TPU v7x, 32 devices: a whole 2x2x4 slice. The times are simulated.
32 devices in a mesh: dp: 16 (over z, x, core), tm: 2 (over y).
Axes of the slice: x: 2, y: 2, z: 4, core: 2. Of those that a mesh axis runs over, the one named last changes fastest.
Arguments:
- src_mel: bfloat16 [2, 128, 640], P('tm', 'dp'), may hold values from -6 to 6
- owner: int32 [2, 128], P('tm', 'dp'), may hold values from 0 to 15, as said below
- dst_pos: int32 [2, 128], P('tm', 'dp'), may hold values from 0 to 7, as said below
- keep: int32 [2, 128], P('tm', 'dp'), may hold values 0 or 1
- cotangent: bfloat16 [16, 1024, 256], P('dp', 'tm'), may hold values from -0.125 to 0.125
- w_pre: bfloat16 [560, 512], replicated, may hold values from -0.25 to 0.25
- b_pre: float32 [512], replicated, may hold values from -3 to 3
- w_ups: bfloat16 [512, 4096], P('tm'), may hold values from -0.1875 to 0.1875
- upsample_bias: float32 [256], replicated, may hold values from -3 to 3
- w_res: bfloat16 [768, 256], replicated, may hold values from -0.21875 to 0.21875
- b_res: float32 [256], replicated, may hold values from -3 to 3
Outputs:
- section_out: bfloat16 [16, 1024, 256], P('dp', 'tm')
- grad_w_pre: float32 [560, 512], replicated
- grad_b_pre: float32 [512], replicated
- grad_w_res: float32 [768, 256], replicated
- grad_b_res: float32 [256], replicated
Inputs may be any that keep to these rules, and one draw needn't show every extreme that they name: Within one tm column, every dp index sends at most one of its segments to each owner, and every owner receives exactly 8 segments. `dst_pos`: the segments received by one owner in one column have positions 0 to 7, each once.
All inputs are finite; a program needn't handle non-finite values. No bound on the sum of `keep` on one device may be relied on, other than what follows from the above.
Results may differ from a plain program's by a relative error of at most 0.009.
The roundings to bfloat16 on the way count: a program that leaves them out, or rounds other values in their place, can miss the bound.
Values may be sent and summed in bfloat16 or wider, within the bound.
No kernel may reach another device: no remote copies, remote signals or barrier semaphores. Data moves between devices by JAX's collectives and lax.ppermute only.
A program may use at most 64 MiB of HBM per device.

v0:
```python
import jax
import jax.numpy as jnp
from jax import lax
from jax.sharding import PartitionSpec as P

KPRE = 7
UPSAMPLE_FACTOR = 8
DILATION_SIZE = 3


def with_halo(block, sides, width):
    for axis, dim in sides:
        count = lax.axis_size(axis)
        forward = [(i, i + 1) for i in range(count - 1)]
        backward = [(target, source) for source, target in forward]
        low = lax.ppermute(
            lax.slice_in_dim(block, block.shape[dim] - width, None, axis=dim), axis, forward
        )
        high = lax.ppermute(lax.slice_in_dim(block, 0, width, axis=dim), axis, backward)
        block = jnp.concatenate([low, block, high], axis=dim)
    return block


def leaky(value):
    return jnp.where(value > 0, value, 0.1 * value)


def negative_slope(value):
    return jnp.where(value > 0, 1.0, 0.1).astype(jnp.float32)


def contract_rows(left, right):
    return lax.dot_general(
        left, right, (((0,), (0,)), ((), ())), preferred_element_type=jnp.float32
    )


def contract_cols(left, right):
    return lax.dot_general(
        left, right, (((1,), (1,)), ((), ())), preferred_element_type=jnp.float32
    )


def local_pass(
    mel_ext,
    gradient_value,
    first_frame0,
    total,
    w_pre,
    b_pre,
    ups_forward,
    ups_backward,
    upsample_bias,
    w_res,
    b_res,
):
    mel_bins = mel_ext.shape[1]
    kpre = w_pre.shape[0] // mel_bins
    edge = kpre // 2 + 1
    frame_count = mel_ext.shape[0] - 2 * edge
    window_width = upsample_bias.shape[0]
    residual_kernel = w_res.shape[0] // window_width
    patches = jnp.concatenate([mel_ext[i : i + frame_count + 2] for i in range(kpre)], axis=1)
    pre = jnp.dot(patches, w_pre, preferred_element_type=jnp.float32) + b_pre
    frame_idx = first_frame0 - 1 + jnp.arange(frame_count + 2, dtype=jnp.int32)
    inside_f = ((frame_idx >= 0) & (frame_idx < total))[:, None]
    act = jnp.where(inside_f, leaky(pre), 0.0).astype(jnp.bfloat16)
    taps = ups_forward(act).reshape(frame_count + 2, 2 * UPSAMPLE_FACTOR, window_width)
    upper_output = taps[1:, :UPSAMPLE_FACTOR] + taps[:-1, UPSAMPLE_FACTOR:]
    sample_count = UPSAMPLE_FACTOR * frame_count
    start_offset = UPSAMPLE_FACTOR // 2 - DILATION_SIZE
    waveform = (
        upper_output.reshape(UPSAMPLE_FACTOR * (frame_count + 1), window_width)[
            start_offset : start_offset + sample_count + 2 * DILATION_SIZE
        ]
        + upsample_bias
    )
    step_index = (
        UPSAMPLE_FACTOR * first_frame0
        - DILATION_SIZE
        + jnp.arange(sample_count + 2 * DILATION_SIZE, dtype=jnp.int32)
    )
    inside_samples = ((step_index >= 0) & (step_index < UPSAMPLE_FACTOR * total))[:, None]
    hidden_state = jnp.where(inside_samples, leaky(waveform), 0.0).astype(jnp.bfloat16)
    column_block = jnp.concatenate(
        [
            hidden_state[kernel_index * DILATION_SIZE : kernel_index * DILATION_SIZE + sample_count]
            for kernel_index in range(residual_kernel)
        ],
        axis=1,
    )
    convolve_fn = jnp.dot(column_block, w_res, preferred_element_type=jnp.float32) + b_res
    output_rows = (waveform[DILATION_SIZE : DILATION_SIZE + sample_count] + convolve_fn).astype(
        jnp.bfloat16
    )
    g_wres = contract_rows(column_block, gradient_value)
    g_bres = jnp.sum(gradient_value.astype(jnp.float32), axis=0)
    backward_pass = contract_cols(gradient_value, w_res)
    hidden_gradient = jnp.zeros((sample_count + 2 * DILATION_SIZE, window_width), jnp.float32)
    for kernel_index in range(residual_kernel):
        hidden_gradient = hidden_gradient + jnp.pad(
            backward_pass[:, kernel_index * window_width : (kernel_index + 1) * window_width],
            (
                (
                    kernel_index * DILATION_SIZE,
                    (residual_kernel - 1 - kernel_index) * DILATION_SIZE,
                ),
                (0, 0),
            ),
        )
    waveform_gradient = jnp.where(
        inside_samples, hidden_gradient * negative_slope(waveform), 0.0
    ) + jnp.pad(gradient_value.astype(jnp.float32), ((DILATION_SIZE, DILATION_SIZE), (0, 0)))
    waveform_gradient = waveform_gradient.astype(jnp.bfloat16)
    d_upper = jnp.pad(waveform_gradient, ((start_offset, start_offset), (0, 0))).reshape(
        frame_count + 1, UPSAMPLE_FACTOR, window_width
    )
    zero_row = jnp.zeros((1, UPSAMPLE_FACTOR, window_width), jnp.bfloat16)
    d_taps = jnp.concatenate(
        [
            jnp.concatenate([zero_row, d_upper], axis=0),
            jnp.concatenate([d_upper, zero_row], axis=0),
        ],
        axis=1,
    )
    d_act = ups_backward(d_taps.reshape(frame_count + 2, 2 * UPSAMPLE_FACTOR * window_width))
    d_pre = jnp.where(inside_f, d_act * negative_slope(pre), 0.0).astype(jnp.bfloat16)
    g_wpre = contract_rows(patches, d_pre)
    g_bpre = jnp.sum(d_pre.astype(jnp.float32), axis=0)
    return (output_rows, (g_wpre, g_bpre, g_wres, g_bres))


def on_device(
    src_mel, owner, dst_pos, keep, cotangent, w_pre, b_pre, w_ups, upsample_bias, w_res, b_res
):
    owners_count = lax.axis_size("dp")
    seg_rows = src_mel[0]
    seg_count = seg_rows.shape[0]
    mel_bins = w_pre.shape[0] // KPRE
    pick = jnp.arange(owners_count, dtype=jnp.int32)[:, None] == owner[0][None, :]
    outgoing = jnp.dot(
        pick.astype(jnp.bfloat16), seg_rows, preferred_element_type=jnp.float32
    ).astype(jnp.bfloat16)
    slot_code = jnp.sum(jnp.where(pick, dst_pos[0][None, :] + 1, 0), axis=1)
    keep_code = jnp.sum(jnp.where(pick, keep[0][None, :], 0), axis=1)
    header = jnp.stack([slot_code, keep_code], axis=1)
    arrived, arrived_header = (
        lax.all_to_all(outgoing, "dp", split_axis=0, concat_axis=0, tiled=True),
        lax.all_to_all(header, "dp", split_axis=0, concat_axis=0, tiled=True),
    )
    place = (arrived_header[:, 0] - 1)[:, None] == jnp.arange(seg_count, dtype=jnp.int32)[None, :]
    mel_segs = contract_rows(place.astype(jnp.bfloat16), arrived).astype(jnp.bfloat16)
    keep_segs = jnp.sum(jnp.where(place, arrived_header[:, 1][:, None], 0), axis=0)
    mel = mel_segs.reshape(seg_count * (mel_segs.shape[1] // mel_bins), mel_bins)
    frame_count = mel.shape[0]
    mel_ext = with_halo(mel, (("tm", 0),), KPRE // 2 + 1)
    first_frame0 = lax.axis_index("tm") * frame_count
    total = lax.axis_size("tm") * frame_count
    cot = cotangent[0]
    marks = jnp.repeat(keep_segs, cot.shape[0] // seg_count)
    gradient_value = jnp.where(marks[:, None] > 0, cot, jnp.zeros_like(cot))
    whole = lax.all_gather(w_ups, "tm", axis=0, tiled=True)

    def ups_forward(act):
        return jnp.dot(act, whole, preferred_element_type=jnp.float32)

    def ups_backward(d_taps):
        return contract_cols(d_taps, whole)

    output_rows, grads = local_pass(
        mel_ext,
        gradient_value,
        first_frame0,
        total,
        w_pre,
        b_pre,
        ups_forward,
        ups_backward,
        upsample_bias,
        w_res,
        b_res,
    )
    within = (
        lax.psum(grads[0].astype(jnp.bfloat16), "tm").astype(jnp.float32),
        lax.psum(grads[1].astype(jnp.bfloat16), "tm").astype(jnp.float32),
        lax.psum(grads[2].astype(jnp.bfloat16), "tm").astype(jnp.float32),
        lax.psum(grads[3].astype(jnp.bfloat16), "tm").astype(jnp.float32),
    )
    summed = lax.psum((within[0], within[1], within[2], within[3]), "dp")
    return (output_rows[None], summed[0], summed[1], summed[2], summed[3])


def solution(mesh):
    in_specs = (
        P("tm", "dp", None),
        P("tm", "dp"),
        P("tm", "dp"),
        P("tm", "dp"),
        P("dp", "tm", None),
        P(),
        P(),
        P("tm", None),
        P(),
        P(),
        P(),
    )
    out_specs = (P("dp", "tm", None), P(), P(), P(), P())
    return jax.shard_map(
        on_device, mesh=mesh, in_specs=in_specs, out_specs=out_specs, check_vma=False
    )
```

profile of v0, /device:TPU:0, one launch (start us, length us, event | category | flops | bytes accessed | tf_op | source)
XLA Modules:
  0.0 200.8 jit_solution(5339003557283982641)
XLA Ops:
  7.3 0.7 all-gather.2.cloned.1.call-update
  8.1 0.7 copy.22
  8.8 7.4 %all-to-all-start = ((s32[16,1,2]{2,1,0:T(1,128)}), s32[16,1,2]{2,1,0:T(1,128)S(1)}, u32[]{:S(2)}, u32[]{:S(2)}) async-start(s32[16,1,2]{2,1,0:T(1,128)} %copy.22), calls=%async_computation | async-start | bytes 16384 | tf_op jit(solution)/shard_map/all_to_all | solution.py:149
  16.2 0.3 fusion.5
  16.5 0.5 broadcast.83
  17.0 0.7 reduce.2
  17.6 0.7 reshape.60
  18.3 4.2 %all-to-all-done = s32[16,1,2]{2,1,0:T(1,128)S(1)} async-done(((s32[16,1,2]{2,1,0:T(1,128)}), s32[16,1,2]{2,1,0:T(1,128)S(1)}, u32[]{:S(2)}, u32[]{:S(2)}) %all-to-all-start) | async-done | bytes 160 | tf_op jit(solution)/shard_map/all_to_all | solution.py:149
  22.5 3.5 %all-to-all-start.1 = ((bf16[16,2,320]{2,1,0:T(2,128)(2,1)}), bf16[16,2,320]{2,1,0:T(2,128)(2,1)S(1)}, u32[]{:S(2)}, u32[]{:S(2)}) async-start(bf16[16,2,320]{2,1,0:T(2,128)(2,1)} %reshape.60), calls=%async_computation.1 | async-start | bytes 49152 | tf_op jit(solution)/shard_map/all_to_all | solution.py:148
  26.4 0.2 fusion.37
  26.6 0.4 fusion.43
  27.2 5.4 %all-to-all-done.1 = bf16[16,2,320]{2,1,0:T(2,128)(2,1)S(1)} async-done(((bf16[16,2,320]{2,1,0:T(2,128)(2,1)}), bf16[16,2,320]{2,1,0:T(2,128)(2,1)S(1)}, u32[]{:S(2)}, u32[]{:S(2)}) %all-to-all-start.1) | async-done | bytes 20512 | tf_op jit(solution)/shard_map/all_to_all | solution.py:148
  32.9 1.3 collective-permute-start.1
  34.2 4.5 %collective-permute-start = (bf16[4,80]{1,0:T(4,128)(2,1)S(1)}, bf16[4,80]{1,0:T(4,128)(2,1)S(1)}, u32[]{:S(2)}, u32[]{:S(2)}) collective-permute-start(bf16[4,80]{1,0:T(4,128)(2,1)S(1)} %get-tuple-element.33), channel_id=1, source_target_pairs={{0,1},{2,3},{4,5},{6,7},{8,9},{10,11},{12,13},{14,15},{16,17},{18,... | collective-permute-start | bytes 1928 | tf_op jit(solution)/shard_map/ppermute | solution.py:16
  38.8 1.3 collective-permute-done
  40.1 0.1 concatenate.31
  40.2 0.2 convolution_add_fusion.1
  40.5 28.7 %all-gather.2.cloned.1.call-done = bf16[512,4096]{1,0:T(8,128)(2,1)} async-done(((bf16[256,4096]{1,0:T(8,128)(2,1)}), bf16[512,4096]{1,0:T(8,128)(2,1)}) %all-gather.2.cloned.1.call-update) | async-done | bytes 4194320 | tf_op jit(solution)/shard_map/all_gather | solution.py:162
  69.1 3.1 %fusion.18 = f32[66,4096]{1,0:T(8,128)S(1)} fusion(bf16[512,4096]{1,0:T(8,128)(2,1)} %all-gather.2.cloned.1.call-done, f32[66,512]{1,0:T(8,128)S(1)} %convolution_add_fusion.1, pred[66]{0:T(512)(128)(4,1)S(1)} %compare_and_fusion), kind=kOutput, calls=%fused_computation.36 | convolution fusion | flops 276993024 | bytes 5410882 | tf_op jit(solution)/shard_map/dot_general | solution.py:165
  72.2 0.4 copy.26
  72.7 0.5 copy-done.6
  73.3 0.3 fusion.12
  73.6 0.1 fusion.14
  74.0 0.2 copy.27
  74.3 1.7 copy-done.1
  75.9 1.4 fusion.42
  77.3 1.1 convolution_convert_fusion
  78.5 1.2 convolution_convert_fusion.1
  79.7 4.9 %all-reduce.8 = (bf16[512]{0:T(512)(128)(2,1)S(1)}, bf16[256]{0:T(256)(128)(2,1)S(1)}) all-reduce(bf16[512]{0:T(512)(128)(2,1)S(1)} %get-tuple-element.36, bf16[256]{0:T(256)(128)(2,1)S(1)} %get-tuple-element.15), channel_id=1, replica_groups=mesh['dp'=16,'tm'=2] {'tm'}, use_global_device_ids=true, to_apply=%region_6.7 | all-reduce | flops 768 | bytes 3072 | tf_op jit(solution)/shard_map/psum | solution.py:185
  84.6 1.1 fusion.2
  85.7 32.6 %all-reduce.13.cloned.1.call-done = (bf16[560,512]{1,0:T(8,128)(2,1)}, bf16[768,256]{1,0:T(8,128)(2,1)}) async-done(((bf16[560,512]{1,0:T(8,128)(2,1)}, bf16[768,256]{1,0:T(8,128)(2,1)}), (bf16[560,512]{1,0:T(8,128)(2,1)}, bf16[768,256]{1,0:T(8,128)(2,1)})) %all-reduce.13.cloned.1.call-update) | async-done | bytes 966672 | tf_op jit(solution)/shard_map/psum | solution.py:184
  118.3 75.7 %all-reduce.14 = (f32[560,512]{1,0:T(8,128)}, f32[512]{0:T(512)}, f32[768,256]{1,0:T(8,128)}, f32[256]{0:T(256)}) all-reduce(bf16[560,512]{1,0:T(8,128)(2,1)} %get-tuple-element.13, bf16[512]{0:T(512)(128)(2,1)S(1)} %get-tuple-element.11, bf16[768,256]{1,0:T(8,128)(2,1)} %get-tuple-element.14, ...), channel_id=1, replica_groups=mesh['dp'=16,'tm'=2] {'dp'}, use_global_device_ids=true, to_apply=%region_4.5 | all-reduce | flops 484096 | bytes 2904576 | tf_op jit(solution)/shard_map/psum | solution.py:189
  (52 shorter events, 1.5 us)
Async XLA Ops:
  7.2 33.0 %copy-start = (bf16[560,512]{1,0:T(8,128)(2,1)S(1)}, bf16[560,512]{1,0:T(8,128)(2,1)}, u32[]{:S(2)}) copy-start(bf16[560,512]{1,0:T(8,128)(2,1)} %param.16) | copy-start | bytes 1720324
  7.2 0.8 copy-start.11
  7.2 0.8 copy-start.8
  7.2 0.8 copy-start.7
  7.2 9.0 %copy-start.9 = (bf16[1,8,640]{2,1,0:T(8,128)(2,1)S(1)}, bf16[1,8,640]{2,1,0:T(8,128)(2,1)}, u32[]{:S(2)}) copy-start(bf16[1,8,640]{2,1,0:T(8,128)(2,1)} %param.11) | copy-start | bytes 30724
  7.2 19.2 %copy-start.4 = (bf16[1,512,256]{2,1,0:T(8,128)(2,1)S(1)}, bf16[1,512,256]{2,1,0:T(8,128)(2,1)}, u32[]{:S(2)}) copy-start(bf16[1,512,256]{2,1,0:T(8,128)(2,1)} %param.15) | copy-start | bytes 786436
  7.2 19.4 %copy-start.2 = (bf16[768,256]{1,0:T(8,128)(2,1)S(1)}, bf16[768,256]{1,0:T(8,128)(2,1)}, u32[]{:S(2)}) copy-start(bf16[768,256]{1,0:T(8,128)(2,1)} %param.20) | copy-start | bytes 1179652
  7.2 61.9 %all-gather.2.cloned.1.call-start = ((), (), s32[]{:S(2)}) async-start(), calls=%async_computation.2 | async-start | bytes 6291456 | tf_op jit(solution)/shard_map/all_gather | solution.py:162
  8.8 13.7 %all-to-all-start = ((s32[16,1,2]{2,1,0:T(1,128)}), s32[16,1,2]{2,1,0:T(1,128)S(1)}, u32[]{:S(2)}, u32[]{:S(2)}) async-start(s32[16,1,2]{2,1,0:T(1,128)} %copy.22), calls=%async_computation | async-start | bytes 16384 | tf_op jit(solution)/shard_map/all_to_all | solution.py:149
  22.5 10.0 %all-to-all-start.1 = ((bf16[16,2,320]{2,1,0:T(2,128)(2,1)}), bf16[16,2,320]{2,1,0:T(2,128)(2,1)S(1)}, u32[]{:S(2)}, u32[]{:S(2)}) async-start(bf16[16,2,320]{2,1,0:T(2,128)(2,1)} %reshape.60), calls=%async_computation.1 | async-start | bytes 49152 | tf_op jit(solution)/shard_map/all_to_all | solution.py:148
  26.0 92.3 %all-reduce.13.cloned.1.call-start = ((), (), s32[]{:S(2)}) async-start(), calls=%async_computation.3 | async-start | bytes 1933312 | tf_op jit(solution)/shard_map/psum | solution.py:184
  27.0 13.2 %copy-start.5 = (f32[512]{0:T(512)S(1)}, f32[512]{0:T(512)}, u32[]{:S(2)}) copy-start(f32[512]{0:T(512)} %param.17) | copy-start | bytes 6148
  32.9 5.9 %collective-permute-start.1 = (bf16[4,80]{1,0:T(4,128)(2,1)S(1)}, bf16[4,80]{1,0:T(4,128)(2,1)S(1)}, u32[]{:S(2)}, u32[]{:S(2)}) collective-permute-start(bf16[4,80]{1,0:T(4,128)(2,1)S(1)} %get-tuple-element.32), channel_id=1, source_target_pairs={{1,0},{3,2},{5,4},{7,6},{9,8},{11,10},{13,12},{15,14},{17,16},{19,... | collective-permute-start | bytes 1928 | tf_op jit(solution)/shard_map/ppermute | solution.py:19
  34.2 5.8 %collective-permute-start = (bf16[4,80]{1,0:T(4,128)(2,1)S(1)}, bf16[4,80]{1,0:T(4,128)(2,1)S(1)}, u32[]{:S(2)}, u32[]{:S(2)}) collective-permute-start(bf16[4,80]{1,0:T(4,128)(2,1)S(1)} %get-tuple-element.33), channel_id=1, source_target_pairs={{0,1},{2,3},{4,5},{6,7},{8,9},{10,11},{12,13},{14,15},{16,17},{18,... | collective-permute-start | bytes 1928 | tf_op jit(solution)/shard_map/ppermute | solution.py:16
  72.6 0.7 copy-start.6
  73.7 2.2 %copy-start.1 = (bf16[512,4096]{1,0:T(8,128)(2,1)S(1)}, bf16[512,4096]{1,0:T(8,128)(2,1)}, u32[]{:S(2)}) copy-start(bf16[512,4096]{1,0:T(8,128)(2,1)} %all-gather.2.cloned.1.call-done) | copy-start | bytes 12582916
  78.5 6.1 %copy-start.3 = (bf16[768,256]{1,0:T(8,128)(2,1)S(1)}, bf16[768,256]{1,0:T(8,128)(2,1)}, u32[]{:S(2)}) copy-start(bf16[768,256]{1,0:T(8,128)(2,1)} %param.20) | copy-start | bytes 1179652
  78.5 6.1 %copy-start.10 = (f32[256]{0:T(256)S(1)}, f32[256]{0:T(256)}, u32[]{:S(2)}) copy-start(f32[256]{0:T(256)} %param.21) | copy-start | bytes 3076
Sparse Core Ops, SparseCore 0:
  9.6 59.4 all-gather.1
  79.8 38.4 all-reduce.12
where the time goes:
time: 201 us
  blocking collectives  80.6 us (40%)
  waiting for transfers between devices  72.7 us (36%)
  starting transfers between devices  16.8 us (8%)
  between operations  14.4 us (7%)
  matrix products  8.92 us (4%)
  local copies, waits for them, and re-layouts  5.73 us (3%)
    psum x1, blocking collectives, on_device(): summed = lax.psum((within[0], within[1], within[2], within[3]), 'dp')  75.7 us
    psum x1, waiting for transfers between devices, on_device(): lax.psum(grads[0].astype(jnp.bfloat16), 'tm').astype(jnp.float32)  32.6 us
    all_gather x1, waiting for transfers between devices, on_device(): whole = lax.all_gather(w_ups, 'tm', axis=0, tiled=True)  28.7 us
    all_to_all x1, starting transfers between devices, on_device(): lax.all_to_all(header, 'dp', split_axis=0, concat_axis=0, tiled=True)  7.36 us
    all_to_all x1, waiting for transfers between devices, on_device(): lax.all_to_all(outgoing, 'dp', split_axis=0, concat_axis=0, tiled=True)  5.38 us
    psum x1, blocking collectives, on_device(): lax.psum(grads[1].astype(jnp.bfloat16), 'tm').astype(jnp.float32)  4.94 us
    ppermute x1, starting transfers between devices, with_halo(): lax.ppermute(lax.slice_in_dim(block, block.shape[dim] - width, None, axis...  4.54 us
    all_to_all x1, waiting for transfers between devices, on_device(): lax.all_to_all(header, 'dp', split_axis=0, concat_axis=0, tiled=True)  4.15 us
  transfers between devices with their start and end apart: 6, of which 5 were waited for; matrix products, arithmetic and copies ran while one was open for 3% of the time, Pallas kernels for 0%

commit v1 on v0

--- a/solution.py
+++ b/solution.py
@@ -138,19 +138,20 @@
     seg_count = seg_rows.shape[0]
     mel_bins = w_pre.shape[0] // KPRE
     pick = jnp.arange(owners_count, dtype=jnp.int32)[:, None] == owner[0][None, :]
+    seg_width = seg_rows.shape[1]
+    header = jnp.stack([dst_pos[0] + 1, keep[0]], axis=1).astype(jnp.bfloat16)
+    seg_ext = jnp.concatenate([seg_rows, header], axis=1)
     outgoing = jnp.dot(
-        pick.astype(jnp.bfloat16), seg_rows, preferred_element_type=jnp.float32
+        pick.astype(jnp.bfloat16), seg_ext, preferred_element_type=jnp.float32
     ).astype(jnp.bfloat16)
-    slot_code = jnp.sum(jnp.where(pick, dst_pos[0][None, :] + 1, 0), axis=1)
-    keep_code = jnp.sum(jnp.where(pick, keep[0][None, :], 0), axis=1)
-    header = jnp.stack([slot_code, keep_code], axis=1)
-    arrived, arrived_header = (
-        lax.all_to_all(outgoing, "dp", split_axis=0, concat_axis=0, tiled=True),
-        lax.all_to_all(header, "dp", split_axis=0, concat_axis=0, tiled=True),
-    )
-    place = (arrived_header[:, 0] - 1)[:, None] == jnp.arange(seg_count, dtype=jnp.int32)[None, :]
-    mel_segs = contract_rows(place.astype(jnp.bfloat16), arrived).astype(jnp.bfloat16)
-    keep_segs = jnp.sum(jnp.where(place, arrived_header[:, 1][:, None], 0), axis=0)
+    arrived = lax.all_to_all(outgoing, "dp", split_axis=0, concat_axis=0, tiled=True)
+    slot_code = arrived[:, seg_width].astype(jnp.int32)
+    keep_code = arrived[:, seg_width + 1].astype(jnp.int32)
+    place = (slot_code - 1)[:, None] == jnp.arange(seg_count, dtype=jnp.int32)[None, :]
+    mel_segs = contract_rows(place.astype(jnp.bfloat16), arrived[:, :seg_width]).astype(
+        jnp.bfloat16
+    )
+    keep_segs = jnp.sum(jnp.where(place, keep_code[:, None], 0), axis=0)
     mel = mel_segs.reshape(seg_count * (mel_segs.shape[1] // mel_bins), mel_bins)
     frame_count = mel.shape[0]
     mel_ext = with_halo(mel, (("tm", 0),), KPRE // 2 + 1)
@@ -180,13 +181,7 @@
         w_res,
         b_res,
     )
-    within = (
-        lax.psum(grads[0].astype(jnp.bfloat16), "tm").astype(jnp.float32),
-        lax.psum(grads[1].astype(jnp.bfloat16), "tm").astype(jnp.float32),
-        lax.psum(grads[2].astype(jnp.bfloat16), "tm").astype(jnp.float32),
-        lax.psum(grads[3].astype(jnp.bfloat16), "tm").astype(jnp.float32),
-    )
-    summed = lax.psum((within[0], within[1], within[2], within[3]), "dp")
+    summed = lax.psum(grads, ("dp", "tm"))
     return (output_rows[None], summed[0], summed[1], summed[2], summed[3])
 
 

time: 201 us -> 224 us (1.11)
  waiting for transfers between devices: 72.7 us -> 137 us
  blocking collectives: 80.6 us -> 39.7 us
  starting transfers between devices: 16.8 us -> 13.3 us
  local copies, waits for them, and re-layouts: 5.73 us -> 8.51 us
    psum x1, waiting for transfers between devices: 32.6 us -> 92.8 us  [on_device(): summed = lax.psum(grads, ('dp', 'tm'))]
    psum x2 -> x1, blocking collectives: 80.6 us -> 39.7 us  [on_device(): summed = lax.psum(grads, ('dp', 'tm'))]
    all_to_all x1 -> x0, starting transfers between devices: 7.36 us -> none  [on_device(): lax.all_to_all(header, 'dp', split_axis=0, concat_axis=0, tiled=True)]
    all_gather x1, waiting for transfers between devices: 28.7 us -> 35.7 us  [on_device(): whole = lax.all_gather(w_ups, 'tm', axis=0, tiled=True)]
    all_to_all x1 -> x0, waiting for transfers between devices: 4.15 us -> none  [on_device(): lax.all_to_all(header, 'dp', split_axis=0, concat_axis=0, tiled=True)]
    all_to_all x1, starting transfers between devices: 3.5 us -> 7.36 us  [on_device(): lax.all_to_all(outgoing, 'dp', split_axis=0, concat_axis=0, tiled=True)]
    unnamed x30 -> x43, local copies, waits for them, and re-layouts: 3.66 us -> 7 us
  transfers between devices with their start and end apart: 6 -> 5, of which waited for: 5 -> 4; matrix products, arithmetic and copies ran while one was open for 3% -> 2% of each run, Pallas kernels for 0% -> 0%
where the time goes in v1:
time: 224 us
  waiting for transfers between devices  137 us (61%)
  blocking collectives  39.7 us (18%)
  between operations  14.4 us (6%)
  starting transfers between devices  13.3 us (6%)
  matrix products  9.26 us (4%)
  local copies, waits for them, and re-layouts  8.51 us (4%)
    psum x1, waiting for transfers between devices, on_device(): summed = lax.psum(grads, ('dp', 'tm'))  92.8 us
    psum x1, blocking collectives, on_device(): summed = lax.psum(grads, ('dp', 'tm'))  39.7 us
    all_gather x1, waiting for transfers between devices, on_device(): whole = lax.all_gather(w_ups, 'tm', axis=0, tiled=True)  35.7 us
    all_to_all x1, starting transfers between devices, on_device(): lax.all_to_all(outgoing, 'dp', split_axis=0, concat_axis=0, tiled=True)  7.36 us
    unnamed x43, local copies, waits for them, and re-layouts  7 us
    all_to_all x1, waiting for transfers between devices, on_device(): lax.all_to_all(outgoing, 'dp', split_axis=0, concat_axis=0, tiled=True)  6.48 us
    ppermute x1, starting transfers between devices, with_halo(): lax.ppermute(lax.slice_in_dim(block, block.shape[dim] - width, None, axis...  4.54 us
  transfers between devices with their start and end apart: 5, of which 4 were waited for; matrix products, arithmetic and copies ran while one was open for 2% of the time, Pallas kernels for 0%

profile of v1, /device:TPU:0, one launch (start us, length us, event | category | flops | bytes accessed | tf_op | source)
XLA Modules:
  0.0 224.1 jit_solution(13383541488804429791)
XLA Ops:
  7.3 0.7 all-gather.2.cloned.1.call-update
  8.2 0.2 fusion.5
  8.4 0.5 broadcast.94
  8.9 0.7 reduce.4
  9.6 0.7 reshape.74
  10.3 7.4 %all-to-all-start = ((bf16[16,2,321]{2,1,0:T(2,128)(2,1)}), bf16[16,2,321]{2,1,0:T(2,128)(2,1)S(1)}, u32[]{:S(2)}, u32[]{:S(2)}) async-start(bf16[16,2,321]{2,1,0:T(2,128)(2,1)} %reshape.74), calls=%async_computation | async-start | bytes 49152 | tf_op jit(solution)/shard_map/all_to_all | solution.py:147
  17.7 6.5 %all-to-all-done = bf16[16,2,321]{2,1,0:T(2,128)(2,1)S(1)} async-done(((bf16[16,2,321]{2,1,0:T(2,128)(2,1)}), bf16[16,2,321]{2,1,0:T(2,128)(2,1)S(1)}, u32[]{:S(2)}, u32[]{:S(2)}) %all-to-all-start) | async-done | bytes 20576 | tf_op jit(solution)/shard_map/all_to_all | solution.py:147
  24.3 0.2 convert_reduce_fusion.2
  24.7 1.3 collective-permute-start.1
  26.3 0.1 fusion.42
  26.5 0.4 fusion.43
  27.1 4.5 %collective-permute-start = (bf16[4,80]{1,0:T(4,128)(2,1)S(1)}, bf16[4,80]{1,0:T(4,128)(2,1)S(1)}, u32[]{:S(2)}, u32[]{:S(2)}) collective-permute-start(bf16[4,80]{1,0:T(4,128)(2,1)S(1)} %get-tuple-element.27), channel_id=1, source_target_pairs={{0,1},{2,3},{4,5},{6,7},{8,9},{10,11},{12,13},{14,15},{16,17},{18,... | collective-permute-start | bytes 1928 | tf_op jit(solution)/shard_map/ppermute | solution.py:16
  31.6 1.3 collective-permute-done
  33.0 0.1 concatenate.36
  33.1 0.2 convolution_add_fusion.1
  33.4 35.7 %all-gather.2.cloned.1.call-done = bf16[512,4096]{1,0:T(8,128)(2,1)} async-done(((bf16[256,4096]{1,0:T(8,128)(2,1)}), bf16[512,4096]{1,0:T(8,128)(2,1)}) %all-gather.2.cloned.1.call-update) | async-done | bytes 4194320 | tf_op jit(solution)/shard_map/all_gather | solution.py:163
  69.1 3.1 %fusion.19 = f32[66,4096]{1,0:T(8,128)S(1)} fusion(bf16[512,4096]{1,0:T(8,128)(2,1)} %all-gather.2.cloned.1.call-done, f32[66,512]{1,0:T(8,128)S(1)} %convolution_add_fusion.1, pred[66]{0:T(512)(128)(4,1)S(1)} %compare_and_fusion), kind=kOutput, calls=%fused_computation.37 | convolution fusion | flops 276993024 | bytes 5410882 | tf_op jit(solution)/shard_map/dot_general | solution.py:166
  72.2 0.4 copy.30
  72.8 0.5 copy-done.12
  73.3 0.3 fusion.12
  73.6 0.1 fusion.14
  74.1 0.2 copy.31
  74.3 1.7 copy-done.1
  76.0 1.4 convert_reduce_fusion
  77.4 1.3 fusion.48
  78.7 1.4 fusion.16
  80.2 0.2 convert_reduce_fusion.1
  80.3 39.7 %all-reduce.7 = (f32[512]{0:T(512)}, f32[256]{0:T(256)}) all-reduce(f32[512]{0:T(512)S(1)} %get-tuple-element.28, f32[256]{0:T(256)S(1)} %convert_reduce_fusion.1), channel_id=1, replica_groups=mesh['dp'=16,'tm'=2] {'dp','tm'}, use_global_device_ids=true, to_apply=%region_3.4 | all-reduce | flops 768 | bytes 6144 | tf_op jit(solution)/shard_map/psum | solution.py:184
  120.0 1.1 fusion.2
  121.1 92.8 %all-reduce.11.cloned.1.call-done = (f32[560,512]{1,0:T(8,128)}, f32[768,256]{1,0:T(8,128)}) async-done(((f32[560,512]{1,0:T(8,128)}, f32[768,256]{1,0:T(8,128)}), (f32[560,512]{1,0:T(8,128)}, f32[768,256]{1,0:T(8,128)})) %all-reduce.11.cloned.1.call-update) | async-done | bytes 1933328 | tf_op jit(solution)/shard_map/psum | solution.py:184
  213.9 2.4 %copy.38 = f32[560,512]{1,0:T(8,128)} copy(f32[560,512]{1,0:T(8,128)} %get-tuple-element.31) | data formatting | bytes 2293760
  216.3 0.9 copy.39
  (62 shorter events, 1.6 us)
Async XLA Ops:
  7.2 25.9 %copy-start = (bf16[560,512]{1,0:T(8,128)(2,1)S(1)}, bf16[560,512]{1,0:T(8,128)(2,1)}, u32[]{:S(2)}) copy-start(bf16[560,512]{1,0:T(8,128)(2,1)} %param.16) | copy-start | bytes 1720324
  7.2 0.8 copy-start.15
  7.2 0.9 copy-start.16
  7.2 1.0 copy-start.13
  7.2 1.0 copy-start.10
  7.2 19.1 %copy-start.2 = (bf16[1,512,256]{2,1,0:T(8,128)(2,1)S(1)}, bf16[1,512,256]{2,1,0:T(8,128)(2,1)}, u32[]{:S(2)}) copy-start(bf16[1,512,256]{2,1,0:T(8,128)(2,1)} %param.15) | copy-start | bytes 786436
  7.2 19.3 %copy-start.8 = (bf16[768,256]{1,0:T(8,128)(2,1)S(1)}, bf16[768,256]{1,0:T(8,128)(2,1)}, u32[]{:S(2)}) copy-start(bf16[768,256]{1,0:T(8,128)(2,1)} %param.20) | copy-start | bytes 1179652
  7.2 61.9 %all-gather.2.cloned.1.call-start = ((), (), s32[]{:S(2)}) async-start(), calls=%async_computation.1 | async-start | bytes 6291456 | tf_op jit(solution)/shard_map/all_gather | solution.py:163
  10.3 13.9 %all-to-all-start = ((bf16[16,2,321]{2,1,0:T(2,128)(2,1)}), bf16[16,2,321]{2,1,0:T(2,128)(2,1)S(1)}, u32[]{:S(2)}, u32[]{:S(2)}) async-start(bf16[16,2,321]{2,1,0:T(2,128)(2,1)} %reshape.74), calls=%async_computation | async-start | bytes 49152 | tf_op jit(solution)/shard_map/all_to_all | solution.py:147
  17.6 196.3 %all-reduce.11.cloned.1.call-start = ((), (), s32[]{:S(2)}) async-start(), calls=%async_computation.2 | async-start | bytes 3866624 | tf_op jit(solution)/shard_map/psum | solution.py:184
  24.7 6.9 %collective-permute-start.1 = (bf16[4,80]{1,0:T(4,128)(2,1)S(1)}, bf16[4,80]{1,0:T(4,128)(2,1)S(1)}, u32[]{:S(2)}, u32[]{:S(2)}) collective-permute-start(bf16[4,80]{1,0:T(4,128)(2,1)S(1)} %get-tuple-element.26), channel_id=1, source_target_pairs={{1,0},{3,2},{5,4},{7,6},{9,8},{11,10},{13,12},{15,14},{17,16},{19,... | collective-permute-start | bytes 1928 | tf_op jit(solution)/shard_map/ppermute | solution.py:19
  26.9 6.2 %copy-start.11 = (f32[512]{0:T(512)S(1)}, f32[512]{0:T(512)}, u32[]{:S(2)}) copy-start(f32[512]{0:T(512)} %param.17) | copy-start | bytes 6148
  27.1 5.8 %collective-permute-start = (bf16[4,80]{1,0:T(4,128)(2,1)S(1)}, bf16[4,80]{1,0:T(4,128)(2,1)S(1)}, u32[]{:S(2)}, u32[]{:S(2)}) collective-permute-start(bf16[4,80]{1,0:T(4,128)(2,1)S(1)} %get-tuple-element.27), channel_id=1, source_target_pairs={{0,1},{2,3},{4,5},{6,7},{8,9},{10,11},{12,13},{14,15},{16,17},{18,... | collective-permute-start | bytes 1928 | tf_op jit(solution)/shard_map/ppermute | solution.py:16
  33.1 39.1 %copy-start.5 = (bf16[66,560]{1,0:T(8,128)(2,1)}, bf16[66,560]{1,0:T(8,128)(2,1)S(1)}, u32[]{:S(2)}) copy-start(bf16[66,560]{1,0:T(8,128)(2,1)S(1)} %concatenate.36) | copy-start | bytes 221764
  33.4 38.8 %copy-start.3 = (f32[66,512]{1,0:T(8,128)}, f32[66,512]{1,0:T(8,128)S(1)}, u32[]{:S(2)}) copy-start(f32[66,512]{1,0:T(8,128)S(1)} %convolution_add_fusion.1) | copy-start | bytes 405508
  72.6 0.7 copy-start.12
  73.8 2.2 copy-start.1
  74.0 2.0 copy-start.4
  76.0 1.4 copy-start.6
  80.1 39.9 %copy-start.9 = (bf16[768,256]{1,0:T(8,128)(2,1)S(1)}, bf16[768,256]{1,0:T(8,128)(2,1)}, u32[]{:S(2)}) copy-start(bf16[768,256]{1,0:T(8,128)(2,1)} %param.20) | copy-start | bytes 1179652
  80.1 39.9 %copy-start.14 = (f32[256]{0:T(256)S(1)}, f32[256]{0:T(256)}, u32[]{:S(2)}) copy-start(f32[256]{0:T(256)} %param.21) | copy-start | bytes 3076
  213.9 2.4 %copy-start.7 = (f32[768,256]{1,0:T(8,128)S(1)}, f32[768,256]{1,0:T(8,128)}, u32[]{:S(2)}) copy-start(f32[768,256]{1,0:T(8,128)} %get-tuple-element.33) | copy-start | bytes 2359300
Sparse Core Ops, SparseCore 0:
  9.6 59.4 all-gather.1
  80.3 133.6 all-reduce.10

commit v2 on v1

--- a/solution.py
+++ b/solution.py
@@ -130,6 +130,39 @@
     return (output_rows, (g_wpre, g_bpre, g_wres, g_bres))
 
 
+def butterfly_psum(parts):
+    dp_size = lax.axis_size("dp")
+    tm_size = lax.axis_size("tm")
+    steps = [("dp", 1)]
+    steps += [("tm", 1 << k) for k in range(tm_size.bit_length() - 1)]
+    steps += [("dp", 1 << k) for k in range(1, dp_size.bit_length() - 1)]
+    flat = jnp.concatenate([p.reshape(-1) for p in parts])
+    unit = 8 * 128 * dp_size * tm_size
+    padded = -(-flat.shape[0] // unit) * unit
+    x = jnp.pad(flat, (0, padded - flat.shape[0])).reshape(padded // 128, 128)
+    for axis, bit in steps:
+        half = x.shape[0] // 2
+        upper = (lax.axis_index(axis) // bit) % 2
+        send = lax.dynamic_slice_in_dim(x, (1 - upper) * half, half)
+        keep = lax.dynamic_slice_in_dim(x, upper * half, half)
+        perm = [(i, i ^ bit) for i in range(lax.axis_size(axis))]
+        x = keep + lax.ppermute(send, axis, perm)
+    for axis, bit in reversed(steps):
+        rows = x.shape[0]
+        upper = (lax.axis_index(axis) // bit) % 2
+        perm = [(i, i ^ bit) for i in range(lax.axis_size(axis))]
+        recv = lax.ppermute(x, axis, perm)
+        both = jnp.zeros((2 * rows, 128), x.dtype)
+        both = lax.dynamic_update_slice_in_dim(both, x, upper * rows, 0)
+        x = lax.dynamic_update_slice_in_dim(both, recv, (1 - upper) * rows, 0)
+    flat = x.reshape(-1)
+    out, at = [], 0
+    for p in parts:
+        out.append(flat[at : at + p.size].reshape(p.shape))
+        at += p.size
+    return tuple(out)
+
+
 def on_device(
     src_mel, owner, dst_pos, keep, cotangent, w_pre, b_pre, w_ups, upsample_bias, w_res, b_res
 ):
@@ -181,7 +214,7 @@
         w_res,
         b_res,
     )
-    summed = lax.psum(grads, ("dp", "tm"))
+    summed = butterfly_psum(grads)
     return (output_rows[None], summed[0], summed[1], summed[2], summed[3])
 
 

time: 224 us -> 155 us (0.69)
  waiting for transfers between devices: 137 us -> 91.1 us
  blocking collectives: 39.7 us -> 0 us
  starting transfers between devices: 13.3 us -> 27.3 us
  local copies, waits for them, and re-layouts: 8.51 us -> 11 us
    psum x1 -> x0, waiting for transfers between devices: 92.8 us -> none  [on_device(): summed = lax.psum(grads, ('dp', 'tm'))]
    ppermute x0 -> x10, waiting for transfers between devices: none -> 47 us  [the longest x5 27.7 us: butterfly_psum(): x = keep + lax.ppermute(send, axis, perm)]
    psum x1 -> x0, blocking collectives: 39.7 us -> none  [on_device(): summed = lax.psum(grads, ('dp', 'tm'))]
    ppermute x0 -> x10, starting transfers between devices: none -> 14.1 us  [the longest x5 7.99 us: butterfly_psum(): recv = lax.ppermute(x, axis, perm)]
    reshape x0 -> x2, local copies, waits for them, and re-layouts: none -> 2.27 us  [butterfly_psum(): out.append(flat[at:at + p.size].reshape(p.shape))]
    unnamed x43 -> x49, local copies, waits for them, and re-layouts: 7 us -> 5.24 us
  transfers between devices with their start and end apart: 5 -> 14, of which waited for: 4 -> 13; matrix products, arithmetic and copies ran while one was open for 2% -> 4% of each run, Pallas kernels for 0% -> 0%
where the time goes in v2:
time: 155 us
  waiting for transfers between devices  91.1 us (59%)
  starting transfers between devices  27.3 us (18%)
  between operations  14.8 us (10%)
  local copies, waits for them, and re-layouts  11 us (7%)
  matrix products  7.37 us (5%)
  other arithmetic  3.41 us (2%)
    all_gather x1, waiting for transfers between devices, on_device(): whole = lax.all_gather(w_ups, 'tm', axis=0, tiled=True)  35.6 us
    ppermute x5, waiting for transfers between devices, butterfly_psum(): x = keep + lax.ppermute(send, axis, perm)  27.7 us
    ppermute x5, waiting for transfers between devices, butterfly_psum(): recv = lax.ppermute(x, axis, perm)  19.4 us
    ppermute x5, starting transfers between devices, butterfly_psum(): recv = lax.ppermute(x, axis, perm)  7.99 us
    all_to_all x1, starting transfers between devices, on_device(): lax.all_to_all(outgoing, 'dp', split_axis=0, concat_axis=0, tiled=True)  7.36 us
    all_to_all x1, waiting for transfers between devices, on_device(): lax.all_to_all(outgoing, 'dp', split_axis=0, concat_axis=0, tiled=True)  6.51 us
    ppermute x5, starting transfers between devices, butterfly_psum(): x = keep + lax.ppermute(send, axis, perm)  6.07 us
    unnamed x49, local copies, waits for them, and re-layouts  5.24 us
  transfers between devices with their start and end apart: 14, of which 13 were waited for; matrix products, arithmetic and copies ran while one was open for 4% of the time, Pallas kernels for 0%

profile of v2, /device:TPU:0, one launch (start us, length us, event | category | flops | bytes accessed | tf_op | source)
XLA Modules:
  0.0 154.9 jit_solution(950576458560107007)
XLA Ops:
  7.3 0.7 all-gather.2.cloned.1.call-update
  9.6 0.7 reshape.101
  10.3 7.4 %all-to-all-start = ((bf16[16,2,321]{2,1,0:T(2,128)(2,1)}), bf16[16,2,321]{2,1,0:T(2,128)(2,1)S(1)}, u32[]{:S(2)}, u32[]{:S(2)}) async-start(bf16[16,2,321]{2,1,0:T(2,128)(2,1)} %reshape.101), calls=%async_computation | async-start | bytes 49152 | tf_op jit(solution)/shard_map/all_to_all | solution.py:180
  17.7 6.5 %all-to-all-done = bf16[16,2,321]{2,1,0:T(2,128)(2,1)S(1)} async-done(((bf16[16,2,321]{2,1,0:T(2,128)(2,1)}), bf16[16,2,321]{2,1,0:T(2,128)(2,1)S(1)}, u32[]{:S(2)}, u32[]{:S(2)}) %all-to-all-start) | async-done | bytes 20576 | tf_op jit(solution)/shard_map/all_to_all | solution.py:180
  24.7 1.3 collective-permute-start.1
  27.3 4.5 %collective-permute-start = (bf16[4,80]{1,0:T(4,128)(2,1)S(1)}, bf16[4,80]{1,0:T(4,128)(2,1)S(1)}, u32[]{:S(2)}, u32[]{:S(2)}) collective-permute-start(bf16[4,80]{1,0:T(4,128)(2,1)S(1)} %get-tuple-element.25), channel_id=1, source_target_pairs={{0,1},{2,3},{4,5},{6,7},{8,9},{10,11},{12,13},{14,15},{16,17},{18,... | collective-permute-start | bytes 1928 | tf_op jit(solution)/shard_map/ppermute | solution.py:16
  31.8 1.3 collective-permute-done
  33.6 35.6 %all-gather.2.cloned.1.call-done = bf16[512,4096]{1,0:T(8,128)(2,1)} async-done(((bf16[256,4096]{1,0:T(8,128)(2,1)}), bf16[512,4096]{1,0:T(8,128)(2,1)}) %all-gather.2.cloned.1.call-update) | async-done | bytes 4194320 | tf_op jit(solution)/shard_map/all_gather | solution.py:196
  69.1 3.1 %fusion.19 = f32[66,4096]{1,0:T(8,128)S(1)} fusion(bf16[512,4096]{1,0:T(8,128)(2,1)} %all-gather.2.cloned.1.call-done, f32[66,512]{1,0:T(8,128)S(1)} %convolution_add_fusion.1, pred[66]{0:T(512)(128)(4,1)S(1)} %compare_and_fusion), kind=kOutput, calls=%fused_computation.47 | convolution fusion | flops 276993024 | bytes 5410882 | tf_op jit(solution)/shard_map/dot_general | solution.py:199
  74.0 1.7 %copy-done.1 = bf16[512,4096]{1,0:T(8,128)(2,1)S(1)} copy-done((bf16[512,4096]{1,0:T(8,128)(2,1)S(1)}, bf16[512,4096]{1,0:T(8,128)(2,1)}, u32[]{:S(2)}) %copy-start.1) | copy-done | bytes 4194328
  75.6 1.4 convert_reduce_fusion
  80.1 2.7 %collective-permute-done.2 = f32[1920,128]{1,0:T(8,128)} collective-permute-done((f32[1920,128]{1,0:T(8,128)S(1)}, f32[1920,128]{1,0:T(8,128)}, u32[]{:S(2)}, u32[]{:S(2)}) %collective-permute-start.2) | collective-permute-done | bytes 983072 | tf_op jit(solution)/shard_map/ppermute | solution.py:149
  82.7 1.3 dynamic-slice_add_fusion
  84.5 12.9 %collective-permute-done.3 = f32[960,128]{1,0:T(8,128)S(1)} collective-permute-done((f32[960,128]{1,0:T(8,128)S(1)}, f32[960,128]{1,0:T(8,128)S(1)}, u32[]{:S(2)}, u32[]{:S(2)}) %collective-permute-start.3) | collective-permute-done | bytes 491552 | tf_op jit(solution)/shard_map/ppermute | solution.py:149
  97.5 1.5 collective-permute-start.4
  99.1 5.7 %collective-permute-done.4 = f32[480,128]{1,0:T(8,128)S(1)} collective-permute-done((f32[480,128]{1,0:T(8,128)S(1)}, f32[480,128]{1,0:T(8,128)S(1)}, u32[]{:S(2)}, u32[]{:S(2)}) %collective-permute-start.4) | collective-permute-done | bytes 245792 | tf_op jit(solution)/shard_map/ppermute | solution.py:149
  104.8 1.6 %collective-permute-start.5 = (f32[240,128]{1,0:T(8,128)S(1)}, f32[240,128]{1,0:T(8,128)S(1)}, u32[]{:S(2)}, u32[]{:S(2)}) collective-permute-start(f32[240,128]{1,0:T(8,128)S(1)} %constant_dynamic-slice_fusion.1), channel_id=1, source_target_pairs={{0,8},{2,10},{4,12},{6,14},{8,0},{10,2},{12,4},{14,6},{16,24},{18,... | collective-permute-start | bytes 368648 | tf_op jit(solution)/shard_map/ppermute | solution.py:149
  106.4 3.4 %collective-permute-done.5 = f32[240,128]{1,0:T(8,128)S(1)} collective-permute-done((f32[240,128]{1,0:T(8,128)S(1)}, f32[240,128]{1,0:T(8,128)S(1)}, u32[]{:S(2)}, u32[]{:S(2)}) %collective-permute-start.5) | collective-permute-done | bytes 122912 | tf_op jit(solution)/shard_map/ppermute | solution.py:149
  109.8 2.5 %collective-permute-start.6 = (f32[120,128]{1,0:T(8,128)S(1)}, f32[120,128]{1,0:T(8,128)S(1)}, u32[]{:S(2)}, u32[]{:S(2)}) collective-permute-start(f32[120,128]{1,0:T(8,128)S(1)} %constant_dynamic-slice_fusion), channel_id=1, source_target_pairs={{0,16},{2,18},{4,20},{6,22},{8,24},{10,26},{12,28},{14,30},{16,0},... | collective-permute-start | bytes 184328 | tf_op jit(solution)/shard_map/ppermute | solution.py:149
  112.3 3.0 %collective-permute-done.6 = f32[120,128]{1,0:T(8,128)S(1)} collective-permute-done((f32[120,128]{1,0:T(8,128)S(1)}, f32[120,128]{1,0:T(8,128)S(1)}, u32[]{:S(2)}, u32[]{:S(2)}) %collective-permute-start.6) | collective-permute-done | bytes 61472 | tf_op jit(solution)/shard_map/ppermute | solution.py:149
  115.4 2.7 %collective-permute-start.7 = (f32[120,128]{1,0:T(8,128)S(1)}, f32[120,128]{1,0:T(8,128)S(1)}, u32[]{:S(2)}, u32[]{:S(2)}) collective-permute-start(f32[120,128]{1,0:T(8,128)S(1)} %get-tuple-element.8), channel_id=1, source_target_pairs={{0,16},{2,18},{4,20},{6,22},{8,24},{10,26},{12,28},{14,30},{16,0},... | collective-permute-start | bytes 184328 | tf_op jit(solution)/shard_map/ppermute | solution.py:154
  118.0 2.6 %collective-permute-done.7 = f32[120,128]{1,0:T(8,128)S(1)} collective-permute-done((f32[120,128]{1,0:T(8,128)S(1)}, f32[120,128]{1,0:T(8,128)S(1)}, u32[]{:S(2)}, u32[]{:S(2)}) %collective-permute-start.7) | collective-permute-done | bytes 61472 | tf_op jit(solution)/shard_map/ppermute | solution.py:154
  120.7 3.1 %collective-permute-start.8 = (f32[240,128]{1,0:T(8,128)S(1)}, f32[240,128]{1,0:T(8,128)S(1)}, u32[]{:S(2)}, u32[]{:S(2)}) collective-permute-start(f32[240,128]{1,0:T(8,128)S(1)} %constant_dynamic-update-slice_fusion.10), channel_id=1, source_target_pairs={{0,8},{2,10},{4,12},{6,14},{8,0},{10,2},{12,4},{14,6},{16,24},{18,... | collective-permute-start | bytes 368648 | tf_op jit(solution)/shard_map/ppermute | solution.py:154
  123.8 2.8 %collective-permute-done.8 = f32[240,128]{1,0:T(8,128)S(1)} collective-permute-done((f32[240,128]{1,0:T(8,128)S(1)}, f32[240,128]{1,0:T(8,128)S(1)}, u32[]{:S(2)}, u32[]{:S(2)}) %collective-permute-start.8) | collective-permute-done | bytes 122912 | tf_op jit(solution)/shard_map/ppermute | solution.py:154
  126.6 1.5 collective-permute-start.9
  128.2 4.6 %collective-permute-done.9 = f32[480,128]{1,0:T(8,128)S(1)} collective-permute-done((f32[480,128]{1,0:T(8,128)S(1)}, f32[480,128]{1,0:T(8,128)S(1)}, u32[]{:S(2)}, u32[]{:S(2)}) %collective-permute-start.9) | collective-permute-done | bytes 245792 | tf_op jit(solution)/shard_map/ppermute | solution.py:154
  132.9 0.7 collective-permute-start.10
  133.7 8.1 %collective-permute-done.10 = f32[960,128]{1,0:T(8,128)S(1)} collective-permute-done((f32[960,128]{1,0:T(8,128)S(1)}, f32[960,128]{1,0:T(8,128)S(1)}, u32[]{:S(2)}, u32[]{:S(2)}) %collective-permute-start.10) | collective-permute-done | bytes 491552 | tf_op jit(solution)/shard_map/ppermute | solution.py:154
  141.9 1.1 fusion.3
  143.2 1.2 collective-permute-done.11
  145.8 1.2 reshape.96
  147.0 1.1 reshape.97
  (115 shorter events, 10.9 us)
Async XLA Ops:
  7.2 26.1 %copy-start = (bf16[560,512]{1,0:T(8,128)(2,1)S(1)}, bf16[560,512]{1,0:T(8,128)(2,1)}, u32[]{:S(2)}) copy-start(bf16[560,512]{1,0:T(8,128)(2,1)} %param.16) | copy-start | bytes 1720324
  7.2 0.8 copy-start.18
  7.2 0.9 copy-start.19
  7.2 1.0 copy-start.16
  7.2 1.0 copy-start.13
  7.2 19.1 %copy-start.2 = (bf16[1,512,256]{2,1,0:T(8,128)(2,1)S(1)}, bf16[1,512,256]{2,1,0:T(8,128)(2,1)}, u32[]{:S(2)}) copy-start(bf16[1,512,256]{2,1,0:T(8,128)(2,1)} %param.15) | copy-start | bytes 786436
  7.2 19.4 %copy-start.5 = (bf16[768,256]{1,0:T(8,128)(2,1)S(1)}, bf16[768,256]{1,0:T(8,128)(2,1)}, u32[]{:S(2)}) copy-start(bf16[768,256]{1,0:T(8,128)(2,1)} %param.20) | copy-start | bytes 1179652
  7.2 61.9 %all-gather.2.cloned.1.call-start = ((), (), s32[]{:S(2)}) async-start(), calls=%async_computation.1 | async-start | bytes 6291456 | tf_op jit(solution)/shard_map/all_gather | solution.py:196
  10.3 13.9 %all-to-all-start = ((bf16[16,2,321]{2,1,0:T(2,128)(2,1)}), bf16[16,2,321]{2,1,0:T(2,128)(2,1)S(1)}, u32[]{:S(2)}, u32[]{:S(2)}) async-start(bf16[16,2,321]{2,1,0:T(2,128)(2,1)} %reshape.101), calls=%async_computation | async-start | bytes 49152 | tf_op jit(solution)/shard_map/all_to_all | solution.py:180
  24.7 7.1 %collective-permute-start.1 = (bf16[4,80]{1,0:T(4,128)(2,1)S(1)}, bf16[4,80]{1,0:T(4,128)(2,1)S(1)}, u32[]{:S(2)}, u32[]{:S(2)}) collective-permute-start(bf16[4,80]{1,0:T(4,128)(2,1)S(1)} %get-tuple-element.24), channel_id=1, source_target_pairs={{1,0},{3,2},{5,4},{7,6},{9,8},{11,10},{13,12},{15,14},{17,16},{19,... | collective-permute-start | bytes 1928 | tf_op jit(solution)/shard_map/ppermute | solution.py:19
  27.1 6.2 %copy-start.14 = (f32[512]{0:T(512)S(1)}, f32[512]{0:T(512)}, u32[]{:S(2)}) copy-start(f32[512]{0:T(512)} %param.17) | copy-start | bytes 6148
  27.3 5.8 %collective-permute-start = (bf16[4,80]{1,0:T(4,128)(2,1)S(1)}, bf16[4,80]{1,0:T(4,128)(2,1)S(1)}, u32[]{:S(2)}, u32[]{:S(2)}) collective-permute-start(bf16[4,80]{1,0:T(4,128)(2,1)S(1)} %get-tuple-element.25), channel_id=1, source_target_pairs={{0,1},{2,3},{4,5},{6,7},{8,9},{10,11},{12,13},{14,15},{16,17},{18,... | collective-permute-start | bytes 1928 | tf_op jit(solution)/shard_map/ppermute | solution.py:16
  73.3 2.4 %copy-start.1 = (bf16[512,4096]{1,0:T(8,128)(2,1)S(1)}, bf16[512,4096]{1,0:T(8,128)(2,1)}, u32[]{:S(2)}) copy-start(bf16[512,4096]{1,0:T(8,128)(2,1)} %all-gather.2.cloned.1.call-done) | copy-start | bytes 12582916
  73.6 4.1 %copy-start.3 = (f32[518,256]{1,0:T(8,128)}, f32[518,256]{1,0:T(8,128)S(1)}, u32[]{:S(2)}) copy-start(f32[518,256]{1,0:T(8,128)S(1)} %get-tuple-element.10) | copy-start | bytes 1591300
  78.0 0.8 copy-start.9
  78.0 0.9 copy-start.11
  80.0 2.8 %collective-permute-start.2 = (f32[1920,128]{1,0:T(8,128)S(1)}, f32[1920,128]{1,0:T(8,128)}, u32[]{:S(2)}, u32[]{:S(2)}) collective-permute-start(f32[1920,128]{1,0:T(8,128)S(1)} %constant_dynamic-slice_fusion.4), channel_id=1, source_target_pairs={{0,2},{2,0},{4,6},{6,4},{8,10},{10,8},{12,14},{14,12},{16,18},{18,... | collective-permute-start | bytes 2949128 | tf_op jit(solution)/shard_map/ppermute | solution.py:149
  84.1 13.3 %collective-permute-start.3 = (f32[960,128]{1,0:T(8,128)S(1)}, f32[960,128]{1,0:T(8,128)S(1)}, u32[]{:S(2)}, u32[]{:S(2)}) collective-permute-start(f32[960,128]{1,0:T(8,128)S(1)} %constant_dynamic-slice_fusion.3), channel_id=1, source_target_pairs={{0,1},{1,0},{2,3},{3,2},{4,5},{5,4},{6,7},{7,6},{8,9},{9,8},{10,11... | collective-permute-start | bytes 1474568 | tf_op jit(solution)/shard_map/ppermute | solution.py:149
  97.5 7.2 %collective-permute-start.4 = (f32[480,128]{1,0:T(8,128)S(1)}, f32[480,128]{1,0:T(8,128)S(1)}, u32[]{:S(2)}, u32[]{:S(2)}) collective-permute-start(f32[480,128]{1,0:T(8,128)S(1)} %constant_dynamic-slice_fusion.2), channel_id=1, source_target_pairs={{0,4},{2,6},{4,0},{6,2},{8,12},{10,14},{12,8},{14,10},{16,20},{18,... | collective-permute-start | bytes 737288 | tf_op jit(solution)/shard_map/ppermute | solution.py:149
  104.8 4.9 %collective-permute-start.5 = (f32[240,128]{1,0:T(8,128)S(1)}, f32[240,128]{1,0:T(8,128)S(1)}, u32[]{:S(2)}, u32[]{:S(2)}) collective-permute-start(f32[240,128]{1,0:T(8,128)S(1)} %constant_dynamic-slice_fusion.1), channel_id=1, source_target_pairs={{0,8},{2,10},{4,12},{6,14},{8,0},{10,2},{12,4},{14,6},{16,24},{18,... | collective-permute-start | bytes 368648 | tf_op jit(solution)/shard_map/ppermute | solution.py:149
  109.8 5.5 %collective-permute-start.6 = (f32[120,128]{1,0:T(8,128)S(1)}, f32[120,128]{1,0:T(8,128)S(1)}, u32[]{:S(2)}, u32[]{:S(2)}) collective-permute-start(f32[120,128]{1,0:T(8,128)S(1)} %constant_dynamic-slice_fusion), channel_id=1, source_target_pairs={{0,16},{2,18},{4,20},{6,22},{8,24},{10,26},{12,28},{14,30},{16,0},... | collective-permute-start | bytes 184328 | tf_op jit(solution)/shard_map/ppermute | solution.py:149
  115.4 5.3 %collective-permute-start.7 = (f32[120,128]{1,0:T(8,128)S(1)}, f32[120,128]{1,0:T(8,128)S(1)}, u32[]{:S(2)}, u32[]{:S(2)}) collective-permute-start(f32[120,128]{1,0:T(8,128)S(1)} %get-tuple-element.8), channel_id=1, source_target_pairs={{0,16},{2,18},{4,20},{6,22},{8,24},{10,26},{12,28},{14,30},{16,0},... | collective-permute-start | bytes 184328 | tf_op jit(solution)/shard_map/ppermute | solution.py:154
  120.7 5.9 %collective-permute-start.8 = (f32[240,128]{1,0:T(8,128)S(1)}, f32[240,128]{1,0:T(8,128)S(1)}, u32[]{:S(2)}, u32[]{:S(2)}) collective-permute-start(f32[240,128]{1,0:T(8,128)S(1)} %constant_dynamic-update-slice_fusion.10), channel_id=1, source_target_pairs={{0,8},{2,10},{4,12},{6,14},{8,0},{10,2},{12,4},{14,6},{16,24},{18,... | collective-permute-start | bytes 368648 | tf_op jit(solution)/shard_map/ppermute | solution.py:154
  126.6 6.3 %collective-permute-start.9 = (f32[480,128]{1,0:T(8,128)S(1)}, f32[480,128]{1,0:T(8,128)S(1)}, u32[]{:S(2)}, u32[]{:S(2)}) collective-permute-start(f32[480,128]{1,0:T(8,128)S(1)} %constant_dynamic-update-slice_fusion.8), channel_id=1, source_target_pairs={{0,4},{2,6},{4,0},{6,2},{8,12},{10,14},{12,8},{14,10},{16,20},{18,... | collective-permute-start | bytes 737288 | tf_op jit(solution)/shard_map/ppermute | solution.py:154
  128.1 13.8 %copy-start.4 = (f32[518,256]{1,0:T(8,128)S(1)}, f32[518,256]{1,0:T(8,128)}, u32[]{:S(2)}) copy-start(f32[518,256]{1,0:T(8,128)} %copy-done.3) | copy-start | bytes 1591300
  128.1 13.8 %copy-start.6 = (bf16[768,256]{1,0:T(8,128)(2,1)S(1)}, bf16[768,256]{1,0:T(8,128)(2,1)}, u32[]{:S(2)}) copy-start(bf16[768,256]{1,0:T(8,128)(2,1)} %param.20) | copy-start | bytes 1179652
  128.1 13.8 %copy-start.8 = (bf16[512,256]{1,0:T(8,128)(2,1)S(1)}, bf16[512,256]{1,0:T(8,128)(2,1)}, u32[]{:S(2)}) copy-start(bf16[512,256]{1,0:T(8,128)(2,1)} %copy-done.7) | copy-start | bytes 786436
  128.1 13.8 %copy-start.10 = (bf16[512,256]{1,0:T(8,128)(2,1)S(1)}, bf16[512,256]{1,0:T(8,128)(2,1)}, u32[]{:S(2)}) copy-start(bf16[512,256]{1,0:T(8,128)(2,1)} %copy-done.9) | copy-start | bytes 786436
  128.2 13.8 %copy-start.12 = (bf16[512,256]{1,0:T(8,128)(2,1)S(1)}, bf16[512,256]{1,0:T(8,128)(2,1)}, u32[]{:S(2)}) copy-start(bf16[512,256]{1,0:T(8,128)(2,1)} %copy-done.11) | copy-start | bytes 786436
  128.2 13.8 %copy-start.17 = (f32[256]{0:T(256)S(1)}, f32[256]{0:T(256)}, u32[]{:S(2)}) copy-start(f32[256]{0:T(256)} %param.21) | copy-start | bytes 3076
  132.9 8.9 %collective-permute-start.10 = (f32[960,128]{1,0:T(8,128)S(1)}, f32[960,128]{1,0:T(8,128)S(1)}, u32[]{:S(2)}, u32[]{:S(2)}) collective-permute-start(f32[960,128]{1,0:T(8,128)S(1)} %constant_dynamic-update-slice_fusion.6), channel_id=1, source_target_pairs={{0,1},{1,0},{2,3},{3,2},{4,5},{5,4},{6,7},{7,6},{8,9},{9,8},{10,11... | collective-permute-start | bytes 1474568 | tf_op jit(solution)/shard_map/ppermute | solution.py:154
  141.8 2.6 %collective-permute-start.11 = (f32[1920,128]{1,0:T(8,128)S(1)}, f32[1920,128]{1,0:T(8,128)S(1)}, u32[]{:S(2)}, u32[]{:S(2)}) collective-permute-start(f32[1920,128]{1,0:T(8,128)S(1)} %constant_dynamic-update-slice_fusion.4), channel_id=1, source_target_pairs={{0,2},{2,0},{4,6},{6,4},{8,10},{10,8},{12,14},{14,12},{16,18},{18,... | collective-permute-start | bytes 2949128 | tf_op jit(solution)/shard_map/ppermute | solution.py:154
  (2 other events, 1.4 us)
Sparse Core Ops, SparseCore 0:
  9.6 59.4 all-gather.1

commit v3 on v2

--- a/solution.py
+++ b/solution.py
@@ -163,6 +163,23 @@
     return tuple(out)
 
 
+def gather_rows(w_ups):
+    dp_size = lax.axis_size("dp")
+    if lax.axis_size("tm") != 2 or dp_size % 2:
+        return lax.all_gather(w_ups, "tm", axis=0, tiled=True)
+    rows, width = w_ups.shape
+    cols = width // 2
+    core = lax.axis_index("dp") % 2
+    tm = lax.axis_index("tm")
+    mine = lax.dynamic_slice_in_dim(w_ups, core * cols, cols, axis=1)
+    got = lax.ppermute(mine, "tm", [(0, 1), (1, 0)])
+    partner = lax.ppermute(got, "dp", [(i, i ^ 1) for i in range(dp_size)])
+    whole = jnp.zeros((2 * rows, width), w_ups.dtype)
+    whole = lax.dynamic_update_slice(whole, w_ups, (tm * rows, 0))
+    whole = lax.dynamic_update_slice(whole, got, ((1 - tm) * rows, core * cols))
+    return lax.dynamic_update_slice(whole, partner, ((1 - tm) * rows, (1 - core) * cols))
+
+
 def on_device(
     src_mel, owner, dst_pos, keep, cotangent, w_pre, b_pre, w_ups, upsample_bias, w_res, b_res
 ):
@@ -193,7 +210,7 @@
     cot = cotangent[0]
     marks = jnp.repeat(keep_segs, cot.shape[0] // seg_count)
     gradient_value = jnp.where(marks[:, None] > 0, cot, jnp.zeros_like(cot))
-    whole = lax.all_gather(w_ups, "tm", axis=0, tiled=True)
+    whole = gather_rows(w_ups)
 
     def ups_forward(act):
         return jnp.dot(act, whole, preferred_element_type=jnp.float32)

time: 155 us -> 139 us (0.90)
  waiting for transfers between devices: 91.1 us -> 54.1 us
  local copies, waits for them, and re-layouts: 11 us -> 37 us
  between operations: 14.8 us -> 1.35 us
  starting transfers between devices: 27.3 us -> 32.6 us
  matrix products: 7.37 us -> 9.6 us
    all_gather x1 -> x0, waiting for transfers between devices: 35.6 us -> none  [on_device(): whole = lax.all_gather(w_ups, 'tm', axis=0, tiled=True)]
    dynamic_update_slice x0 -> x3, local copies, waits for them, and re-layouts: none -> 22.8 us  [the longest x1 10.7 us: gather_rows(): whole = lax.dynamic_update_slice(whole, got, ((1 - tm) * rows, core * cols))]
    ppermute x0 -> x2, waiting for transfers between devices: none -> 5.85 us  [the longest x1 5.85 us: gather_rows(): got = lax.ppermute(mine, 'tm', [(0, 1), (1, 0)])]
    all_to_all x1, waiting for transfers between devices: 6.51 us -> 2.6 us  [on_device(): lax.all_to_all(outgoing, 'dp', split_axis=0, concat_axis=0, tiled=True)]
    ppermute x5, starting transfers between devices: 6.07 us -> 9.36 us  [butterfly_psum(): x = keep + lax.ppermute(send, axis, perm)]
    ppermute x0 -> x2, starting transfers between devices: none -> 2.97 us  [the longest x1 2.97 us: gather_rows(): got = lax.ppermute(mine, 'tm', [(0, 1), (1, 0)])]
    broadcast_in_dim x0 -> x1, local copies, waits for them, and re-layouts: none -> 2.46 us  [gather_rows(): whole = jnp.zeros((2 * rows, width), w_ups.dtype)]
    dynamic_slice x0 -> x1, local copies, waits for them, and re-layouts: none -> 2.37 us  [gather_rows(): mine = lax.dynamic_slice_in_dim(w_ups, core * cols, cols, axis=1)]
  transfers between devices with their start and end apart: 14 -> 15, of which waited for: 13 -> 13; matrix products, arithmetic and copies ran while one was open for 4% -> 15% of each run, Pallas kernels for 0% -> 0%
where the time goes in v3:
time: 139 us; the launch traced here: 138 us
  waiting for transfers between devices  54.1 us (39%)
  local copies, waits for them, and re-layouts  37 us (27%)
  starting transfers between devices  32.6 us (23%)
  matrix products  9.6 us (7%)
  other arithmetic  3.38 us (2%)
    ppermute x5, waiting for transfers between devices, butterfly_psum(): x = keep + lax.ppermute(send, axis, perm)  26 us
    ppermute x5, waiting for transfers between devices, butterfly_psum(): recv = lax.ppermute(x, axis, perm)  18.4 us
    dynamic_update_slice x1, local copies, waits for them, and re-layouts, gather_rows(): whole = lax.dynamic_update_slice(whole, got, ((1 - tm) * rows, core * cols))  10.7 us
    dynamic_update_slice x1, local copies, waits for them, and re-layouts, gather_rows(): lax.dynamic_update_slice(whole, partner, ((1 - tm) * rows, (1 - core) * c...  10.6 us
    ppermute x5, starting transfers between devices, butterfly_psum(): recv = lax.ppermute(x, axis, perm)  9.46 us
    ppermute x5, starting transfers between devices, butterfly_psum(): x = keep + lax.ppermute(send, axis, perm)  9.36 us
    all_to_all x1, starting transfers between devices, on_device(): lax.all_to_all(outgoing, 'dp', split_axis=0, concat_axis=0, tiled=True)  5.91 us
    ppermute x1, waiting for transfers between devices, gather_rows(): got = lax.ppermute(mine, 'tm', [(0, 1), (1, 0)])  5.85 us
  transfers between devices with their start and end apart: 15, of which 13 were waited for; matrix products, arithmetic and copies ran while one was open for 15% of the time, Pallas kernels for 0%

profile of v3, /device:TPU:0, one launch (start us, length us, event | category | flops | bytes accessed | tf_op | source)
XLA Modules:
  0.0 138.1 jit_solution(7975119282346305381)
XLA Ops:
  0.7 2.4 %constant_dynamic-slice_fusion.5 = bf16[256,2048]{1,0:T(8,128)(2,1)} fusion(bf16[256,4096]{1,0:T(8,128)(2,1)} %param.18, s32[]{:T(128)S(6)} %select_n.148), kind=kLoop, calls=%fused_computation.86 | loop fusion | bytes 2097156 | tf_op jit(solution)/shard_map/dynamic_slice | solution.py:174
  3.1 3.0 %collective-permute-start.2 = (bf16[256,2048]{1,0:T(8,128)(2,1)}, bf16[256,2048]{1,0:T(8,128)(2,1)}, u32[]{:S(2)}, u32[]{:S(2)}) collective-permute-start(bf16[256,2048]{1,0:T(8,128)(2,1)} %constant_dynamic-slice_fusion.5), channel_id=1, source_target_pairs={{0,1},{1,0},{2,3},{3,2},{4,5},{5,4},{6,7},{7,6},{8,9},{9,8},{10,11... | collective-permute-start | bytes 3145736 | tf_op jit(solution)/shard_map/ppermute | solution.py:175
  8.3 5.9 %all-to-all-start = ((bf16[16,2,321]{2,1,0:T(2,128)(2,1)}), bf16[16,2,321]{2,1,0:T(2,128)(2,1)S(1)}, u32[]{:S(2)}, u32[]{:S(2)}) async-start(bf16[16,2,321]{2,1,0:T(2,128)(2,1)} %reshape.101), calls=%async_computation | async-start | bytes 49152 | tf_op jit(solution)/shard_map/all_to_all | solution.py:197
  14.3 2.5 %broadcast_in_dim.103 = bf16[512,4096]{1,0:T(8,128)(2,1)} broadcast(bf16[]{:T(256)} %constant.149.clone.1), dimensions={} | broadcast | bytes 4194306 | tf_op jit(solution)/shard_map/broadcast_in_dim | solution.py:177
  16.8 1.5 %constant_dynamic-update-slice_fusion.12 = bf16[512,4096]{1,0:T(8,128)(2,1)} fusion(bf16[512,4096]{1,0:T(8,128)(2,1)} %broadcast_in_dim.103, bf16[256,4096]{1,0:T(8,128)(2,1)S(1)} %copy-done.1, s32[]{:T(128)S(6)} %select_n.146), kind=kLoop, calls=%fused_computation.87 | loop fusion | bytes 4194308 | tf_op jit(solution)/shard_map/dynamic_update_slice | solution.py:178
  18.2 2.6 %all-to-all-done = bf16[16,2,321]{2,1,0:T(2,128)(2,1)S(1)} async-done(((bf16[16,2,321]{2,1,0:T(2,128)(2,1)}), bf16[16,2,321]{2,1,0:T(2,128)(2,1)S(1)}, u32[]{:S(2)}, u32[]{:S(2)}) %all-to-all-start) | async-done | bytes 20576 | tf_op jit(solution)/shard_map/all_to_all | solution.py:197
  21.4 1.3 collective-permute-start.1
  23.7 5.8 %collective-permute-done.2 = bf16[256,2048]{1,0:T(8,128)(2,1)} collective-permute-done((bf16[256,2048]{1,0:T(8,128)(2,1)}, bf16[256,2048]{1,0:T(8,128)(2,1)}, u32[]{:S(2)}, u32[]{:S(2)}) %collective-permute-start.2) | collective-permute-done | bytes 1048608 | tf_op jit(solution)/shard_map/ppermute | solution.py:175
  29.7 3.6 %collective-permute-start = (bf16[4,80]{1,0:T(4,128)(2,1)S(1)}, bf16[4,80]{1,0:T(4,128)(2,1)S(1)}, u32[]{:S(2)}, u32[]{:S(2)}) collective-permute-start(bf16[4,80]{1,0:T(4,128)(2,1)S(1)} %get-tuple-element.25), channel_id=1, source_target_pairs={{0,1},{2,3},{4,5},{6,7},{8,9},{10,11},{12,13},{14,15},{16,17},{18,... | collective-permute-start | bytes 1928 | tf_op jit(solution)/shard_map/ppermute | solution.py:16
  33.4 1.3 collective-permute-done
  35.1 10.7 %dynamic_update_slice.40 = bf16[512,4096]{1,0:T(8,128)(2,1)} dynamic-update-slice(bf16[512,4096]{1,0:T(8,128)(2,1)} %constant_dynamic-update-slice_fusion.12, bf16[256,2048]{1,0:T(8,128)(2,1)} %collective-permute-done.2, s32[]{:T(128)S(6)} %select_n.149, s32[]{:T(128)S(6)} %select_n.148) | dynamic-update-slice | bytes 2097156 | tf_op jit(solution)/shard_map/dynamic_update_slice | solution.py:179
  45.8 10.6 %dynamic_update_slice.41 = bf16[512,4096]{1,0:T(8,128)(2,1)} dynamic-update-slice(bf16[512,4096]{1,0:T(8,128)(2,1)} %dynamic_update_slice.40, bf16[256,2048]{1,0:T(8,128)(2,1)} %collective-permute-done.3, s32[]{:T(128)S(6)} %select_n.149, s32[]{:T(128)S(6)} %select_n.150) | dynamic-update-slice | bytes 2097156 | tf_op jit(solution)/shard_map/dynamic_update_slice | solution.py:180
  56.4 3.1 %fusion.19 = f32[66,4096]{1,0:T(8,128)S(1)} fusion(bf16[512,4096]{1,0:T(8,128)(2,1)} %dynamic_update_slice.41, f32[66,512]{1,0:T(8,128)S(1)} %convolution_add_fusion.1, pred[66]{0:T(512)(128)(4,1)S(1)} %compare_and_fusion), kind=kOutput, calls=%fused_computation.47 | convolution fusion | flops 276993024 | bytes 5410882 | tf_op jit(solution)/shard_map/dot_general | solution.py:216
  61.3 3.6 %convert_reduce_fusion = (f32[512]{0:T(512)S(1)}, bf16[66,512]{1,0:T(8,128)(2,1)S(1)}) fusion(f32[66,512]{1,0:T(8,128)S(1)} %convolution_add_fusion.1, bf16[66,4096]{1,0:T(8,128)(2,1)S(1)} %bitcast.56, bf16[512,4096]{1,0:T(8,128)(2,1)} %dynamic_update_slice.41, pred[66]{0:T(512)(128)(4,1)S(1)} %compare_and_fusion), kind=kOutput, calls=%fused_computation.44 | convolution fusion | flops 277060096 | bytes 4939842 | tf_op jit(solution)/shard_map/dot_general | solution.py:39
  67.9 2.7 %collective-permute-done.4 = f32[1920,128]{1,0:T(8,128)} collective-permute-done((f32[1920,128]{1,0:T(8,128)S(1)}, f32[1920,128]{1,0:T(8,128)}, u32[]{:S(2)}, u32[]{:S(2)}) %collective-permute-start.4) | collective-permute-done | bytes 983072 | tf_op jit(solution)/shard_map/ppermute | solution.py:149
  70.6 1.3 dynamic-slice_add_fusion
  72.0 3.4 %collective-permute-start.5 = (f32[960,128]{1,0:T(8,128)S(1)}, f32[960,128]{1,0:T(8,128)S(1)}, u32[]{:S(2)}, u32[]{:S(2)}) collective-permute-start(f32[960,128]{1,0:T(8,128)S(1)} %constant_dynamic-slice_fusion.3), channel_id=1, source_target_pairs={{0,1},{1,0},{2,3},{3,2},{4,5},{5,4},{6,7},{7,6},{8,9},{9,8},{10,11... | collective-permute-start | bytes 1474568 | tf_op jit(solution)/shard_map/ppermute | solution.py:149
  75.4 11.5 %collective-permute-done.5 = f32[960,128]{1,0:T(8,128)S(1)} collective-permute-done((f32[960,128]{1,0:T(8,128)S(1)}, f32[960,128]{1,0:T(8,128)S(1)}, u32[]{:S(2)}, u32[]{:S(2)}) %collective-permute-start.5) | collective-permute-done | bytes 491552 | tf_op jit(solution)/shard_map/ppermute | solution.py:149
  87.0 1.6 %collective-permute-start.6 = (f32[480,128]{1,0:T(8,128)S(1)}, f32[480,128]{1,0:T(8,128)S(1)}, u32[]{:S(2)}, u32[]{:S(2)}) collective-permute-start(f32[480,128]{1,0:T(8,128)S(1)} %constant_dynamic-slice_fusion.2), channel_id=1, source_target_pairs={{0,4},{2,6},{4,0},{6,2},{8,12},{10,14},{12,8},{14,10},{16,20},{18,... | collective-permute-start | bytes 737288 | tf_op jit(solution)/shard_map/ppermute | solution.py:149
  88.6 6.0 %collective-permute-done.6 = f32[480,128]{1,0:T(8,128)S(1)} collective-permute-done((f32[480,128]{1,0:T(8,128)S(1)}, f32[480,128]{1,0:T(8,128)S(1)}, u32[]{:S(2)}, u32[]{:S(2)}) %collective-permute-start.6) | collective-permute-done | bytes 245792 | tf_op jit(solution)/shard_map/ppermute | solution.py:149
  94.6 1.6 %collective-permute-start.7 = (f32[240,128]{1,0:T(8,128)S(1)}, f32[240,128]{1,0:T(8,128)S(1)}, u32[]{:S(2)}, u32[]{:S(2)}) collective-permute-start(f32[240,128]{1,0:T(8,128)S(1)} %constant_dynamic-slice_fusion.1), channel_id=1, source_target_pairs={{0,8},{2,10},{4,12},{6,14},{8,0},{10,2},{12,4},{14,6},{16,24},{18,... | collective-permute-start | bytes 368648 | tf_op jit(solution)/shard_map/ppermute | solution.py:149
  96.3 3.3 %collective-permute-done.7 = f32[240,128]{1,0:T(8,128)S(1)} collective-permute-done((f32[240,128]{1,0:T(8,128)S(1)}, f32[240,128]{1,0:T(8,128)S(1)}, u32[]{:S(2)}, u32[]{:S(2)}) %collective-permute-start.7) | collective-permute-done | bytes 122912 | tf_op jit(solution)/shard_map/ppermute | solution.py:149
  99.6 2.7 %collective-permute-start.8 = (f32[120,128]{1,0:T(8,128)S(1)}, f32[120,128]{1,0:T(8,128)S(1)}, u32[]{:S(2)}, u32[]{:S(2)}) collective-permute-start(f32[120,128]{1,0:T(8,128)S(1)} %constant_dynamic-slice_fusion), channel_id=1, source_target_pairs={{0,16},{2,18},{4,20},{6,22},{8,24},{10,26},{12,28},{14,30},{16,0},... | collective-permute-start | bytes 184328 | tf_op jit(solution)/shard_map/ppermute | solution.py:149
  102.3 2.5 %collective-permute-done.8 = f32[120,128]{1,0:T(8,128)S(1)} collective-permute-done((f32[120,128]{1,0:T(8,128)S(1)}, f32[120,128]{1,0:T(8,128)S(1)}, u32[]{:S(2)}, u32[]{:S(2)}) %collective-permute-start.8) | collective-permute-done | bytes 61472 | tf_op jit(solution)/shard_map/ppermute | solution.py:149
  104.8 2.7 %collective-permute-start.9 = (f32[120,128]{1,0:T(8,128)S(1)}, f32[120,128]{1,0:T(8,128)S(1)}, u32[]{:S(2)}, u32[]{:S(2)}) collective-permute-start(f32[120,128]{1,0:T(8,128)S(1)} %get-tuple-element.8), channel_id=1, source_target_pairs={{0,16},{2,18},{4,20},{6,22},{8,24},{10,26},{12,28},{14,30},{16,0},... | collective-permute-start | bytes 184328 | tf_op jit(solution)/shard_map/ppermute | solution.py:154
  107.5 2.6 %collective-permute-done.9 = f32[120,128]{1,0:T(8,128)S(1)} collective-permute-done((f32[120,128]{1,0:T(8,128)S(1)}, f32[120,128]{1,0:T(8,128)S(1)}, u32[]{:S(2)}, u32[]{:S(2)}) %collective-permute-start.9) | collective-permute-done | bytes 61472 | tf_op jit(solution)/shard_map/ppermute | solution.py:154
  110.1 3.6 %collective-permute-start.10 = (f32[240,128]{1,0:T(8,128)S(1)}, f32[240,128]{1,0:T(8,128)S(1)}, u32[]{:S(2)}, u32[]{:S(2)}) collective-permute-start(f32[240,128]{1,0:T(8,128)S(1)} %constant_dynamic-update-slice_fusion.10), channel_id=1, source_target_pairs={{0,8},{2,10},{4,12},{6,14},{8,0},{10,2},{12,4},{14,6},{16,24},{18,... | collective-permute-start | bytes 368648 | tf_op jit(solution)/shard_map/ppermute | solution.py:154
  113.7 2.8 %collective-permute-done.10 = f32[240,128]{1,0:T(8,128)S(1)} collective-permute-done((f32[240,128]{1,0:T(8,128)S(1)}, f32[240,128]{1,0:T(8,128)S(1)}, u32[]{:S(2)}, u32[]{:S(2)}) %collective-permute-start.10) | collective-permute-done | bytes 122912 | tf_op jit(solution)/shard_map/ppermute | solution.py:154
  116.6 1.6 %collective-permute-start.11 = (f32[480,128]{1,0:T(8,128)S(1)}, f32[480,128]{1,0:T(8,128)S(1)}, u32[]{:S(2)}, u32[]{:S(2)}) collective-permute-start(f32[480,128]{1,0:T(8,128)S(1)} %constant_dynamic-update-slice_fusion.8), channel_id=1, source_target_pairs={{0,4},{2,6},{4,0},{6,2},{8,12},{10,14},{12,8},{14,10},{16,20},{18,... | collective-permute-start | bytes 737288 | tf_op jit(solution)/shard_map/ppermute | solution.py:154
  118.3 4.6 %collective-permute-done.11 = f32[480,128]{1,0:T(8,128)S(1)} collective-permute-done((f32[480,128]{1,0:T(8,128)S(1)}, f32[480,128]{1,0:T(8,128)S(1)}, u32[]{:S(2)}, u32[]{:S(2)}) %collective-permute-start.11) | collective-permute-done | bytes 245792 | tf_op jit(solution)/shard_map/ppermute | solution.py:154
  122.9 1.6 %collective-permute-start.12 = (f32[960,128]{1,0:T(8,128)S(1)}, f32[960,128]{1,0:T(8,128)S(1)}, u32[]{:S(2)}, u32[]{:S(2)}) collective-permute-start(f32[960,128]{1,0:T(8,128)S(1)} %constant_dynamic-update-slice_fusion.6), channel_id=1, source_target_pairs={{0,1},{1,0},{2,3},{3,2},{4,5},{5,4},{6,7},{7,6},{8,9},{9,8},{10,11... | collective-permute-start | bytes 1474568 | tf_op jit(solution)/shard_map/ppermute | solution.py:154
  124.5 7.2 %collective-permute-done.12 = f32[960,128]{1,0:T(8,128)S(1)} collective-permute-done((f32[960,128]{1,0:T(8,128)S(1)}, f32[960,128]{1,0:T(8,128)S(1)}, u32[]{:S(2)}, u32[]{:S(2)}) %collective-permute-start.12) | collective-permute-done | bytes 491552 | tf_op jit(solution)/shard_map/ppermute | solution.py:154
  (121 shorter events, 15.7 us)
Async XLA Ops:
  0.6 34.2 %copy-start = (bf16[560,512]{1,0:T(8,128)(2,1)S(1)}, bf16[560,512]{1,0:T(8,128)(2,1)}, u32[]{:S(2)}) copy-start(bf16[560,512]{1,0:T(8,128)(2,1)} %param.16) | copy-start | bytes 1720324
  0.6 5.4 %copy-start.18 = (s32[1,8]{1,0:T(1,128)S(1)}, s32[1,8]{1,0:T(1,128)}, u32[]{:S(2)}) copy-start(s32[1,8]{1,0:T(1,128)} %param.13) | copy-start | bytes 100
  0.7 5.5 %copy-start.19 = (s32[1,8]{1,0:T(1,128)S(1)}, s32[1,8]{1,0:T(1,128)}, u32[]{:S(2)}) copy-start(s32[1,8]{1,0:T(1,128)} %param.14) | copy-start | bytes 100
  0.7 5.6 %copy-start.16 = (s32[1,8]{1,0:T(1,128)S(1)}, s32[1,8]{1,0:T(1,128)}, u32[]{:S(2)}) copy-start(s32[1,8]{1,0:T(1,128)} %param.12) | copy-start | bytes 100
  0.7 5.6 %copy-start.13 = (bf16[1,8,640]{2,1,0:T(8,128)(2,1)S(1)}, bf16[1,8,640]{2,1,0:T(8,128)(2,1)}, u32[]{:S(2)}) copy-start(bf16[1,8,640]{2,1,0:T(8,128)(2,1)} %param.11) | copy-start | bytes 30724
  3.1 26.4 %collective-permute-start.2 = (bf16[256,2048]{1,0:T(8,128)(2,1)}, bf16[256,2048]{1,0:T(8,128)(2,1)}, u32[]{:S(2)}, u32[]{:S(2)}) collective-permute-start(bf16[256,2048]{1,0:T(8,128)(2,1)} %constant_dynamic-slice_fusion.5), channel_id=1, source_target_pairs={{0,1},{1,0},{2,3},{3,2},{4,5},{5,4},{6,7},{7,6},{8,9},{9,8},{10,11... | collective-permute-start | bytes 3145736 | tf_op jit(solution)/shard_map/ppermute | solution.py:175
  8.3 12.5 %all-to-all-start = ((bf16[16,2,321]{2,1,0:T(2,128)(2,1)}), bf16[16,2,321]{2,1,0:T(2,128)(2,1)S(1)}, u32[]{:S(2)}, u32[]{:S(2)}) async-start(bf16[16,2,321]{2,1,0:T(2,128)(2,1)} %reshape.101), calls=%async_computation | async-start | bytes 49152 | tf_op jit(solution)/shard_map/all_to_all | solution.py:197
  14.3 2.5 %copy-start.1 = (bf16[256,4096]{1,0:T(8,128)(2,1)S(1)}, bf16[256,4096]{1,0:T(8,128)(2,1)}, u32[]{:S(2)}) copy-start(bf16[256,4096]{1,0:T(8,128)(2,1)} %param.18) | copy-start | bytes 6291460
  16.7 6.2 %copy-start.2 = (bf16[1,512,256]{2,1,0:T(8,128)(2,1)S(1)}, bf16[1,512,256]{2,1,0:T(8,128)(2,1)}, u32[]{:S(2)}) copy-start(bf16[1,512,256]{2,1,0:T(8,128)(2,1)} %param.15) | copy-start | bytes 786436
  16.7 6.3 %copy-start.5 = (bf16[768,256]{1,0:T(8,128)(2,1)S(1)}, bf16[768,256]{1,0:T(8,128)(2,1)}, u32[]{:S(2)}) copy-start(bf16[768,256]{1,0:T(8,128)(2,1)} %param.20) | copy-start | bytes 1179652
  21.4 12.0 %collective-permute-start.1 = (bf16[4,80]{1,0:T(4,128)(2,1)S(1)}, bf16[4,80]{1,0:T(4,128)(2,1)S(1)}, u32[]{:S(2)}, u32[]{:S(2)}) collective-permute-start(bf16[4,80]{1,0:T(4,128)(2,1)S(1)} %get-tuple-element.24), channel_id=1, source_target_pairs={{1,0},{3,2},{5,4},{7,6},{9,8},{11,10},{13,12},{15,14},{17,16},{19,... | collective-permute-start | bytes 1928 | tf_op jit(solution)/shard_map/ppermute | solution.py:19
  23.5 11.3 %copy-start.14 = (f32[512]{0:T(512)S(1)}, f32[512]{0:T(512)}, u32[]{:S(2)}) copy-start(f32[512]{0:T(512)} %param.17) | copy-start | bytes 6148
  29.5 16.3 %collective-permute-start.3 = (bf16[256,2048]{1,0:T(8,128)(2,1)}, bf16[256,2048]{1,0:T(8,128)(2,1)}, u32[]{:S(2)}, u32[]{:S(2)}) collective-permute-start(bf16[256,2048]{1,0:T(8,128)(2,1)} %collective-permute-done.2), channel_id=1, source_target_pairs={{0,2},{2,0},{4,6},{6,4},{8,10},{10,8},{12,14},{14,12},{16,18},{18,... | collective-permute-start | bytes 3145736 | tf_op jit(solution)/shard_map/ppermute | solution.py:176
  29.7 4.9 %collective-permute-start = (bf16[4,80]{1,0:T(4,128)(2,1)S(1)}, bf16[4,80]{1,0:T(4,128)(2,1)S(1)}, u32[]{:S(2)}, u32[]{:S(2)}) collective-permute-start(bf16[4,80]{1,0:T(4,128)(2,1)S(1)} %get-tuple-element.25), channel_id=1, source_target_pairs={{0,1},{2,3},{4,5},{6,7},{8,9},{10,11},{12,13},{14,15},{16,17},{18,... | collective-permute-start | bytes 1928 | tf_op jit(solution)/shard_map/ppermute | solution.py:16
  60.9 4.7 %copy-start.3 = (f32[518,256]{1,0:T(8,128)}, f32[518,256]{1,0:T(8,128)S(1)}, u32[]{:S(2)}) copy-start(f32[518,256]{1,0:T(8,128)S(1)} %get-tuple-element.10) | copy-start | bytes 1591300
  65.8 0.9 copy-start.11
  67.8 2.8 %collective-permute-start.4 = (f32[1920,128]{1,0:T(8,128)S(1)}, f32[1920,128]{1,0:T(8,128)}, u32[]{:S(2)}, u32[]{:S(2)}) collective-permute-start(f32[1920,128]{1,0:T(8,128)S(1)} %constant_dynamic-slice_fusion.4), channel_id=1, source_target_pairs={{0,2},{2,0},{4,6},{6,4},{8,10},{10,8},{12,14},{14,12},{16,18},{18,... | collective-permute-start | bytes 2949128 | tf_op jit(solution)/shard_map/ppermute | solution.py:149
  72.0 15.0 %collective-permute-start.5 = (f32[960,128]{1,0:T(8,128)S(1)}, f32[960,128]{1,0:T(8,128)S(1)}, u32[]{:S(2)}, u32[]{:S(2)}) collective-permute-start(f32[960,128]{1,0:T(8,128)S(1)} %constant_dynamic-slice_fusion.3), channel_id=1, source_target_pairs={{0,1},{1,0},{2,3},{3,2},{4,5},{5,4},{6,7},{7,6},{8,9},{9,8},{10,11... | collective-permute-start | bytes 1474568 | tf_op jit(solution)/shard_map/ppermute | solution.py:149
  87.0 7.6 %collective-permute-start.6 = (f32[480,128]{1,0:T(8,128)S(1)}, f32[480,128]{1,0:T(8,128)S(1)}, u32[]{:S(2)}, u32[]{:S(2)}) collective-permute-start(f32[480,128]{1,0:T(8,128)S(1)} %constant_dynamic-slice_fusion.2), channel_id=1, source_target_pairs={{0,4},{2,6},{4,0},{6,2},{8,12},{10,14},{12,8},{14,10},{16,20},{18,... | collective-permute-start | bytes 737288 | tf_op jit(solution)/shard_map/ppermute | solution.py:149
  94.6 4.9 %collective-permute-start.7 = (f32[240,128]{1,0:T(8,128)S(1)}, f32[240,128]{1,0:T(8,128)S(1)}, u32[]{:S(2)}, u32[]{:S(2)}) collective-permute-start(f32[240,128]{1,0:T(8,128)S(1)} %constant_dynamic-slice_fusion.1), channel_id=1, source_target_pairs={{0,8},{2,10},{4,12},{6,14},{8,0},{10,2},{12,4},{14,6},{16,24},{18,... | collective-permute-start | bytes 368648 | tf_op jit(solution)/shard_map/ppermute | solution.py:149
  99.6 5.2 %collective-permute-start.8 = (f32[120,128]{1,0:T(8,128)S(1)}, f32[120,128]{1,0:T(8,128)S(1)}, u32[]{:S(2)}, u32[]{:S(2)}) collective-permute-start(f32[120,128]{1,0:T(8,128)S(1)} %constant_dynamic-slice_fusion), channel_id=1, source_target_pairs={{0,16},{2,18},{4,20},{6,22},{8,24},{10,26},{12,28},{14,30},{16,0},... | collective-permute-start | bytes 184328 | tf_op jit(solution)/shard_map/ppermute | solution.py:149
  104.8 5.3 %collective-permute-start.9 = (f32[120,128]{1,0:T(8,128)S(1)}, f32[120,128]{1,0:T(8,128)S(1)}, u32[]{:S(2)}, u32[]{:S(2)}) collective-permute-start(f32[120,128]{1,0:T(8,128)S(1)} %get-tuple-element.8), channel_id=1, source_target_pairs={{0,16},{2,18},{4,20},{6,22},{8,24},{10,26},{12,28},{14,30},{16,0},... | collective-permute-start | bytes 184328 | tf_op jit(solution)/shard_map/ppermute | solution.py:154
  110.1 6.4 %collective-permute-start.10 = (f32[240,128]{1,0:T(8,128)S(1)}, f32[240,128]{1,0:T(8,128)S(1)}, u32[]{:S(2)}, u32[]{:S(2)}) collective-permute-start(f32[240,128]{1,0:T(8,128)S(1)} %constant_dynamic-update-slice_fusion.10), channel_id=1, source_target_pairs={{0,8},{2,10},{4,12},{6,14},{8,0},{10,2},{12,4},{14,6},{16,24},{18,... | collective-permute-start | bytes 368648 | tf_op jit(solution)/shard_map/ppermute | solution.py:154
  116.6 6.3 %collective-permute-start.11 = (f32[480,128]{1,0:T(8,128)S(1)}, f32[480,128]{1,0:T(8,128)S(1)}, u32[]{:S(2)}, u32[]{:S(2)}) collective-permute-start(f32[480,128]{1,0:T(8,128)S(1)} %constant_dynamic-update-slice_fusion.8), channel_id=1, source_target_pairs={{0,4},{2,6},{4,0},{6,2},{8,12},{10,14},{12,8},{14,10},{16,20},{18,... | collective-permute-start | bytes 737288 | tf_op jit(solution)/shard_map/ppermute | solution.py:154
  118.2 13.7 %copy-start.4 = (f32[518,256]{1,0:T(8,128)S(1)}, f32[518,256]{1,0:T(8,128)}, u32[]{:S(2)}) copy-start(f32[518,256]{1,0:T(8,128)} %copy-done.3) | copy-start | bytes 1591300
  118.2 13.7 %copy-start.6 = (bf16[768,256]{1,0:T(8,128)(2,1)S(1)}, bf16[768,256]{1,0:T(8,128)(2,1)}, u32[]{:S(2)}) copy-start(bf16[768,256]{1,0:T(8,128)(2,1)} %param.20) | copy-start | bytes 1179652
  118.2 13.7 %copy-start.8 = (bf16[512,256]{1,0:T(8,128)(2,1)S(1)}, bf16[512,256]{1,0:T(8,128)(2,1)}, u32[]{:S(2)}) copy-start(bf16[512,256]{1,0:T(8,128)(2,1)} %copy-done.7) | copy-start | bytes 786436
  118.2 13.7 %copy-start.10 = (bf16[512,256]{1,0:T(8,128)(2,1)S(1)}, bf16[512,256]{1,0:T(8,128)(2,1)}, u32[]{:S(2)}) copy-start(bf16[512,256]{1,0:T(8,128)(2,1)} %copy-done.9) | copy-start | bytes 786436
  118.2 13.7 %copy-start.12 = (bf16[512,256]{1,0:T(8,128)(2,1)S(1)}, bf16[512,256]{1,0:T(8,128)(2,1)}, u32[]{:S(2)}) copy-start(bf16[512,256]{1,0:T(8,128)(2,1)} %copy-done.11) | copy-start | bytes 786436
  118.2 13.7 %copy-start.17 = (f32[256]{0:T(256)S(1)}, f32[256]{0:T(256)}, u32[]{:S(2)}) copy-start(f32[256]{0:T(256)} %param.21) | copy-start | bytes 3076
  122.9 8.9 %collective-permute-start.12 = (f32[960,128]{1,0:T(8,128)S(1)}, f32[960,128]{1,0:T(8,128)S(1)}, u32[]{:S(2)}, u32[]{:S(2)}) collective-permute-start(f32[960,128]{1,0:T(8,128)S(1)} %constant_dynamic-update-slice_fusion.6), channel_id=1, source_target_pairs={{0,1},{1,0},{2,3},{3,2},{4,5},{5,4},{6,7},{7,6},{8,9},{9,8},{10,11... | collective-permute-start | bytes 1474568 | tf_op jit(solution)/shard_map/ppermute | solution.py:154
  131.8 2.6 %collective-permute-start.13 = (f32[1920,128]{1,0:T(8,128)S(1)}, f32[1920,128]{1,0:T(8,128)S(1)}, u32[]{:S(2)}, u32[]{:S(2)}) collective-permute-start(f32[1920,128]{1,0:T(8,128)S(1)} %constant_dynamic-update-slice_fusion.4), channel_id=1, source_target_pairs={{0,2},{2,0},{4,6},{6,4},{8,10},{10,8},{12,14},{14,12},{16,18},{18,... | collective-permute-start | bytes 2949128 | tf_op jit(solution)/shard_map/ppermute | solution.py:154
  (3 other events, 2.2 us)

commit v4 on v3

--- a/solution.py
+++ b/solution.py
@@ -163,21 +163,45 @@
     return tuple(out)
 
 
-def gather_rows(w_ups):
+def ups_functions(w_ups):
     dp_size = lax.axis_size("dp")
     if lax.axis_size("tm") != 2 or dp_size % 2:
-        return lax.all_gather(w_ups, "tm", axis=0, tiled=True)
+        whole = lax.all_gather(w_ups, "tm", axis=0, tiled=True)
+        return (
+            lambda act: jnp.dot(act, whole, preferred_element_type=jnp.float32),
+            lambda d_taps: contract_cols(d_taps, whole),
+        )
     rows, width = w_ups.shape
     cols = width // 2
     core = lax.axis_index("dp") % 2
     tm = lax.axis_index("tm")
-    mine = lax.dynamic_slice_in_dim(w_ups, core * cols, cols, axis=1)
+    mine = jnp.where(core == 0, w_ups[:, :cols], w_ups[:, cols:])
     got = lax.ppermute(mine, "tm", [(0, 1), (1, 0)])
     partner = lax.ppermute(got, "dp", [(i, i ^ 1) for i in range(dp_size)])
-    whole = jnp.zeros((2 * rows, width), w_ups.dtype)
-    whole = lax.dynamic_update_slice(whole, w_ups, (tm * rows, 0))
-    whole = lax.dynamic_update_slice(whole, got, ((1 - tm) * rows, core * cols))
-    return lax.dynamic_update_slice(whole, partner, ((1 - tm) * rows, (1 - core) * cols))
+    low = jnp.where(core == 0, got, partner)
+    high = jnp.where(core == 0, partner, got)
+
+    def forward(act):
+        own_act = lax.dynamic_slice_in_dim(act, tm * rows, rows, axis=1)
+        other_act = lax.dynamic_slice_in_dim(act, (1 - tm) * rows, rows, axis=1)
+        own = jnp.dot(own_act, w_ups, preferred_element_type=jnp.float32)
+        other = jnp.concatenate(
+            [
+                jnp.dot(other_act, low, preferred_element_type=jnp.float32),
+                jnp.dot(other_act, high, preferred_element_type=jnp.float32),
+            ],
+            axis=1,
+        )
+        return own + other
+
+    def backward(d_taps):
+        own = contract_cols(d_taps, w_ups)
+        other = contract_cols(d_taps[:, :cols], low) + contract_cols(d_taps[:, cols:], high)
+        return jnp.where(
+            tm == 0, jnp.concatenate([own, other], axis=1), jnp.concatenate([other, own], axis=1)
+        )
+
+    return forward, backward
 
 
 def on_device(
@@ -210,13 +234,7 @@
     cot = cotangent[0]
     marks = jnp.repeat(keep_segs, cot.shape[0] // seg_count)
     gradient_value = jnp.where(marks[:, None] > 0, cot, jnp.zeros_like(cot))
-    whole = gather_rows(w_ups)
-
-    def ups_forward(act):
-        return jnp.dot(act, whole, preferred_element_type=jnp.float32)
-
-    def ups_backward(d_taps):
-        return contract_cols(d_taps, whole)
+    ups_forward, ups_backward = ups_functions(w_ups)
 
     output_rows, grads = local_pass(
         mel_ext,

time: 139 us -> 115 us (0.83)
  local copies, waits for them, and re-layouts: 37 us -> 12.9 us
  other arithmetic: 3.38 us -> 7.51 us
  matrix products: 9.6 us -> 6.45 us
    dynamic_update_slice x3 -> x0, local copies, waits for them, and re-layouts: 22.8 us -> none  [the longest x1 10.7 us: gather_rows(): whole = lax.dynamic_update_slice(whole, got, ((1 - tm) * rows, core * cols))]
    all_to_all x1, waiting for transfers between devices: 2.6 us -> 5.48 us  [on_device(): lax.all_to_all(outgoing, 'dp', split_axis=0, concat_axis=0, tiled=True)]
    broadcast_in_dim x1 -> x0, local copies, waits for them, and re-layouts: 2.46 us -> none  [gather_rows(): whole = jnp.zeros((2 * rows, width), w_ups.dtype)]
    dynamic_slice x1 -> x0, local copies, waits for them, and re-layouts: 2.37 us -> none  [gather_rows(): mine = lax.dynamic_slice_in_dim(w_ups, core * cols, cols, axis=1)]
    dot_general x2 -> x4, matrix products: 4.06 us -> 2.1 us  [contract_cols(): lax.dot_general(left, right, (((1,), (1,)), ((), ())), preferred_element_...]
    ppermute x2, waiting for transfers between devices: 5.85 us -> 3.96 us  [the longest x1 3.95 us: ups_functions(): got = lax.ppermute(mine, 'tm', [(0, 1), (1, 0)])]
    dot_general x1 -> x3, matrix products: 3.08 us -> 1.2 us  [the longest x1 0.5 us: forward(): own = jnp.dot(own_act, w_ups, preferred_element_type=jnp.float32)]
    select_n x0 -> x1, other arithmetic: none -> 1.76 us  [ups_functions(): mine = jnp.where(core == 0, w_ups[:, :cols], w_ups[:, cols:])]
  transfers between devices with their start and end apart: 15 -> 15, of which waited for: 13 -> 13; matrix products, arithmetic and copies ran while one was open for 15% -> 10% of each run, Pallas kernels for 0% -> 0%
where the time goes in v4:
time: 115 us
  waiting for transfers between devices  55.1 us (48%)
  starting transfers between devices  31.6 us (27%)
  local copies, waits for them, and re-layouts  12.9 us (11%)
  other arithmetic  7.51 us (7%)
  matrix products  6.45 us (6%)
  between operations  1.41 us (1%)
    ppermute x5, waiting for transfers between devices, butterfly_psum(): x = keep + lax.ppermute(send, axis, perm)  26 us
    ppermute x5, waiting for transfers between devices, butterfly_psum(): recv = lax.ppermute(x, axis, perm)  18.4 us
    ppermute x5, starting transfers between devices, butterfly_psum(): recv = lax.ppermute(x, axis, perm)  9.46 us
    ppermute x5, starting transfers between devices, butterfly_psum(): x = keep + lax.ppermute(send, axis, perm)  8.25 us
    all_to_all x1, starting transfers between devices, on_device(): lax.all_to_all(outgoing, 'dp', split_axis=0, concat_axis=0, tiled=True)  5.91 us
    all_to_all x1, waiting for transfers between devices, on_device(): lax.all_to_all(outgoing, 'dp', split_axis=0, concat_axis=0, tiled=True)  5.48 us
    unnamed x59, local copies, waits for them, and re-layouts  4.64 us
    ppermute x1, waiting for transfers between devices, ups_functions(): got = lax.ppermute(mine, 'tm', [(0, 1), (1, 0)])  3.95 us
  transfers between devices with their start and end apart: 15, of which 13 were waited for; matrix products, arithmetic and copies ran while one was open for 10% of the time, Pallas kernels for 0%

profile of v4, /device:TPU:0, one launch (start us, length us, event | category | flops | bytes accessed | tf_op | source)
XLA Modules:
  0.0 115.0 jit_solution(13931281202473461076)
XLA Ops:
  0.7 1.8 %slice_select_fusion = bf16[256,2048]{1,0:T(8,128)(2,1)S(1)} fusion(bf16[256,4096]{1,0:T(8,128)(2,1)} %param.18, pred[]{:T(512)S(6)} %eq.58), kind=kLoop, calls=%fused_computation.21 | loop fusion | flops 524288 | bytes 3145729 | tf_op jit(solution)/shard_map/jit(_where)/select_n | solution.py:178
  2.5 3.0 %collective-permute-start.2 = (bf16[256,2048]{1,0:T(8,128)(2,1)S(1)}, bf16[256,2048]{1,0:T(8,128)(2,1)S(1)}, u32[]{:S(2)}, u32[]{:S(2)}) collective-permute-start(bf16[256,2048]{1,0:T(8,128)(2,1)S(1)} %slice_select_fusion), channel_id=1, source_target_pairs={{0,1},{1,0},{2,3},{3,2},{4,5},{5,4},{6,7},{7,6},{8,9},{9,8},{10,11... | collective-permute-start | bytes 3145736 | tf_op jit(solution)/shard_map/ppermute | solution.py:179
  7.8 5.9 %all-to-all-start = ((bf16[16,2,321]{2,1,0:T(2,128)(2,1)}), bf16[16,2,321]{2,1,0:T(2,128)(2,1)S(1)}, u32[]{:S(2)}, u32[]{:S(2)}) async-start(bf16[16,2,321]{2,1,0:T(2,128)(2,1)} %reshape.101), calls=%async_computation | async-start | bytes 49152 | tf_op jit(solution)/shard_map/all_to_all | solution.py:221
  14.8 5.5 %all-to-all-done = bf16[16,2,321]{2,1,0:T(2,128)(2,1)S(1)} async-done(((bf16[16,2,321]{2,1,0:T(2,128)(2,1)}), bf16[16,2,321]{2,1,0:T(2,128)(2,1)S(1)}, u32[]{:S(2)}, u32[]{:S(2)}) %all-to-all-start) | async-done | bytes 20576 | tf_op jit(solution)/shard_map/all_to_all | solution.py:221
  20.8 1.3 %collective-permute-start.1 = (bf16[4,80]{1,0:T(4,128)(2,1)S(1)}, bf16[4,80]{1,0:T(4,128)(2,1)S(1)}, u32[]{:S(2)}, u32[]{:S(2)}) collective-permute-start(bf16[4,80]{1,0:T(4,128)(2,1)S(1)} %get-tuple-element.26), channel_id=1, source_target_pairs={{1,0},{3,2},{5,4},{7,6},{9,8},{11,10},{13,12},{15,14},{17,16},{19,... | collective-permute-start | bytes 1928 | tf_op jit(solution)/shard_map/ppermute | solution.py:19
  23.6 1.2 %fusion.53 = (f32[512,256]{1,0:T(8,128)}, f32[512,256]{1,0:T(8,128)}, f32[512,256]{1,0:T(8,128)}) fusion(f32[512,768]{1,0:T(8,128)S(1)} %fusion.51), kind=kLoop, calls=%fused_computation.119 | loop fusion | bytes 3145728 | tf_op jit(solution)/shard_map/slice | solution.py:102
  24.7 4.0 %collective-permute-done.2 = bf16[256,2048]{1,0:T(8,128)(2,1)S(1)} collective-permute-done((bf16[256,2048]{1,0:T(8,128)(2,1)S(1)}, bf16[256,2048]{1,0:T(8,128)(2,1)S(1)}, u32[]{:S(2)}, u32[]{:S(2)}) %collective-permute-start.2) | collective-permute-done | bytes 1048608 | tf_op jit(solution)/shard_map/ppermute | solution.py:179
  28.8 3.6 %collective-permute-start = (bf16[4,80]{1,0:T(4,128)(2,1)S(1)}, bf16[4,80]{1,0:T(4,128)(2,1)S(1)}, u32[]{:S(2)}, u32[]{:S(2)}) collective-permute-start(bf16[4,80]{1,0:T(4,128)(2,1)S(1)} %get-tuple-element.27), channel_id=1, source_target_pairs={{0,1},{2,3},{4,5},{6,7},{8,9},{10,11},{12,13},{14,15},{16,17},{18,... | collective-permute-start | bytes 1928 | tf_op jit(solution)/shard_map/ppermute | solution.py:16
  32.5 1.3 %collective-permute-done = bf16[4,80]{1,0:T(4,128)(2,1)S(1)} collective-permute-done((bf16[4,80]{1,0:T(4,128)(2,1)S(1)}, bf16[4,80]{1,0:T(4,128)(2,1)S(1)}, u32[]{:S(2)}, u32[]{:S(2)}) %collective-permute-start) | collective-permute-done | bytes 672 | tf_op jit(solution)/shard_map/ppermute | solution.py:16
  37.7 1.2 %copy-done.1 = bf16[256,4096]{1,0:T(8,128)(2,1)S(1)} copy-done((bf16[256,4096]{1,0:T(8,128)(2,1)S(1)}, bf16[256,4096]{1,0:T(8,128)(2,1)}, u32[]{:S(2)}) %copy-start.1) | copy-done | bytes 2097176
  45.9 2.7 %collective-permute-done.4 = f32[1920,128]{1,0:T(8,128)} collective-permute-done((f32[1920,128]{1,0:T(8,128)S(1)}, f32[1920,128]{1,0:T(8,128)}, u32[]{:S(2)}, u32[]{:S(2)}) %collective-permute-start.4) | collective-permute-done | bytes 983072 | tf_op jit(solution)/shard_map/ppermute | solution.py:149
  48.6 1.3 %dynamic-slice_add_fusion = f32[1920,128]{1,0:T(8,128)S(1)} fusion(f32[1920,128]{1,0:T(8,128)} %collective-permute-done.4, f32[3840,128]{1,0:T(8,128)S(1)} %fusion, s32[]{:T(128)S(6)} %select_n.179), kind=kLoop, calls=%fused_computation.24 | loop fusion | flops 245760 | bytes 2949124 | tf_op jit(solution)/shard_map/add | solution.py:149
  50.0 2.3 %collective-permute-start.5 = (f32[960,128]{1,0:T(8,128)S(1)}, f32[960,128]{1,0:T(8,128)S(1)}, u32[]{:S(2)}, u32[]{:S(2)}) collective-permute-start(f32[960,128]{1,0:T(8,128)S(1)} %constant_dynamic-slice_fusion.3), channel_id=1, source_target_pairs={{0,1},{1,0},{2,3},{3,2},{4,5},{5,4},{6,7},{7,6},{8,9},{9,8},{10,11... | collective-permute-start | bytes 1474568 | tf_op jit(solution)/shard_map/ppermute | solution.py:149
  52.3 11.5 %collective-permute-done.5 = f32[960,128]{1,0:T(8,128)S(1)} collective-permute-done((f32[960,128]{1,0:T(8,128)S(1)}, f32[960,128]{1,0:T(8,128)S(1)}, u32[]{:S(2)}, u32[]{:S(2)}) %collective-permute-start.5) | collective-permute-done | bytes 491552 | tf_op jit(solution)/shard_map/ppermute | solution.py:149
  63.9 1.6 %collective-permute-start.6 = (f32[480,128]{1,0:T(8,128)S(1)}, f32[480,128]{1,0:T(8,128)S(1)}, u32[]{:S(2)}, u32[]{:S(2)}) collective-permute-start(f32[480,128]{1,0:T(8,128)S(1)} %constant_dynamic-slice_fusion.2), channel_id=1, source_target_pairs={{0,4},{2,6},{4,0},{6,2},{8,12},{10,14},{12,8},{14,10},{16,20},{18,... | collective-permute-start | bytes 737288 | tf_op jit(solution)/shard_map/ppermute | solution.py:149
  65.5 6.0 %collective-permute-done.6 = f32[480,128]{1,0:T(8,128)S(1)} collective-permute-done((f32[480,128]{1,0:T(8,128)S(1)}, f32[480,128]{1,0:T(8,128)S(1)}, u32[]{:S(2)}, u32[]{:S(2)}) %collective-permute-start.6) | collective-permute-done | bytes 245792 | tf_op jit(solution)/shard_map/ppermute | solution.py:149
  71.5 1.6 %collective-permute-start.7 = (f32[240,128]{1,0:T(8,128)S(1)}, f32[240,128]{1,0:T(8,128)S(1)}, u32[]{:S(2)}, u32[]{:S(2)}) collective-permute-start(f32[240,128]{1,0:T(8,128)S(1)} %constant_dynamic-slice_fusion.1), channel_id=1, source_target_pairs={{0,8},{2,10},{4,12},{6,14},{8,0},{10,2},{12,4},{14,6},{16,24},{18,... | collective-permute-start | bytes 368648 | tf_op jit(solution)/shard_map/ppermute | solution.py:149
  73.2 3.3 %collective-permute-done.7 = f32[240,128]{1,0:T(8,128)S(1)} collective-permute-done((f32[240,128]{1,0:T(8,128)S(1)}, f32[240,128]{1,0:T(8,128)S(1)}, u32[]{:S(2)}, u32[]{:S(2)}) %collective-permute-start.7) | collective-permute-done | bytes 122912 | tf_op jit(solution)/shard_map/ppermute | solution.py:149
  76.5 2.7 %collective-permute-start.8 = (f32[120,128]{1,0:T(8,128)S(1)}, f32[120,128]{1,0:T(8,128)S(1)}, u32[]{:S(2)}, u32[]{:S(2)}) collective-permute-start(f32[120,128]{1,0:T(8,128)S(1)} %constant_dynamic-slice_fusion), channel_id=1, source_target_pairs={{0,16},{2,18},{4,20},{6,22},{8,24},{10,26},{12,28},{14,30},{16,0},... | collective-permute-start | bytes 184328 | tf_op jit(solution)/shard_map/ppermute | solution.py:149
  79.1 2.5 %collective-permute-done.8 = f32[120,128]{1,0:T(8,128)S(1)} collective-permute-done((f32[120,128]{1,0:T(8,128)S(1)}, f32[120,128]{1,0:T(8,128)S(1)}, u32[]{:S(2)}, u32[]{:S(2)}) %collective-permute-start.8) | collective-permute-done | bytes 61472 | tf_op jit(solution)/shard_map/ppermute | solution.py:149
  81.7 2.7 %collective-permute-start.9 = (f32[120,128]{1,0:T(8,128)S(1)}, f32[120,128]{1,0:T(8,128)S(1)}, u32[]{:S(2)}, u32[]{:S(2)}) collective-permute-start(f32[120,128]{1,0:T(8,128)S(1)} %get-tuple-element.8), channel_id=1, source_target_pairs={{0,16},{2,18},{4,20},{6,22},{8,24},{10,26},{12,28},{14,30},{16,0},... | collective-permute-start | bytes 184328 | tf_op jit(solution)/shard_map/ppermute | solution.py:154
  84.4 2.6 %collective-permute-done.9 = f32[120,128]{1,0:T(8,128)S(1)} collective-permute-done((f32[120,128]{1,0:T(8,128)S(1)}, f32[120,128]{1,0:T(8,128)S(1)}, u32[]{:S(2)}, u32[]{:S(2)}) %collective-permute-start.9) | collective-permute-done | bytes 61472 | tf_op jit(solution)/shard_map/ppermute | solution.py:154
  87.0 3.6 %collective-permute-start.10 = (f32[240,128]{1,0:T(8,128)S(1)}, f32[240,128]{1,0:T(8,128)S(1)}, u32[]{:S(2)}, u32[]{:S(2)}) collective-permute-start(f32[240,128]{1,0:T(8,128)S(1)} %constant_dynamic-update-slice_fusion.10), channel_id=1, source_target_pairs={{0,8},{2,10},{4,12},{6,14},{8,0},{10,2},{12,4},{14,6},{16,24},{18,... | collective-permute-start | bytes 368648 | tf_op jit(solution)/shard_map/ppermute | solution.py:154
  90.6 2.8 %collective-permute-done.10 = f32[240,128]{1,0:T(8,128)S(1)} collective-permute-done((f32[240,128]{1,0:T(8,128)S(1)}, f32[240,128]{1,0:T(8,128)S(1)}, u32[]{:S(2)}, u32[]{:S(2)}) %collective-permute-start.10) | collective-permute-done | bytes 122912 | tf_op jit(solution)/shard_map/ppermute | solution.py:154
  93.5 1.6 %collective-permute-start.11 = (f32[480,128]{1,0:T(8,128)S(1)}, f32[480,128]{1,0:T(8,128)S(1)}, u32[]{:S(2)}, u32[]{:S(2)}) collective-permute-start(f32[480,128]{1,0:T(8,128)S(1)} %constant_dynamic-update-slice_fusion.8), channel_id=1, source_target_pairs={{0,4},{2,6},{4,0},{6,2},{8,12},{10,14},{12,8},{14,10},{16,20},{18,... | collective-permute-start | bytes 737288 | tf_op jit(solution)/shard_map/ppermute | solution.py:154
  95.2 4.6 %collective-permute-done.11 = f32[480,128]{1,0:T(8,128)S(1)} collective-permute-done((f32[480,128]{1,0:T(8,128)S(1)}, f32[480,128]{1,0:T(8,128)S(1)}, u32[]{:S(2)}, u32[]{:S(2)}) %collective-permute-start.11) | collective-permute-done | bytes 245792 | tf_op jit(solution)/shard_map/ppermute | solution.py:154
  99.7 1.6 %collective-permute-start.12 = (f32[960,128]{1,0:T(8,128)S(1)}, f32[960,128]{1,0:T(8,128)S(1)}, u32[]{:S(2)}, u32[]{:S(2)}) collective-permute-start(f32[960,128]{1,0:T(8,128)S(1)} %constant_dynamic-update-slice_fusion.6), channel_id=1, source_target_pairs={{0,1},{1,0},{2,3},{3,2},{4,5},{5,4},{6,7},{7,6},{8,9},{9,8},{10,11... | collective-permute-start | bytes 1474568 | tf_op jit(solution)/shard_map/ppermute | solution.py:154
  101.4 7.2 %collective-permute-done.12 = f32[960,128]{1,0:T(8,128)S(1)} collective-permute-done((f32[960,128]{1,0:T(8,128)S(1)}, f32[960,128]{1,0:T(8,128)S(1)}, u32[]{:S(2)}, u32[]{:S(2)}) %collective-permute-start.12) | collective-permute-done | bytes 491552 | tf_op jit(solution)/shard_map/ppermute | solution.py:154
  108.8 1.1 fusion.3
  110.1 1.2 %collective-permute-done.13 = f32[1920,128]{1,0:T(8,128)S(1)} collective-permute-done((f32[1920,128]{1,0:T(8,128)S(1)}, f32[1920,128]{1,0:T(8,128)S(1)}, u32[]{:S(2)}, u32[]{:S(2)}) %collective-permute-start.13) | collective-permute-done | bytes 983072 | tf_op jit(solution)/shard_map/ppermute | solution.py:154
  112.7 1.2 %reshape.96 = f32[560,512]{1,0:T(8,128)} reshape(f32[2240,128]{1,0:T(8,128)S(1)} %slice.160) | data formatting | bytes 2293760 | tf_op jit(solution)/shard_map/reshape | solution.py:161
  113.9 1.1 reshape.97
  (132 shorter events, 18.2 us)
Async XLA Ops:
  0.6 35.4 %copy-start = (bf16[560,512]{1,0:T(8,128)(2,1)S(1)}, bf16[560,512]{1,0:T(8,128)(2,1)}, u32[]{:S(2)}) copy-start(bf16[560,512]{1,0:T(8,128)(2,1)} %param.16) | copy-start | bytes 1720324
  0.6 4.9 %copy-start.23 = (s32[1,8]{1,0:T(1,128)S(1)}, s32[1,8]{1,0:T(1,128)}, u32[]{:S(2)}) copy-start(s32[1,8]{1,0:T(1,128)} %param.13) | copy-start | bytes 100
  0.7 5.0 %copy-start.24 = (s32[1,8]{1,0:T(1,128)S(1)}, s32[1,8]{1,0:T(1,128)}, u32[]{:S(2)}) copy-start(s32[1,8]{1,0:T(1,128)} %param.14) | copy-start | bytes 100
  0.7 5.1 %copy-start.21 = (s32[1,8]{1,0:T(1,128)S(1)}, s32[1,8]{1,0:T(1,128)}, u32[]{:S(2)}) copy-start(s32[1,8]{1,0:T(1,128)} %param.12) | copy-start | bytes 100
  0.7 5.1 %copy-start.16 = (bf16[1,8,640]{2,1,0:T(8,128)(2,1)S(1)}, bf16[1,8,640]{2,1,0:T(8,128)(2,1)}, u32[]{:S(2)}) copy-start(bf16[1,8,640]{2,1,0:T(8,128)(2,1)} %param.11) | copy-start | bytes 30724
  0.7 21.7 %copy-start.2 = (bf16[1,512,256]{2,1,0:T(8,128)(2,1)S(1)}, bf16[1,512,256]{2,1,0:T(8,128)(2,1)}, u32[]{:S(2)}) copy-start(bf16[1,512,256]{2,1,0:T(8,128)(2,1)} %param.15) | copy-start | bytes 786436
  0.7 22.4 %copy-start.8 = (bf16[768,256]{1,0:T(8,128)(2,1)S(1)}, bf16[768,256]{1,0:T(8,128)(2,1)}, u32[]{:S(2)}) copy-start(bf16[768,256]{1,0:T(8,128)(2,1)} %param.20) | copy-start | bytes 1179652
  2.5 26.2 %collective-permute-start.2 = (bf16[256,2048]{1,0:T(8,128)(2,1)S(1)}, bf16[256,2048]{1,0:T(8,128)(2,1)S(1)}, u32[]{:S(2)}, u32[]{:S(2)}) collective-permute-start(bf16[256,2048]{1,0:T(8,128)(2,1)S(1)} %slice_select_fusion), channel_id=1, source_target_pairs={{0,1},{1,0},{2,3},{3,2},{4,5},{5,4},{6,7},{7,6},{8,9},{9,8},{10,11... | collective-permute-start | bytes 3145736 | tf_op jit(solution)/shard_map/ppermute | solution.py:179
  7.8 12.5 %all-to-all-start = ((bf16[16,2,321]{2,1,0:T(2,128)(2,1)}), bf16[16,2,321]{2,1,0:T(2,128)(2,1)S(1)}, u32[]{:S(2)}, u32[]{:S(2)}) async-start(bf16[16,2,321]{2,1,0:T(2,128)(2,1)} %reshape.101), calls=%async_computation | async-start | bytes 49152 | tf_op jit(solution)/shard_map/all_to_all | solution.py:221
  20.8 11.7 %collective-permute-start.1 = (bf16[4,80]{1,0:T(4,128)(2,1)S(1)}, bf16[4,80]{1,0:T(4,128)(2,1)S(1)}, u32[]{:S(2)}, u32[]{:S(2)}) collective-permute-start(bf16[4,80]{1,0:T(4,128)(2,1)S(1)} %get-tuple-element.26), channel_id=1, source_target_pairs={{1,0},{3,2},{5,4},{7,6},{9,8},{11,10},{13,12},{15,14},{17,16},{19,... | collective-permute-start | bytes 1928 | tf_op jit(solution)/shard_map/ppermute | solution.py:19
  28.7 8.3 %collective-permute-start.3 = (bf16[256,2048]{1,0:T(8,128)(2,1)S(1)}, bf16[256,2048]{1,0:T(8,128)(2,1)S(1)}, u32[]{:S(2)}, u32[]{:S(2)}) collective-permute-start(bf16[256,2048]{1,0:T(8,128)(2,1)S(1)} %collective-permute-done.2), channel_id=1, source_target_pairs={{0,2},{2,0},{4,6},{6,4},{8,10},{10,8},{12,14},{14,12},{16,18},{18,... | collective-permute-start | bytes 3145736 | tf_op jit(solution)/shard_map/ppermute | solution.py:180
  28.8 4.9 %collective-permute-start = (bf16[4,80]{1,0:T(4,128)(2,1)S(1)}, bf16[4,80]{1,0:T(4,128)(2,1)S(1)}, u32[]{:S(2)}, u32[]{:S(2)}) collective-permute-start(bf16[4,80]{1,0:T(4,128)(2,1)S(1)} %get-tuple-element.27), channel_id=1, source_target_pairs={{0,1},{2,3},{4,5},{6,7},{8,9},{10,11},{12,13},{14,15},{16,17},{18,... | collective-permute-start | bytes 1928 | tf_op jit(solution)/shard_map/ppermute | solution.py:16
  37.3 1.6 %copy-start.1 = (bf16[256,4096]{1,0:T(8,128)(2,1)S(1)}, bf16[256,4096]{1,0:T(8,128)(2,1)}, u32[]{:S(2)}) copy-start(bf16[256,4096]{1,0:T(8,128)(2,1)} %param.18) | copy-start | bytes 6291460
  39.8 1.3 %copy-start.7 = (f32[512,256]{1,0:T(8,128)S(1)}, f32[512,256]{1,0:T(8,128)}, u32[]{:S(2)}) copy-start(f32[512,256]{1,0:T(8,128)} %get-tuple-element.15) | copy-start | bytes 1572868
  39.8 1.3 %copy-start.17 = (pred[518]{0:T(1024)(128)(4,1)S(1)}, pred[518]{0:T(1024)(128)(4,1)}, u32[]{:S(2)}) copy-start(pred[518]{0:T(1024)(128)(4,1)} %fusion.45) | copy-start | bytes 1558
  41.5 2.8 %copy-start.3 = (f32[518,256]{1,0:T(8,128)}, f32[518,256]{1,0:T(8,128)S(1)}, u32[]{:S(2)}) copy-start(f32[518,256]{1,0:T(8,128)S(1)} %get-tuple-element.12) | copy-start | bytes 1591300
  45.8 2.8 %collective-permute-start.4 = (f32[1920,128]{1,0:T(8,128)S(1)}, f32[1920,128]{1,0:T(8,128)}, u32[]{:S(2)}, u32[]{:S(2)}) collective-permute-start(f32[1920,128]{1,0:T(8,128)S(1)} %constant_dynamic-slice_fusion.4), channel_id=1, source_target_pairs={{0,2},{2,0},{4,6},{6,4},{8,10},{10,8},{12,14},{14,12},{16,18},{18,... | collective-permute-start | bytes 2949128 | tf_op jit(solution)/shard_map/ppermute | solution.py:149
  50.0 13.9 %collective-permute-start.5 = (f32[960,128]{1,0:T(8,128)S(1)}, f32[960,128]{1,0:T(8,128)S(1)}, u32[]{:S(2)}, u32[]{:S(2)}) collective-permute-start(f32[960,128]{1,0:T(8,128)S(1)} %constant_dynamic-slice_fusion.3), channel_id=1, source_target_pairs={{0,1},{1,0},{2,3},{3,2},{4,5},{5,4},{6,7},{7,6},{8,9},{9,8},{10,11... | collective-permute-start | bytes 1474568 | tf_op jit(solution)/shard_map/ppermute | solution.py:149
  63.9 7.6 %collective-permute-start.6 = (f32[480,128]{1,0:T(8,128)S(1)}, f32[480,128]{1,0:T(8,128)S(1)}, u32[]{:S(2)}, u32[]{:S(2)}) collective-permute-start(f32[480,128]{1,0:T(8,128)S(1)} %constant_dynamic-slice_fusion.2), channel_id=1, source_target_pairs={{0,4},{2,6},{4,0},{6,2},{8,12},{10,14},{12,8},{14,10},{16,20},{18,... | collective-permute-start | bytes 737288 | tf_op jit(solution)/shard_map/ppermute | solution.py:149
  71.5 4.9 %collective-permute-start.7 = (f32[240,128]{1,0:T(8,128)S(1)}, f32[240,128]{1,0:T(8,128)S(1)}, u32[]{:S(2)}, u32[]{:S(2)}) collective-permute-start(f32[240,128]{1,0:T(8,128)S(1)} %constant_dynamic-slice_fusion.1), channel_id=1, source_target_pairs={{0,8},{2,10},{4,12},{6,14},{8,0},{10,2},{12,4},{14,6},{16,24},{18,... | collective-permute-start | bytes 368648 | tf_op jit(solution)/shard_map/ppermute | solution.py:149
  76.5 5.2 %collective-permute-start.8 = (f32[120,128]{1,0:T(8,128)S(1)}, f32[120,128]{1,0:T(8,128)S(1)}, u32[]{:S(2)}, u32[]{:S(2)}) collective-permute-start(f32[120,128]{1,0:T(8,128)S(1)} %constant_dynamic-slice_fusion), channel_id=1, source_target_pairs={{0,16},{2,18},{4,20},{6,22},{8,24},{10,26},{12,28},{14,30},{16,0},... | collective-permute-start | bytes 184328 | tf_op jit(solution)/shard_map/ppermute | solution.py:149
  81.7 5.3 %collective-permute-start.9 = (f32[120,128]{1,0:T(8,128)S(1)}, f32[120,128]{1,0:T(8,128)S(1)}, u32[]{:S(2)}, u32[]{:S(2)}) collective-permute-start(f32[120,128]{1,0:T(8,128)S(1)} %get-tuple-element.8), channel_id=1, source_target_pairs={{0,16},{2,18},{4,20},{6,22},{8,24},{10,26},{12,28},{14,30},{16,0},... | collective-permute-start | bytes 184328 | tf_op jit(solution)/shard_map/ppermute | solution.py:154
  87.0 6.4 %collective-permute-start.10 = (f32[240,128]{1,0:T(8,128)S(1)}, f32[240,128]{1,0:T(8,128)S(1)}, u32[]{:S(2)}, u32[]{:S(2)}) collective-permute-start(f32[240,128]{1,0:T(8,128)S(1)} %constant_dynamic-update-slice_fusion.10), channel_id=1, source_target_pairs={{0,8},{2,10},{4,12},{6,14},{8,0},{10,2},{12,4},{14,6},{16,24},{18,... | collective-permute-start | bytes 368648 | tf_op jit(solution)/shard_map/ppermute | solution.py:154
  93.5 6.3 %collective-permute-start.11 = (f32[480,128]{1,0:T(8,128)S(1)}, f32[480,128]{1,0:T(8,128)S(1)}, u32[]{:S(2)}, u32[]{:S(2)}) collective-permute-start(f32[480,128]{1,0:T(8,128)S(1)} %constant_dynamic-update-slice_fusion.8), channel_id=1, source_target_pairs={{0,4},{2,6},{4,0},{6,2},{8,12},{10,14},{12,8},{14,10},{16,20},{18,... | collective-permute-start | bytes 737288 | tf_op jit(solution)/shard_map/ppermute | solution.py:154
  95.1 13.7 %copy-start.4 = (f32[518,256]{1,0:T(8,128)S(1)}, f32[518,256]{1,0:T(8,128)}, u32[]{:S(2)}) copy-start(f32[518,256]{1,0:T(8,128)} %copy-done.3) | copy-start | bytes 1591300
  95.1 13.7 %copy-start.9 = (bf16[768,256]{1,0:T(8,128)(2,1)S(1)}, bf16[768,256]{1,0:T(8,128)(2,1)}, u32[]{:S(2)}) copy-start(bf16[768,256]{1,0:T(8,128)(2,1)} %param.20) | copy-start | bytes 1179652
  95.1 13.7 %copy-start.11 = (bf16[512,256]{1,0:T(8,128)(2,1)S(1)}, bf16[512,256]{1,0:T(8,128)(2,1)}, u32[]{:S(2)}) copy-start(bf16[512,256]{1,0:T(8,128)(2,1)} %copy-done.10) | copy-start | bytes 786436
  95.1 13.7 %copy-start.13 = (bf16[512,256]{1,0:T(8,128)(2,1)S(1)}, bf16[512,256]{1,0:T(8,128)(2,1)}, u32[]{:S(2)}) copy-start(bf16[512,256]{1,0:T(8,128)(2,1)} %copy-done.12) | copy-start | bytes 786436
  95.1 13.7 %copy-start.15 = (bf16[512,256]{1,0:T(8,128)(2,1)S(1)}, bf16[512,256]{1,0:T(8,128)(2,1)}, u32[]{:S(2)}) copy-start(bf16[512,256]{1,0:T(8,128)(2,1)} %copy-done.14) | copy-start | bytes 786436
  95.1 13.7 %copy-start.22 = (f32[256]{0:T(256)S(1)}, f32[256]{0:T(256)}, u32[]{:S(2)}) copy-start(f32[256]{0:T(256)} %param.21) | copy-start | bytes 3076
  99.7 8.9 %collective-permute-start.12 = (f32[960,128]{1,0:T(8,128)S(1)}, f32[960,128]{1,0:T(8,128)S(1)}, u32[]{:S(2)}, u32[]{:S(2)}) collective-permute-start(f32[960,128]{1,0:T(8,128)S(1)} %constant_dynamic-update-slice_fusion.6), channel_id=1, source_target_pairs={{0,1},{1,0},{2,3},{3,2},{4,5},{5,4},{6,7},{7,6},{8,9},{9,8},{10,11... | collective-permute-start | bytes 1474568 | tf_op jit(solution)/shard_map/ppermute | solution.py:154
  108.7 2.6 %collective-permute-start.13 = (f32[1920,128]{1,0:T(8,128)S(1)}, f32[1920,128]{1,0:T(8,128)S(1)}, u32[]{:S(2)}, u32[]{:S(2)}) collective-permute-start(f32[1920,128]{1,0:T(8,128)S(1)} %constant_dynamic-update-slice_fusion.4), channel_id=1, source_target_pairs={{0,2},{2,0},{4,6},{6,4},{8,10},{10,8},{12,14},{14,12},{16,18},{18,... | collective-permute-start | bytes 2949128 | tf_op jit(solution)/shard_map/ppermute | solution.py:154
  (8 other events, 8.3 us)

commit v5 on v4

--- a/solution.py
+++ b/solution.py
@@ -133,35 +133,76 @@
 def butterfly_psum(parts):
     dp_size = lax.axis_size("dp")
     tm_size = lax.axis_size("tm")
-    steps = [("dp", 1)]
-    steps += [("tm", 1 << k) for k in range(tm_size.bit_length() - 1)]
-    steps += [("dp", 1 << k) for k in range(1, dp_size.bit_length() - 1)]
+    axes = ("dp", "tm")
+    later = [("tm", 1 << k) for k in range(tm_size.bit_length() - 1)]
+    later += [("dp", 1 << k) for k in range(1, dp_size.bit_length() - 1)]
+    swapped = list(later)
+    for i in range(0, len(swapped) - 1, 2):
+        swapped[i], swapped[i + 1] = swapped[i + 1], swapped[i]
+    sizes = {"dp": dp_size, "tm": tm_size}
+
+    def linear(idx):
+        return idx["dp"] * tm_size + idx["tm"]
+
+    def pairs(choice):
+        out = []
+        for d in range(dp_size):
+            for t in range(tm_size):
+                idx = {"dp": d, "tm": t}
+                axis, bit = choice(d % 2)
+                other = dict(idx)
+                other[axis] = idx[axis] ^ bit
+                out.append((linear(idx), linear(other)))
+        return out
+
+    core = lax.axis_index("dp") % 2
+    position = {"dp": lax.axis_index("dp"), "tm": lax.axis_index("tm")}
+
+    def upper_of(step):
+        a0, b0 = later[step]
+        a1, b1 = swapped[step]
+        return jnp.where(
+            core == 0, (position[a0] // b0) % 2, (position[a1] // b1) % 2
+        )
+
     flat = jnp.concatenate([p.reshape(-1) for p in parts])
     unit = 8 * 128 * dp_size * tm_size
     padded = -(-flat.shape[0] // unit) * unit
     x = jnp.pad(flat, (0, padded - flat.shape[0])).reshape(padded // 128, 128)
-    for axis, bit in steps:
+    halving = [None] + list(range(len(later) - 1))
+    for step in halving:
         half = x.shape[0] // 2
-        upper = (lax.axis_index(axis) // bit) % 2
+        if step is None:
+            upper = core
+            perm = [(i, i ^ tm_size) for i in range(dp_size * tm_size)]
+        else:
+            upper = upper_of(step)
+            perm = pairs(lambda c, s=step: (later if c == 0 else swapped)[s])
         send = lax.dynamic_slice_in_dim(x, (1 - upper) * half, half)
         keep = lax.dynamic_slice_in_dim(x, upper * half, half)
-        perm = [(i, i ^ bit) for i in range(lax.axis_size(axis))]
-        x = keep + lax.ppermute(send, axis, perm)
-    for axis, bit in reversed(steps):
+        x = keep + lax.ppermute(send, axes, perm)
+    if later:
+        last = len(later) - 1
+        perm = pairs(lambda c: (later if c == 0 else swapped)[last])
+        x = x + lax.ppermute(x, axes, perm)
+    for step in reversed(halving):
         rows = x.shape[0]
-        upper = (lax.axis_index(axis) // bit) % 2
-        perm = [(i, i ^ bit) for i in range(lax.axis_size(axis))]
-        recv = lax.ppermute(x, axis, perm)
-        both = jnp.zeros((2 * rows, 128), x.dtype)
-        both = lax.dynamic_update_slice_in_dim(both, x, upper * rows, 0)
-        x = lax.dynamic_update_slice_in_dim(both, recv, (1 - upper) * rows, 0)
+        if step is None:
+            upper = core
+            perm = [(i, i ^ tm_size) for i in range(dp_size * tm_size)]
+        else:
+            upper = upper_of(step)
+            perm = pairs(lambda c, s=step: (later if c == 0 else swapped)[s])
+        recv = lax.ppermute(x, axes, perm)
+        x = jnp.where(
+            upper == 0, jnp.concatenate([x, recv]), jnp.concatenate([recv, x])
+        )
     flat = x.reshape(-1)
     out, at = [], 0
     for p in parts:
         out.append(flat[at : at + p.size].reshape(p.shape))
         at += p.size
     return tuple(out)
-
 
 def ups_functions(w_ups):
     dp_size = lax.axis_size("dp")

time: 115 us -> 108 us (0.939)
  the two profiles are of different devices: /device:TPU:0 before, /device:TPU:31 now
where the time goes in v5:
time: 108 us
  waiting for transfers between devices  57.7 us (53%)
  starting transfers between devices  22.2 us (21%)
  local copies, waits for them, and re-layouts  12.4 us (11%)
  other arithmetic  7.83 us (7%)
  matrix products  6.5 us (6%)
  between operations  1.37 us (1%)
    ppermute x4, waiting for transfers between devices, butterfly_psum(): recv = lax.ppermute(x, axes, perm)  22.3 us
    ppermute x4, waiting for transfers between devices, butterfly_psum(): x = keep + lax.ppermute(send, axes, perm)  21.2 us
    ppermute x4, starting transfers between devices, butterfly_psum(): recv = lax.ppermute(x, axes, perm)  7.48 us
    all_to_all x1, starting transfers between devices, on_device(): lax.all_to_all(outgoing, 'dp', split_axis=0, concat_axis=0, tiled=True)  6.61 us
    ppermute x1, waiting for transfers between devices, ups_functions(): got = lax.ppermute(mine, 'tm', [(0, 1), (1, 0)])  6.21 us
    unnamed x59, local copies, waits for them, and re-layouts  4.65 us
    ppermute x1, waiting for transfers between devices, butterfly_psum(): x = x + lax.ppermute(x, axes, perm)  3.72 us
    ppermute x1, starting transfers between devices, with_halo(): lax.ppermute(lax.slice_in_dim(block, 0, width, axis=dim), axis, backward)  3.14 us
  transfers between devices with their start and end apart: 14, of which 12 were waited for; matrix products, arithmetic and copies ran while one was open for 10% of the time, Pallas kernels for 0%

profile of v5, /device:TPU:31, one launch (start us, length us, event | category | flops | bytes accessed | tf_op | source)
XLA Modules:
  0.0 107.9 jit_solution(5292378377395293067)
XLA Ops:
  0.7 1.8 %slice_select_fusion = bf16[256,2048]{1,0:T(8,128)(2,1)S(1)} fusion(bf16[256,4096]{1,0:T(8,128)(2,1)} %param.18, pred[]{:T(512)S(6)} %eq.77), kind=kLoop, calls=%fused_computation.22 | loop fusion | flops 524288 | bytes 3145729 | tf_op jit(solution)/shard_map/jit(_where)/select_n | solution.py:219
  4.4 0.7 reshape.101
  5.1 6.6 %all-to-all-start = ((bf16[16,2,321]{2,1,0:T(2,128)(2,1)}), bf16[16,2,321]{2,1,0:T(2,128)(2,1)S(1)}, u32[]{:S(2)}, u32[]{:S(2)}) async-start(bf16[16,2,321]{2,1,0:T(2,128)(2,1)} %reshape.101), calls=%async_computation | async-start | bytes 49152 | tf_op jit(solution)/shard_map/all_to_all | solution.py:262
  12.8 1.3 %all-to-all-done = bf16[16,2,321]{2,1,0:T(2,128)(2,1)S(1)} async-done(((bf16[16,2,321]{2,1,0:T(2,128)(2,1)}), bf16[16,2,321]{2,1,0:T(2,128)(2,1)S(1)}, u32[]{:S(2)}, u32[]{:S(2)}) %all-to-all-start) | async-done | bytes 20576 | tf_op jit(solution)/shard_map/all_to_all | solution.py:262
  14.6 3.1 %collective-permute-start.1 = (bf16[4,80]{1,0:T(4,128)(2,1)S(1)}, bf16[4,80]{1,0:T(4,128)(2,1)S(1)}, u32[]{:S(2)}, u32[]{:S(2)}) collective-permute-start(bf16[4,80]{1,0:T(4,128)(2,1)S(1)} %get-tuple-element.24), channel_id=1, source_target_pairs={{1,0},{3,2},{5,4},{7,6},{9,8},{11,10},{13,12},{15,14},{17,16},{19,... | collective-permute-start | bytes 1928 | tf_op jit(solution)/shard_map/ppermute | solution.py:19
  18.0 0.7 convert_reduce_fusion.1
  19.2 1.2 %fusion.53 = (f32[512,256]{1,0:T(8,128)}, f32[512,256]{1,0:T(8,128)}, f32[512,256]{1,0:T(8,128)}) fusion(f32[512,768]{1,0:T(8,128)S(1)} %fusion.51), kind=kLoop, calls=%fused_computation.111 | loop fusion | bytes 3145728 | tf_op jit(solution)/shard_map/slice | solution.py:102
  20.4 6.2 %collective-permute-done.2 = bf16[256,2048]{1,0:T(8,128)(2,1)S(1)} collective-permute-done((bf16[256,2048]{1,0:T(8,128)(2,1)S(1)}, bf16[256,2048]{1,0:T(8,128)(2,1)S(1)}, u32[]{:S(2)}, u32[]{:S(2)}) %collective-permute-start.2) | collective-permute-done | bytes 1048608 | tf_op jit(solution)/shard_map/ppermute | solution.py:220
  26.6 1.5 %collective-permute-start.3 = (bf16[256,2048]{1,0:T(8,128)(2,1)S(1)}, bf16[256,2048]{1,0:T(8,128)(2,1)S(1)}, u32[]{:S(2)}, u32[]{:S(2)}) collective-permute-start(bf16[256,2048]{1,0:T(8,128)(2,1)S(1)} %collective-permute-done.2), channel_id=1, source_target_pairs={{0,2},{2,0},{4,6},{6,4},{8,10},{10,8},{12,14},{14,12},{16,18},{18,... | collective-permute-start | bytes 3145736 | tf_op jit(solution)/shard_map/ppermute | solution.py:221
  28.3 1.3 %collective-permute-start = (bf16[4,80]{1,0:T(4,128)(2,1)S(1)}, bf16[4,80]{1,0:T(4,128)(2,1)S(1)}, u32[]{:S(2)}, u32[]{:S(2)}) collective-permute-start(bf16[4,80]{1,0:T(4,128)(2,1)S(1)} %get-tuple-element.25), channel_id=1, source_target_pairs={{0,1},{2,3},{4,5},{6,7},{8,9},{10,11},{12,13},{14,15},{16,17},{18,... | collective-permute-start | bytes 1928 | tf_op jit(solution)/shard_map/ppermute | solution.py:16
  29.6 3.0 %collective-permute-done = bf16[4,80]{1,0:T(4,128)(2,1)S(1)} collective-permute-done((bf16[4,80]{1,0:T(4,128)(2,1)S(1)}, bf16[4,80]{1,0:T(4,128)(2,1)S(1)}, u32[]{:S(2)}, u32[]{:S(2)}) %collective-permute-start) | collective-permute-done | bytes 672 | tf_op jit(solution)/shard_map/ppermute | solution.py:16
  32.6 0.7 pad_maximum_fusion.3
  33.9 0.9 concatenate.72
  34.9 0.9 fusion.24
  36.5 1.2 %copy-done.1 = bf16[256,4096]{1,0:T(8,128)(2,1)S(1)} copy-done((bf16[256,4096]{1,0:T(8,128)(2,1)S(1)}, bf16[256,4096]{1,0:T(8,128)(2,1)}, u32[]{:S(2)}) %copy-start.1) | copy-done | bytes 2097176
  38.8 0.8 copy-done.5
  40.7 0.8 fusion.57
  44.7 1.2 %collective-permute-start.4 = (f32[1920,128]{1,0:T(8,128)S(1)}, f32[1920,128]{1,0:T(8,128)}, u32[]{:S(2)}, u32[]{:S(2)}) collective-permute-start(f32[1920,128]{1,0:T(8,128)S(1)} %constant_dynamic-slice_fusion.3), channel_id=1, source_target_pairs={{0,2},{1,3},{2,0},{3,1},{4,6},{5,7},{6,4},{7,5},{8,10},{9,11},{10,... | collective-permute-start | bytes 2949128 | tf_op jit(solution)/shard_map/ppermute | solution.py:183
  45.9 2.3 %collective-permute-done.4 = f32[1920,128]{1,0:T(8,128)} collective-permute-done((f32[1920,128]{1,0:T(8,128)S(1)}, f32[1920,128]{1,0:T(8,128)}, u32[]{:S(2)}, u32[]{:S(2)}) %collective-permute-start.4) | collective-permute-done | bytes 983072 | tf_op jit(solution)/shard_map/ppermute | solution.py:183
  48.3 1.3 %dynamic-slice_add_fusion = f32[1920,128]{1,0:T(8,128)S(1)} fusion(f32[1920,128]{1,0:T(8,128)} %collective-permute-done.4, f32[3840,128]{1,0:T(8,128)S(1)} %fusion, s32[]{:T(128)S(6)} %select_n.229), kind=kLoop, calls=%fused_computation.26 | loop fusion | flops 245760 | bytes 2949124 | tf_op jit(solution)/shard_map/add | solution.py:183
  49.9 7.7 %collective-permute-done.5 = f32[960,128]{1,0:T(8,128)S(1)} collective-permute-done((f32[960,128]{1,0:T(8,128)S(1)}, f32[960,128]{1,0:T(8,128)S(1)}, u32[]{:S(2)}, u32[]{:S(2)}) %collective-permute-start.5) | collective-permute-done | bytes 491552 | tf_op jit(solution)/shard_map/ppermute | solution.py:183
  57.9 5.3 %collective-permute-done.6 = f32[480,128]{1,0:T(8,128)S(1)} collective-permute-done((f32[480,128]{1,0:T(8,128)S(1)}, f32[480,128]{1,0:T(8,128)S(1)}, u32[]{:S(2)}, u32[]{:S(2)}) %collective-permute-start.6) | collective-permute-done | bytes 245792 | tf_op jit(solution)/shard_map/ppermute | solution.py:183
  63.3 5.9 %collective-permute-done.7 = f32[240,128]{1,0:T(8,128)S(1)} collective-permute-done((f32[240,128]{1,0:T(8,128)S(1)}, f32[240,128]{1,0:T(8,128)S(1)}, u32[]{:S(2)}, u32[]{:S(2)}) %collective-permute-start.7) | collective-permute-done | bytes 122912 | tf_op jit(solution)/shard_map/ppermute | solution.py:183
  69.4 3.7 %collective-permute-done.8 = f32[240,128]{1,0:T(8,128)S(1)} collective-permute-done((f32[240,128]{1,0:T(8,128)S(1)}, f32[240,128]{1,0:T(8,128)S(1)}, u32[]{:S(2)}, u32[]{:S(2)}) %collective-permute-start.8) | collective-permute-done | bytes 122912 | tf_op jit(solution)/shard_map/ppermute | solution.py:187
  73.2 6.1 %collective-permute-done.9 = f32[240,128]{1,0:T(8,128)S(1)} collective-permute-done((f32[240,128]{1,0:T(8,128)S(1)}, f32[240,128]{1,0:T(8,128)S(1)}, u32[]{:S(2)}, u32[]{:S(2)}) %collective-permute-start.9) | collective-permute-done | bytes 122912 | tf_op jit(solution)/shard_map/ppermute | solution.py:196
  79.4 5.0 %collective-permute-done.10 = f32[480,128]{1,0:T(8,128)S(1)} collective-permute-done((f32[480,128]{1,0:T(8,128)S(1)}, f32[480,128]{1,0:T(8,128)S(1)}, u32[]{:S(2)}, u32[]{:S(2)}) %collective-permute-start.10) | collective-permute-done | bytes 245792 | tf_op jit(solution)/shard_map/ppermute | solution.py:196
  84.8 10.0 %collective-permute-done.11 = f32[960,128]{1,0:T(8,128)S(1)} collective-permute-done((f32[960,128]{1,0:T(8,128)S(1)}, f32[960,128]{1,0:T(8,128)S(1)}, u32[]{:S(2)}, u32[]{:S(2)}) %collective-permute-start.11) | collective-permute-done | bytes 491552 | tf_op jit(solution)/shard_map/ppermute | solution.py:196
  94.9 7.0 %collective-permute-start.12 = (f32[1920,128]{1,0:T(8,128)S(1)}, f32[1920,128]{1,0:T(8,128)S(1)}, u32[]{:S(2)}, u32[]{:S(2)}) collective-permute-start(f32[1920,128]{1,0:T(8,128)S(1)} %maximum_select_fusion.1), channel_id=1, source_target_pairs={{0,2},{1,3},{2,0},{3,1},{4,6},{5,7},{6,4},{7,5},{8,10},{9,11},{10,... | collective-permute-start | bytes 2949128 | tf_op jit(solution)/shard_map/ppermute | solution.py:196
  102.0 1.1 %fusion.3 = bf16[1,512,256]{2,1,0:T(8,128)(2,1)} fusion(bf16[768,256]{1,0:T(8,128)(2,1)S(1)} %copy-done.9, f32[518,256]{1,0:T(8,128)S(1)} %copy-done.4, bf16[512,256]{1,0:T(8,128)(2,1)S(1)} %copy-done.13, bf16[512,256]{1,0:T(8,128)(2,1)S(1)} %copy-done.15, bf16[512,256]{1,0:T(8,128)(2,1)S(1)} %copy-done.11, f32[256]{0:T(256)S(1)} %copy-done.22), kind=kOutput, calls=%fused_computation.12 | convolution fusion | flops 204079104 | bytes 1967104 | tf_op jit(solution)/shard_map/dot_general | solution.py:92
  103.1 1.1 collective-permute-done.12
  105.6 1.2 %reshape.96 = f32[560,512]{1,0:T(8,128)} reshape(f32[2240,128]{1,0:T(8,128)S(1)} %slice.160) | data formatting | bytes 2293760 | tf_op jit(solution)/shard_map/reshape | solution.py:203
  106.8 1.1 %reshape.97 = f32[768,256]{1,0:T(8,128)} reshape(f32[1536,128]{1,0:T(8,128)S(1)} %slice.162) | data formatting | bytes 1572864 | tf_op jit(solution)/shard_map/reshape | solution.py:203
  (119 shorter events, 13.6 us)
Async XLA Ops:
  0.6 34.2 %copy-start = (bf16[560,512]{1,0:T(8,128)(2,1)S(1)}, bf16[560,512]{1,0:T(8,128)(2,1)}, u32[]{:S(2)}) copy-start(bf16[560,512]{1,0:T(8,128)(2,1)} %param.16) | copy-start | bytes 1720324
  0.6 2.1 %copy-start.23 = (s32[1,8]{1,0:T(1,128)S(1)}, s32[1,8]{1,0:T(1,128)}, u32[]{:S(2)}) copy-start(s32[1,8]{1,0:T(1,128)} %param.13) | copy-start | bytes 100
  0.7 2.2 %copy-start.24 = (s32[1,8]{1,0:T(1,128)S(1)}, s32[1,8]{1,0:T(1,128)}, u32[]{:S(2)}) copy-start(s32[1,8]{1,0:T(1,128)} %param.14) | copy-start | bytes 100
  0.7 2.3 %copy-start.21 = (s32[1,8]{1,0:T(1,128)S(1)}, s32[1,8]{1,0:T(1,128)}, u32[]{:S(2)}) copy-start(s32[1,8]{1,0:T(1,128)} %param.12) | copy-start | bytes 100
  0.7 2.3 %copy-start.16 = (bf16[1,8,640]{2,1,0:T(8,128)(2,1)S(1)}, bf16[1,8,640]{2,1,0:T(8,128)(2,1)}, u32[]{:S(2)}) copy-start(bf16[1,8,640]{2,1,0:T(8,128)(2,1)} %param.11) | copy-start | bytes 30724
  0.7 17.4 %copy-start.2 = (bf16[1,512,256]{2,1,0:T(8,128)(2,1)S(1)}, bf16[1,512,256]{2,1,0:T(8,128)(2,1)}, u32[]{:S(2)}) copy-start(bf16[1,512,256]{2,1,0:T(8,128)(2,1)} %param.15) | copy-start | bytes 786436
  0.7 18.1 %copy-start.8 = (bf16[768,256]{1,0:T(8,128)(2,1)S(1)}, bf16[768,256]{1,0:T(8,128)(2,1)}, u32[]{:S(2)}) copy-start(bf16[768,256]{1,0:T(8,128)(2,1)} %param.20) | copy-start | bytes 1179652
  2.5 24.1 %collective-permute-start.2 = (bf16[256,2048]{1,0:T(8,128)(2,1)S(1)}, bf16[256,2048]{1,0:T(8,128)(2,1)S(1)}, u32[]{:S(2)}, u32[]{:S(2)}) collective-permute-start(bf16[256,2048]{1,0:T(8,128)(2,1)S(1)} %slice_select_fusion), channel_id=1, source_target_pairs={{0,1},{1,0},{2,3},{3,2},{4,5},{5,4},{6,7},{7,6},{8,9},{9,8},{10,11... | collective-permute-start | bytes 3145736 | tf_op jit(solution)/shard_map/ppermute | solution.py:220
  5.1 9.0 %all-to-all-start = ((bf16[16,2,321]{2,1,0:T(2,128)(2,1)}), bf16[16,2,321]{2,1,0:T(2,128)(2,1)S(1)}, u32[]{:S(2)}, u32[]{:S(2)}) async-start(bf16[16,2,321]{2,1,0:T(2,128)(2,1)} %reshape.101), calls=%async_computation | async-start | bytes 49152 | tf_op jit(solution)/shard_map/all_to_all | solution.py:262
  14.6 15.0 %collective-permute-start.1 = (bf16[4,80]{1,0:T(4,128)(2,1)S(1)}, bf16[4,80]{1,0:T(4,128)(2,1)S(1)}, u32[]{:S(2)}, u32[]{:S(2)}) collective-permute-start(bf16[4,80]{1,0:T(4,128)(2,1)S(1)} %get-tuple-element.24), channel_id=1, source_target_pairs={{1,0},{3,2},{5,4},{7,6},{9,8},{11,10},{13,12},{15,14},{17,16},{19,... | collective-permute-start | bytes 1928 | tf_op jit(solution)/shard_map/ppermute | solution.py:19
  26.6 9.2 %collective-permute-start.3 = (bf16[256,2048]{1,0:T(8,128)(2,1)S(1)}, bf16[256,2048]{1,0:T(8,128)(2,1)S(1)}, u32[]{:S(2)}, u32[]{:S(2)}) collective-permute-start(bf16[256,2048]{1,0:T(8,128)(2,1)S(1)} %collective-permute-done.2), channel_id=1, source_target_pairs={{0,2},{2,0},{4,6},{6,4},{8,10},{10,8},{12,14},{14,12},{16,18},{18,... | collective-permute-start | bytes 3145736 | tf_op jit(solution)/shard_map/ppermute | solution.py:221
  28.3 4.3 %collective-permute-start = (bf16[4,80]{1,0:T(4,128)(2,1)S(1)}, bf16[4,80]{1,0:T(4,128)(2,1)S(1)}, u32[]{:S(2)}, u32[]{:S(2)}) collective-permute-start(bf16[4,80]{1,0:T(4,128)(2,1)S(1)} %get-tuple-element.25), channel_id=1, source_target_pairs={{0,1},{2,3},{4,5},{6,7},{8,9},{10,11},{12,13},{14,15},{16,17},{18,... | collective-permute-start | bytes 1928 | tf_op jit(solution)/shard_map/ppermute | solution.py:16
  36.2 1.6 %copy-start.1 = (bf16[256,4096]{1,0:T(8,128)(2,1)S(1)}, bf16[256,4096]{1,0:T(8,128)(2,1)}, u32[]{:S(2)}) copy-start(bf16[256,4096]{1,0:T(8,128)(2,1)} %param.18) | copy-start | bytes 6291460
  38.7 1.3 %copy-start.7 = (f32[512,256]{1,0:T(8,128)S(1)}, f32[512,256]{1,0:T(8,128)}, u32[]{:S(2)}) copy-start(f32[512,256]{1,0:T(8,128)} %get-tuple-element.13) | copy-start | bytes 1572868
  38.7 1.3 %copy-start.17 = (pred[518]{0:T(1024)(128)(4,1)S(1)}, pred[518]{0:T(1024)(128)(4,1)}, u32[]{:S(2)}) copy-start(pred[518]{0:T(1024)(128)(4,1)} %fusion.42) | copy-start | bytes 1558
  38.7 1.3 %copy-start.20 = (f32[256]{0:T(256)S(1)}, f32[256]{0:T(256)}, u32[]{:S(2)}) copy-start(f32[256]{0:T(256)} %param.19) | copy-start | bytes 3076
  40.3 2.9 %copy-start.3 = (f32[518,256]{1,0:T(8,128)}, f32[518,256]{1,0:T(8,128)S(1)}, u32[]{:S(2)}) copy-start(f32[518,256]{1,0:T(8,128)S(1)} %get-tuple-element.10) | copy-start | bytes 1591300
  44.7 3.5 %collective-permute-start.4 = (f32[1920,128]{1,0:T(8,128)S(1)}, f32[1920,128]{1,0:T(8,128)}, u32[]{:S(2)}, u32[]{:S(2)}) collective-permute-start(f32[1920,128]{1,0:T(8,128)S(1)} %constant_dynamic-slice_fusion.3), channel_id=1, source_target_pairs={{0,2},{1,3},{2,0},{3,1},{4,6},{5,7},{6,4},{7,5},{8,10},{9,11},{10,... | collective-permute-start | bytes 2949128 | tf_op jit(solution)/shard_map/ppermute | solution.py:183
  49.6 8.0 %collective-permute-start.5 = (f32[960,128]{1,0:T(8,128)S(1)}, f32[960,128]{1,0:T(8,128)S(1)}, u32[]{:S(2)}, u32[]{:S(2)}) collective-permute-start(f32[960,128]{1,0:T(8,128)S(1)} %constant_dynamic-slice_fusion.2), channel_id=1, source_target_pairs={{0,1},{1,0},{2,6},{3,7},{4,5},{5,4},{6,2},{7,3},{8,9},{9,8},{10,14... | collective-permute-start | bytes 1474568 | tf_op jit(solution)/shard_map/ppermute | solution.py:183
  57.8 5.4 %collective-permute-start.6 = (f32[480,128]{1,0:T(8,128)S(1)}, f32[480,128]{1,0:T(8,128)S(1)}, u32[]{:S(2)}, u32[]{:S(2)}) collective-permute-start(f32[480,128]{1,0:T(8,128)S(1)} %constant_dynamic-slice_fusion.1), channel_id=1, source_target_pairs={{0,4},{1,5},{2,3},{3,2},{4,0},{5,1},{6,7},{7,6},{8,12},{9,13},{10,... | collective-permute-start | bytes 737288 | tf_op jit(solution)/shard_map/ppermute | solution.py:183
  63.2 6.0 %collective-permute-start.7 = (f32[240,128]{1,0:T(8,128)S(1)}, f32[240,128]{1,0:T(8,128)S(1)}, u32[]{:S(2)}, u32[]{:S(2)}) collective-permute-start(f32[240,128]{1,0:T(8,128)S(1)} %constant_dynamic-slice_fusion), channel_id=1, source_target_pairs={{0,8},{1,9},{2,18},{3,19},{4,12},{5,13},{6,22},{7,23},{8,0},{9,1},... | collective-permute-start | bytes 368648 | tf_op jit(solution)/shard_map/ppermute | solution.py:183
  69.2 32.7 %copy-start.4 = (f32[518,256]{1,0:T(8,128)S(1)}, f32[518,256]{1,0:T(8,128)}, u32[]{:S(2)}) copy-start(f32[518,256]{1,0:T(8,128)} %copy-done.3) | copy-start | bytes 1591300
  69.2 32.7 %copy-start.9 = (bf16[768,256]{1,0:T(8,128)(2,1)S(1)}, bf16[768,256]{1,0:T(8,128)(2,1)}, u32[]{:S(2)}) copy-start(bf16[768,256]{1,0:T(8,128)(2,1)} %param.20) | copy-start | bytes 1179652
  69.3 32.7 %copy-start.11 = (bf16[512,256]{1,0:T(8,128)(2,1)S(1)}, bf16[512,256]{1,0:T(8,128)(2,1)}, u32[]{:S(2)}) copy-start(bf16[512,256]{1,0:T(8,128)(2,1)} %copy-done.10) | copy-start | bytes 786436
  69.3 32.7 %copy-start.13 = (bf16[512,256]{1,0:T(8,128)(2,1)S(1)}, bf16[512,256]{1,0:T(8,128)(2,1)}, u32[]{:S(2)}) copy-start(bf16[512,256]{1,0:T(8,128)(2,1)} %copy-done.12) | copy-start | bytes 786436
  69.3 32.7 %copy-start.15 = (bf16[512,256]{1,0:T(8,128)(2,1)S(1)}, bf16[512,256]{1,0:T(8,128)(2,1)}, u32[]{:S(2)}) copy-start(bf16[512,256]{1,0:T(8,128)(2,1)} %copy-done.14) | copy-start | bytes 786436
  69.3 32.7 %copy-start.22 = (f32[256]{0:T(256)S(1)}, f32[256]{0:T(256)}, u32[]{:S(2)}) copy-start(f32[256]{0:T(256)} %param.21) | copy-start | bytes 3076
  69.3 3.8 %collective-permute-start.8 = (f32[240,128]{1,0:T(8,128)S(1)}, f32[240,128]{1,0:T(8,128)S(1)}, u32[]{:S(2)}, u32[]{:S(2)}) collective-permute-start(f32[240,128]{1,0:T(8,128)S(1)} %dynamic-slice_add_fusion.3), channel_id=1, source_target_pairs={{0,16},{1,17},{2,10},{3,11},{4,20},{5,21},{6,14},{7,15},{8,24},{9,... | collective-permute-start | bytes 368648 | tf_op jit(solution)/shard_map/ppermute | solution.py:187
  73.1 6.2 %collective-permute-start.9 = (f32[240,128]{1,0:T(8,128)S(1)}, f32[240,128]{1,0:T(8,128)S(1)}, u32[]{:S(2)}, u32[]{:S(2)}) collective-permute-start(f32[240,128]{1,0:T(8,128)S(1)} %add.210), channel_id=1, source_target_pairs={{0,8},{1,9},{2,18},{3,19},{4,12},{5,13},{6,22},{7,23},{8,0},{9,1},... | collective-permute-start | bytes 368648 | tf_op jit(solution)/shard_map/ppermute | solution.py:196
  79.4 5.1 %collective-permute-start.10 = (f32[480,128]{1,0:T(8,128)S(1)}, f32[480,128]{1,0:T(8,128)S(1)}, u32[]{:S(2)}, u32[]{:S(2)}) collective-permute-start(f32[480,128]{1,0:T(8,128)S(1)} %maximum_select_fusion.3), channel_id=1, source_target_pairs={{0,4},{1,5},{2,3},{3,2},{4,0},{5,1},{6,7},{7,6},{8,12},{9,13},{10,... | collective-permute-start | bytes 737288 | tf_op jit(solution)/shard_map/ppermute | solution.py:196
  84.5 10.3 %collective-permute-start.11 = (f32[960,128]{1,0:T(8,128)S(1)}, f32[960,128]{1,0:T(8,128)S(1)}, u32[]{:S(2)}, u32[]{:S(2)}) collective-permute-start(f32[960,128]{1,0:T(8,128)S(1)} %maximum_select_fusion.2), channel_id=1, source_target_pairs={{0,1},{1,0},{2,6},{3,7},{4,5},{5,4},{6,2},{7,3},{8,9},{9,8},{10,14... | collective-permute-start | bytes 1474568 | tf_op jit(solution)/shard_map/ppermute | solution.py:196
  94.9 9.2 %collective-permute-start.12 = (f32[1920,128]{1,0:T(8,128)S(1)}, f32[1920,128]{1,0:T(8,128)S(1)}, u32[]{:S(2)}, u32[]{:S(2)}) collective-permute-start(f32[1920,128]{1,0:T(8,128)S(1)} %maximum_select_fusion.1), channel_id=1, source_target_pairs={{0,2},{1,3},{2,0},{3,1},{4,6},{5,7},{6,4},{7,5},{8,10},{9,11},{10,... | collective-permute-start | bytes 2949128 | tf_op jit(solution)/shard_map/ppermute | solution.py:196
  (7 other events, 7.1 us)

commit v6 on v4

--- a/solution.py
+++ b/solution.py
@@ -133,35 +133,70 @@
 def butterfly_psum(parts):
     dp_size = lax.axis_size("dp")
     tm_size = lax.axis_size("tm")
-    steps = [("dp", 1)]
-    steps += [("tm", 1 << k) for k in range(tm_size.bit_length() - 1)]
-    steps += [("dp", 1 << k) for k in range(1, dp_size.bit_length() - 1)]
+    axes = ("dp", "tm")
+    levels = [("tm", 1 << k) for k in range(tm_size.bit_length() - 1)]
+    levels += [("dp", 1 << k) for k in range(1, dp_size.bit_length() - 1)]
+    groups = [levels[i : i + 2] for i in range(0, len(levels), 2)]
+    orders = (groups, groups[::-1])
+    count = dp_size * tm_size
+
+    def perm_of(step, offset):
+        out = []
+        for d in range(dp_size):
+            for t in range(tm_size):
+                idx = {"dp": d, "tm": t}
+                for j, (axis, bit) in enumerate(orders[d % 2][step]):
+                    if (offset >> j) & 1:
+                        idx[axis] = idx[axis] ^ bit
+                out.append((d * tm_size + t, idx["dp"] * tm_size + idx["tm"]))
+        return out
+
+    core = lax.axis_index("dp") % 2
+    position = {"dp": lax.axis_index("dp"), "tm": lax.axis_index("tm")}
+
+    def slot_of(step):
+        def one(group):
+            return sum(((position[a] // b) % 2) << j for j, (a, b) in enumerate(group))
+
+        return jnp.where(core == 0, one(orders[0][step]), one(orders[1][step]))
+
     flat = jnp.concatenate([p.reshape(-1) for p in parts])
-    unit = 8 * 128 * dp_size * tm_size
+    unit = 8 * 128 * count
     padded = -(-flat.shape[0] // unit) * unit
     x = jnp.pad(flat, (0, padded - flat.shape[0])).reshape(padded // 128, 128)
-    for axis, bit in steps:
-        half = x.shape[0] // 2
-        upper = (lax.axis_index(axis) // bit) % 2
-        send = lax.dynamic_slice_in_dim(x, (1 - upper) * half, half)
-        keep = lax.dynamic_slice_in_dim(x, upper * half, half)
-        perm = [(i, i ^ bit) for i in range(lax.axis_size(axis))]
-        x = keep + lax.ppermute(send, axis, perm)
-    for axis, bit in reversed(steps):
-        rows = x.shape[0]
-        upper = (lax.axis_index(axis) // bit) % 2
-        perm = [(i, i ^ bit) for i in range(lax.axis_size(axis))]
-        recv = lax.ppermute(x, axis, perm)
-        both = jnp.zeros((2 * rows, 128), x.dtype)
-        both = lax.dynamic_update_slice_in_dim(both, x, upper * rows, 0)
-        x = lax.dynamic_update_slice_in_dim(both, recv, (1 - upper) * rows, 0)
+    core_perm = [(i, i ^ tm_size) for i in range(count)]
+    half = x.shape[0] // 2
+    send = lax.dynamic_slice_in_dim(x, (1 - core) * half, half)
+    x = lax.dynamic_slice_in_dim(x, core * half, half) + lax.ppermute(send, axes, core_perm)
+    for step in range(len(groups)):
+        radix = 1 << len(groups[step])
+        piece = x.shape[0] // radix
+        slot = slot_of(step)
+        total = lax.dynamic_slice_in_dim(x, slot * piece, piece)
+        for offset in range(1, radix):
+            send = lax.dynamic_slice_in_dim(x, (slot ^ offset) * piece, piece)
+            total = total + lax.ppermute(send, axes, perm_of(step, offset))
+        x = total
+    for step in reversed(range(len(groups))):
+        radix = 1 << len(groups[step])
+        slot = slot_of(step)
+        got = [x] + [lax.ppermute(x, axes, perm_of(step, o)) for o in range(1, radix)]
+        pieces = []
+        for q in range(radix):
+            source = slot ^ q
+            chosen = got[radix - 1]
+            for o in range(radix - 2, -1, -1):
+                chosen = jnp.where(source == o, got[o], chosen)
+            pieces.append(chosen)
+        x = jnp.concatenate(pieces)
+    recv = lax.ppermute(x, axes, core_perm)
+    x = jnp.where(core == 0, jnp.concatenate([x, recv]), jnp.concatenate([recv, x]))
     flat = x.reshape(-1)
     out, at = [], 0
     for p in parts:
         out.append(flat[at : at + p.size].reshape(p.shape))
         at += p.size
     return tuple(out)
-
 
 def ups_functions(w_ups):
     dp_size = lax.axis_size("dp")

time: 115 us -> 108 us (0.939)
  waiting for transfers between devices: 55.1 us -> 45.2 us
  other arithmetic: 7.51 us -> 9.41 us
    ppermute x10 -> x14, waiting for transfers between devices: 44.4 us -> 25.6 us  [the longest x6 12.6 us: butterfly_psum(): total = total + lax.ppermute(send, axes, perm_of(step, offset))]
    ppermute x1, waiting for transfers between devices: 3.95 us -> 16.2 us  [ups_functions(): got = lax.ppermute(mine, 'tm', [(0, 1), (1, 0)])]
    all_to_all x1, waiting for transfers between devices: 5.48 us -> 2.13 us  [on_device(): lax.all_to_all(outgoing, 'dp', split_axis=0, concat_axis=0, tiled=True)]
    all_to_all x1, starting transfers between devices: 5.91 us -> 7.36 us  [on_device(): lax.all_to_all(outgoing, 'dp', split_axis=0, concat_axis=0, tiled=True)]
    ppermute x1, starting transfers between devices: 3.03 us -> 1.61 us  [ups_functions(): got = lax.ppermute(mine, 'tm', [(0, 1), (1, 0)])]
    unnamed x59 -> x55, local copies, waits for them, and re-layouts: 4.64 us -> 5.28 us
    ppermute x10 -> x14, starting transfers between devices: 17.7 us -> 18 us  [the longest x6 8.32 us: butterfly_psum(): lax.ppermute(x, axes, perm_of(step, o))]
  transfers between devices with their start and end apart: 15 -> 19, of which waited for: 13 -> 15; matrix products, arithmetic and copies ran while one was open for 10% -> 10% of each run, Pallas kernels for 0% -> 0%
where the time goes in v6:
time: 108 us
  waiting for transfers between devices  45.2 us (42%)
  starting transfers between devices  31.7 us (29%)
  local copies, waits for them, and re-layouts  13 us (12%)
  other arithmetic  9.41 us (9%)
  matrix products  7.18 us (7%)
  between operations  1.42 us (1%)
    ppermute x1, waiting for transfers between devices, ups_functions(): got = lax.ppermute(mine, 'tm', [(0, 1), (1, 0)])  16.2 us
    ppermute x6, waiting for transfers between devices, butterfly_psum(): total = total + lax.ppermute(send, axes, perm_of(step, offset))  12.6 us
    ppermute x6, waiting for transfers between devices, butterfly_psum(): lax.ppermute(x, axes, perm_of(step, o))  9.33 us
    ppermute x6, starting transfers between devices, butterfly_psum(): lax.ppermute(x, axes, perm_of(step, o))  8.32 us
    ppermute x6, starting transfers between devices, butterfly_psum(): total = total + lax.ppermute(send, axes, perm_of(step, offset))  7.98 us
    all_to_all x1, starting transfers between devices, on_device(): lax.all_to_all(outgoing, 'dp', split_axis=0, concat_axis=0, tiled=True)  7.36 us
    unnamed x55, local copies, waits for them, and re-layouts  5.28 us
    ppermute x1, starting transfers between devices, with_halo(): lax.ppermute(lax.slice_in_dim(block, block.shape[dim] - width, None, axis...  3.41 us
  transfers between devices with their start and end apart: 19, of which 15 were waited for; matrix products, arithmetic and copies ran while one was open for 10% of the time, Pallas kernels for 0%

profile of v6, /device:TPU:0, one launch (start us, length us, event | category | flops | bytes accessed | tf_op | source)
XLA Modules:
  0.0 107.9 jit_solution(10600037648119705495)
XLA Ops:
  5.1 7.4 %all-to-all-start = ((bf16[16,2,321]{2,1,0:T(2,128)(2,1)}), bf16[16,2,321]{2,1,0:T(2,128)(2,1)S(1)}, u32[]{:S(2)}, u32[]{:S(2)}) async-start(bf16[16,2,321]{2,1,0:T(2,128)(2,1)} %reshape.101), calls=%async_computation | async-start | bytes 49152 | tf_op jit(solution)/shard_map/all_to_all | solution.py:256
  12.4 1.7 %slice_select_fusion = bf16[256,2048]{1,0:T(8,128)(2,1)S(1)} fusion(bf16[256,4096]{1,0:T(8,128)(2,1)} %param.18, pred[]{:T(512)S(6)} %eq.142), kind=kLoop, calls=%fused_computation.21 | loop fusion | flops 524288 | bytes 3145729 | tf_op jit(solution)/shard_map/jit(_where)/select_n | solution.py:213
  14.1 1.6 %collective-permute-start.2 = (bf16[256,2048]{1,0:T(8,128)(2,1)S(1)}, bf16[256,2048]{1,0:T(8,128)(2,1)S(1)}, u32[]{:S(2)}, u32[]{:S(2)}) collective-permute-start(bf16[256,2048]{1,0:T(8,128)(2,1)S(1)} %slice_select_fusion), channel_id=1, source_target_pairs={{0,1},{1,0},{2,3},{3,2},{4,5},{5,4},{6,7},{7,6},{8,9},{9,8},{10,11... | collective-permute-start | bytes 3145736 | tf_op jit(solution)/shard_map/ppermute | solution.py:214
  16.9 2.1 %all-to-all-done = bf16[16,2,321]{2,1,0:T(2,128)(2,1)S(1)} async-done(((bf16[16,2,321]{2,1,0:T(2,128)(2,1)}), bf16[16,2,321]{2,1,0:T(2,128)(2,1)S(1)}, u32[]{:S(2)}, u32[]{:S(2)}) %all-to-all-start) | async-done | bytes 20576 | tf_op jit(solution)/shard_map/all_to_all | solution.py:256
  19.8 1.3 %collective-permute-start.1 = (bf16[4,80]{1,0:T(4,128)(2,1)S(1)}, bf16[4,80]{1,0:T(4,128)(2,1)S(1)}, u32[]{:S(2)}, u32[]{:S(2)}) collective-permute-start(bf16[4,80]{1,0:T(4,128)(2,1)S(1)} %get-tuple-element.44), channel_id=1, source_target_pairs={{1,0},{3,2},{5,4},{7,6},{9,8},{11,10},{13,12},{15,14},{17,16},{19,... | collective-permute-start | bytes 1928 | tf_op jit(solution)/shard_map/ppermute | solution.py:19
  22.3 1.2 %fusion.53 = (f32[512,256]{1,0:T(8,128)}, f32[512,256]{1,0:T(8,128)}, f32[512,256]{1,0:T(8,128)}) fusion(f32[512,768]{1,0:T(8,128)S(1)} %fusion.51), kind=kLoop, calls=%fused_computation.130 | loop fusion | bytes 3145728 | tf_op jit(solution)/shard_map/slice | solution.py:102
  23.5 16.2 %collective-permute-done.2 = bf16[256,2048]{1,0:T(8,128)(2,1)S(1)} collective-permute-done((bf16[256,2048]{1,0:T(8,128)(2,1)S(1)}, bf16[256,2048]{1,0:T(8,128)(2,1)S(1)}, u32[]{:S(2)}, u32[]{:S(2)}) %collective-permute-start.2) | collective-permute-done | bytes 1048608 | tf_op jit(solution)/shard_map/ppermute | solution.py:214
  39.8 3.4 %collective-permute-start = (bf16[4,80]{1,0:T(4,128)(2,1)S(1)}, bf16[4,80]{1,0:T(4,128)(2,1)S(1)}, u32[]{:S(2)}, u32[]{:S(2)}) collective-permute-start(bf16[4,80]{1,0:T(4,128)(2,1)S(1)} %get-tuple-element.45), channel_id=1, source_target_pairs={{0,1},{2,3},{4,5},{6,7},{8,9},{10,11},{12,13},{14,15},{16,17},{18,... | collective-permute-start | bytes 1928 | tf_op jit(solution)/shard_map/ppermute | solution.py:16
  43.2 1.3 %collective-permute-done = bf16[4,80]{1,0:T(4,128)(2,1)S(1)} collective-permute-done((bf16[4,80]{1,0:T(4,128)(2,1)S(1)}, bf16[4,80]{1,0:T(4,128)(2,1)S(1)}, u32[]{:S(2)}, u32[]{:S(2)}) %collective-permute-start) | collective-permute-done | bytes 672 | tf_op jit(solution)/shard_map/ppermute | solution.py:16
  48.4 1.2 %copy-done.1 = bf16[256,4096]{1,0:T(8,128)(2,1)S(1)} copy-done((bf16[256,4096]{1,0:T(8,128)(2,1)S(1)}, bf16[256,4096]{1,0:T(8,128)(2,1)}, u32[]{:S(2)}) %copy-start.1) | copy-done | bytes 2097176
  57.2 2.6 %collective-permute-done.4 = f32[1920,128]{1,0:T(8,128)} collective-permute-done((f32[1920,128]{1,0:T(8,128)S(1)}, f32[1920,128]{1,0:T(8,128)}, u32[]{:S(2)}, u32[]{:S(2)}) %collective-permute-start.4) | collective-permute-done | bytes 983072 | tf_op jit(solution)/shard_map/ppermute | solution.py:170
  59.8 1.3 %dynamic-slice_add_fusion = f32[1920,128]{1,0:T(8,128)S(1)} fusion(f32[1920,128]{1,0:T(8,128)} %collective-permute-done.4, f32[3840,128]{1,0:T(8,128)S(1)} %fusion, s32[]{:T(128)S(6)} %select_n.365), kind=kLoop, calls=%fused_computation.25 | loop fusion | flops 245760 | bytes 2949124 | tf_op jit(solution)/shard_map/add | solution.py:170
  61.2 2.3 %collective-permute-start.5 = (f32[480,128]{1,0:T(8,128)S(1)}, f32[480,128]{1,0:T(8,128)S(1)}, u32[]{:S(2)}, u32[]{:S(2)}) collective-permute-start(f32[480,128]{1,0:T(8,128)S(1)} %get-tuple-element.24), channel_id=1, source_target_pairs={{0,1},{1,0},{2,10},{3,11},{4,5},{5,4},{6,14},{7,15},{8,9},{9,8},{1... | collective-permute-start | bytes 737288 | tf_op jit(solution)/shard_map/ppermute | solution.py:178
  63.5 1.2 %collective-permute-start.7 = (f32[480,128]{1,0:T(8,128)S(1)}, f32[480,128]{1,0:T(8,128)S(1)}, u32[]{:S(2)}, u32[]{:S(2)}) collective-permute-start(f32[480,128]{1,0:T(8,128)S(1)} %get-tuple-element.25), channel_id=1, source_target_pairs={{0,5},{1,4},{2,26},{3,27},{4,1},{5,0},{6,30},{7,31},{8,13},{9,12},... | collective-permute-start | bytes 737288 | tf_op jit(solution)/shard_map/ppermute | solution.py:178
  65.2 4.7 %collective-permute-done.5 = f32[480,128]{1,0:T(8,128)S(1)} collective-permute-done((f32[480,128]{1,0:T(8,128)S(1)}, f32[480,128]{1,0:T(8,128)S(1)}, u32[]{:S(2)}, u32[]{:S(2)}) %collective-permute-start.5) | collective-permute-done | bytes 245792 | tf_op jit(solution)/shard_map/ppermute | solution.py:178
  70.6 1.4 %collective-permute-done.6 = f32[480,128]{1,0:T(8,128)S(1)} collective-permute-done((f32[480,128]{1,0:T(8,128)S(1)}, f32[480,128]{1,0:T(8,128)S(1)}, u32[]{:S(2)}, u32[]{:S(2)}) %collective-permute-start.6) | collective-permute-done | bytes 245792 | tf_op jit(solution)/shard_map/ppermute | solution.py:178
  72.1 1.6 %collective-permute-start.8 = (f32[120,128]{1,0:T(8,128)S(1)}, f32[120,128]{1,0:T(8,128)S(1)}, u32[]{:S(2)}, u32[]{:S(2)}) collective-permute-start(f32[120,128]{1,0:T(8,128)S(1)} %get-tuple-element.34), channel_id=1, source_target_pairs={{0,8},{1,9},{2,3},{3,2},{4,12},{5,13},{6,7},{7,6},{8,0},{9,1},{10,... | collective-permute-start | bytes 184328 | tf_op jit(solution)/shard_map/ppermute | solution.py:178
  73.7 2.4 %collective-permute-start.10 = (f32[120,128]{1,0:T(8,128)S(1)}, f32[120,128]{1,0:T(8,128)S(1)}, u32[]{:S(2)}, u32[]{:S(2)}) collective-permute-start(f32[120,128]{1,0:T(8,128)S(1)} %get-tuple-element.35), channel_id=1, source_target_pairs={{0,24},{1,25},{2,7},{3,6},{4,28},{5,29},{6,3},{7,2},{8,16},{9,17},... | collective-permute-start | bytes 184328 | tf_op jit(solution)/shard_map/ppermute | solution.py:178
  76.1 1.1 %collective-permute-done.8 = f32[120,128]{1,0:T(8,128)S(1)} collective-permute-done((f32[120,128]{1,0:T(8,128)S(1)}, f32[120,128]{1,0:T(8,128)S(1)}, u32[]{:S(2)}, u32[]{:S(2)}) %collective-permute-start.8) | collective-permute-done | bytes 61472 | tf_op jit(solution)/shard_map/ppermute | solution.py:178
  77.2 2.6 %collective-permute-done.10 = f32[120,128]{1,0:T(8,128)S(1)} collective-permute-done((f32[120,128]{1,0:T(8,128)S(1)}, f32[120,128]{1,0:T(8,128)S(1)}, u32[]{:S(2)}, u32[]{:S(2)}) %collective-permute-start.10) | collective-permute-done | bytes 61472 | tf_op jit(solution)/shard_map/ppermute | solution.py:178
  79.7 2.1 %collective-permute-done.9 = f32[120,128]{1,0:T(8,128)S(1)} collective-permute-done((f32[120,128]{1,0:T(8,128)S(1)}, f32[120,128]{1,0:T(8,128)S(1)}, u32[]{:S(2)}, u32[]{:S(2)}) %collective-permute-start.9) | collective-permute-done | bytes 61472 | tf_op jit(solution)/shard_map/ppermute | solution.py:178
  81.9 1.6 %collective-permute-start.13 = (f32[120,128]{1,0:T(8,128)S(1)}, f32[120,128]{1,0:T(8,128)S(1)}, u32[]{:S(2)}, u32[]{:S(2)}) collective-permute-start(f32[120,128]{1,0:T(8,128)S(1)} %add_add_fusion.1), channel_id=1, source_target_pairs={{0,24},{1,25},{2,7},{3,6},{4,28},{5,29},{6,3},{7,2},{8,16},{9,17},... | collective-permute-start | bytes 184328 | tf_op jit(solution)/shard_map/ppermute | solution.py:183
  83.5 2.8 %collective-permute-start.11 = (f32[120,128]{1,0:T(8,128)S(1)}, f32[120,128]{1,0:T(8,128)S(1)}, u32[]{:S(2)}, u32[]{:S(2)}) collective-permute-start(f32[120,128]{1,0:T(8,128)S(1)} %add_add_fusion.1), channel_id=1, source_target_pairs={{0,8},{1,9},{2,3},{3,2},{4,12},{5,13},{6,7},{7,6},{8,0},{9,1},{10,... | collective-permute-start | bytes 184328 | tf_op jit(solution)/shard_map/ppermute | solution.py:183
  86.3 1.6 %collective-permute-done.13 = f32[120,128]{1,0:T(8,128)S(1)} collective-permute-done((f32[120,128]{1,0:T(8,128)S(1)}, f32[120,128]{1,0:T(8,128)S(1)}, u32[]{:S(2)}, u32[]{:S(2)}) %collective-permute-start.13) | collective-permute-done | bytes 61472 | tf_op jit(solution)/shard_map/ppermute | solution.py:183
  88.0 1.3 %collective-permute-done.12 = f32[120,128]{1,0:T(8,128)S(1)} collective-permute-done((f32[120,128]{1,0:T(8,128)S(1)}, f32[120,128]{1,0:T(8,128)S(1)}, u32[]{:S(2)}, u32[]{:S(2)}) %collective-permute-start.12) | collective-permute-done | bytes 61472 | tf_op jit(solution)/shard_map/ppermute | solution.py:183
  89.4 3.2 %collective-permute-start.16 = (f32[480,128]{1,0:T(8,128)S(1)}, f32[480,128]{1,0:T(8,128)S(1)}, u32[]{:S(2)}, u32[]{:S(2)}) collective-permute-start(f32[480,128]{1,0:T(8,128)S(1)} %pad_maximum_fusion.4), channel_id=1, source_target_pairs={{0,5},{1,4},{2,26},{3,27},{4,1},{5,0},{6,30},{7,31},{8,13},{9,12},... | collective-permute-start | bytes 737288 | tf_op jit(solution)/shard_map/ppermute | solution.py:183
  93.2 3.6 %collective-permute-done.16 = f32[480,128]{1,0:T(8,128)S(1)} collective-permute-done((f32[480,128]{1,0:T(8,128)S(1)}, f32[480,128]{1,0:T(8,128)S(1)}, u32[]{:S(2)}, u32[]{:S(2)}) %collective-permute-start.16) | collective-permute-done | bytes 245792 | tf_op jit(solution)/shard_map/ppermute | solution.py:183
  96.8 2.8 %collective-permute-done.15 = f32[480,128]{1,0:T(8,128)S(1)} collective-permute-done((f32[480,128]{1,0:T(8,128)S(1)}, f32[480,128]{1,0:T(8,128)S(1)}, u32[]{:S(2)}, u32[]{:S(2)}) %collective-permute-start.15) | collective-permute-done | bytes 245792 | tf_op jit(solution)/shard_map/ppermute | solution.py:183
  100.0 1.6 %collective-permute-start.17 = (f32[1920,128]{1,0:T(8,128)S(1)}, f32[1920,128]{1,0:T(8,128)S(1)}, u32[]{:S(2)}, u32[]{:S(2)}) collective-permute-start(f32[1920,128]{1,0:T(8,128)S(1)} %pad_maximum_fusion), channel_id=1, source_target_pairs={{0,2},{1,3},{2,0},{3,1},{4,6},{5,7},{6,4},{7,5},{8,10},{9,11},{10,... | collective-permute-start | bytes 2949128 | tf_op jit(solution)/shard_map/ppermute | solution.py:192
  101.7 1.1 %fusion.3 = bf16[1,512,256]{2,1,0:T(8,128)(2,1)} fusion(bf16[768,256]{1,0:T(8,128)(2,1)S(1)} %copy-done.9, f32[518,256]{1,0:T(8,128)S(1)} %copy-done.4, bf16[512,256]{1,0:T(8,128)(2,1)S(1)} %copy-done.13, bf16[512,256]{1,0:T(8,128)(2,1)S(1)} %copy-done.15, bf16[512,256]{1,0:T(8,128)(2,1)S(1)} %copy-done.11, f32[256]{0:T(256)S(1)} %copy-done.20), kind=kOutput, calls=%fused_computation.11 | convolution fusion | flops 204079104 | bytes 1967104 | tf_op jit(solution)/shard_map/dot_general | solution.py:92
  105.6 1.2 %reshape.96 = f32[560,512]{1,0:T(8,128)} reshape(f32[2240,128]{1,0:T(8,128)S(1)} %slice.160) | data formatting | bytes 2293760 | tf_op jit(solution)/shard_map/reshape | solution.py:197
  106.8 1.1 %reshape.97 = f32[768,256]{1,0:T(8,128)} reshape(f32[1536,128]{1,0:T(8,128)S(1)} %slice.162) | data formatting | bytes 1572864 | tf_op jit(solution)/shard_map/reshape | solution.py:197
  (127 shorter events, 23.9 us)
Async XLA Ops:
  0.6 46.1 %copy-start = (bf16[560,512]{1,0:T(8,128)(2,1)S(1)}, bf16[560,512]{1,0:T(8,128)(2,1)}, u32[]{:S(2)}) copy-start(bf16[560,512]{1,0:T(8,128)(2,1)} %param.16) | copy-start | bytes 1720324
  0.6 20.5 %copy-start.2 = (bf16[1,512,256]{2,1,0:T(8,128)(2,1)S(1)}, bf16[1,512,256]{2,1,0:T(8,128)(2,1)}, u32[]{:S(2)}) copy-start(bf16[1,512,256]{2,1,0:T(8,128)(2,1)} %param.15) | copy-start | bytes 786436
  0.7 21.2 %copy-start.8 = (bf16[768,256]{1,0:T(8,128)(2,1)S(1)}, bf16[768,256]{1,0:T(8,128)(2,1)}, u32[]{:S(2)}) copy-start(bf16[768,256]{1,0:T(8,128)(2,1)} %param.20) | copy-start | bytes 1179652
  5.1 13.9 %all-to-all-start = ((bf16[16,2,321]{2,1,0:T(2,128)(2,1)}), bf16[16,2,321]{2,1,0:T(2,128)(2,1)S(1)}, u32[]{:S(2)}, u32[]{:S(2)}) async-start(bf16[16,2,321]{2,1,0:T(2,128)(2,1)} %reshape.101), calls=%async_computation | async-start | bytes 49152 | tf_op jit(solution)/shard_map/all_to_all | solution.py:256
  14.1 25.5 %collective-permute-start.2 = (bf16[256,2048]{1,0:T(8,128)(2,1)S(1)}, bf16[256,2048]{1,0:T(8,128)(2,1)S(1)}, u32[]{:S(2)}, u32[]{:S(2)}) collective-permute-start(bf16[256,2048]{1,0:T(8,128)(2,1)S(1)} %slice_select_fusion), channel_id=1, source_target_pairs={{0,1},{1,0},{2,3},{3,2},{4,5},{5,4},{6,7},{7,6},{8,9},{9,8},{10,11... | collective-permute-start | bytes 3145736 | tf_op jit(solution)/shard_map/ppermute | solution.py:214
  19.8 23.4 %collective-permute-start.1 = (bf16[4,80]{1,0:T(4,128)(2,1)S(1)}, bf16[4,80]{1,0:T(4,128)(2,1)S(1)}, u32[]{:S(2)}, u32[]{:S(2)}) collective-permute-start(bf16[4,80]{1,0:T(4,128)(2,1)S(1)} %get-tuple-element.44), channel_id=1, source_target_pairs={{1,0},{3,2},{5,4},{7,6},{9,8},{11,10},{13,12},{15,14},{17,16},{19,... | collective-permute-start | bytes 1928 | tf_op jit(solution)/shard_map/ppermute | solution.py:19
  39.6 8.1 %collective-permute-start.3 = (bf16[256,2048]{1,0:T(8,128)(2,1)S(1)}, bf16[256,2048]{1,0:T(8,128)(2,1)S(1)}, u32[]{:S(2)}, u32[]{:S(2)}) collective-permute-start(bf16[256,2048]{1,0:T(8,128)(2,1)S(1)} %collective-permute-done.2), channel_id=1, source_target_pairs={{0,2},{2,0},{4,6},{6,4},{8,10},{10,8},{12,14},{14,12},{16,18},{18,... | collective-permute-start | bytes 3145736 | tf_op jit(solution)/shard_map/ppermute | solution.py:215
  39.8 4.7 %collective-permute-start = (bf16[4,80]{1,0:T(4,128)(2,1)S(1)}, bf16[4,80]{1,0:T(4,128)(2,1)S(1)}, u32[]{:S(2)}, u32[]{:S(2)}) collective-permute-start(bf16[4,80]{1,0:T(4,128)(2,1)S(1)} %get-tuple-element.45), channel_id=1, source_target_pairs={{0,1},{2,3},{4,5},{6,7},{8,9},{10,11},{12,13},{14,15},{16,17},{18,... | collective-permute-start | bytes 1928 | tf_op jit(solution)/shard_map/ppermute | solution.py:16
  48.1 1.6 %copy-start.1 = (bf16[256,4096]{1,0:T(8,128)(2,1)S(1)}, bf16[256,4096]{1,0:T(8,128)(2,1)}, u32[]{:S(2)}) copy-start(bf16[256,4096]{1,0:T(8,128)(2,1)} %param.18) | copy-start | bytes 6291460
  50.5 1.3 %copy-start.7 = (f32[512,256]{1,0:T(8,128)S(1)}, f32[512,256]{1,0:T(8,128)}, u32[]{:S(2)}) copy-start(f32[512,256]{1,0:T(8,128)} %get-tuple-element.21) | copy-start | bytes 1572868
  50.6 1.3 %copy-start.16 = (pred[518]{0:T(1024)(128)(4,1)S(1)}, pred[518]{0:T(1024)(128)(4,1)}, u32[]{:S(2)}) copy-start(pred[518]{0:T(1024)(128)(4,1)} %fusion.42) | copy-start | bytes 1558
  50.6 1.3 %copy-start.19 = (f32[256]{0:T(256)S(1)}, f32[256]{0:T(256)}, u32[]{:S(2)}) copy-start(f32[256]{0:T(256)} %param.19) | copy-start | bytes 3076
  57.0 2.8 %collective-permute-start.4 = (f32[1920,128]{1,0:T(8,128)S(1)}, f32[1920,128]{1,0:T(8,128)}, u32[]{:S(2)}, u32[]{:S(2)}) collective-permute-start(f32[1920,128]{1,0:T(8,128)S(1)} %constant_dynamic-slice_fusion.6), channel_id=1, source_target_pairs={{0,2},{1,3},{2,0},{3,1},{4,6},{5,7},{6,4},{7,5},{8,10},{9,11},{10,... | collective-permute-start | bytes 2949128 | tf_op jit(solution)/shard_map/ppermute | solution.py:170
  61.2 8.7 %collective-permute-start.5 = (f32[480,128]{1,0:T(8,128)S(1)}, f32[480,128]{1,0:T(8,128)S(1)}, u32[]{:S(2)}, u32[]{:S(2)}) collective-permute-start(f32[480,128]{1,0:T(8,128)S(1)} %get-tuple-element.24), channel_id=1, source_target_pairs={{0,1},{1,0},{2,10},{3,11},{4,5},{5,4},{6,14},{7,15},{8,9},{9,8},{1... | collective-permute-start | bytes 737288 | tf_op jit(solution)/shard_map/ppermute | solution.py:178
  63.5 7.1 %collective-permute-start.7 = (f32[480,128]{1,0:T(8,128)S(1)}, f32[480,128]{1,0:T(8,128)S(1)}, u32[]{:S(2)}, u32[]{:S(2)}) collective-permute-start(f32[480,128]{1,0:T(8,128)S(1)} %get-tuple-element.25), channel_id=1, source_target_pairs={{0,5},{1,4},{2,26},{3,27},{4,1},{5,0},{6,30},{7,31},{8,13},{9,12},... | collective-permute-start | bytes 737288 | tf_op jit(solution)/shard_map/ppermute | solution.py:178
  64.7 7.3 %collective-permute-start.6 = (f32[480,128]{1,0:T(8,128)S(1)}, f32[480,128]{1,0:T(8,128)S(1)}, u32[]{:S(2)}, u32[]{:S(2)}) collective-permute-start(f32[480,128]{1,0:T(8,128)S(1)} %get-tuple-element.26), channel_id=1, source_target_pairs={{0,4},{1,5},{2,18},{3,19},{4,0},{5,1},{6,22},{7,23},{8,12},{9,13},... | collective-permute-start | bytes 737288 | tf_op jit(solution)/shard_map/ppermute | solution.py:178
  72.1 5.1 %collective-permute-start.8 = (f32[120,128]{1,0:T(8,128)S(1)}, f32[120,128]{1,0:T(8,128)S(1)}, u32[]{:S(2)}, u32[]{:S(2)}) collective-permute-start(f32[120,128]{1,0:T(8,128)S(1)} %get-tuple-element.34), channel_id=1, source_target_pairs={{0,8},{1,9},{2,3},{3,2},{4,12},{5,13},{6,7},{7,6},{8,0},{9,1},{10,... | collective-permute-start | bytes 184328 | tf_op jit(solution)/shard_map/ppermute | solution.py:178
  73.7 6.0 %collective-permute-start.10 = (f32[120,128]{1,0:T(8,128)S(1)}, f32[120,128]{1,0:T(8,128)S(1)}, u32[]{:S(2)}, u32[]{:S(2)}) collective-permute-start(f32[120,128]{1,0:T(8,128)S(1)} %get-tuple-element.35), channel_id=1, source_target_pairs={{0,24},{1,25},{2,7},{3,6},{4,28},{5,29},{6,3},{7,2},{8,16},{9,17},... | collective-permute-start | bytes 184328 | tf_op jit(solution)/shard_map/ppermute | solution.py:178
  76.1 5.8 %collective-permute-start.9 = (f32[120,128]{1,0:T(8,128)S(1)}, f32[120,128]{1,0:T(8,128)S(1)}, u32[]{:S(2)}, u32[]{:S(2)}) collective-permute-start(f32[120,128]{1,0:T(8,128)S(1)} %get-tuple-element.36), channel_id=1, source_target_pairs={{0,16},{1,17},{2,6},{3,7},{4,20},{5,21},{6,2},{7,3},{8,24},{9,25},... | collective-permute-start | bytes 184328 | tf_op jit(solution)/shard_map/ppermute | solution.py:178
  81.9 6.1 %collective-permute-start.13 = (f32[120,128]{1,0:T(8,128)S(1)}, f32[120,128]{1,0:T(8,128)S(1)}, u32[]{:S(2)}, u32[]{:S(2)}) collective-permute-start(f32[120,128]{1,0:T(8,128)S(1)} %add_add_fusion.1), channel_id=1, source_target_pairs={{0,24},{1,25},{2,7},{3,6},{4,28},{5,29},{6,3},{7,2},{8,16},{9,17},... | collective-permute-start | bytes 184328 | tf_op jit(solution)/shard_map/ppermute | solution.py:183
  83.5 5.8 %collective-permute-start.12 = (f32[120,128]{1,0:T(8,128)S(1)}, f32[120,128]{1,0:T(8,128)S(1)}, u32[]{:S(2)}, u32[]{:S(2)}) collective-permute-start(f32[120,128]{1,0:T(8,128)S(1)} %add_add_fusion.1), channel_id=1, source_target_pairs={{0,16},{1,17},{2,6},{3,7},{4,20},{5,21},{6,2},{7,3},{8,24},{9,25},... | collective-permute-start | bytes 184328 | tf_op jit(solution)/shard_map/ppermute | solution.py:183
  83.5 5.8 %collective-permute-start.11 = (f32[120,128]{1,0:T(8,128)S(1)}, f32[120,128]{1,0:T(8,128)S(1)}, u32[]{:S(2)}, u32[]{:S(2)}) collective-permute-start(f32[120,128]{1,0:T(8,128)S(1)} %add_add_fusion.1), channel_id=1, source_target_pairs={{0,8},{1,9},{2,3},{3,2},{4,12},{5,13},{6,7},{7,6},{8,0},{9,1},{10,... | collective-permute-start | bytes 184328 | tf_op jit(solution)/shard_map/ppermute | solution.py:183
  89.4 7.4 %collective-permute-start.16 = (f32[480,128]{1,0:T(8,128)S(1)}, f32[480,128]{1,0:T(8,128)S(1)}, u32[]{:S(2)}, u32[]{:S(2)}) collective-permute-start(f32[480,128]{1,0:T(8,128)S(1)} %pad_maximum_fusion.4), channel_id=1, source_target_pairs={{0,5},{1,4},{2,26},{3,27},{4,1},{5,0},{6,30},{7,31},{8,13},{9,12},... | collective-permute-start | bytes 737288 | tf_op jit(solution)/shard_map/ppermute | solution.py:183
  92.6 7.0 %collective-permute-start.15 = (f32[480,128]{1,0:T(8,128)S(1)}, f32[480,128]{1,0:T(8,128)S(1)}, u32[]{:S(2)}, u32[]{:S(2)}) collective-permute-start(f32[480,128]{1,0:T(8,128)S(1)} %pad_maximum_fusion.4), channel_id=1, source_target_pairs={{0,4},{1,5},{2,18},{3,19},{4,0},{5,1},{6,22},{7,23},{8,12},{9,13},... | collective-permute-start | bytes 737288 | tf_op jit(solution)/shard_map/ppermute | solution.py:183
  92.8 6.8 %collective-permute-start.14 = (f32[480,128]{1,0:T(8,128)S(1)}, f32[480,128]{1,0:T(8,128)S(1)}, u32[]{:S(2)}, u32[]{:S(2)}) collective-permute-start(f32[480,128]{1,0:T(8,128)S(1)} %pad_maximum_fusion.4), channel_id=1, source_target_pairs={{0,1},{1,0},{2,10},{3,11},{4,5},{5,4},{6,14},{7,15},{8,9},{9,8},{1... | collective-permute-start | bytes 737288 | tf_op jit(solution)/shard_map/ppermute | solution.py:183
  99.8 1.9 %copy-start.4 = (f32[518,256]{1,0:T(8,128)S(1)}, f32[518,256]{1,0:T(8,128)}, u32[]{:S(2)}) copy-start(f32[518,256]{1,0:T(8,128)} %copy-done.3) | copy-start | bytes 1591300
  99.8 1.9 %copy-start.9 = (bf16[768,256]{1,0:T(8,128)(2,1)S(1)}, bf16[768,256]{1,0:T(8,128)(2,1)}, u32[]{:S(2)}) copy-start(bf16[768,256]{1,0:T(8,128)(2,1)} %param.20) | copy-start | bytes 1179652
  99.8 1.8 %copy-start.11 = (bf16[512,256]{1,0:T(8,128)(2,1)S(1)}, bf16[512,256]{1,0:T(8,128)(2,1)}, u32[]{:S(2)}) copy-start(bf16[512,256]{1,0:T(8,128)(2,1)} %copy-done.10) | copy-start | bytes 786436
  99.8 1.8 %copy-start.13 = (bf16[512,256]{1,0:T(8,128)(2,1)S(1)}, bf16[512,256]{1,0:T(8,128)(2,1)}, u32[]{:S(2)}) copy-start(bf16[512,256]{1,0:T(8,128)(2,1)} %copy-done.12) | copy-start | bytes 786436
  99.9 1.8 %copy-start.15 = (bf16[512,256]{1,0:T(8,128)(2,1)S(1)}, bf16[512,256]{1,0:T(8,128)(2,1)}, u32[]{:S(2)}) copy-start(bf16[512,256]{1,0:T(8,128)(2,1)} %copy-done.14) | copy-start | bytes 786436
  99.9 1.8 %copy-start.20 = (f32[256]{0:T(256)S(1)}, f32[256]{0:T(256)}, u32[]{:S(2)}) copy-start(f32[256]{0:T(256)} %param.21) | copy-start | bytes 3076
  100.0 3.8 %collective-permute-start.17 = (f32[1920,128]{1,0:T(8,128)S(1)}, f32[1920,128]{1,0:T(8,128)S(1)}, u32[]{:S(2)}, u32[]{:S(2)}) collective-permute-start(f32[1920,128]{1,0:T(8,128)S(1)} %pad_maximum_fusion), channel_id=1, source_target_pairs={{0,2},{1,3},{2,0},{3,1},{4,6},{5,7},{6,4},{7,5},{8,10},{9,11},{10,... | collective-permute-start | bytes 2949128 | tf_op jit(solution)/shard_map/ppermute | solution.py:192
  (8 other events, 7.6 us)

commit v7 on v6

--- a/solution.py
+++ b/solution.py
@@ -242,22 +242,20 @@
 def on_device(
     src_mel, owner, dst_pos, keep, cotangent, w_pre, b_pre, w_ups, upsample_bias, w_res, b_res
 ):
-    owners_count = lax.axis_size("dp")
     seg_rows = src_mel[0]
     seg_count = seg_rows.shape[0]
     mel_bins = w_pre.shape[0] // KPRE
-    pick = jnp.arange(owners_count, dtype=jnp.int32)[:, None] == owner[0][None, :]
     seg_width = seg_rows.shape[1]
-    header = jnp.stack([dst_pos[0] + 1, keep[0]], axis=1).astype(jnp.bfloat16)
+    header = jnp.stack([dst_pos[0] + 1, keep[0], owner[0]], axis=1).astype(jnp.bfloat16)
     seg_ext = jnp.concatenate([seg_rows, header], axis=1)
-    outgoing = jnp.dot(
-        pick.astype(jnp.bfloat16), seg_ext, preferred_element_type=jnp.float32
-    ).astype(jnp.bfloat16)
-    arrived = lax.all_to_all(outgoing, "dp", split_axis=0, concat_axis=0, tiled=True)
-    slot_code = arrived[:, seg_width].astype(jnp.int32)
-    keep_code = arrived[:, seg_width + 1].astype(jnp.int32)
-    place = (slot_code - 1)[:, None] == jnp.arange(seg_count, dtype=jnp.int32)[None, :]
-    mel_segs = contract_rows(place.astype(jnp.bfloat16), arrived[:, :seg_width]).astype(
+    gathered = lax.all_gather(seg_ext, "dp", axis=0, tiled=True)
+    slot_code = gathered[:, seg_width].astype(jnp.int32)
+    keep_code = gathered[:, seg_width + 1].astype(jnp.int32)
+    mine = gathered[:, seg_width + 2].astype(jnp.int32) == lax.axis_index("dp")
+    place = mine[:, None] & (
+        (slot_code - 1)[:, None] == jnp.arange(seg_count, dtype=jnp.int32)[None, :]
+    )
+    mel_segs = contract_rows(place.astype(jnp.bfloat16), gathered[:, :seg_width]).astype(
         jnp.bfloat16
     )
     keep_segs = jnp.sum(jnp.where(place, keep_code[:, None], 0), axis=0)

time: 108 us -> 123 us (1.14)
  blocking collectives: 0 us -> 23.6 us
  starting transfers between devices: 31.7 us -> 23.1 us
    all_gather x0 -> x1, blocking collectives: none -> 23.6 us  [on_device(): gathered = lax.all_gather(seg_ext, 'dp', axis=0, tiled=True)]
    all_to_all x1 -> x0, starting transfers between devices: 7.36 us -> none  [on_device(): lax.all_to_all(outgoing, 'dp', split_axis=0, concat_axis=0, tiled=True)]
    ppermute x1, waiting for transfers between devices: 16.2 us -> 21.7 us  [ups_functions(): got = lax.ppermute(mine, 'tm', [(0, 1), (1, 0)])]
    all_to_all x1 -> x0, waiting for transfers between devices: 2.13 us -> none  [on_device(): lax.all_to_all(outgoing, 'dp', split_axis=0, concat_axis=0, tiled=True)]
    ppermute x6, waiting for transfers between devices: 12.6 us -> 11 us  [butterfly_psum(): total = total + lax.ppermute(send, axes, perm_of(step, offset))]
    ppermute x1, starting transfers between devices: 1.61 us -> 0.07 us  [ups_functions(): got = lax.ppermute(mine, 'tm', [(0, 1), (1, 0)])]
    ppermute x1, waiting for transfers between devices: 1.26 us -> 0.01 us  [with_halo(): lax.ppermute(lax.slice_in_dim(block, block.shape[dim] - width, None, axis...]
    unnamed x55 -> x50, local copies, waits for them, and re-layouts: 5.28 us -> 4.46 us
  transfers between devices with their start and end apart: 19 -> 18, of which waited for: 15 -> 13; matrix products, arithmetic and copies ran while one was open for 10% -> 9% of each run, Pallas kernels for 0% -> 0%
where the time goes in v7:
time: 123 us
  waiting for transfers between devices  45.5 us (37%)
  blocking collectives  23.6 us (19%)
  starting transfers between devices  23.1 us (19%)
  local copies, waits for them, and re-layouts  11.8 us (10%)
  other arithmetic  10.4 us (8%)
  matrix products  7.29 us (6%)
  between operations  1.26 us (1%)
    all_gather x1, blocking collectives, on_device(): gathered = lax.all_gather(seg_ext, 'dp', axis=0, tiled=True)  23.6 us
    ppermute x1, waiting for transfers between devices, ups_functions(): got = lax.ppermute(mine, 'tm', [(0, 1), (1, 0)])  21.7 us
    ppermute x6, waiting for transfers between devices, butterfly_psum(): total = total + lax.ppermute(send, axes, perm_of(step, offset))  11 us
    ppermute x6, waiting for transfers between devices, butterfly_psum(): lax.ppermute(x, axes, perm_of(step, o))  9.46 us
    ppermute x6, starting transfers between devices, butterfly_psum(): lax.ppermute(x, axes, perm_of(step, o))  8 us
    ppermute x6, starting transfers between devices, butterfly_psum(): total = total + lax.ppermute(send, axes, perm_of(step, offset))  7.09 us
    ppermute x1, starting transfers between devices, with_halo(): lax.ppermute(lax.slice_in_dim(block, block.shape[dim] - width, None, axis...  4.54 us
    unnamed x50, local copies, waits for them, and re-layouts  4.46 us
  transfers between devices with their start and end apart: 18, of which 13 were waited for; matrix products, arithmetic and copies ran while one was open for 9% of the time, Pallas kernels for 0%

profile of v7, /device:TPU:0, one launch (start us, length us, event | category | flops | bytes accessed | tf_op | source)
XLA Modules:
  0.0 122.8 jit_solution(15562826771619706983)
XLA Ops:
  3.8 23.6 %all_gather.3 = bf16[128,643]{1,0:T(8,128)(2,1)S(1)} all-gather(bf16[8,643]{1,0:T(8,128)(2,1)S(1)} %pad_maximum_fusion.8), channel_id=1, replica_groups=mesh['dp'=16,'tm'=2] {'dp'}, dimensions={0}, use_global_device_ids=true | all-gather | bytes 174896 | tf_op jit(solution)/shard_map/all_gather | solution.py:251
  28.0 1.3 %collective-permute-start.1 = (bf16[4,80]{1,0:T(4,128)(2,1)S(1)}, bf16[4,80]{1,0:T(4,128)(2,1)S(1)}, u32[]{:S(2)}, u32[]{:S(2)}) collective-permute-start(bf16[4,80]{1,0:T(4,128)(2,1)S(1)} %get-tuple-element.44), channel_id=1, source_target_pairs={{1,0},{3,2},{5,4},{7,6},{9,8},{11,10},{13,12},{15,14},{17,16},{19,... | collective-permute-start | bytes 1928 | tf_op jit(solution)/shard_map/ppermute | solution.py:19
  29.3 4.5 %collective-permute-start = (bf16[4,80]{1,0:T(4,128)(2,1)S(1)}, bf16[4,80]{1,0:T(4,128)(2,1)S(1)}, u32[]{:S(2)}, u32[]{:S(2)}) collective-permute-start(bf16[4,80]{1,0:T(4,128)(2,1)S(1)} %get-tuple-element.45), channel_id=1, source_target_pairs={{0,1},{2,3},{4,5},{6,7},{8,9},{10,11},{12,13},{14,15},{16,17},{18,... | collective-permute-start | bytes 1928 | tf_op jit(solution)/shard_map/ppermute | solution.py:16
  33.9 1.7 %slice_select_fusion = bf16[256,2048]{1,0:T(8,128)(2,1)S(1)} fusion(bf16[256,4096]{1,0:T(8,128)(2,1)} %param.18, pred[]{:T(512)S(6)} %eq.132), kind=kLoop, calls=%fused_computation.19 | loop fusion | flops 524288 | bytes 3145729 | tf_op jit(solution)/shard_map/jit(_where)/select_n | solution.py:213
  37.3 1.4 %fusion.47 = f32[512,768]{1,0:T(8,128)S(1)} fusion(bf16[768,256]{1,0:T(8,128)(2,1)} %param.20, bf16[1,512,256]{2,1,0:T(8,128)(2,1)S(1)} %copy-done.2, pred[512]{0:T(512)(128)(4,1)S(1)} %gt.27), kind=kOutput, calls=%fused_computation.124 | convolution fusion | flops 201457664 | bytes 2228736 | tf_op jit(solution)/shard_map/dot_general | solution.py:39
  38.7 21.7 %collective-permute-done.2 = bf16[256,2048]{1,0:T(8,128)(2,1)S(1)} collective-permute-done((bf16[256,2048]{1,0:T(8,128)(2,1)S(1)}, bf16[256,2048]{1,0:T(8,128)(2,1)S(1)}, u32[]{:S(2)}, u32[]{:S(2)}) %collective-permute-start.2) | collective-permute-done | bytes 1048608 | tf_op jit(solution)/shard_map/ppermute | solution.py:214
  61.0 1.2 fusion.49
  63.5 0.9 concatenate.62
  66.1 1.2 copy-done.1
  75.3 2.3 %collective-permute-done.4 = f32[1920,128]{1,0:T(8,128)} collective-permute-done((f32[1920,128]{1,0:T(8,128)S(1)}, f32[1920,128]{1,0:T(8,128)}, u32[]{:S(2)}, u32[]{:S(2)}) %collective-permute-start.4) | collective-permute-done | bytes 983072 | tf_op jit(solution)/shard_map/ppermute | solution.py:170
  77.6 1.3 %dynamic-slice_add_fusion = f32[1920,128]{1,0:T(8,128)S(1)} fusion(f32[1920,128]{1,0:T(8,128)} %collective-permute-done.4, f32[3840,128]{1,0:T(8,128)S(1)} %fusion, s32[]{:T(128)S(6)} %select_n.365), kind=kLoop, calls=%fused_computation.23 | loop fusion | flops 245760 | bytes 2949124 | tf_op jit(solution)/shard_map/add | solution.py:170
  79.4 3.2 %collective-permute-start.6 = (f32[480,128]{1,0:T(8,128)S(1)}, f32[480,128]{1,0:T(8,128)S(1)}, u32[]{:S(2)}, u32[]{:S(2)}) collective-permute-start(f32[480,128]{1,0:T(8,128)S(1)} %get-tuple-element.26), channel_id=1, source_target_pairs={{0,4},{1,5},{2,18},{3,19},{4,0},{5,1},{6,22},{7,23},{8,12},{9,13},... | collective-permute-start | bytes 737288 | tf_op jit(solution)/shard_map/ppermute | solution.py:178
  82.6 5.3 %collective-permute-done.5 = f32[480,128]{1,0:T(8,128)S(1)} collective-permute-done((f32[480,128]{1,0:T(8,128)S(1)}, f32[480,128]{1,0:T(8,128)S(1)}, u32[]{:S(2)}, u32[]{:S(2)}) %collective-permute-start.5) | collective-permute-done | bytes 245792 | tf_op jit(solution)/shard_map/ppermute | solution.py:178
  87.9 1.5 %collective-permute-done.6 = f32[480,128]{1,0:T(8,128)S(1)} collective-permute-done((f32[480,128]{1,0:T(8,128)S(1)}, f32[480,128]{1,0:T(8,128)S(1)}, u32[]{:S(2)}, u32[]{:S(2)}) %collective-permute-start.6) | collective-permute-done | bytes 245792 | tf_op jit(solution)/shard_map/ppermute | solution.py:178
  89.6 3.4 %collective-permute-start.9 = (f32[120,128]{1,0:T(8,128)S(1)}, f32[120,128]{1,0:T(8,128)S(1)}, u32[]{:S(2)}, u32[]{:S(2)}) collective-permute-start(f32[120,128]{1,0:T(8,128)S(1)} %get-tuple-element.36), channel_id=1, source_target_pairs={{0,16},{1,17},{2,6},{3,7},{4,20},{5,21},{6,2},{7,3},{8,24},{9,25},... | collective-permute-start | bytes 184328 | tf_op jit(solution)/shard_map/ppermute | solution.py:178
  93.0 1.4 %collective-permute-done.8 = f32[120,128]{1,0:T(8,128)S(1)} collective-permute-done((f32[120,128]{1,0:T(8,128)S(1)}, f32[120,128]{1,0:T(8,128)S(1)}, u32[]{:S(2)}, u32[]{:S(2)}) %collective-permute-start.8) | collective-permute-done | bytes 61472 | tf_op jit(solution)/shard_map/ppermute | solution.py:178
  94.4 1.3 %collective-permute-done.10 = f32[120,128]{1,0:T(8,128)S(1)} collective-permute-done((f32[120,128]{1,0:T(8,128)S(1)}, f32[120,128]{1,0:T(8,128)S(1)}, u32[]{:S(2)}, u32[]{:S(2)}) %collective-permute-start.10) | collective-permute-done | bytes 61472 | tf_op jit(solution)/shard_map/ppermute | solution.py:178
  95.7 1.5 %collective-permute-done.9 = f32[120,128]{1,0:T(8,128)S(1)} collective-permute-done((f32[120,128]{1,0:T(8,128)S(1)}, f32[120,128]{1,0:T(8,128)S(1)}, u32[]{:S(2)}, u32[]{:S(2)}) %collective-permute-start.9) | collective-permute-done | bytes 61472 | tf_op jit(solution)/shard_map/ppermute | solution.py:178
  97.2 2.1 %collective-permute-start.13 = (f32[120,128]{1,0:T(8,128)S(1)}, f32[120,128]{1,0:T(8,128)S(1)}, u32[]{:S(2)}, u32[]{:S(2)}) collective-permute-start(f32[120,128]{1,0:T(8,128)S(1)} %add_add_fusion.1), channel_id=1, source_target_pairs={{0,24},{1,25},{2,7},{3,6},{4,28},{5,29},{6,3},{7,2},{8,16},{9,17},... | collective-permute-start | bytes 184328 | tf_op jit(solution)/shard_map/ppermute | solution.py:183
  99.3 2.4 %collective-permute-start.11 = (f32[120,128]{1,0:T(8,128)S(1)}, f32[120,128]{1,0:T(8,128)S(1)}, u32[]{:S(2)}, u32[]{:S(2)}) collective-permute-start(f32[120,128]{1,0:T(8,128)S(1)} %add_add_fusion.1), channel_id=1, source_target_pairs={{0,8},{1,9},{2,3},{3,2},{4,12},{5,13},{6,7},{7,6},{8,0},{9,1},{10,... | collective-permute-start | bytes 184328 | tf_op jit(solution)/shard_map/ppermute | solution.py:183
  101.6 1.6 %collective-permute-done.13 = f32[120,128]{1,0:T(8,128)S(1)} collective-permute-done((f32[120,128]{1,0:T(8,128)S(1)}, f32[120,128]{1,0:T(8,128)S(1)}, u32[]{:S(2)}, u32[]{:S(2)}) %collective-permute-start.13) | collective-permute-done | bytes 61472 | tf_op jit(solution)/shard_map/ppermute | solution.py:183
  103.3 1.6 %collective-permute-done.12 = f32[120,128]{1,0:T(8,128)S(1)} collective-permute-done((f32[120,128]{1,0:T(8,128)S(1)}, f32[120,128]{1,0:T(8,128)S(1)}, u32[]{:S(2)}, u32[]{:S(2)}) %collective-permute-start.12) | collective-permute-done | bytes 61472 | tf_op jit(solution)/shard_map/ppermute | solution.py:183
  105.0 1.5 %collective-permute-start.15 = (f32[480,128]{1,0:T(8,128)S(1)}, f32[480,128]{1,0:T(8,128)S(1)}, u32[]{:S(2)}, u32[]{:S(2)}) collective-permute-start(f32[480,128]{1,0:T(8,128)S(1)} %pad_maximum_fusion.4), channel_id=1, source_target_pairs={{0,4},{1,5},{2,18},{3,19},{4,0},{5,1},{6,22},{7,23},{8,12},{9,13},... | collective-permute-start | bytes 737288 | tf_op jit(solution)/shard_map/ppermute | solution.py:183
  106.5 2.0 %collective-permute-start.14 = (f32[480,128]{1,0:T(8,128)S(1)}, f32[480,128]{1,0:T(8,128)S(1)}, u32[]{:S(2)}, u32[]{:S(2)}) collective-permute-start(f32[480,128]{1,0:T(8,128)S(1)} %pad_maximum_fusion.4), channel_id=1, source_target_pairs={{0,1},{1,0},{2,10},{3,11},{4,5},{5,4},{6,14},{7,15},{8,9},{9,8},{1... | collective-permute-start | bytes 737288 | tf_op jit(solution)/shard_map/ppermute | solution.py:183
  108.5 3.7 %collective-permute-done.16 = f32[480,128]{1,0:T(8,128)S(1)} collective-permute-done((f32[480,128]{1,0:T(8,128)S(1)}, f32[480,128]{1,0:T(8,128)S(1)}, u32[]{:S(2)}, u32[]{:S(2)}) %collective-permute-start.16) | collective-permute-done | bytes 245792 | tf_op jit(solution)/shard_map/ppermute | solution.py:183
  112.2 1.1 collective-permute-done.15
  113.3 1.4 %collective-permute-done.14 = f32[480,128]{1,0:T(8,128)S(1)} collective-permute-done((f32[480,128]{1,0:T(8,128)S(1)}, f32[480,128]{1,0:T(8,128)S(1)}, u32[]{:S(2)}, u32[]{:S(2)}) %collective-permute-start.14) | collective-permute-done | bytes 245792 | tf_op jit(solution)/shard_map/ppermute | solution.py:183
  115.1 1.5 %collective-permute-start.17 = (f32[1920,128]{1,0:T(8,128)S(1)}, f32[1920,128]{1,0:T(8,128)S(1)}, u32[]{:S(2)}, u32[]{:S(2)}) collective-permute-start(f32[1920,128]{1,0:T(8,128)S(1)} %pad_maximum_fusion), channel_id=1, source_target_pairs={{0,2},{1,3},{2,0},{3,1},{4,6},{5,7},{6,4},{7,5},{8,10},{9,11},{10,... | collective-permute-start | bytes 2949128 | tf_op jit(solution)/shard_map/ppermute | solution.py:192
  116.7 1.1 fusion.3
  117.8 1.1 collective-permute-done.17
  120.6 1.2 reshape.94
  121.7 1.1 reshape.95
  (122 shorter events, 19.6 us)
Async XLA Ops:
  0.6 63.8 %copy-start = (bf16[560,512]{1,0:T(8,128)(2,1)S(1)}, bf16[560,512]{1,0:T(8,128)(2,1)}, u32[]{:S(2)}) copy-start(bf16[560,512]{1,0:T(8,128)(2,1)} %param.16) | copy-start | bytes 1720324
  0.6 35.8 %copy-start.2 = (bf16[1,512,256]{2,1,0:T(8,128)(2,1)S(1)}, bf16[1,512,256]{2,1,0:T(8,128)(2,1)}, u32[]{:S(2)}) copy-start(bf16[1,512,256]{2,1,0:T(8,128)(2,1)} %param.15) | copy-start | bytes 786436
  28.0 34.2 %collective-permute-start.1 = (bf16[4,80]{1,0:T(4,128)(2,1)S(1)}, bf16[4,80]{1,0:T(4,128)(2,1)S(1)}, u32[]{:S(2)}, u32[]{:S(2)}) collective-permute-start(bf16[4,80]{1,0:T(4,128)(2,1)S(1)} %get-tuple-element.44), channel_id=1, source_target_pairs={{1,0},{3,2},{5,4},{7,6},{9,8},{11,10},{13,12},{15,14},{17,16},{19,... | collective-permute-start | bytes 1928 | tf_op jit(solution)/shard_map/ppermute | solution.py:19
  29.3 32.9 %collective-permute-start = (bf16[4,80]{1,0:T(4,128)(2,1)S(1)}, bf16[4,80]{1,0:T(4,128)(2,1)S(1)}, u32[]{:S(2)}, u32[]{:S(2)}) collective-permute-start(bf16[4,80]{1,0:T(4,128)(2,1)S(1)} %get-tuple-element.45), channel_id=1, source_target_pairs={{0,1},{2,3},{4,5},{6,7},{8,9},{10,11},{12,13},{14,15},{16,17},{18,... | collective-permute-start | bytes 1928 | tf_op jit(solution)/shard_map/ppermute | solution.py:16
  35.5 24.9 %collective-permute-start.2 = (bf16[256,2048]{1,0:T(8,128)(2,1)S(1)}, bf16[256,2048]{1,0:T(8,128)(2,1)S(1)}, u32[]{:S(2)}, u32[]{:S(2)}) collective-permute-start(bf16[256,2048]{1,0:T(8,128)(2,1)S(1)} %slice_select_fusion), channel_id=1, source_target_pairs={{0,1},{1,0},{2,3},{3,2},{4,5},{5,4},{6,7},{7,6},{8,9},{9,8},{10,11... | collective-permute-start | bytes 3145736 | tf_op jit(solution)/shard_map/ppermute | solution.py:214
  60.4 5.0 %collective-permute-start.3 = (bf16[256,2048]{1,0:T(8,128)(2,1)S(1)}, bf16[256,2048]{1,0:T(8,128)(2,1)S(1)}, u32[]{:S(2)}, u32[]{:S(2)}) collective-permute-start(bf16[256,2048]{1,0:T(8,128)(2,1)S(1)} %collective-permute-done.2), channel_id=1, source_target_pairs={{0,2},{2,0},{4,6},{6,4},{8,10},{10,8},{12,14},{14,12},{16,18},{18,... | collective-permute-start | bytes 3145736 | tf_op jit(solution)/shard_map/ppermute | solution.py:215
  65.8 1.6 %copy-start.1 = (bf16[256,4096]{1,0:T(8,128)(2,1)S(1)}, bf16[256,4096]{1,0:T(8,128)(2,1)}, u32[]{:S(2)}) copy-start(bf16[256,4096]{1,0:T(8,128)(2,1)} %param.18) | copy-start | bytes 6291460
  68.2 1.0 copy-start.5
  68.3 1.2 copy-start.6
  68.3 1.3 %copy-start.7 = (f32[512,256]{1,0:T(8,128)S(1)}, f32[512,256]{1,0:T(8,128)}, u32[]{:S(2)}) copy-start(f32[512,256]{1,0:T(8,128)} %get-tuple-element.21) | copy-start | bytes 1572868
  68.3 1.3 %copy-start.15 = (pred[518]{0:T(1024)(128)(4,1)S(1)}, pred[518]{0:T(1024)(128)(4,1)}, u32[]{:S(2)}) copy-start(pred[518]{0:T(1024)(128)(4,1)} %fusion.38) | copy-start | bytes 1558
  68.3 1.3 %copy-start.18 = (f32[256]{0:T(256)S(1)}, f32[256]{0:T(256)}, u32[]{:S(2)}) copy-start(f32[256]{0:T(256)} %param.19) | copy-start | bytes 3076
  74.7 2.9 %collective-permute-start.4 = (f32[1920,128]{1,0:T(8,128)S(1)}, f32[1920,128]{1,0:T(8,128)}, u32[]{:S(2)}, u32[]{:S(2)}) collective-permute-start(f32[1920,128]{1,0:T(8,128)S(1)} %constant_dynamic-slice_fusion.6), channel_id=1, source_target_pairs={{0,2},{1,3},{2,0},{3,1},{4,6},{5,7},{6,4},{7,5},{8,10},{9,11},{10,... | collective-permute-start | bytes 2949128 | tf_op jit(solution)/shard_map/ppermute | solution.py:170
  79.0 8.9 %collective-permute-start.5 = (f32[480,128]{1,0:T(8,128)S(1)}, f32[480,128]{1,0:T(8,128)S(1)}, u32[]{:S(2)}, u32[]{:S(2)}) collective-permute-start(f32[480,128]{1,0:T(8,128)S(1)} %get-tuple-element.24), channel_id=1, source_target_pairs={{0,1},{1,0},{2,10},{3,11},{4,5},{5,4},{6,14},{7,15},{8,9},{9,8},{1... | collective-permute-start | bytes 737288 | tf_op jit(solution)/shard_map/ppermute | solution.py:178
  79.4 8.6 %collective-permute-start.7 = (f32[480,128]{1,0:T(8,128)S(1)}, f32[480,128]{1,0:T(8,128)S(1)}, u32[]{:S(2)}, u32[]{:S(2)}) collective-permute-start(f32[480,128]{1,0:T(8,128)S(1)} %get-tuple-element.25), channel_id=1, source_target_pairs={{0,5},{1,4},{2,26},{3,27},{4,1},{5,0},{6,30},{7,31},{8,13},{9,12},... | collective-permute-start | bytes 737288 | tf_op jit(solution)/shard_map/ppermute | solution.py:178
  79.4 10.0 %collective-permute-start.6 = (f32[480,128]{1,0:T(8,128)S(1)}, f32[480,128]{1,0:T(8,128)S(1)}, u32[]{:S(2)}, u32[]{:S(2)}) collective-permute-start(f32[480,128]{1,0:T(8,128)S(1)} %get-tuple-element.26), channel_id=1, source_target_pairs={{0,4},{1,5},{2,18},{3,19},{4,0},{5,1},{6,22},{7,23},{8,12},{9,13},... | collective-permute-start | bytes 737288 | tf_op jit(solution)/shard_map/ppermute | solution.py:178
  89.4 5.0 %collective-permute-start.8 = (f32[120,128]{1,0:T(8,128)S(1)}, f32[120,128]{1,0:T(8,128)S(1)}, u32[]{:S(2)}, u32[]{:S(2)}) collective-permute-start(f32[120,128]{1,0:T(8,128)S(1)} %get-tuple-element.34), channel_id=1, source_target_pairs={{0,8},{1,9},{2,3},{3,2},{4,12},{5,13},{6,7},{7,6},{8,0},{9,1},{10,... | collective-permute-start | bytes 184328 | tf_op jit(solution)/shard_map/ppermute | solution.py:178
  89.5 6.2 %collective-permute-start.10 = (f32[120,128]{1,0:T(8,128)S(1)}, f32[120,128]{1,0:T(8,128)S(1)}, u32[]{:S(2)}, u32[]{:S(2)}) collective-permute-start(f32[120,128]{1,0:T(8,128)S(1)} %get-tuple-element.35), channel_id=1, source_target_pairs={{0,24},{1,25},{2,7},{3,6},{4,28},{5,29},{6,3},{7,2},{8,16},{9,17},... | collective-permute-start | bytes 184328 | tf_op jit(solution)/shard_map/ppermute | solution.py:178
  89.6 7.6 %collective-permute-start.9 = (f32[120,128]{1,0:T(8,128)S(1)}, f32[120,128]{1,0:T(8,128)S(1)}, u32[]{:S(2)}, u32[]{:S(2)}) collective-permute-start(f32[120,128]{1,0:T(8,128)S(1)} %get-tuple-element.36), channel_id=1, source_target_pairs={{0,16},{1,17},{2,6},{3,7},{4,20},{5,21},{6,2},{7,3},{8,24},{9,25},... | collective-permute-start | bytes 184328 | tf_op jit(solution)/shard_map/ppermute | solution.py:178
  97.2 6.1 %collective-permute-start.13 = (f32[120,128]{1,0:T(8,128)S(1)}, f32[120,128]{1,0:T(8,128)S(1)}, u32[]{:S(2)}, u32[]{:S(2)}) collective-permute-start(f32[120,128]{1,0:T(8,128)S(1)} %add_add_fusion.1), channel_id=1, source_target_pairs={{0,24},{1,25},{2,7},{3,6},{4,28},{5,29},{6,3},{7,2},{8,16},{9,17},... | collective-permute-start | bytes 184328 | tf_op jit(solution)/shard_map/ppermute | solution.py:183
  99.3 5.6 %collective-permute-start.12 = (f32[120,128]{1,0:T(8,128)S(1)}, f32[120,128]{1,0:T(8,128)S(1)}, u32[]{:S(2)}, u32[]{:S(2)}) collective-permute-start(f32[120,128]{1,0:T(8,128)S(1)} %add_add_fusion.1), channel_id=1, source_target_pairs={{0,16},{1,17},{2,6},{3,7},{4,20},{5,21},{6,2},{7,3},{8,24},{9,25},... | collective-permute-start | bytes 184328 | tf_op jit(solution)/shard_map/ppermute | solution.py:183
  99.3 5.6 %collective-permute-start.11 = (f32[120,128]{1,0:T(8,128)S(1)}, f32[120,128]{1,0:T(8,128)S(1)}, u32[]{:S(2)}, u32[]{:S(2)}) collective-permute-start(f32[120,128]{1,0:T(8,128)S(1)} %add_add_fusion.1), channel_id=1, source_target_pairs={{0,8},{1,9},{2,3},{3,2},{4,12},{5,13},{6,7},{7,6},{8,0},{9,1},{10,... | collective-permute-start | bytes 184328 | tf_op jit(solution)/shard_map/ppermute | solution.py:183
  104.9 7.3 %collective-permute-start.16 = (f32[480,128]{1,0:T(8,128)S(1)}, f32[480,128]{1,0:T(8,128)S(1)}, u32[]{:S(2)}, u32[]{:S(2)}) collective-permute-start(f32[480,128]{1,0:T(8,128)S(1)} %pad_maximum_fusion.4), channel_id=1, source_target_pairs={{0,5},{1,4},{2,26},{3,27},{4,1},{5,0},{6,30},{7,31},{8,13},{9,12},... | collective-permute-start | bytes 737288 | tf_op jit(solution)/shard_map/ppermute | solution.py:183
  105.0 8.3 %collective-permute-start.15 = (f32[480,128]{1,0:T(8,128)S(1)}, f32[480,128]{1,0:T(8,128)S(1)}, u32[]{:S(2)}, u32[]{:S(2)}) collective-permute-start(f32[480,128]{1,0:T(8,128)S(1)} %pad_maximum_fusion.4), channel_id=1, source_target_pairs={{0,4},{1,5},{2,18},{3,19},{4,0},{5,1},{6,22},{7,23},{8,12},{9,13},... | collective-permute-start | bytes 737288 | tf_op jit(solution)/shard_map/ppermute | solution.py:183
  106.5 8.2 %collective-permute-start.14 = (f32[480,128]{1,0:T(8,128)S(1)}, f32[480,128]{1,0:T(8,128)S(1)}, u32[]{:S(2)}, u32[]{:S(2)}) collective-permute-start(f32[480,128]{1,0:T(8,128)S(1)} %pad_maximum_fusion.4), channel_id=1, source_target_pairs={{0,1},{1,0},{2,10},{3,11},{4,5},{5,4},{6,14},{7,15},{8,9},{9,8},{1... | collective-permute-start | bytes 737288 | tf_op jit(solution)/shard_map/ppermute | solution.py:183
  114.9 1.7 %copy-start.4 = (f32[518,256]{1,0:T(8,128)S(1)}, f32[518,256]{1,0:T(8,128)}, u32[]{:S(2)}) copy-start(f32[518,256]{1,0:T(8,128)} %copy-done.3) | copy-start | bytes 1591300
  114.9 1.7 %copy-start.8 = (bf16[768,256]{1,0:T(8,128)(2,1)S(1)}, bf16[768,256]{1,0:T(8,128)(2,1)}, u32[]{:S(2)}) copy-start(bf16[768,256]{1,0:T(8,128)(2,1)} %param.20) | copy-start | bytes 1179652
  115.0 1.7 %copy-start.10 = (bf16[512,256]{1,0:T(8,128)(2,1)S(1)}, bf16[512,256]{1,0:T(8,128)(2,1)}, u32[]{:S(2)}) copy-start(bf16[512,256]{1,0:T(8,128)(2,1)} %copy-done.9) | copy-start | bytes 786436
  115.0 1.7 %copy-start.12 = (bf16[512,256]{1,0:T(8,128)(2,1)S(1)}, bf16[512,256]{1,0:T(8,128)(2,1)}, u32[]{:S(2)}) copy-start(bf16[512,256]{1,0:T(8,128)(2,1)} %copy-done.11) | copy-start | bytes 786436
  115.0 1.7 %copy-start.14 = (bf16[512,256]{1,0:T(8,128)(2,1)S(1)}, bf16[512,256]{1,0:T(8,128)(2,1)}, u32[]{:S(2)}) copy-start(bf16[512,256]{1,0:T(8,128)(2,1)} %copy-done.13) | copy-start | bytes 786436
  115.0 1.7 %copy-start.19 = (f32[256]{0:T(256)S(1)}, f32[256]{0:T(256)}, u32[]{:S(2)}) copy-start(f32[256]{0:T(256)} %param.21) | copy-start | bytes 3076
  115.1 3.7 %collective-permute-start.17 = (f32[1920,128]{1,0:T(8,128)S(1)}, f32[1920,128]{1,0:T(8,128)S(1)}, u32[]{:S(2)}, u32[]{:S(2)}) collective-permute-start(f32[1920,128]{1,0:T(8,128)S(1)} %pad_maximum_fusion), channel_id=1, source_target_pairs={{0,2},{1,3},{2,0},{3,1},{4,6},{5,7},{6,4},{7,5},{8,10},{9,11},{10,... | collective-permute-start | bytes 2949128 | tf_op jit(solution)/shard_map/ppermute | solution.py:192
  (6 other events, 5.3 us)

commit v8 on v6

--- a/solution.py
+++ b/solution.py
@@ -211,8 +211,14 @@
     core = lax.axis_index("dp") % 2
     tm = lax.axis_index("tm")
     mine = jnp.where(core == 0, w_ups[:, :cols], w_ups[:, cols:])
-    got = lax.ppermute(mine, "tm", [(0, 1), (1, 0)])
-    partner = lax.ppermute(got, "dp", [(i, i ^ 1) for i in range(dp_size)])
+    split = rows // 2
+    got_parts = [
+        lax.ppermute(mine[:split], "tm", [(0, 1), (1, 0)]),
+        lax.ppermute(mine[split:], "tm", [(0, 1), (1, 0)]),
+    ]
+    swap = [(i, i ^ 1) for i in range(dp_size)]
+    partner = jnp.concatenate([lax.ppermute(part, "dp", swap) for part in got_parts])
+    got = jnp.concatenate(got_parts)
     low = jnp.where(core == 0, got, partner)
     high = jnp.where(core == 0, partner, got)
 

time: 108 us -> 105 us (0.972)
  waiting for transfers between devices: 45.2 us -> 40.1 us
  starting transfers between devices: 31.7 us -> 33.6 us
    ppermute x2 -> x4, waiting for transfers between devices: 16.2 us -> 0.35 us  [the longest x2 0.34 us: ups_functions(): lax.ppermute(part, 'dp', swap)]
    ppermute x1, waiting for transfers between devices: 0.01 us -> 13.9 us  [with_halo(): lax.ppermute(lax.slice_in_dim(block, 0, width, axis=dim), axis, backward)]
    all_to_all x1, waiting for transfers between devices: 2.13 us -> 0.59 us  [on_device(): lax.all_to_all(outgoing, 'dp', split_axis=0, concat_axis=0, tiled=True)]
    ppermute x1, waiting for transfers between devices: 1.26 us -> 0.01 us  [with_halo(): lax.ppermute(lax.slice_in_dim(block, block.shape[dim] - width, None, axis...]
    ppermute x1, starting transfers between devices: 3.41 us -> 4.54 us  [with_halo(): lax.ppermute(lax.slice_in_dim(block, block.shape[dim] - width, None, axis...]
    ppermute x2 -> x4, starting transfers between devices: 1.62 us -> 2.68 us  [the longest x1 1.55 us: ups_functions(): lax.ppermute(mine[split:], 'tm', [(0, 1), (1, 0)])]
    unnamed x55 -> x51, local copies, waits for them, and re-layouts: 5.28 us -> 5.29 us
  transfers between devices with their start and end apart: 19 -> 21, of which waited for: 15 -> 14; matrix products, arithmetic and copies ran while one was open for 10% -> 11% of each run, Pallas kernels for 0% -> 0%
where the time goes in v8:
time: 105 us
  waiting for transfers between devices  40.1 us (38%)
  starting transfers between devices  33.6 us (32%)
  local copies, waits for them, and re-layouts  13.1 us (12%)
  other arithmetic  9.4 us (9%)
  matrix products  7.17 us (7%)
  between operations  1.32 us (1%)
    ppermute x1, waiting for transfers between devices, with_halo(): lax.ppermute(lax.slice_in_dim(block, 0, width, axis=dim), axis, backward)  13.9 us
    ppermute x6, waiting for transfers between devices, butterfly_psum(): total = total + lax.ppermute(send, axes, perm_of(step, offset))  12.6 us
    ppermute x6, waiting for transfers between devices, butterfly_psum(): lax.ppermute(x, axes, perm_of(step, o))  9.26 us
    ppermute x6, starting transfers between devices, butterfly_psum(): lax.ppermute(x, axes, perm_of(step, o))  8.01 us
    ppermute x6, starting transfers between devices, butterfly_psum(): total = total + lax.ppermute(send, axes, perm_of(step, offset))  7.66 us
    all_to_all x1, starting transfers between devices, on_device(): lax.all_to_all(outgoing, 'dp', split_axis=0, concat_axis=0, tiled=True)  7.36 us
    unnamed x51, local copies, waits for them, and re-layouts  5.29 us
    ppermute x1, starting transfers between devices, with_halo(): lax.ppermute(lax.slice_in_dim(block, block.shape[dim] - width, None, axis...  4.54 us
  transfers between devices with their start and end apart: 21, of which 14 were waited for; matrix products, arithmetic and copies ran while one was open for 11% of the time, Pallas kernels for 0%

profile of v8, /device:TPU:0, one launch (start us, length us, event | category | flops | bytes accessed | tf_op | source)
XLA Modules:
  0.0 104.6 jit_solution(4902210088176596601)
XLA Ops:
  5.0 7.4 %all-to-all-start = ((bf16[16,2,321]{2,1,0:T(2,128)(2,1)}), bf16[16,2,321]{2,1,0:T(2,128)(2,1)S(1)}, u32[]{:S(2)}, u32[]{:S(2)}) async-start(bf16[16,2,321]{2,1,0:T(2,128)(2,1)} %reshape.101), calls=%async_computation | async-start | bytes 49152 | tf_op jit(solution)/shard_map/all_to_all | solution.py:262
  12.4 1.7 %slice_select_fusion = bf16[256,2048]{1,0:T(8,128)(2,1)S(1)} fusion(bf16[256,4096]{1,0:T(8,128)(2,1)} %param.18, pred[]{:T(512)S(6)} %eq.142), kind=kLoop, calls=%fused_computation.21 | loop fusion | flops 524288 | bytes 3145729 | tf_op jit(solution)/shard_map/jit(_where)/select_n | solution.py:213
  14.1 1.0 fusion.54
  15.1 1.5 %collective-permute-start.3 = (bf16[128,2048]{1,0:T(8,128)(2,1)}, bf16[128,2048]{1,0:T(8,128)(2,1)S(1)}, u32[]{:S(2)}, u32[]{:S(2)}) collective-permute-start(bf16[128,2048]{1,0:T(8,128)(2,1)} %get-tuple-element.22), channel_id=1, source_target_pairs={{0,1},{1,0},{2,3},{3,2},{4,5},{5,4},{6,7},{7,6},{8,9},{9,8},{10,11... | collective-permute-start | bytes 1572872 | tf_op jit(solution)/shard_map/ppermute | solution.py:217
  20.6 1.3 %collective-permute-start.1 = (bf16[4,80]{1,0:T(4,128)(2,1)S(1)}, bf16[4,80]{1,0:T(4,128)(2,1)S(1)}, u32[]{:S(2)}, u32[]{:S(2)}) collective-permute-start(bf16[4,80]{1,0:T(4,128)(2,1)S(1)} %get-tuple-element.46), channel_id=1, source_target_pairs={{1,0},{3,2},{5,4},{7,6},{9,8},{11,10},{13,12},{15,14},{17,16},{19,... | collective-permute-start | bytes 1928 | tf_op jit(solution)/shard_map/ppermute | solution.py:19
  21.9 4.5 %collective-permute-start = (bf16[4,80]{1,0:T(4,128)(2,1)S(1)}, bf16[4,80]{1,0:T(4,128)(2,1)S(1)}, u32[]{:S(2)}, u32[]{:S(2)}) collective-permute-start(bf16[4,80]{1,0:T(4,128)(2,1)S(1)} %get-tuple-element.47), channel_id=1, source_target_pairs={{0,1},{2,3},{4,5},{6,7},{8,9},{10,11},{12,13},{14,15},{16,17},{18,... | collective-permute-start | bytes 1928 | tf_op jit(solution)/shard_map/ppermute | solution.py:16
  27.1 13.9 %collective-permute-done.1 = bf16[4,80]{1,0:T(4,128)(2,1)S(1)} collective-permute-done((bf16[4,80]{1,0:T(4,128)(2,1)S(1)}, bf16[4,80]{1,0:T(4,128)(2,1)S(1)}, u32[]{:S(2)}, u32[]{:S(2)}) %collective-permute-start.1) | collective-permute-done | bytes 672 | tf_op jit(solution)/shard_map/ppermute | solution.py:19
  44.8 1.1 %constant_dynamic-update-slice_fusion.3 = bf16[256,2048]{1,0:T(8,128)(2,1)S(1)} fusion(bf16[128,2048]{1,0:T(8,128)(2,1)} %collective-permute-done.2), kind=kLoop, calls=%fused_computation.73 | loop fusion | bytes 1048576
  47.1 1.2 %copy-done.1 = bf16[256,4096]{1,0:T(8,128)(2,1)S(1)} copy-done((bf16[256,4096]{1,0:T(8,128)(2,1)S(1)}, bf16[256,4096]{1,0:T(8,128)(2,1)}, u32[]{:S(2)}) %copy-start.1) | copy-done | bytes 2097176
  55.0 2.3 %collective-permute-done.6 = f32[1920,128]{1,0:T(8,128)} collective-permute-done((f32[1920,128]{1,0:T(8,128)S(1)}, f32[1920,128]{1,0:T(8,128)}, u32[]{:S(2)}, u32[]{:S(2)}) %collective-permute-start.6) | collective-permute-done | bytes 983072 | tf_op jit(solution)/shard_map/ppermute | solution.py:170
  57.3 1.3 %dynamic-slice_add_fusion = f32[1920,128]{1,0:T(8,128)S(1)} fusion(f32[1920,128]{1,0:T(8,128)} %collective-permute-done.6, f32[3840,128]{1,0:T(8,128)S(1)} %fusion, s32[]{:T(128)S(6)} %select_n.365), kind=kLoop, calls=%fused_computation.25 | loop fusion | flops 245760 | bytes 2949124 | tf_op jit(solution)/shard_map/add | solution.py:170
  58.7 1.6 %collective-permute-start.7 = (f32[480,128]{1,0:T(8,128)S(1)}, f32[480,128]{1,0:T(8,128)S(1)}, u32[]{:S(2)}, u32[]{:S(2)}) collective-permute-start(f32[480,128]{1,0:T(8,128)S(1)} %get-tuple-element.26), channel_id=1, source_target_pairs={{0,1},{1,0},{2,10},{3,11},{4,5},{5,4},{6,14},{7,15},{8,9},{9,8},{1... | collective-permute-start | bytes 737288 | tf_op jit(solution)/shard_map/ppermute | solution.py:178
  60.3 1.6 %collective-permute-start.9 = (f32[480,128]{1,0:T(8,128)S(1)}, f32[480,128]{1,0:T(8,128)S(1)}, u32[]{:S(2)}, u32[]{:S(2)}) collective-permute-start(f32[480,128]{1,0:T(8,128)S(1)} %get-tuple-element.27), channel_id=1, source_target_pairs={{0,5},{1,4},{2,26},{3,27},{4,1},{5,0},{6,30},{7,31},{8,13},{9,12},... | collective-permute-start | bytes 737288 | tf_op jit(solution)/shard_map/ppermute | solution.py:178
  62.2 5.3 %collective-permute-done.7 = f32[480,128]{1,0:T(8,128)S(1)} collective-permute-done((f32[480,128]{1,0:T(8,128)S(1)}, f32[480,128]{1,0:T(8,128)S(1)}, u32[]{:S(2)}, u32[]{:S(2)}) %collective-permute-start.7) | collective-permute-done | bytes 245792 | tf_op jit(solution)/shard_map/ppermute | solution.py:178
  67.6 1.5 %collective-permute-done.8 = f32[480,128]{1,0:T(8,128)S(1)} collective-permute-done((f32[480,128]{1,0:T(8,128)S(1)}, f32[480,128]{1,0:T(8,128)S(1)}, u32[]{:S(2)}, u32[]{:S(2)}) %collective-permute-start.8) | collective-permute-done | bytes 245792 | tf_op jit(solution)/shard_map/ppermute | solution.py:178
  69.2 1.7 %collective-permute-start.10 = (f32[120,128]{1,0:T(8,128)S(1)}, f32[120,128]{1,0:T(8,128)S(1)}, u32[]{:S(2)}, u32[]{:S(2)}) collective-permute-start(f32[120,128]{1,0:T(8,128)S(1)} %get-tuple-element.36), channel_id=1, source_target_pairs={{0,8},{1,9},{2,3},{3,2},{4,12},{5,13},{6,7},{7,6},{8,0},{9,1},{10,... | collective-permute-start | bytes 184328 | tf_op jit(solution)/shard_map/ppermute | solution.py:178
  70.9 2.4 %collective-permute-start.12 = (f32[120,128]{1,0:T(8,128)S(1)}, f32[120,128]{1,0:T(8,128)S(1)}, u32[]{:S(2)}, u32[]{:S(2)}) collective-permute-start(f32[120,128]{1,0:T(8,128)S(1)} %get-tuple-element.37), channel_id=1, source_target_pairs={{0,24},{1,25},{2,7},{3,6},{4,28},{5,29},{6,3},{7,2},{8,16},{9,17},... | collective-permute-start | bytes 184328 | tf_op jit(solution)/shard_map/ppermute | solution.py:178
  73.3 1.6 %collective-permute-done.10 = f32[120,128]{1,0:T(8,128)S(1)} collective-permute-done((f32[120,128]{1,0:T(8,128)S(1)}, f32[120,128]{1,0:T(8,128)S(1)}, u32[]{:S(2)}, u32[]{:S(2)}) %collective-permute-start.10) | collective-permute-done | bytes 61472 | tf_op jit(solution)/shard_map/ppermute | solution.py:178
  74.9 2.0 %collective-permute-done.12 = f32[120,128]{1,0:T(8,128)S(1)} collective-permute-done((f32[120,128]{1,0:T(8,128)S(1)}, f32[120,128]{1,0:T(8,128)S(1)}, u32[]{:S(2)}, u32[]{:S(2)}) %collective-permute-start.12) | collective-permute-done | bytes 61472 | tf_op jit(solution)/shard_map/ppermute | solution.py:178
  76.9 2.1 %collective-permute-done.11 = f32[120,128]{1,0:T(8,128)S(1)} collective-permute-done((f32[120,128]{1,0:T(8,128)S(1)}, f32[120,128]{1,0:T(8,128)S(1)}, u32[]{:S(2)}, u32[]{:S(2)}) %collective-permute-start.11) | collective-permute-done | bytes 61472 | tf_op jit(solution)/shard_map/ppermute | solution.py:178
  79.1 1.6 %collective-permute-start.15 = (f32[120,128]{1,0:T(8,128)S(1)}, f32[120,128]{1,0:T(8,128)S(1)}, u32[]{:S(2)}, u32[]{:S(2)}) collective-permute-start(f32[120,128]{1,0:T(8,128)S(1)} %add_add_fusion.1), channel_id=1, source_target_pairs={{0,24},{1,25},{2,7},{3,6},{4,28},{5,29},{6,3},{7,2},{8,16},{9,17},... | collective-permute-start | bytes 184328 | tf_op jit(solution)/shard_map/ppermute | solution.py:183
  80.7 2.8 %collective-permute-start.13 = (f32[120,128]{1,0:T(8,128)S(1)}, f32[120,128]{1,0:T(8,128)S(1)}, u32[]{:S(2)}, u32[]{:S(2)}) collective-permute-start(f32[120,128]{1,0:T(8,128)S(1)} %add_add_fusion.1), channel_id=1, source_target_pairs={{0,8},{1,9},{2,3},{3,2},{4,12},{5,13},{6,7},{7,6},{8,0},{9,1},{10,... | collective-permute-start | bytes 184328 | tf_op jit(solution)/shard_map/ppermute | solution.py:183
  83.5 1.6 %collective-permute-done.15 = f32[120,128]{1,0:T(8,128)S(1)} collective-permute-done((f32[120,128]{1,0:T(8,128)S(1)}, f32[120,128]{1,0:T(8,128)S(1)}, u32[]{:S(2)}, u32[]{:S(2)}) %collective-permute-start.15) | collective-permute-done | bytes 61472 | tf_op jit(solution)/shard_map/ppermute | solution.py:183
  85.1 1.3 %collective-permute-done.14 = f32[120,128]{1,0:T(8,128)S(1)} collective-permute-done((f32[120,128]{1,0:T(8,128)S(1)}, f32[120,128]{1,0:T(8,128)S(1)}, u32[]{:S(2)}, u32[]{:S(2)}) %collective-permute-start.14) | collective-permute-done | bytes 61472 | tf_op jit(solution)/shard_map/ppermute | solution.py:183
  86.5 2.6 %collective-permute-start.18 = (f32[480,128]{1,0:T(8,128)S(1)}, f32[480,128]{1,0:T(8,128)S(1)}, u32[]{:S(2)}, u32[]{:S(2)}) collective-permute-start(f32[480,128]{1,0:T(8,128)S(1)} %pad_maximum_fusion.4), channel_id=1, source_target_pairs={{0,5},{1,4},{2,26},{3,27},{4,1},{5,0},{6,30},{7,31},{8,13},{9,12},... | collective-permute-start | bytes 737288 | tf_op jit(solution)/shard_map/ppermute | solution.py:183
  90.1 3.7 %collective-permute-done.18 = f32[480,128]{1,0:T(8,128)S(1)} collective-permute-done((f32[480,128]{1,0:T(8,128)S(1)}, f32[480,128]{1,0:T(8,128)S(1)}, u32[]{:S(2)}, u32[]{:S(2)}) %collective-permute-start.18) | collective-permute-done | bytes 245792 | tf_op jit(solution)/shard_map/ppermute | solution.py:183
  93.7 2.6 %collective-permute-done.17 = f32[480,128]{1,0:T(8,128)S(1)} collective-permute-done((f32[480,128]{1,0:T(8,128)S(1)}, f32[480,128]{1,0:T(8,128)S(1)}, u32[]{:S(2)}, u32[]{:S(2)}) %collective-permute-start.17) | collective-permute-done | bytes 245792 | tf_op jit(solution)/shard_map/ppermute | solution.py:183
  96.8 1.6 %collective-permute-start.19 = (f32[1920,128]{1,0:T(8,128)S(1)}, f32[1920,128]{1,0:T(8,128)S(1)}, u32[]{:S(2)}, u32[]{:S(2)}) collective-permute-start(f32[1920,128]{1,0:T(8,128)S(1)} %pad_maximum_fusion), channel_id=1, source_target_pairs={{0,2},{1,3},{2,0},{3,1},{4,6},{5,7},{6,4},{7,5},{8,10},{9,11},{10,... | collective-permute-start | bytes 2949128 | tf_op jit(solution)/shard_map/ppermute | solution.py:192
  98.4 1.1 %fusion.3 = bf16[1,512,256]{2,1,0:T(8,128)(2,1)} fusion(bf16[768,256]{1,0:T(8,128)(2,1)S(1)} %copy-done.6, f32[518,256]{1,0:T(8,128)S(1)} %copy-done.4, bf16[512,256]{1,0:T(8,128)(2,1)S(1)} %copy-done.10, bf16[512,256]{1,0:T(8,128)(2,1)S(1)} %copy-done.12, bf16[512,256]{1,0:T(8,128)(2,1)S(1)} %copy-done.8, f32[256]{0:T(256)S(1)} %copy-done.17), kind=kOutput, calls=%fused_computation.11 | convolution fusion | flops 204079104 | bytes 1967104 | tf_op jit(solution)/shard_map/dot_general | solution.py:92
  99.5 1.1 %collective-permute-done.19 = f32[1920,128]{1,0:T(8,128)S(1)} collective-permute-done((f32[1920,128]{1,0:T(8,128)S(1)}, f32[1920,128]{1,0:T(8,128)S(1)}, u32[]{:S(2)}, u32[]{:S(2)}) %collective-permute-start.19) | collective-permute-done | bytes 983072 | tf_op jit(solution)/shard_map/ppermute | solution.py:192
  102.3 1.2 %reshape.96 = f32[560,512]{1,0:T(8,128)} reshape(f32[2240,128]{1,0:T(8,128)S(1)} %slice.170) | data formatting | bytes 2293760 | tf_op jit(solution)/shard_map/reshape | solution.py:197
  103.5 1.1 %reshape.97 = f32[768,256]{1,0:T(8,128)} reshape(f32[1536,128]{1,0:T(8,128)S(1)} %slice.172) | data formatting | bytes 1572864 | tf_op jit(solution)/shard_map/reshape | solution.py:197
  (130 shorter events, 23.7 us)
Async XLA Ops:
  0.6 42.6 %copy-start = (bf16[560,512]{1,0:T(8,128)(2,1)S(1)}, bf16[560,512]{1,0:T(8,128)(2,1)}, u32[]{:S(2)}) copy-start(bf16[560,512]{1,0:T(8,128)(2,1)} %param.16) | copy-start | bytes 1720324
  5.0 13.9 %all-to-all-start = ((bf16[16,2,321]{2,1,0:T(2,128)(2,1)}), bf16[16,2,321]{2,1,0:T(2,128)(2,1)S(1)}, u32[]{:S(2)}, u32[]{:S(2)}) async-start(bf16[16,2,321]{2,1,0:T(2,128)(2,1)} %reshape.101), calls=%async_computation | async-start | bytes 49152 | tf_op jit(solution)/shard_map/all_to_all | solution.py:262
  12.4 7.3 %copy-start.2 = (bf16[1,512,256]{2,1,0:T(8,128)(2,1)S(1)}, bf16[1,512,256]{2,1,0:T(8,128)(2,1)}, u32[]{:S(2)}) copy-start(bf16[1,512,256]{2,1,0:T(8,128)(2,1)} %param.15) | copy-start | bytes 786436
  14.1 12.4 %copy-start.5 = (bf16[768,256]{1,0:T(8,128)(2,1)S(1)}, bf16[768,256]{1,0:T(8,128)(2,1)}, u32[]{:S(2)}) copy-start(bf16[768,256]{1,0:T(8,128)(2,1)} %param.20) | copy-start | bytes 1179652
  15.1 29.1 %collective-permute-start.3 = (bf16[128,2048]{1,0:T(8,128)(2,1)}, bf16[128,2048]{1,0:T(8,128)(2,1)S(1)}, u32[]{:S(2)}, u32[]{:S(2)}) collective-permute-start(bf16[128,2048]{1,0:T(8,128)(2,1)} %get-tuple-element.22), channel_id=1, source_target_pairs={{0,1},{1,0},{2,3},{3,2},{4,5},{5,4},{6,7},{7,6},{8,9},{9,8},{10,11... | collective-permute-start | bytes 1572872 | tf_op jit(solution)/shard_map/ppermute | solution.py:217
  16.7 26.5 %collective-permute-start.2 = (bf16[128,2048]{1,0:T(8,128)(2,1)}, bf16[128,2048]{1,0:T(8,128)(2,1)}, u32[]{:S(2)}, u32[]{:S(2)}) collective-permute-start(bf16[128,2048]{1,0:T(8,128)(2,1)} %get-tuple-element.23), channel_id=1, source_target_pairs={{0,1},{1,0},{2,3},{3,2},{4,5},{5,4},{6,7},{7,6},{8,9},{9,8},{10,11... | collective-permute-start | bytes 1572872 | tf_op jit(solution)/shard_map/ppermute | solution.py:216
  20.6 20.3 %collective-permute-start.1 = (bf16[4,80]{1,0:T(4,128)(2,1)S(1)}, bf16[4,80]{1,0:T(4,128)(2,1)S(1)}, u32[]{:S(2)}, u32[]{:S(2)}) collective-permute-start(bf16[4,80]{1,0:T(4,128)(2,1)S(1)} %get-tuple-element.46), channel_id=1, source_target_pairs={{1,0},{3,2},{5,4},{7,6},{9,8},{11,10},{13,12},{15,14},{17,16},{19,... | collective-permute-start | bytes 1928 | tf_op jit(solution)/shard_map/ppermute | solution.py:19
  21.9 19.0 %collective-permute-start = (bf16[4,80]{1,0:T(4,128)(2,1)S(1)}, bf16[4,80]{1,0:T(4,128)(2,1)S(1)}, u32[]{:S(2)}, u32[]{:S(2)}) collective-permute-start(bf16[4,80]{1,0:T(4,128)(2,1)S(1)} %get-tuple-element.47), channel_id=1, source_target_pairs={{0,1},{2,3},{4,5},{6,7},{8,9},{10,11},{12,13},{14,15},{16,17},{18,... | collective-permute-start | bytes 1928 | tf_op jit(solution)/shard_map/ppermute | solution.py:16
  43.2 2.7 %collective-permute-start.4 = (bf16[128,2048]{1,0:T(8,128)(2,1)}, bf16[128,2048]{1,0:T(8,128)(2,1)S(1)}, u32[]{:S(2)}, u32[]{:S(2)}) collective-permute-start(bf16[128,2048]{1,0:T(8,128)(2,1)} %collective-permute-done.2), channel_id=1, source_target_pairs={{0,2},{2,0},{4,6},{6,4},{8,10},{10,8},{12,14},{14,12},{16,18},{18,... | collective-permute-start | bytes 1572872 | tf_op jit(solution)/shard_map/ppermute | solution.py:220
  44.2 2.1 %collective-permute-start.5 = (bf16[128,2048]{1,0:T(8,128)(2,1)S(1)}, bf16[128,2048]{1,0:T(8,128)(2,1)S(1)}, u32[]{:S(2)}, u32[]{:S(2)}) collective-permute-start(bf16[128,2048]{1,0:T(8,128)(2,1)S(1)} %collective-permute-done.3), channel_id=1, source_target_pairs={{0,2},{2,0},{4,6},{6,4},{8,10},{10,8},{12,14},{14,12},{16,18},{18,... | collective-permute-start | bytes 1572872 | tf_op jit(solution)/shard_map/ppermute | solution.py:220
  46.7 1.6 %copy-start.1 = (bf16[256,4096]{1,0:T(8,128)(2,1)S(1)}, bf16[256,4096]{1,0:T(8,128)(2,1)}, u32[]{:S(2)}) copy-start(bf16[256,4096]{1,0:T(8,128)(2,1)} %param.18) | copy-start | bytes 6291460
  50.2 1.6 %copy-start.3 = (f32[518,256]{1,0:T(8,128)}, f32[518,256]{1,0:T(8,128)S(1)}, u32[]{:S(2)}) copy-start(f32[518,256]{1,0:T(8,128)S(1)} %get-tuple-element.18) | copy-start | bytes 1591300
  54.5 2.8 %collective-permute-start.6 = (f32[1920,128]{1,0:T(8,128)S(1)}, f32[1920,128]{1,0:T(8,128)}, u32[]{:S(2)}, u32[]{:S(2)}) collective-permute-start(f32[1920,128]{1,0:T(8,128)S(1)} %constant_dynamic-slice_fusion.6), channel_id=1, source_target_pairs={{0,2},{1,3},{2,0},{3,1},{4,6},{5,7},{6,4},{7,5},{8,10},{9,11},{10,... | collective-permute-start | bytes 2949128 | tf_op jit(solution)/shard_map/ppermute | solution.py:170
  58.7 8.9 %collective-permute-start.7 = (f32[480,128]{1,0:T(8,128)S(1)}, f32[480,128]{1,0:T(8,128)S(1)}, u32[]{:S(2)}, u32[]{:S(2)}) collective-permute-start(f32[480,128]{1,0:T(8,128)S(1)} %get-tuple-element.26), channel_id=1, source_target_pairs={{0,1},{1,0},{2,10},{3,11},{4,5},{5,4},{6,14},{7,15},{8,9},{9,8},{1... | collective-permute-start | bytes 737288 | tf_op jit(solution)/shard_map/ppermute | solution.py:178
  60.3 7.3 %collective-permute-start.9 = (f32[480,128]{1,0:T(8,128)S(1)}, f32[480,128]{1,0:T(8,128)S(1)}, u32[]{:S(2)}, u32[]{:S(2)}) collective-permute-start(f32[480,128]{1,0:T(8,128)S(1)} %get-tuple-element.27), channel_id=1, source_target_pairs={{0,5},{1,4},{2,26},{3,27},{4,1},{5,0},{6,30},{7,31},{8,13},{9,12},... | collective-permute-start | bytes 737288 | tf_op jit(solution)/shard_map/ppermute | solution.py:178
  61.9 7.2 %collective-permute-start.8 = (f32[480,128]{1,0:T(8,128)S(1)}, f32[480,128]{1,0:T(8,128)S(1)}, u32[]{:S(2)}, u32[]{:S(2)}) collective-permute-start(f32[480,128]{1,0:T(8,128)S(1)} %get-tuple-element.28), channel_id=1, source_target_pairs={{0,4},{1,5},{2,18},{3,19},{4,0},{5,1},{6,22},{7,23},{8,12},{9,13},... | collective-permute-start | bytes 737288 | tf_op jit(solution)/shard_map/ppermute | solution.py:178
  69.2 5.7 %collective-permute-start.10 = (f32[120,128]{1,0:T(8,128)S(1)}, f32[120,128]{1,0:T(8,128)S(1)}, u32[]{:S(2)}, u32[]{:S(2)}) collective-permute-start(f32[120,128]{1,0:T(8,128)S(1)} %get-tuple-element.36), channel_id=1, source_target_pairs={{0,8},{1,9},{2,3},{3,2},{4,12},{5,13},{6,7},{7,6},{8,0},{9,1},{10,... | collective-permute-start | bytes 184328 | tf_op jit(solution)/shard_map/ppermute | solution.py:178
  70.9 6.0 %collective-permute-start.12 = (f32[120,128]{1,0:T(8,128)S(1)}, f32[120,128]{1,0:T(8,128)S(1)}, u32[]{:S(2)}, u32[]{:S(2)}) collective-permute-start(f32[120,128]{1,0:T(8,128)S(1)} %get-tuple-element.37), channel_id=1, source_target_pairs={{0,24},{1,25},{2,7},{3,6},{4,28},{5,29},{6,3},{7,2},{8,16},{9,17},... | collective-permute-start | bytes 184328 | tf_op jit(solution)/shard_map/ppermute | solution.py:178
  73.3 5.8 %collective-permute-start.11 = (f32[120,128]{1,0:T(8,128)S(1)}, f32[120,128]{1,0:T(8,128)S(1)}, u32[]{:S(2)}, u32[]{:S(2)}) collective-permute-start(f32[120,128]{1,0:T(8,128)S(1)} %get-tuple-element.38), channel_id=1, source_target_pairs={{0,16},{1,17},{2,6},{3,7},{4,20},{5,21},{6,2},{7,3},{8,24},{9,25},... | collective-permute-start | bytes 184328 | tf_op jit(solution)/shard_map/ppermute | solution.py:178
  79.1 6.1 %collective-permute-start.15 = (f32[120,128]{1,0:T(8,128)S(1)}, f32[120,128]{1,0:T(8,128)S(1)}, u32[]{:S(2)}, u32[]{:S(2)}) collective-permute-start(f32[120,128]{1,0:T(8,128)S(1)} %add_add_fusion.1), channel_id=1, source_target_pairs={{0,24},{1,25},{2,7},{3,6},{4,28},{5,29},{6,3},{7,2},{8,16},{9,17},... | collective-permute-start | bytes 184328 | tf_op jit(solution)/shard_map/ppermute | solution.py:183
  80.7 5.8 %collective-permute-start.14 = (f32[120,128]{1,0:T(8,128)S(1)}, f32[120,128]{1,0:T(8,128)S(1)}, u32[]{:S(2)}, u32[]{:S(2)}) collective-permute-start(f32[120,128]{1,0:T(8,128)S(1)} %add_add_fusion.1), channel_id=1, source_target_pairs={{0,16},{1,17},{2,6},{3,7},{4,20},{5,21},{6,2},{7,3},{8,24},{9,25},... | collective-permute-start | bytes 184328 | tf_op jit(solution)/shard_map/ppermute | solution.py:183
  80.7 5.8 %collective-permute-start.13 = (f32[120,128]{1,0:T(8,128)S(1)}, f32[120,128]{1,0:T(8,128)S(1)}, u32[]{:S(2)}, u32[]{:S(2)}) collective-permute-start(f32[120,128]{1,0:T(8,128)S(1)} %add_add_fusion.1), channel_id=1, source_target_pairs={{0,8},{1,9},{2,3},{3,2},{4,12},{5,13},{6,7},{7,6},{8,0},{9,1},{10,... | collective-permute-start | bytes 184328 | tf_op jit(solution)/shard_map/ppermute | solution.py:183
  86.5 7.2 %collective-permute-start.18 = (f32[480,128]{1,0:T(8,128)S(1)}, f32[480,128]{1,0:T(8,128)S(1)}, u32[]{:S(2)}, u32[]{:S(2)}) collective-permute-start(f32[480,128]{1,0:T(8,128)S(1)} %pad_maximum_fusion.4), channel_id=1, source_target_pairs={{0,5},{1,4},{2,26},{3,27},{4,1},{5,0},{6,30},{7,31},{8,13},{9,12},... | collective-permute-start | bytes 737288 | tf_op jit(solution)/shard_map/ppermute | solution.py:183
  89.2 7.2 %collective-permute-start.17 = (f32[480,128]{1,0:T(8,128)S(1)}, f32[480,128]{1,0:T(8,128)S(1)}, u32[]{:S(2)}, u32[]{:S(2)}) collective-permute-start(f32[480,128]{1,0:T(8,128)S(1)} %pad_maximum_fusion.4), channel_id=1, source_target_pairs={{0,4},{1,5},{2,18},{3,19},{4,0},{5,1},{6,22},{7,23},{8,12},{9,13},... | collective-permute-start | bytes 737288 | tf_op jit(solution)/shard_map/ppermute | solution.py:183
  89.6 6.8 %collective-permute-start.16 = (f32[480,128]{1,0:T(8,128)S(1)}, f32[480,128]{1,0:T(8,128)S(1)}, u32[]{:S(2)}, u32[]{:S(2)}) collective-permute-start(f32[480,128]{1,0:T(8,128)S(1)} %pad_maximum_fusion.4), channel_id=1, source_target_pairs={{0,1},{1,0},{2,10},{3,11},{4,5},{5,4},{6,14},{7,15},{8,9},{9,8},{1... | collective-permute-start | bytes 737288 | tf_op jit(solution)/shard_map/ppermute | solution.py:183
  96.6 1.8 %copy-start.4 = (f32[518,256]{1,0:T(8,128)S(1)}, f32[518,256]{1,0:T(8,128)}, u32[]{:S(2)}) copy-start(f32[518,256]{1,0:T(8,128)} %copy-done.3) | copy-start | bytes 1591300
  96.6 1.8 %copy-start.6 = (bf16[768,256]{1,0:T(8,128)(2,1)S(1)}, bf16[768,256]{1,0:T(8,128)(2,1)}, u32[]{:S(2)}) copy-start(bf16[768,256]{1,0:T(8,128)(2,1)} %param.20) | copy-start | bytes 1179652
  96.6 1.8 %copy-start.8 = (bf16[512,256]{1,0:T(8,128)(2,1)S(1)}, bf16[512,256]{1,0:T(8,128)(2,1)}, u32[]{:S(2)}) copy-start(bf16[512,256]{1,0:T(8,128)(2,1)} %copy-done.7) | copy-start | bytes 786436
  96.6 1.8 %copy-start.10 = (bf16[512,256]{1,0:T(8,128)(2,1)S(1)}, bf16[512,256]{1,0:T(8,128)(2,1)}, u32[]{:S(2)}) copy-start(bf16[512,256]{1,0:T(8,128)(2,1)} %copy-done.9) | copy-start | bytes 786436
  96.6 1.8 %copy-start.12 = (bf16[512,256]{1,0:T(8,128)(2,1)S(1)}, bf16[512,256]{1,0:T(8,128)(2,1)}, u32[]{:S(2)}) copy-start(bf16[512,256]{1,0:T(8,128)(2,1)} %copy-done.11) | copy-start | bytes 786436
  96.7 1.8 %copy-start.17 = (f32[256]{0:T(256)S(1)}, f32[256]{0:T(256)}, u32[]{:S(2)}) copy-start(f32[256]{0:T(256)} %param.21) | copy-start | bytes 3076
  96.8 3.8 %collective-permute-start.19 = (f32[1920,128]{1,0:T(8,128)S(1)}, f32[1920,128]{1,0:T(8,128)S(1)}, u32[]{:S(2)}, u32[]{:S(2)}) collective-permute-start(f32[1920,128]{1,0:T(8,128)S(1)} %pad_maximum_fusion), channel_id=1, source_target_pairs={{0,2},{1,3},{2,0},{3,1},{4,6},{5,7},{6,4},{7,5},{8,10},{9,11},{10,... | collective-permute-start | bytes 2949128 | tf_op jit(solution)/shard_map/ppermute | solution.py:192
  (7 other events, 6.0 us)

commit v9 on v8

--- a/solution.py
+++ b/solution.py
@@ -130,6 +130,23 @@
     return (output_rows, (g_wpre, g_bpre, g_wres, g_bres))
 
 
+def tile_rows(value):
+    if value.ndim == 2 and value.shape[0] % 8 == 0 and value.shape[1] % 128 == 0:
+        r, c = value.shape
+        value = value.reshape(r // 8, 8, c // 128, 128).transpose(0, 2, 1, 3)
+    return jnp.pad(value.reshape(-1), (0, -value.size % 128)).reshape(-1, 128)
+
+
+def untile_rows(rows, shape):
+    if len(shape) == 2 and shape[0] % 8 == 0 and shape[1] % 128 == 0:
+        r, c = shape
+        return rows.reshape(r // 8, c // 128, 8, 128).transpose(0, 2, 1, 3).reshape(shape)
+    size = 1
+    for n in shape:
+        size *= n
+    return rows.reshape(-1)[:size].reshape(shape)
+
+
 def butterfly_psum(parts):
     dp_size = lax.axis_size("dp")
     tm_size = lax.axis_size("tm")
@@ -160,7 +177,8 @@
 
         return jnp.where(core == 0, one(orders[0][step]), one(orders[1][step]))
 
-    flat = jnp.concatenate([p.reshape(-1) for p in parts])
+    tiles = [tile_rows(p) for p in parts]
+    flat = jnp.concatenate([t.reshape(-1) for t in tiles])
     unit = 8 * 128 * count
     padded = -(-flat.shape[0] // unit) * unit
     x = jnp.pad(flat, (0, padded - flat.shape[0])).reshape(padded // 128, 128)
@@ -191,11 +209,10 @@
         x = jnp.concatenate(pieces)
     recv = lax.ppermute(x, axes, core_perm)
     x = jnp.where(core == 0, jnp.concatenate([x, recv]), jnp.concatenate([recv, x]))
-    flat = x.reshape(-1)
     out, at = [], 0
-    for p in parts:
-        out.append(flat[at : at + p.size].reshape(p.shape))
-        at += p.size
+    for p, t in zip(parts, tiles):
+        out.append(untile_rows(x[at : at + t.shape[0]], p.shape))
+        at += t.shape[0]
     return tuple(out)
 
 def ups_functions(w_ups):

time: 105 us -> 103 us (0.981)
  other arithmetic: 9.4 us -> 7.14 us
  waiting for transfers between devices: 40.1 us -> 41.5 us
    reshape x2, local copies, waits for them, and re-layouts: 2.27 us -> 1.14 us  [untile_rows(): return rows.reshape(-1)[:size].reshape(shape)]
    all_to_all x1, waiting for transfers between devices: 0.59 us -> 1.71 us  [on_device(): lax.all_to_all(outgoing, 'dp', split_axis=0, concat_axis=0, tiled=True)]
    unnamed x51 -> x45, local copies, waits for them, and re-layouts: 5.29 us -> 5.4 us
  transfers between devices with their start and end apart: 21 -> 21, of which waited for: 14 -> 13; matrix products, arithmetic and copies ran while one was open for 11% -> 8% of each run, Pallas kernels for 0% -> 0%
where the time goes in v9:
time: 103 us; the launch traced here: 102 us
  waiting for transfers between devices  41.5 us (40%)
  starting transfers between devices  33 us (32%)
  local copies, waits for them, and re-layouts  12.8 us (12%)
  other arithmetic  7.14 us (7%)
  matrix products  6.39 us (6%)
  between operations  1.41 us (1%)
    ppermute x1, waiting for transfers between devices, with_halo(): lax.ppermute(lax.slice_in_dim(block, 0, width, axis=dim), axis, backward)  14.3 us
    ppermute x6, waiting for transfers between devices, butterfly_psum(): total = total + lax.ppermute(send, axes, perm_of(step, offset))  12.6 us
    ppermute x6, waiting for transfers between devices, butterfly_psum(): lax.ppermute(x, axes, perm_of(step, o))  9.25 us
    ppermute x6, starting transfers between devices, butterfly_psum(): lax.ppermute(x, axes, perm_of(step, o))  8.01 us
    ppermute x6, starting transfers between devices, butterfly_psum(): total = total + lax.ppermute(send, axes, perm_of(step, offset))  7.65 us
    all_to_all x1, starting transfers between devices, on_device(): lax.all_to_all(outgoing, 'dp', split_axis=0, concat_axis=0, tiled=True)  7.36 us
    unnamed x45, local copies, waits for them, and re-layouts  5.4 us
    ppermute x1, starting transfers between devices, with_halo(): lax.ppermute(lax.slice_in_dim(block, block.shape[dim] - width, None, axis...  4.54 us
  transfers between devices with their start and end apart: 21, of which 13 were waited for; matrix products, arithmetic and copies ran while one was open for 8% of the time, Pallas kernels for 0%

profile of v9, /device:TPU:0, one launch (start us, length us, event | category | flops | bytes accessed | tf_op | source)
XLA Modules:
  0.0 102.2 jit_solution(6399223900189406701)
XLA Ops:
  5.0 7.4 %all-to-all-start = ((bf16[16,2,321]{2,1,0:T(2,128)(2,1)}), bf16[16,2,321]{2,1,0:T(2,128)(2,1)S(1)}, u32[]{:S(2)}, u32[]{:S(2)}) async-start(bf16[16,2,321]{2,1,0:T(2,128)(2,1)} %reshape.119), calls=%async_computation | async-start | bytes 49152 | tf_op jit(solution)/shard_map/all_to_all | solution.py:279
  12.4 1.7 %slice_select_fusion = bf16[256,2048]{1,0:T(8,128)(2,1)S(1)} fusion(bf16[256,4096]{1,0:T(8,128)(2,1)} %param.18, pred[]{:T(512)S(6)} %eq.142), kind=kLoop, calls=%fused_computation.19 | loop fusion | flops 524288 | bytes 3145729 | tf_op jit(solution)/shard_map/jit(_where)/select_n | solution.py:230
  15.1 1.5 %collective-permute-start.3 = (bf16[128,2048]{1,0:T(8,128)(2,1)}, bf16[128,2048]{1,0:T(8,128)(2,1)}, u32[]{:S(2)}, u32[]{:S(2)}) collective-permute-start(bf16[128,2048]{1,0:T(8,128)(2,1)} %get-tuple-element.22), channel_id=1, source_target_pairs={{0,1},{1,0},{2,3},{3,2},{4,5},{5,4},{6,7},{7,6},{8,9},{9,8},{10,11... | collective-permute-start | bytes 1572872 | tf_op jit(solution)/shard_map/ppermute | solution.py:234
  17.2 1.7 %all-to-all-done = bf16[16,2,321]{2,1,0:T(2,128)(2,1)S(1)} async-done(((bf16[16,2,321]{2,1,0:T(2,128)(2,1)}), bf16[16,2,321]{2,1,0:T(2,128)(2,1)S(1)}, u32[]{:S(2)}, u32[]{:S(2)}) %all-to-all-start) | async-done | bytes 20576 | tf_op jit(solution)/shard_map/all_to_all | solution.py:279
  20.1 1.3 %collective-permute-start.1 = (bf16[4,80]{1,0:T(4,128)(2,1)S(1)}, bf16[4,80]{1,0:T(4,128)(2,1)S(1)}, u32[]{:S(2)}, u32[]{:S(2)}) collective-permute-start(bf16[4,80]{1,0:T(4,128)(2,1)S(1)} %get-tuple-element.48), channel_id=1, source_target_pairs={{1,0},{3,2},{5,4},{7,6},{9,8},{11,10},{13,12},{15,14},{17,16},{19,... | collective-permute-start | bytes 1928 | tf_op jit(solution)/shard_map/ppermute | solution.py:19
  21.4 4.5 %collective-permute-start = (bf16[4,80]{1,0:T(4,128)(2,1)S(1)}, bf16[4,80]{1,0:T(4,128)(2,1)S(1)}, u32[]{:S(2)}, u32[]{:S(2)}) collective-permute-start(bf16[4,80]{1,0:T(4,128)(2,1)S(1)} %get-tuple-element.49), channel_id=1, source_target_pairs={{0,1},{2,3},{4,5},{6,7},{8,9},{10,11},{12,13},{14,15},{16,17},{18,... | collective-permute-start | bytes 1928 | tf_op jit(solution)/shard_map/ppermute | solution.py:16
  26.6 14.3 %collective-permute-done.1 = bf16[4,80]{1,0:T(4,128)(2,1)S(1)} collective-permute-done((bf16[4,80]{1,0:T(4,128)(2,1)S(1)}, bf16[4,80]{1,0:T(4,128)(2,1)S(1)}, u32[]{:S(2)}, u32[]{:S(2)}) %collective-permute-start.1) | collective-permute-done | bytes 672 | tf_op jit(solution)/shard_map/ppermute | solution.py:19
  42.1 1.1 %constant_dynamic-update-slice_fusion.3 = bf16[256,2048]{1,0:T(8,128)(2,1)S(1)} fusion(bf16[128,2048]{1,0:T(8,128)(2,1)} %collective-permute-done.2), kind=kLoop, calls=%fused_computation.74 | loop fusion | bytes 1048576
  43.2 1.1 %constant_dynamic-update-slice_fusion.2 = bf16[256,2048]{1,0:T(8,128)(2,1)S(1)} fusion(bf16[256,2048]{1,0:T(8,128)(2,1)S(1)} %constant_dynamic-update-slice_fusion.3, bf16[128,2048]{1,0:T(8,128)(2,1)} %collective-permute-done.3), kind=kLoop, calls=%fused_computation.73 | loop fusion | bytes 1048576 | tf_op jit(solution)/shard_map/concatenate | solution.py:238
  45.1 1.2 %copy-done.1 = bf16[256,4096]{1,0:T(8,128)(2,1)S(1)} copy-done((bf16[256,4096]{1,0:T(8,128)(2,1)S(1)}, bf16[256,4096]{1,0:T(8,128)(2,1)}, u32[]{:S(2)}) %copy-start.1) | copy-done | bytes 2097176
  53.0 2.6 %collective-permute-done.6 = f32[1920,128]{1,0:T(8,128)} collective-permute-done((f32[1920,128]{1,0:T(8,128)S(1)}, f32[1920,128]{1,0:T(8,128)}, u32[]{:S(2)}, u32[]{:S(2)}) %collective-permute-start.6) | collective-permute-done | bytes 983072 | tf_op jit(solution)/shard_map/ppermute | solution.py:188
  55.6 1.3 %dynamic-slice_add_fusion = f32[1920,128]{1,0:T(8,128)S(1)} fusion(f32[1920,128]{1,0:T(8,128)} %collective-permute-done.6, f32[3840,128]{1,0:T(8,128)S(1)} %fusion, s32[]{:T(128)S(6)} %select_n.365), kind=kLoop, calls=%fused_computation.23 | loop fusion | flops 245760 | bytes 2949124 | tf_op jit(solution)/shard_map/add | solution.py:188
  56.9 1.6 %collective-permute-start.7 = (f32[480,128]{1,0:T(8,128)S(1)}, f32[480,128]{1,0:T(8,128)S(1)}, u32[]{:S(2)}, u32[]{:S(2)}) collective-permute-start(f32[480,128]{1,0:T(8,128)S(1)} %get-tuple-element.26), channel_id=1, source_target_pairs={{0,1},{1,0},{2,10},{3,11},{4,5},{5,4},{6,14},{7,15},{8,9},{9,8},{1... | collective-permute-start | bytes 737288 | tf_op jit(solution)/shard_map/ppermute | solution.py:196
  58.5 1.6 %collective-permute-start.9 = (f32[480,128]{1,0:T(8,128)S(1)}, f32[480,128]{1,0:T(8,128)S(1)}, u32[]{:S(2)}, u32[]{:S(2)}) collective-permute-start(f32[480,128]{1,0:T(8,128)S(1)} %get-tuple-element.27), channel_id=1, source_target_pairs={{0,5},{1,4},{2,26},{3,27},{4,1},{5,0},{6,30},{7,31},{8,13},{9,12},... | collective-permute-start | bytes 737288 | tf_op jit(solution)/shard_map/ppermute | solution.py:196
  60.5 5.3 %collective-permute-done.7 = f32[480,128]{1,0:T(8,128)S(1)} collective-permute-done((f32[480,128]{1,0:T(8,128)S(1)}, f32[480,128]{1,0:T(8,128)S(1)}, u32[]{:S(2)}, u32[]{:S(2)}) %collective-permute-start.7) | collective-permute-done | bytes 245792 | tf_op jit(solution)/shard_map/ppermute | solution.py:196
  65.8 1.5 %collective-permute-done.8 = f32[480,128]{1,0:T(8,128)S(1)} collective-permute-done((f32[480,128]{1,0:T(8,128)S(1)}, f32[480,128]{1,0:T(8,128)S(1)}, u32[]{:S(2)}, u32[]{:S(2)}) %collective-permute-start.8) | collective-permute-done | bytes 245792 | tf_op jit(solution)/shard_map/ppermute | solution.py:196
  67.4 1.7 %collective-permute-start.10 = (f32[120,128]{1,0:T(8,128)S(1)}, f32[120,128]{1,0:T(8,128)S(1)}, u32[]{:S(2)}, u32[]{:S(2)}) collective-permute-start(f32[120,128]{1,0:T(8,128)S(1)} %get-tuple-element.38), channel_id=1, source_target_pairs={{0,8},{1,9},{2,3},{3,2},{4,12},{5,13},{6,7},{7,6},{8,0},{9,1},{10,... | collective-permute-start | bytes 184328 | tf_op jit(solution)/shard_map/ppermute | solution.py:196
  69.2 2.4 %collective-permute-start.12 = (f32[120,128]{1,0:T(8,128)S(1)}, f32[120,128]{1,0:T(8,128)S(1)}, u32[]{:S(2)}, u32[]{:S(2)}) collective-permute-start(f32[120,128]{1,0:T(8,128)S(1)} %get-tuple-element.39), channel_id=1, source_target_pairs={{0,24},{1,25},{2,7},{3,6},{4,28},{5,29},{6,3},{7,2},{8,16},{9,17},... | collective-permute-start | bytes 184328 | tf_op jit(solution)/shard_map/ppermute | solution.py:196
  71.5 1.4 %collective-permute-done.10 = f32[120,128]{1,0:T(8,128)S(1)} collective-permute-done((f32[120,128]{1,0:T(8,128)S(1)}, f32[120,128]{1,0:T(8,128)S(1)}, u32[]{:S(2)}, u32[]{:S(2)}) %collective-permute-start.10) | collective-permute-done | bytes 61472 | tf_op jit(solution)/shard_map/ppermute | solution.py:196
  72.9 2.2 %collective-permute-done.12 = f32[120,128]{1,0:T(8,128)S(1)} collective-permute-done((f32[120,128]{1,0:T(8,128)S(1)}, f32[120,128]{1,0:T(8,128)S(1)}, u32[]{:S(2)}, u32[]{:S(2)}) %collective-permute-start.12) | collective-permute-done | bytes 61472 | tf_op jit(solution)/shard_map/ppermute | solution.py:196
  75.2 2.1 %collective-permute-done.11 = f32[120,128]{1,0:T(8,128)S(1)} collective-permute-done((f32[120,128]{1,0:T(8,128)S(1)}, f32[120,128]{1,0:T(8,128)S(1)}, u32[]{:S(2)}, u32[]{:S(2)}) %collective-permute-start.11) | collective-permute-done | bytes 61472 | tf_op jit(solution)/shard_map/ppermute | solution.py:196
  77.3 1.6 %collective-permute-start.15 = (f32[120,128]{1,0:T(8,128)S(1)}, f32[120,128]{1,0:T(8,128)S(1)}, u32[]{:S(2)}, u32[]{:S(2)}) collective-permute-start(f32[120,128]{1,0:T(8,128)S(1)} %add_add_fusion.1), channel_id=1, source_target_pairs={{0,24},{1,25},{2,7},{3,6},{4,28},{5,29},{6,3},{7,2},{8,16},{9,17},... | collective-permute-start | bytes 184328 | tf_op jit(solution)/shard_map/ppermute | solution.py:201
  78.9 2.8 %collective-permute-start.13 = (f32[120,128]{1,0:T(8,128)S(1)}, f32[120,128]{1,0:T(8,128)S(1)}, u32[]{:S(2)}, u32[]{:S(2)}) collective-permute-start(f32[120,128]{1,0:T(8,128)S(1)} %add_add_fusion.1), channel_id=1, source_target_pairs={{0,8},{1,9},{2,3},{3,2},{4,12},{5,13},{6,7},{7,6},{8,0},{9,1},{10,... | collective-permute-start | bytes 184328 | tf_op jit(solution)/shard_map/ppermute | solution.py:201
  81.8 1.6 %collective-permute-done.15 = f32[120,128]{1,0:T(8,128)S(1)} collective-permute-done((f32[120,128]{1,0:T(8,128)S(1)}, f32[120,128]{1,0:T(8,128)S(1)}, u32[]{:S(2)}, u32[]{:S(2)}) %collective-permute-start.15) | collective-permute-done | bytes 61472 | tf_op jit(solution)/shard_map/ppermute | solution.py:201
  83.4 1.3 %collective-permute-done.14 = f32[120,128]{1,0:T(8,128)S(1)} collective-permute-done((f32[120,128]{1,0:T(8,128)S(1)}, f32[120,128]{1,0:T(8,128)S(1)}, u32[]{:S(2)}, u32[]{:S(2)}) %collective-permute-start.14) | collective-permute-done | bytes 61472 | tf_op jit(solution)/shard_map/ppermute | solution.py:201
  84.8 2.9 %collective-permute-start.18 = (f32[480,128]{1,0:T(8,128)S(1)}, f32[480,128]{1,0:T(8,128)S(1)}, u32[]{:S(2)}, u32[]{:S(2)}) collective-permute-start(f32[480,128]{1,0:T(8,128)S(1)} %pad_maximum_fusion.3), channel_id=1, source_target_pairs={{0,5},{1,4},{2,26},{3,27},{4,1},{5,0},{6,30},{7,31},{8,13},{9,12},... | collective-permute-start | bytes 737288 | tf_op jit(solution)/shard_map/ppermute | solution.py:201
  88.3 3.7 %collective-permute-done.18 = f32[480,128]{1,0:T(8,128)S(1)} collective-permute-done((f32[480,128]{1,0:T(8,128)S(1)}, f32[480,128]{1,0:T(8,128)S(1)}, u32[]{:S(2)}, u32[]{:S(2)}) %collective-permute-start.18) | collective-permute-done | bytes 245792 | tf_op jit(solution)/shard_map/ppermute | solution.py:201
  92.0 2.6 %collective-permute-done.17 = f32[480,128]{1,0:T(8,128)S(1)} collective-permute-done((f32[480,128]{1,0:T(8,128)S(1)}, f32[480,128]{1,0:T(8,128)S(1)}, u32[]{:S(2)}, u32[]{:S(2)}) %collective-permute-start.17) | collective-permute-done | bytes 245792 | tf_op jit(solution)/shard_map/ppermute | solution.py:201
  95.1 1.4 %collective-permute-start.19 = (f32[1920,128]{1,0:T(8,128)S(1)}, f32[1920,128]{1,0:T(8,128)S(1)}, u32[]{:S(2)}, u32[]{:S(2)}) collective-permute-start(f32[1920,128]{1,0:T(8,128)S(1)} %pad_maximum_fusion), channel_id=1, source_target_pairs={{0,2},{1,3},{2,0},{3,1},{4,6},{5,7},{6,4},{7,5},{8,10},{9,11},{10,... | collective-permute-start | bytes 2949128 | tf_op jit(solution)/shard_map/ppermute | solution.py:210
  96.5 1.1 %fusion.3 = bf16[1,512,256]{2,1,0:T(8,128)(2,1)} fusion(bf16[768,256]{1,0:T(8,128)(2,1)S(1)} %copy-done.12, f32[518,256]{1,0:T(8,128)S(1)} %copy-done.4, bf16[512,256]{1,0:T(8,128)(2,1)S(1)} %copy-done.8, bf16[512,256]{1,0:T(8,128)(2,1)S(1)} %copy-done.10, bf16[512,256]{1,0:T(8,128)(2,1)S(1)} %copy-done.6, f32[256]{0:T(256)S(1)} %copy-done.15), kind=kOutput, calls=%fused_computation.9 | convolution fusion | flops 204079104 | bytes 1967104 | tf_op jit(solution)/shard_map/dot_general | solution.py:92
  97.5 1.1 %collective-permute-done.19 = f32[1920,128]{1,0:T(8,128)S(1)} collective-permute-done((f32[1920,128]{1,0:T(8,128)S(1)}, f32[1920,128]{1,0:T(8,128)S(1)}, u32[]{:S(2)}, u32[]{:S(2)}) %collective-permute-start.19) | collective-permute-done | bytes 983072 | tf_op jit(solution)/shard_map/ppermute | solution.py:210
  101.1 1.1 %slice.160 = f32[2240,128]{1,0:T(8,128)} slice(f32[3840,128]{1,0:T(8,128)S(1)} %broadcast_select_fusion.2), slice={[0:2240], [0:128]} | slice | bytes 2293760 | tf_op jit(solution)/shard_map/slice | solution.py:214
  (125 shorter events, 20.0 us)
Async XLA Ops:
  0.6 40.6 %copy-start = (bf16[560,512]{1,0:T(8,128)(2,1)S(1)}, bf16[560,512]{1,0:T(8,128)(2,1)}, u32[]{:S(2)}) copy-start(bf16[560,512]{1,0:T(8,128)(2,1)} %param.16) | copy-start | bytes 1720324
  5.0 13.9 %all-to-all-start = ((bf16[16,2,321]{2,1,0:T(2,128)(2,1)}), bf16[16,2,321]{2,1,0:T(2,128)(2,1)S(1)}, u32[]{:S(2)}, u32[]{:S(2)}) async-start(bf16[16,2,321]{2,1,0:T(2,128)(2,1)} %reshape.119), calls=%async_computation | async-start | bytes 49152 | tf_op jit(solution)/shard_map/all_to_all | solution.py:279
  12.4 7.3 %copy-start.2 = (bf16[1,512,256]{2,1,0:T(8,128)(2,1)S(1)}, bf16[1,512,256]{2,1,0:T(8,128)(2,1)}, u32[]{:S(2)}) copy-start(bf16[1,512,256]{2,1,0:T(8,128)(2,1)} %param.15) | copy-start | bytes 786436
  14.1 11.8 %copy-start.11 = (bf16[768,256]{1,0:T(8,128)(2,1)S(1)}, bf16[768,256]{1,0:T(8,128)(2,1)}, u32[]{:S(2)}) copy-start(bf16[768,256]{1,0:T(8,128)(2,1)} %param.20) | copy-start | bytes 1179652
  15.1 26.4 %collective-permute-start.3 = (bf16[128,2048]{1,0:T(8,128)(2,1)}, bf16[128,2048]{1,0:T(8,128)(2,1)}, u32[]{:S(2)}, u32[]{:S(2)}) collective-permute-start(bf16[128,2048]{1,0:T(8,128)(2,1)} %get-tuple-element.22), channel_id=1, source_target_pairs={{0,1},{1,0},{2,3},{3,2},{4,5},{5,4},{6,7},{7,6},{8,9},{9,8},{10,11... | collective-permute-start | bytes 1572872 | tf_op jit(solution)/shard_map/ppermute | solution.py:234
  16.7 24.4 %collective-permute-start.2 = (bf16[128,2048]{1,0:T(8,128)(2,1)}, bf16[128,2048]{1,0:T(8,128)(2,1)}, u32[]{:S(2)}, u32[]{:S(2)}) collective-permute-start(bf16[128,2048]{1,0:T(8,128)(2,1)} %get-tuple-element.23), channel_id=1, source_target_pairs={{0,1},{1,0},{2,3},{3,2},{4,5},{5,4},{6,7},{7,6},{8,9},{9,8},{10,11... | collective-permute-start | bytes 1572872 | tf_op jit(solution)/shard_map/ppermute | solution.py:233
  20.1 20.9 %collective-permute-start.1 = (bf16[4,80]{1,0:T(4,128)(2,1)S(1)}, bf16[4,80]{1,0:T(4,128)(2,1)S(1)}, u32[]{:S(2)}, u32[]{:S(2)}) collective-permute-start(bf16[4,80]{1,0:T(4,128)(2,1)S(1)} %get-tuple-element.48), channel_id=1, source_target_pairs={{1,0},{3,2},{5,4},{7,6},{9,8},{11,10},{13,12},{15,14},{17,16},{19,... | collective-permute-start | bytes 1928 | tf_op jit(solution)/shard_map/ppermute | solution.py:19
  21.4 19.6 %collective-permute-start = (bf16[4,80]{1,0:T(4,128)(2,1)S(1)}, bf16[4,80]{1,0:T(4,128)(2,1)S(1)}, u32[]{:S(2)}, u32[]{:S(2)}) collective-permute-start(bf16[4,80]{1,0:T(4,128)(2,1)S(1)} %get-tuple-element.49), channel_id=1, source_target_pairs={{0,1},{2,3},{4,5},{6,7},{8,9},{10,11},{12,13},{14,15},{16,17},{18,... | collective-permute-start | bytes 1928 | tf_op jit(solution)/shard_map/ppermute | solution.py:16
  26.3 14.9 %copy-start.13 = (f32[512]{0:T(512)S(1)}, f32[512]{0:T(512)}, u32[]{:S(2)}) copy-start(f32[512]{0:T(512)} %param.17) | copy-start | bytes 6148
  41.1 3.1 %collective-permute-start.4 = (bf16[128,2048]{1,0:T(8,128)(2,1)}, bf16[128,2048]{1,0:T(8,128)(2,1)S(1)}, u32[]{:S(2)}, u32[]{:S(2)}) collective-permute-start(bf16[128,2048]{1,0:T(8,128)(2,1)} %collective-permute-done.2), channel_id=1, source_target_pairs={{0,2},{2,0},{4,6},{6,4},{8,10},{10,8},{12,14},{14,12},{16,18},{18,... | collective-permute-start | bytes 1572872 | tf_op jit(solution)/shard_map/ppermute | solution.py:237
  41.5 2.8 %collective-permute-start.5 = (bf16[128,2048]{1,0:T(8,128)(2,1)}, bf16[128,2048]{1,0:T(8,128)(2,1)S(1)}, u32[]{:S(2)}, u32[]{:S(2)}) collective-permute-start(bf16[128,2048]{1,0:T(8,128)(2,1)} %collective-permute-done.3), channel_id=1, source_target_pairs={{0,2},{2,0},{4,6},{6,4},{8,10},{10,8},{12,14},{14,12},{16,18},{18,... | collective-permute-start | bytes 1572872 | tf_op jit(solution)/shard_map/ppermute | solution.py:237
  44.7 1.6 %copy-start.1 = (bf16[256,4096]{1,0:T(8,128)(2,1)S(1)}, bf16[256,4096]{1,0:T(8,128)(2,1)}, u32[]{:S(2)}) copy-start(bf16[256,4096]{1,0:T(8,128)(2,1)} %param.18) | copy-start | bytes 6291460
  48.2 1.6 %copy-start.3 = (f32[518,256]{1,0:T(8,128)}, f32[518,256]{1,0:T(8,128)S(1)}, u32[]{:S(2)}) copy-start(f32[518,256]{1,0:T(8,128)S(1)} %get-tuple-element.18) | copy-start | bytes 1591300
  52.8 2.8 %collective-permute-start.6 = (f32[1920,128]{1,0:T(8,128)S(1)}, f32[1920,128]{1,0:T(8,128)}, u32[]{:S(2)}, u32[]{:S(2)}) collective-permute-start(f32[1920,128]{1,0:T(8,128)S(1)} %constant_dynamic-slice_fusion.6), channel_id=1, source_target_pairs={{0,2},{1,3},{2,0},{3,1},{4,6},{5,7},{6,4},{7,5},{8,10},{9,11},{10,... | collective-permute-start | bytes 2949128 | tf_op jit(solution)/shard_map/ppermute | solution.py:188
  56.9 8.9 %collective-permute-start.7 = (f32[480,128]{1,0:T(8,128)S(1)}, f32[480,128]{1,0:T(8,128)S(1)}, u32[]{:S(2)}, u32[]{:S(2)}) collective-permute-start(f32[480,128]{1,0:T(8,128)S(1)} %get-tuple-element.26), channel_id=1, source_target_pairs={{0,1},{1,0},{2,10},{3,11},{4,5},{5,4},{6,14},{7,15},{8,9},{9,8},{1... | collective-permute-start | bytes 737288 | tf_op jit(solution)/shard_map/ppermute | solution.py:196
  58.5 7.3 %collective-permute-start.9 = (f32[480,128]{1,0:T(8,128)S(1)}, f32[480,128]{1,0:T(8,128)S(1)}, u32[]{:S(2)}, u32[]{:S(2)}) collective-permute-start(f32[480,128]{1,0:T(8,128)S(1)} %get-tuple-element.27), channel_id=1, source_target_pairs={{0,5},{1,4},{2,26},{3,27},{4,1},{5,0},{6,30},{7,31},{8,13},{9,12},... | collective-permute-start | bytes 737288 | tf_op jit(solution)/shard_map/ppermute | solution.py:196
  60.1 7.2 %collective-permute-start.8 = (f32[480,128]{1,0:T(8,128)S(1)}, f32[480,128]{1,0:T(8,128)S(1)}, u32[]{:S(2)}, u32[]{:S(2)}) collective-permute-start(f32[480,128]{1,0:T(8,128)S(1)} %get-tuple-element.28), channel_id=1, source_target_pairs={{0,4},{1,5},{2,18},{3,19},{4,0},{5,1},{6,22},{7,23},{8,12},{9,13},... | collective-permute-start | bytes 737288 | tf_op jit(solution)/shard_map/ppermute | solution.py:196
  67.4 5.5 %collective-permute-start.10 = (f32[120,128]{1,0:T(8,128)S(1)}, f32[120,128]{1,0:T(8,128)S(1)}, u32[]{:S(2)}, u32[]{:S(2)}) collective-permute-start(f32[120,128]{1,0:T(8,128)S(1)} %get-tuple-element.38), channel_id=1, source_target_pairs={{0,8},{1,9},{2,3},{3,2},{4,12},{5,13},{6,7},{7,6},{8,0},{9,1},{10,... | collective-permute-start | bytes 184328 | tf_op jit(solution)/shard_map/ppermute | solution.py:196
  69.2 6.0 %collective-permute-start.12 = (f32[120,128]{1,0:T(8,128)S(1)}, f32[120,128]{1,0:T(8,128)S(1)}, u32[]{:S(2)}, u32[]{:S(2)}) collective-permute-start(f32[120,128]{1,0:T(8,128)S(1)} %get-tuple-element.39), channel_id=1, source_target_pairs={{0,24},{1,25},{2,7},{3,6},{4,28},{5,29},{6,3},{7,2},{8,16},{9,17},... | collective-permute-start | bytes 184328 | tf_op jit(solution)/shard_map/ppermute | solution.py:196
  71.5 5.8 %collective-permute-start.11 = (f32[120,128]{1,0:T(8,128)S(1)}, f32[120,128]{1,0:T(8,128)S(1)}, u32[]{:S(2)}, u32[]{:S(2)}) collective-permute-start(f32[120,128]{1,0:T(8,128)S(1)} %get-tuple-element.40), channel_id=1, source_target_pairs={{0,16},{1,17},{2,6},{3,7},{4,20},{5,21},{6,2},{7,3},{8,24},{9,25},... | collective-permute-start | bytes 184328 | tf_op jit(solution)/shard_map/ppermute | solution.py:196
  77.3 6.1 %collective-permute-start.15 = (f32[120,128]{1,0:T(8,128)S(1)}, f32[120,128]{1,0:T(8,128)S(1)}, u32[]{:S(2)}, u32[]{:S(2)}) collective-permute-start(f32[120,128]{1,0:T(8,128)S(1)} %add_add_fusion.1), channel_id=1, source_target_pairs={{0,24},{1,25},{2,7},{3,6},{4,28},{5,29},{6,3},{7,2},{8,16},{9,17},... | collective-permute-start | bytes 184328 | tf_op jit(solution)/shard_map/ppermute | solution.py:201
  78.9 5.8 %collective-permute-start.14 = (f32[120,128]{1,0:T(8,128)S(1)}, f32[120,128]{1,0:T(8,128)S(1)}, u32[]{:S(2)}, u32[]{:S(2)}) collective-permute-start(f32[120,128]{1,0:T(8,128)S(1)} %add_add_fusion.1), channel_id=1, source_target_pairs={{0,16},{1,17},{2,6},{3,7},{4,20},{5,21},{6,2},{7,3},{8,24},{9,25},... | collective-permute-start | bytes 184328 | tf_op jit(solution)/shard_map/ppermute | solution.py:201
  78.9 5.8 %collective-permute-start.13 = (f32[120,128]{1,0:T(8,128)S(1)}, f32[120,128]{1,0:T(8,128)S(1)}, u32[]{:S(2)}, u32[]{:S(2)}) collective-permute-start(f32[120,128]{1,0:T(8,128)S(1)} %add_add_fusion.1), channel_id=1, source_target_pairs={{0,8},{1,9},{2,3},{3,2},{4,12},{5,13},{6,7},{7,6},{8,0},{9,1},{10,... | collective-permute-start | bytes 184328 | tf_op jit(solution)/shard_map/ppermute | solution.py:201
  84.8 7.2 %collective-permute-start.18 = (f32[480,128]{1,0:T(8,128)S(1)}, f32[480,128]{1,0:T(8,128)S(1)}, u32[]{:S(2)}, u32[]{:S(2)}) collective-permute-start(f32[480,128]{1,0:T(8,128)S(1)} %pad_maximum_fusion.3), channel_id=1, source_target_pairs={{0,5},{1,4},{2,26},{3,27},{4,1},{5,0},{6,30},{7,31},{8,13},{9,12},... | collective-permute-start | bytes 737288 | tf_op jit(solution)/shard_map/ppermute | solution.py:201
  87.7 7.0 %collective-permute-start.17 = (f32[480,128]{1,0:T(8,128)S(1)}, f32[480,128]{1,0:T(8,128)S(1)}, u32[]{:S(2)}, u32[]{:S(2)}) collective-permute-start(f32[480,128]{1,0:T(8,128)S(1)} %pad_maximum_fusion.3), channel_id=1, source_target_pairs={{0,4},{1,5},{2,18},{3,19},{4,0},{5,1},{6,22},{7,23},{8,12},{9,13},... | collective-permute-start | bytes 737288 | tf_op jit(solution)/shard_map/ppermute | solution.py:201
  87.8 6.8 %collective-permute-start.16 = (f32[480,128]{1,0:T(8,128)S(1)}, f32[480,128]{1,0:T(8,128)S(1)}, u32[]{:S(2)}, u32[]{:S(2)}) collective-permute-start(f32[480,128]{1,0:T(8,128)S(1)} %pad_maximum_fusion.3), channel_id=1, source_target_pairs={{0,1},{1,0},{2,10},{3,11},{4,5},{5,4},{6,14},{7,15},{8,9},{9,8},{1... | collective-permute-start | bytes 737288 | tf_op jit(solution)/shard_map/ppermute | solution.py:201
  94.8 1.6 %copy-start.4 = (f32[518,256]{1,0:T(8,128)S(1)}, f32[518,256]{1,0:T(8,128)}, u32[]{:S(2)}) copy-start(f32[518,256]{1,0:T(8,128)} %copy-done.3) | copy-start | bytes 1591300
  94.9 1.6 %copy-start.6 = (bf16[512,256]{1,0:T(8,128)(2,1)S(1)}, bf16[512,256]{1,0:T(8,128)(2,1)}, u32[]{:S(2)}) copy-start(bf16[512,256]{1,0:T(8,128)(2,1)} %copy-done.5) | copy-start | bytes 786436
  94.9 1.6 %copy-start.8 = (bf16[512,256]{1,0:T(8,128)(2,1)S(1)}, bf16[512,256]{1,0:T(8,128)(2,1)}, u32[]{:S(2)}) copy-start(bf16[512,256]{1,0:T(8,128)(2,1)} %copy-done.7) | copy-start | bytes 786436
  94.9 1.6 %copy-start.10 = (bf16[512,256]{1,0:T(8,128)(2,1)S(1)}, bf16[512,256]{1,0:T(8,128)(2,1)}, u32[]{:S(2)}) copy-start(bf16[512,256]{1,0:T(8,128)(2,1)} %copy-done.9) | copy-start | bytes 786436
  94.9 1.6 %copy-start.12 = (bf16[768,256]{1,0:T(8,128)(2,1)S(1)}, bf16[768,256]{1,0:T(8,128)(2,1)}, u32[]{:S(2)}) copy-start(bf16[768,256]{1,0:T(8,128)(2,1)} %param.20) | copy-start | bytes 1179652
  95.1 3.6 %collective-permute-start.19 = (f32[1920,128]{1,0:T(8,128)S(1)}, f32[1920,128]{1,0:T(8,128)S(1)}, u32[]{:S(2)}, u32[]{:S(2)}) collective-permute-start(f32[1920,128]{1,0:T(8,128)S(1)} %pad_maximum_fusion), channel_id=1, source_target_pairs={{0,2},{1,3},{2,0},{3,1},{4,6},{5,7},{6,4},{7,5},{8,10},{9,11},{10,... | collective-permute-start | bytes 2949128 | tf_op jit(solution)/shard_map/ppermute | solution.py:210
  (5 other events, 4.6 us)

commit v10 on v9

--- a/solution.py
+++ b/solution.py
@@ -222,6 +222,7 @@
         return (
             lambda act: jnp.dot(act, whole, preferred_element_type=jnp.float32),
             lambda d_taps: contract_cols(d_taps, whole),
+            whole,
         )
     rows, width = w_ups.shape
     cols = width // 2
@@ -259,13 +260,15 @@
             tm == 0, jnp.concatenate([own, other], axis=1), jnp.concatenate([other, own], axis=1)
         )
 
-    return forward, backward
+    return forward, backward, got_parts[0]
 
 
 def on_device(
     src_mel, owner, dst_pos, keep, cotangent, w_pre, b_pre, w_ups, upsample_bias, w_res, b_res
 ):
     owners_count = lax.axis_size("dp")
+    ups_forward, ups_backward, ready = ups_functions(w_ups)
+    src_mel, _ = lax.optimization_barrier((src_mel, ready))
     seg_rows = src_mel[0]
     seg_count = seg_rows.shape[0]
     mel_bins = w_pre.shape[0] // KPRE
@@ -292,8 +295,6 @@
     cot = cotangent[0]
     marks = jnp.repeat(keep_segs, cot.shape[0] // seg_count)
     gradient_value = jnp.where(marks[:, None] > 0, cot, jnp.zeros_like(cot))
-    ups_forward, ups_backward = ups_functions(w_ups)
-
     output_rows, grads = local_pass(
         mel_ext,
         gradient_value,

time: 103 us -> 117 us (1.14)
  waiting for transfers between devices: 41.5 us -> 51.1 us
  local copies, waits for them, and re-layouts: 12.8 us -> 16 us
    ppermute x1, waiting for transfers between devices: 0.01 us -> 22.4 us  [ups_functions(): lax.ppermute(mine[:split], 'tm', [(0, 1), (1, 0)])]
    ppermute x1, waiting for transfers between devices: 14.3 us -> 0.01 us  [with_halo(): lax.ppermute(lax.slice_in_dim(block, 0, width, axis=dim), axis, backward)]
    all_to_all x1, waiting for transfers between devices: 1.71 us -> 3.74 us  [on_device(): lax.all_to_all(outgoing, 'dp', split_axis=0, concat_axis=0, tiled=True)]
    unnamed x45 -> x63, local copies, waits for them, and re-layouts: 5.4 us -> 7.01 us
    ppermute x6, waiting for transfers between devices: 12.6 us -> 11.1 us  [butterfly_psum(): total = total + lax.ppermute(send, axes, perm_of(step, offset))]
    ppermute x1, starting transfers between devices: 1.55 us -> 3.03 us  [ups_functions(): lax.ppermute(mine[split:], 'tm', [(0, 1), (1, 0)])]
    dot_general x1, matrix products: 0.25 us -> 1.61 us  [local_pass(): pre = jnp.dot(patches, w_pre, preferred_element_type=jnp.float32) + b_pre]
    all_to_all x1, starting transfers between devices: 7.36 us -> 6.13 us  [on_device(): lax.all_to_all(outgoing, 'dp', split_axis=0, concat_axis=0, tiled=True)]
  transfers between devices with their start and end apart: 21 -> 21, of which waited for: 13 -> 15; matrix products, arithmetic and copies ran while one was open for 8% -> 12% of each run, Pallas kernels for 0% -> 0%
where the time goes in v10:
time: 117 us; the launch traced here: 116 us
  waiting for transfers between devices  51.1 us (44%)
  starting transfers between devices  33.1 us (28%)
  local copies, waits for them, and re-layouts  16 us (14%)
  other arithmetic  7.56 us (6%)
  matrix products  7.05 us (6%)
  between operations  1.45 us (1%)
    ppermute x1, waiting for transfers between devices, ups_functions(): lax.ppermute(mine[:split], 'tm', [(0, 1), (1, 0)])  22.4 us
    ppermute x6, waiting for transfers between devices, butterfly_psum(): total = total + lax.ppermute(send, axes, perm_of(step, offset))  11.1 us
    ppermute x6, waiting for transfers between devices, butterfly_psum(): lax.ppermute(x, axes, perm_of(step, o))  9.85 us
    ppermute x6, starting transfers between devices, butterfly_psum(): lax.ppermute(x, axes, perm_of(step, o))  8.46 us
    ppermute x6, starting transfers between devices, butterfly_psum(): total = total + lax.ppermute(send, axes, perm_of(step, offset))  7.43 us
    unnamed x63, local copies, waits for them, and re-layouts  7.01 us
    all_to_all x1, starting transfers between devices, on_device(): lax.all_to_all(outgoing, 'dp', split_axis=0, concat_axis=0, tiled=True)  6.13 us
    ppermute x1, starting transfers between devices, with_halo(): lax.ppermute(lax.slice_in_dim(block, block.shape[dim] - width, None, axis...  4.53 us
  transfers between devices with their start and end apart: 21, of which 15 were waited for; matrix products, arithmetic and copies ran while one was open for 12% of the time, Pallas kernels for 0%

profile of v10, /device:TPU:0, one launch (start us, length us, event | category | flops | bytes accessed | tf_op | source)
XLA Modules:
  0.0 116.3 jit_solution(17900926496193342255)
XLA Ops:
  0.7 1.7 %slice_select_fusion = bf16[256,2048]{1,0:T(8,128)(2,1)S(1)} fusion(bf16[256,4096]{1,0:T(8,128)(2,1)} %param.18, pred[]{:T(512)S(6)} %eq.138), kind=kLoop, calls=%fused_computation.19 | loop fusion | flops 524288 | bytes 3145729 | tf_op jit(solution)/shard_map/jit(_where)/select_n | solution.py:231
  2.5 3.0 %collective-permute-start.3 = (bf16[128,2048]{1,0:T(8,128)(2,1)S(1)}, bf16[128,2048]{1,0:T(8,128)(2,1)}, u32[]{:S(2)}, u32[]{:S(2)}) collective-permute-start(bf16[128,2048]{1,0:T(8,128)(2,1)S(1)} %get-tuple-element.24), channel_id=1, source_target_pairs={{0,1},{1,0},{2,3},{3,2},{4,5},{5,4},{6,7},{7,6},{8,9},{9,8},{10,11... | collective-permute-start | bytes 1572872 | tf_op jit(solution)/shard_map/ppermute | solution.py:235
  6.4 22.4 %collective-permute-done = bf16[128,2048]{1,0:T(8,128)(2,1)} collective-permute-done((bf16[128,2048]{1,0:T(8,128)(2,1)S(1)}, bf16[128,2048]{1,0:T(8,128)(2,1)}, u32[]{:S(2)}, u32[]{:S(2)}) %collective-permute-start) | collective-permute-done | bytes 524320 | tf_op jit(solution)/shard_map/ppermute | solution.py:234
  30.9 6.1 %all-to-all-start = ((bf16[16,2,321]{2,1,0:T(2,128)(2,1)}), bf16[16,2,321]{2,1,0:T(2,128)(2,1)S(1)}, u32[]{:S(2)}, u32[]{:S(2)}) async-start(bf16[16,2,321]{2,1,0:T(2,128)(2,1)} %reshape.119), calls=%async_computation | async-start | bytes 49152 | tf_op jit(solution)/shard_map/all_to_all | solution.py:282
  37.4 1.1 constant_dynamic-update-slice_fusion.3
  39.9 3.7 %all-to-all-done = bf16[16,2,321]{2,1,0:T(2,128)(2,1)S(1)} async-done(((bf16[16,2,321]{2,1,0:T(2,128)(2,1)}), bf16[16,2,321]{2,1,0:T(2,128)(2,1)S(1)}, u32[]{:S(2)}, u32[]{:S(2)}) %all-to-all-start) | async-done | bytes 20576 | tf_op jit(solution)/shard_map/all_to_all | solution.py:282
  46.0 1.3 %collective-permute-start.2 = (bf16[4,80]{1,0:T(4,128)(2,1)S(1)}, bf16[4,80]{1,0:T(4,128)(2,1)S(1)}, u32[]{:S(2)}, u32[]{:S(2)}) collective-permute-start(bf16[4,80]{1,0:T(4,128)(2,1)S(1)} %get-tuple-element.50), channel_id=1, source_target_pairs={{1,0},{3,2},{5,4},{7,6},{9,8},{11,10},{13,12},{15,14},{17,16},{19,... | collective-permute-start | bytes 1928 | tf_op jit(solution)/shard_map/ppermute | solution.py:19
  48.6 4.5 %collective-permute-start.1 = (bf16[4,80]{1,0:T(4,128)(2,1)S(1)}, bf16[4,80]{1,0:T(4,128)(2,1)S(1)}, u32[]{:S(2)}, u32[]{:S(2)}) collective-permute-start(bf16[4,80]{1,0:T(4,128)(2,1)S(1)} %get-tuple-element.51), channel_id=1, source_target_pairs={{0,1},{2,3},{4,5},{6,7},{8,9},{10,11},{12,13},{14,15},{16,17},{18,... | collective-permute-start | bytes 1928 | tf_op jit(solution)/shard_map/ppermute | solution.py:16
  54.6 1.6 %fusion.27 = (bf16[66,512]{1,0:T(8,128)(2,1)S(1)}, f32[66,512]{1,0:T(8,128)}) fusion(pred[66]{0:T(512)(128)(4,1)} %compare_and_fusion, f32[512]{0:T(512)} %param.17, bf16[66,560]{1,0:T(8,128)(2,1)S(1)} %concatenate.68, bf16[560,512]{1,0:T(8,128)(2,1)S(1)} %copy-done), kind=kOutput, calls=%fused_computation.60 | convolution fusion | flops 38049792 | bytes 852226 | tf_op jit(solution)/shard_map/dot_general | solution.py:64
  56.3 1.1 constant_dynamic-update-slice_fusion.5
  57.4 1.1 constant_dynamic-update-slice_fusion.4
  59.2 1.2 %copy-done.1 = bf16[256,4096]{1,0:T(8,128)(2,1)S(1)} copy-done((bf16[256,4096]{1,0:T(8,128)(2,1)S(1)}, bf16[256,4096]{1,0:T(8,128)(2,1)}, u32[]{:S(2)}) %copy-start.1) | copy-done | bytes 2097176
  67.7 2.6 %collective-permute-done.6 = f32[1920,128]{1,0:T(8,128)} collective-permute-done((f32[1920,128]{1,0:T(8,128)S(1)}, f32[1920,128]{1,0:T(8,128)}, u32[]{:S(2)}, u32[]{:S(2)}) %collective-permute-start.6) | collective-permute-done | bytes 983072 | tf_op jit(solution)/shard_map/ppermute | solution.py:188
  70.3 1.3 %dynamic-slice_add_fusion = f32[1920,128]{1,0:T(8,128)S(1)} fusion(f32[1920,128]{1,0:T(8,128)} %collective-permute-done.6, f32[3840,128]{1,0:T(8,128)S(1)} %fusion, s32[]{:T(128)S(6)} %select_n.365), kind=kLoop, calls=%fused_computation.23 | loop fusion | flops 245760 | bytes 2949124 | tf_op jit(solution)/shard_map/add | solution.py:188
  71.7 2.3 %collective-permute-start.7 = (f32[480,128]{1,0:T(8,128)S(1)}, f32[480,128]{1,0:T(8,128)S(1)}, u32[]{:S(2)}, u32[]{:S(2)}) collective-permute-start(f32[480,128]{1,0:T(8,128)S(1)} %get-tuple-element.28), channel_id=1, source_target_pairs={{0,1},{1,0},{2,10},{3,11},{4,5},{5,4},{6,14},{7,15},{8,9},{9,8},{1... | collective-permute-start | bytes 737288 | tf_op jit(solution)/shard_map/ppermute | solution.py:196
  74.0 1.5 %collective-permute-start.8 = (f32[480,128]{1,0:T(8,128)S(1)}, f32[480,128]{1,0:T(8,128)S(1)}, u32[]{:S(2)}, u32[]{:S(2)}) collective-permute-start(f32[480,128]{1,0:T(8,128)S(1)} %get-tuple-element.30), channel_id=1, source_target_pairs={{0,4},{1,5},{2,18},{3,19},{4,0},{5,1},{6,22},{7,23},{8,12},{9,13},... | collective-permute-start | bytes 737288 | tf_op jit(solution)/shard_map/ppermute | solution.py:196
  75.5 4.8 %collective-permute-done.7 = f32[480,128]{1,0:T(8,128)S(1)} collective-permute-done((f32[480,128]{1,0:T(8,128)S(1)}, f32[480,128]{1,0:T(8,128)S(1)}, u32[]{:S(2)}, u32[]{:S(2)}) %collective-permute-start.7) | collective-permute-done | bytes 245792 | tf_op jit(solution)/shard_map/ppermute | solution.py:196
  81.1 1.3 %collective-permute-done.8 = f32[480,128]{1,0:T(8,128)S(1)} collective-permute-done((f32[480,128]{1,0:T(8,128)S(1)}, f32[480,128]{1,0:T(8,128)S(1)}, u32[]{:S(2)}, u32[]{:S(2)}) %collective-permute-start.8) | collective-permute-done | bytes 245792 | tf_op jit(solution)/shard_map/ppermute | solution.py:196
  82.9 1.5 %collective-permute-start.12 = (f32[120,128]{1,0:T(8,128)S(1)}, f32[120,128]{1,0:T(8,128)S(1)}, u32[]{:S(2)}, u32[]{:S(2)}) collective-permute-start(f32[120,128]{1,0:T(8,128)S(1)} %get-tuple-element.41), channel_id=1, source_target_pairs={{0,24},{1,25},{2,7},{3,6},{4,28},{5,29},{6,3},{7,2},{8,16},{9,17},... | collective-permute-start | bytes 184328 | tf_op jit(solution)/shard_map/ppermute | solution.py:196
  84.4 1.6 %collective-permute-start.11 = (f32[120,128]{1,0:T(8,128)S(1)}, f32[120,128]{1,0:T(8,128)S(1)}, u32[]{:S(2)}, u32[]{:S(2)}) collective-permute-start(f32[120,128]{1,0:T(8,128)S(1)} %get-tuple-element.42), channel_id=1, source_target_pairs={{0,16},{1,17},{2,6},{3,7},{4,20},{5,21},{6,2},{7,3},{8,24},{9,25},... | collective-permute-start | bytes 184328 | tf_op jit(solution)/shard_map/ppermute | solution.py:196
  86.8 2.1 %collective-permute-done.12 = f32[120,128]{1,0:T(8,128)S(1)} collective-permute-done((f32[120,128]{1,0:T(8,128)S(1)}, f32[120,128]{1,0:T(8,128)S(1)}, u32[]{:S(2)}, u32[]{:S(2)}) %collective-permute-start.12) | collective-permute-done | bytes 61472 | tf_op jit(solution)/shard_map/ppermute | solution.py:196
  89.0 1.3 %collective-permute-done.11 = f32[120,128]{1,0:T(8,128)S(1)} collective-permute-done((f32[120,128]{1,0:T(8,128)S(1)}, f32[120,128]{1,0:T(8,128)S(1)}, u32[]{:S(2)}, u32[]{:S(2)}) %collective-permute-start.11) | collective-permute-done | bytes 61472 | tf_op jit(solution)/shard_map/ppermute | solution.py:196
  90.3 2.3 %collective-permute-start.15 = (f32[120,128]{1,0:T(8,128)S(1)}, f32[120,128]{1,0:T(8,128)S(1)}, u32[]{:S(2)}, u32[]{:S(2)}) collective-permute-start(f32[120,128]{1,0:T(8,128)S(1)} %add_add_fusion.1), channel_id=1, source_target_pairs={{0,24},{1,25},{2,7},{3,6},{4,28},{5,29},{6,3},{7,2},{8,16},{9,17},... | collective-permute-start | bytes 184328 | tf_op jit(solution)/shard_map/ppermute | solution.py:201
  92.6 2.1 %collective-permute-start.13 = (f32[120,128]{1,0:T(8,128)S(1)}, f32[120,128]{1,0:T(8,128)S(1)}, u32[]{:S(2)}, u32[]{:S(2)}) collective-permute-start(f32[120,128]{1,0:T(8,128)S(1)} %add_add_fusion.1), channel_id=1, source_target_pairs={{0,8},{1,9},{2,3},{3,2},{4,12},{5,13},{6,7},{7,6},{8,0},{9,1},{10,... | collective-permute-start | bytes 184328 | tf_op jit(solution)/shard_map/ppermute | solution.py:201
  94.8 1.6 %collective-permute-done.15 = f32[120,128]{1,0:T(8,128)S(1)} collective-permute-done((f32[120,128]{1,0:T(8,128)S(1)}, f32[120,128]{1,0:T(8,128)S(1)}, u32[]{:S(2)}, u32[]{:S(2)}) %collective-permute-start.15) | collective-permute-done | bytes 61472 | tf_op jit(solution)/shard_map/ppermute | solution.py:201
  96.4 1.4 %collective-permute-done.14 = f32[120,128]{1,0:T(8,128)S(1)} collective-permute-done((f32[120,128]{1,0:T(8,128)S(1)}, f32[120,128]{1,0:T(8,128)S(1)}, u32[]{:S(2)}, u32[]{:S(2)}) %collective-permute-start.14) | collective-permute-done | bytes 61472 | tf_op jit(solution)/shard_map/ppermute | solution.py:201
  97.8 2.3 %collective-permute-start.18 = (f32[480,128]{1,0:T(8,128)S(1)}, f32[480,128]{1,0:T(8,128)S(1)}, u32[]{:S(2)}, u32[]{:S(2)}) collective-permute-start(f32[480,128]{1,0:T(8,128)S(1)} %pad_maximum_fusion.3), channel_id=1, source_target_pairs={{0,5},{1,4},{2,26},{3,27},{4,1},{5,0},{6,30},{7,31},{8,13},{9,12},... | collective-permute-start | bytes 737288 | tf_op jit(solution)/shard_map/ppermute | solution.py:201
  100.1 1.7 %collective-permute-start.17 = (f32[480,128]{1,0:T(8,128)S(1)}, f32[480,128]{1,0:T(8,128)S(1)}, u32[]{:S(2)}, u32[]{:S(2)}) collective-permute-start(f32[480,128]{1,0:T(8,128)S(1)} %pad_maximum_fusion.3), channel_id=1, source_target_pairs={{0,4},{1,5},{2,18},{3,19},{4,0},{5,1},{6,22},{7,23},{8,12},{9,13},... | collective-permute-start | bytes 737288 | tf_op jit(solution)/shard_map/ppermute | solution.py:201
  101.8 3.2 %collective-permute-done.18 = f32[480,128]{1,0:T(8,128)S(1)} collective-permute-done((f32[480,128]{1,0:T(8,128)S(1)}, f32[480,128]{1,0:T(8,128)S(1)}, u32[]{:S(2)}, u32[]{:S(2)}) %collective-permute-start.18) | collective-permute-done | bytes 245792 | tf_op jit(solution)/shard_map/ppermute | solution.py:201
  105.0 3.7 %collective-permute-done.17 = f32[480,128]{1,0:T(8,128)S(1)} collective-permute-done((f32[480,128]{1,0:T(8,128)S(1)}, f32[480,128]{1,0:T(8,128)S(1)}, u32[]{:S(2)}, u32[]{:S(2)}) %collective-permute-start.17) | collective-permute-done | bytes 245792 | tf_op jit(solution)/shard_map/ppermute | solution.py:201
  109.1 1.4 %collective-permute-start.19 = (f32[1920,128]{1,0:T(8,128)S(1)}, f32[1920,128]{1,0:T(8,128)S(1)}, u32[]{:S(2)}, u32[]{:S(2)}) collective-permute-start(f32[1920,128]{1,0:T(8,128)S(1)} %pad_maximum_fusion), channel_id=1, source_target_pairs={{0,2},{1,3},{2,0},{3,1},{4,6},{5,7},{6,4},{7,5},{8,10},{9,11},{10,... | collective-permute-start | bytes 2949128 | tf_op jit(solution)/shard_map/ppermute | solution.py:210
  110.5 1.1 fusion.3
  (143 shorter events, 24.7 us)
Async XLA Ops:
  0.6 54.0 %copy-start = (bf16[560,512]{1,0:T(8,128)(2,1)S(1)}, bf16[560,512]{1,0:T(8,128)(2,1)}, u32[]{:S(2)}) copy-start(bf16[560,512]{1,0:T(8,128)(2,1)} %param.16) | copy-start | bytes 1720324
  0.7 5.0 %copy-start.23 = (s32[1,8]{1,0:T(1,128)S(1)}, s32[1,8]{1,0:T(1,128)}, u32[]{:S(2)}) copy-start(s32[1,8]{1,0:T(1,128)} %param.14) | copy-start | bytes 100
  0.7 5.1 %copy-start.24 = (s32[1,8]{1,0:T(1,128)S(1)}, s32[1,8]{1,0:T(1,128)}, u32[]{:S(2)}) copy-start(s32[1,8]{1,0:T(1,128)} %param.13) | copy-start | bytes 100
  0.7 28.1 %copy-start.17 = (bf16[1,8,640]{2,1,0:T(8,128)(2,1)S(1)}, bf16[1,8,640]{2,1,0:T(8,128)(2,1)}, u32[]{:S(2)}) copy-start(bf16[1,8,640]{2,1,0:T(8,128)(2,1)} %param.11) | copy-start | bytes 30724
  0.7 28.1 %copy-start.21 = (s32[1,8]{1,0:T(1,128)S(1)}, s32[1,8]{1,0:T(1,128)}, u32[]{:S(2)}) copy-start(s32[1,8]{1,0:T(1,128)} %param.12) | copy-start | bytes 100
  2.4 41.9 %copy-start.2 = (bf16[1,512,256]{2,1,0:T(8,128)(2,1)S(1)}, bf16[1,512,256]{2,1,0:T(8,128)(2,1)}, u32[]{:S(2)}) copy-start(bf16[1,512,256]{2,1,0:T(8,128)(2,1)} %param.15) | copy-start | bytes 786436
  2.5 44.8 %copy-start.15 = (bf16[768,256]{1,0:T(8,128)(2,1)S(1)}, bf16[768,256]{1,0:T(8,128)(2,1)}, u32[]{:S(2)}) copy-start(bf16[768,256]{1,0:T(8,128)(2,1)} %param.20) | copy-start | bytes 1179652
  2.5 36.0 %collective-permute-start.3 = (bf16[128,2048]{1,0:T(8,128)(2,1)S(1)}, bf16[128,2048]{1,0:T(8,128)(2,1)}, u32[]{:S(2)}, u32[]{:S(2)}) collective-permute-start(bf16[128,2048]{1,0:T(8,128)(2,1)S(1)} %get-tuple-element.24), channel_id=1, source_target_pairs={{0,1},{1,0},{2,3},{3,2},{4,5},{5,4},{6,7},{7,6},{8,9},{9,8},{10,11... | collective-permute-start | bytes 1572872 | tf_op jit(solution)/shard_map/ppermute | solution.py:235
  5.5 23.3 %collective-permute-start = (bf16[128,2048]{1,0:T(8,128)(2,1)S(1)}, bf16[128,2048]{1,0:T(8,128)(2,1)}, u32[]{:S(2)}, u32[]{:S(2)}) collective-permute-start(bf16[128,2048]{1,0:T(8,128)(2,1)S(1)} %get-tuple-element.25), channel_id=1, source_target_pairs={{0,1},{1,0},{2,3},{3,2},{4,5},{5,4},{6,7},{7,6},{8,9},{9,8},{10,11... | collective-permute-start | bytes 1572872 | tf_op jit(solution)/shard_map/ppermute | solution.py:234
  30.9 12.7 %all-to-all-start = ((bf16[16,2,321]{2,1,0:T(2,128)(2,1)}), bf16[16,2,321]{2,1,0:T(2,128)(2,1)S(1)}, u32[]{:S(2)}, u32[]{:S(2)}) async-start(bf16[16,2,321]{2,1,0:T(2,128)(2,1)} %reshape.119), calls=%async_computation | async-start | bytes 49152 | tf_op jit(solution)/shard_map/all_to_all | solution.py:282
  37.0 19.2 %collective-permute-start.4 = (bf16[128,2048]{1,0:T(8,128)(2,1)}, bf16[128,2048]{1,0:T(8,128)(2,1)}, u32[]{:S(2)}, u32[]{:S(2)}) collective-permute-start(bf16[128,2048]{1,0:T(8,128)(2,1)} %collective-permute-done), channel_id=1, source_target_pairs={{0,2},{2,0},{4,6},{6,4},{8,10},{10,8},{12,14},{14,12},{16,18},{18,... | collective-permute-start | bytes 1572872 | tf_op jit(solution)/shard_map/ppermute | solution.py:238
  38.5 18.8 %collective-permute-start.5 = (bf16[128,2048]{1,0:T(8,128)(2,1)}, bf16[128,2048]{1,0:T(8,128)(2,1)}, u32[]{:S(2)}, u32[]{:S(2)}) collective-permute-start(bf16[128,2048]{1,0:T(8,128)(2,1)} %collective-permute-done.3), channel_id=1, source_target_pairs={{0,2},{2,0},{4,6},{6,4},{8,10},{10,8},{12,14},{14,12},{16,18},{18,... | collective-permute-start | bytes 1572872 | tf_op jit(solution)/shard_map/ppermute | solution.py:238
  46.0 8.1 %collective-permute-start.2 = (bf16[4,80]{1,0:T(4,128)(2,1)S(1)}, bf16[4,80]{1,0:T(4,128)(2,1)S(1)}, u32[]{:S(2)}, u32[]{:S(2)}) collective-permute-start(bf16[4,80]{1,0:T(4,128)(2,1)S(1)} %get-tuple-element.50), channel_id=1, source_target_pairs={{1,0},{3,2},{5,4},{7,6},{9,8},{11,10},{13,12},{15,14},{17,16},{19,... | collective-permute-start | bytes 1928 | tf_op jit(solution)/shard_map/ppermute | solution.py:19
  47.7 5.5 %copy-start.7 = (bf16[256,512]{0,1:T(8,128)(2,1)S(1)}, bf16[256,512]{0,1:T(8,128)(2,1)}, u32[]{:S(2)}) copy-start(bf16[256,512]{0,1:T(8,128)(2,1)} %get-tuple-element.34) | copy-start | bytes 786436
  48.6 5.8 %collective-permute-start.1 = (bf16[4,80]{1,0:T(4,128)(2,1)S(1)}, bf16[4,80]{1,0:T(4,128)(2,1)S(1)}, u32[]{:S(2)}, u32[]{:S(2)}) collective-permute-start(bf16[4,80]{1,0:T(4,128)(2,1)S(1)} %get-tuple-element.51), channel_id=1, source_target_pairs={{0,1},{2,3},{4,5},{6,7},{8,9},{10,11},{12,13},{14,15},{16,17},{18,... | collective-permute-start | bytes 1928 | tf_op jit(solution)/shard_map/ppermute | solution.py:16
  62.6 1.6 %copy-start.3 = (f32[518,256]{1,0:T(8,128)}, f32[518,256]{1,0:T(8,128)S(1)}, u32[]{:S(2)}) copy-start(f32[518,256]{1,0:T(8,128)S(1)} %get-tuple-element.20) | copy-start | bytes 1591300
  67.5 2.8 %collective-permute-start.6 = (f32[1920,128]{1,0:T(8,128)S(1)}, f32[1920,128]{1,0:T(8,128)}, u32[]{:S(2)}, u32[]{:S(2)}) collective-permute-start(f32[1920,128]{1,0:T(8,128)S(1)} %constant_dynamic-slice_fusion.6), channel_id=1, source_target_pairs={{0,2},{1,3},{2,0},{3,1},{4,6},{5,7},{6,4},{7,5},{8,10},{9,11},{10,... | collective-permute-start | bytes 2949128 | tf_op jit(solution)/shard_map/ppermute | solution.py:188
  71.7 8.7 %collective-permute-start.7 = (f32[480,128]{1,0:T(8,128)S(1)}, f32[480,128]{1,0:T(8,128)S(1)}, u32[]{:S(2)}, u32[]{:S(2)}) collective-permute-start(f32[480,128]{1,0:T(8,128)S(1)} %get-tuple-element.28), channel_id=1, source_target_pairs={{0,1},{1,0},{2,10},{3,11},{4,5},{5,4},{6,14},{7,15},{8,9},{9,8},{1... | collective-permute-start | bytes 737288 | tf_op jit(solution)/shard_map/ppermute | solution.py:196
  74.0 7.1 %collective-permute-start.9 = (f32[480,128]{1,0:T(8,128)S(1)}, f32[480,128]{1,0:T(8,128)S(1)}, u32[]{:S(2)}, u32[]{:S(2)}) collective-permute-start(f32[480,128]{1,0:T(8,128)S(1)} %get-tuple-element.29), channel_id=1, source_target_pairs={{0,5},{1,4},{2,26},{3,27},{4,1},{5,0},{6,30},{7,31},{8,13},{9,12},... | collective-permute-start | bytes 737288 | tf_op jit(solution)/shard_map/ppermute | solution.py:196
  74.0 8.4 %collective-permute-start.8 = (f32[480,128]{1,0:T(8,128)S(1)}, f32[480,128]{1,0:T(8,128)S(1)}, u32[]{:S(2)}, u32[]{:S(2)}) collective-permute-start(f32[480,128]{1,0:T(8,128)S(1)} %get-tuple-element.30), channel_id=1, source_target_pairs={{0,4},{1,5},{2,18},{3,19},{4,0},{5,1},{6,22},{7,23},{8,12},{9,13},... | collective-permute-start | bytes 737288 | tf_op jit(solution)/shard_map/ppermute | solution.py:196
  82.5 4.4 %collective-permute-start.10 = (f32[120,128]{1,0:T(8,128)S(1)}, f32[120,128]{1,0:T(8,128)S(1)}, u32[]{:S(2)}, u32[]{:S(2)}) collective-permute-start(f32[120,128]{1,0:T(8,128)S(1)} %get-tuple-element.40), channel_id=1, source_target_pairs={{0,8},{1,9},{2,3},{3,2},{4,12},{5,13},{6,7},{7,6},{8,0},{9,1},{10,... | collective-permute-start | bytes 184328 | tf_op jit(solution)/shard_map/ppermute | solution.py:196
  82.9 6.0 %collective-permute-start.12 = (f32[120,128]{1,0:T(8,128)S(1)}, f32[120,128]{1,0:T(8,128)S(1)}, u32[]{:S(2)}, u32[]{:S(2)}) collective-permute-start(f32[120,128]{1,0:T(8,128)S(1)} %get-tuple-element.41), channel_id=1, source_target_pairs={{0,24},{1,25},{2,7},{3,6},{4,28},{5,29},{6,3},{7,2},{8,16},{9,17},... | collective-permute-start | bytes 184328 | tf_op jit(solution)/shard_map/ppermute | solution.py:196
  84.4 5.8 %collective-permute-start.11 = (f32[120,128]{1,0:T(8,128)S(1)}, f32[120,128]{1,0:T(8,128)S(1)}, u32[]{:S(2)}, u32[]{:S(2)}) collective-permute-start(f32[120,128]{1,0:T(8,128)S(1)} %get-tuple-element.42), channel_id=1, source_target_pairs={{0,16},{1,17},{2,6},{3,7},{4,20},{5,21},{6,2},{7,3},{8,24},{9,25},... | collective-permute-start | bytes 184328 | tf_op jit(solution)/shard_map/ppermute | solution.py:196
  90.3 6.1 %collective-permute-start.15 = (f32[120,128]{1,0:T(8,128)S(1)}, f32[120,128]{1,0:T(8,128)S(1)}, u32[]{:S(2)}, u32[]{:S(2)}) collective-permute-start(f32[120,128]{1,0:T(8,128)S(1)} %add_add_fusion.1), channel_id=1, source_target_pairs={{0,24},{1,25},{2,7},{3,6},{4,28},{5,29},{6,3},{7,2},{8,16},{9,17},... | collective-permute-start | bytes 184328 | tf_op jit(solution)/shard_map/ppermute | solution.py:201
  92.6 5.1 %collective-permute-start.14 = (f32[120,128]{1,0:T(8,128)S(1)}, f32[120,128]{1,0:T(8,128)S(1)}, u32[]{:S(2)}, u32[]{:S(2)}) collective-permute-start(f32[120,128]{1,0:T(8,128)S(1)} %add_add_fusion.1), channel_id=1, source_target_pairs={{0,16},{1,17},{2,6},{3,7},{4,20},{5,21},{6,2},{7,3},{8,24},{9,25},... | collective-permute-start | bytes 184328 | tf_op jit(solution)/shard_map/ppermute | solution.py:201
  92.6 5.1 %collective-permute-start.13 = (f32[120,128]{1,0:T(8,128)S(1)}, f32[120,128]{1,0:T(8,128)S(1)}, u32[]{:S(2)}, u32[]{:S(2)}) collective-permute-start(f32[120,128]{1,0:T(8,128)S(1)} %add_add_fusion.1), channel_id=1, source_target_pairs={{0,8},{1,9},{2,3},{3,2},{4,12},{5,13},{6,7},{7,6},{8,0},{9,1},{10,... | collective-permute-start | bytes 184328 | tf_op jit(solution)/shard_map/ppermute | solution.py:201
  97.8 7.2 %collective-permute-start.18 = (f32[480,128]{1,0:T(8,128)S(1)}, f32[480,128]{1,0:T(8,128)S(1)}, u32[]{:S(2)}, u32[]{:S(2)}) collective-permute-start(f32[480,128]{1,0:T(8,128)S(1)} %pad_maximum_fusion.3), channel_id=1, source_target_pairs={{0,5},{1,4},{2,26},{3,27},{4,1},{5,0},{6,30},{7,31},{8,13},{9,12},... | collective-permute-start | bytes 737288 | tf_op jit(solution)/shard_map/ppermute | solution.py:201
  100.1 8.5 %collective-permute-start.17 = (f32[480,128]{1,0:T(8,128)S(1)}, f32[480,128]{1,0:T(8,128)S(1)}, u32[]{:S(2)}, u32[]{:S(2)}) collective-permute-start(f32[480,128]{1,0:T(8,128)S(1)} %pad_maximum_fusion.3), channel_id=1, source_target_pairs={{0,4},{1,5},{2,18},{3,19},{4,0},{5,1},{6,22},{7,23},{8,12},{9,13},... | collective-permute-start | bytes 737288 | tf_op jit(solution)/shard_map/ppermute | solution.py:201
  101.8 6.8 %collective-permute-start.16 = (f32[480,128]{1,0:T(8,128)S(1)}, f32[480,128]{1,0:T(8,128)S(1)}, u32[]{:S(2)}, u32[]{:S(2)}) collective-permute-start(f32[480,128]{1,0:T(8,128)S(1)} %pad_maximum_fusion.3), channel_id=1, source_target_pairs={{0,1},{1,0},{2,10},{3,11},{4,5},{5,4},{6,14},{7,15},{8,9},{9,8},{1... | collective-permute-start | bytes 737288 | tf_op jit(solution)/shard_map/ppermute | solution.py:201
  108.9 1.6 %copy-start.4 = (f32[518,256]{1,0:T(8,128)S(1)}, f32[518,256]{1,0:T(8,128)}, u32[]{:S(2)}) copy-start(f32[518,256]{1,0:T(8,128)} %copy-done.3) | copy-start | bytes 1591300
  108.9 1.6 %copy-start.9 = (bf16[512,256]{1,0:T(8,128)(2,1)S(1)}, bf16[512,256]{1,0:T(8,128)(2,1)}, u32[]{:S(2)}) copy-start(bf16[512,256]{1,0:T(8,128)(2,1)} %copy-done.8) | copy-start | bytes 786436
  109.1 3.6 %collective-permute-start.19 = (f32[1920,128]{1,0:T(8,128)S(1)}, f32[1920,128]{1,0:T(8,128)S(1)}, u32[]{:S(2)}, u32[]{:S(2)}) collective-permute-start(f32[1920,128]{1,0:T(8,128)S(1)} %pad_maximum_fusion), channel_id=1, source_target_pairs={{0,2},{1,3},{2,0},{3,1},{4,6},{5,7},{6,4},{7,5},{8,10},{9,11},{10,... | collective-permute-start | bytes 2949128 | tf_op jit(solution)/shard_map/ppermute | solution.py:210
  (14 other events, 16.9 us)

commit v11 on v10

--- a/solution.py
+++ b/solution.py
@@ -229,10 +229,9 @@
     core = lax.axis_index("dp") % 2
     tm = lax.axis_index("tm")
     mine = jnp.where(core == 0, w_ups[:, :cols], w_ups[:, cols:])
-    split = rows // 2
+    bounds = [0, 16, rows // 2, rows] if rows % 32 == 0 and rows > 32 else [0, rows]
     got_parts = [
-        lax.ppermute(mine[:split], "tm", [(0, 1), (1, 0)]),
-        lax.ppermute(mine[split:], "tm", [(0, 1), (1, 0)]),
+        lax.ppermute(mine[lo:hi], "tm", [(0, 1), (1, 0)]) for lo, hi in zip(bounds, bounds[1:])
     ]
     swap = [(i, i ^ 1) for i in range(dp_size)]
     partner = jnp.concatenate([lax.ppermute(part, "dp", swap) for part in got_parts])

time: 117 us -> 99.3 us (0.85)
  waiting for transfers between devices: 51.1 us -> 30.4 us
  starting transfers between devices: 33.1 us -> 35.2 us
    ppermute x2 -> x3, waiting for transfers between devices: 22.4 us -> 0.01 us  [ups_functions(): lax.ppermute(mine[lo:hi], 'tm', [(0, 1), (1, 0)])]
    ppermute x2 -> x3, starting transfers between devices: 3.11 us -> 5.06 us  [ups_functions(): lax.ppermute(mine[lo:hi], 'tm', [(0, 1), (1, 0)])]
    slice x1 -> x3, local copies, waits for them, and re-layouts: 0.07 us -> 1.67 us  [ups_functions(): mine[lo:hi]]
    all_to_all x1, waiting for transfers between devices: 3.74 us -> 5.31 us  [on_device(): lax.all_to_all(outgoing, 'dp', split_axis=0, concat_axis=0, tiled=True)]
    unnamed x63 -> x65, local copies, waits for them, and re-layouts: 7.01 us -> 7.62 us
  transfers between devices with their start and end apart: 21 -> 23, of which waited for: 15 -> 15; matrix products, arithmetic and copies ran while one was open for 12% -> 16% of each run, Pallas kernels for 0% -> 0%
where the time goes in v11:
time: 99.3 us; the launch traced here: 98.7 us
  starting transfers between devices  35.2 us (35%)
  waiting for transfers between devices  30.4 us (31%)
  local copies, waits for them, and re-layouts  17.1 us (17%)
  other arithmetic  7.56 us (8%)
  matrix products  7.05 us (7%)
  between operations  1.34 us (1%)
    ppermute x6, waiting for transfers between devices, butterfly_psum(): total = total + lax.ppermute(send, axes, perm_of(step, offset))  11.1 us
    ppermute x6, waiting for transfers between devices, butterfly_psum(): lax.ppermute(x, axes, perm_of(step, o))  9.85 us
    ppermute x6, starting transfers between devices, butterfly_psum(): lax.ppermute(x, axes, perm_of(step, o))  8.46 us
    unnamed x65, local copies, waits for them, and re-layouts  7.62 us
    ppermute x6, starting transfers between devices, butterfly_psum(): total = total + lax.ppermute(send, axes, perm_of(step, offset))  7.43 us
    all_to_all x1, starting transfers between devices, on_device(): lax.all_to_all(outgoing, 'dp', split_axis=0, concat_axis=0, tiled=True)  5.91 us
    all_to_all x1, waiting for transfers between devices, on_device(): lax.all_to_all(outgoing, 'dp', split_axis=0, concat_axis=0, tiled=True)  5.31 us
    ppermute x3, starting transfers between devices, ups_functions(): lax.ppermute(mine[lo:hi], 'tm', [(0, 1), (1, 0)])  5.06 us
  transfers between devices with their start and end apart: 23, of which 15 were waited for; matrix products, arithmetic and copies ran while one was open for 16% of the time, Pallas kernels for 0%

profile of v11, /device:TPU:0, one launch (start us, length us, event | category | flops | bytes accessed | tf_op | source)
XLA Modules:
  0.0 98.7 jit_solution(3549961136414619023)
XLA Ops:
  0.7 1.7 %slice_select_fusion = bf16[256,2048]{1,0:T(8,128)(2,1)S(1)} fusion(bf16[256,4096]{1,0:T(8,128)(2,1)} %param.18, pred[]{:T(512)S(6)} %eq.138), kind=kLoop, calls=%fused_computation.19 | loop fusion | flops 524288 | bytes 3145729 | tf_op jit(solution)/shard_map/jit(_where)/select_n | solution.py:231
  2.4 3.0 %collective-permute-start = (bf16[16,2048]{1,0:T(8,128)(2,1)S(1)}, bf16[16,2048]{1,0:T(8,128)(2,1)}, u32[]{:S(2)}, u32[]{:S(2)}) collective-permute-start(bf16[16,2048]{1,0:T(8,128)(2,1)S(1)} %slice.138), channel_id=1, source_target_pairs={{0,1},{1,0},{2,3},{3,2},{4,5},{5,4},{6,7},{7,6},{8,9},{9,8},{10,11... | collective-permute-start | bytes 196616 | tf_op jit(solution)/shard_map/ppermute | solution.py:234
  7.2 2.0 %collective-permute-start.4 = (bf16[128,2048]{1,0:T(8,128)(2,1)}, bf16[128,2048]{1,0:T(8,128)(2,1)}, u32[]{:S(2)}, u32[]{:S(2)}) collective-permute-start(bf16[128,2048]{1,0:T(8,128)(2,1)} %slice.151), channel_id=1, source_target_pairs={{0,1},{1,0},{2,3},{3,2},{4,5},{5,4},{6,7},{7,6},{8,9},{9,8},{10,11... | collective-permute-start | bytes 1572872 | tf_op jit(solution)/shard_map/ppermute | solution.py:234
  12.0 5.9 %all-to-all-start = ((bf16[16,2,321]{2,1,0:T(2,128)(2,1)}), bf16[16,2,321]{2,1,0:T(2,128)(2,1)S(1)}, u32[]{:S(2)}, u32[]{:S(2)}) async-start(bf16[16,2,321]{2,1,0:T(2,128)(2,1)} %reshape.119), calls=%async_computation | async-start | bytes 49152 | tf_op jit(solution)/shard_map/all_to_all | solution.py:281
  19.2 5.3 %all-to-all-done = bf16[16,2,321]{2,1,0:T(2,128)(2,1)S(1)} async-done(((bf16[16,2,321]{2,1,0:T(2,128)(2,1)}), bf16[16,2,321]{2,1,0:T(2,128)(2,1)S(1)}, u32[]{:S(2)}, u32[]{:S(2)}) %all-to-all-start) | async-done | bytes 20576 | tf_op jit(solution)/shard_map/all_to_all | solution.py:281
  26.9 1.3 %collective-permute-start.2 = (bf16[4,80]{1,0:T(4,128)(2,1)S(1)}, bf16[4,80]{1,0:T(4,128)(2,1)S(1)}, u32[]{:S(2)}, u32[]{:S(2)}) collective-permute-start(bf16[4,80]{1,0:T(4,128)(2,1)S(1)} %get-tuple-element.48), channel_id=1, source_target_pairs={{1,0},{3,2},{5,4},{7,6},{9,8},{11,10},{13,12},{15,14},{17,16},{19,... | collective-permute-start | bytes 1928 | tf_op jit(solution)/shard_map/ppermute | solution.py:19
  29.5 4.5 %collective-permute-start.1 = (bf16[4,80]{1,0:T(4,128)(2,1)S(1)}, bf16[4,80]{1,0:T(4,128)(2,1)S(1)}, u32[]{:S(2)}, u32[]{:S(2)}) collective-permute-start(bf16[4,80]{1,0:T(4,128)(2,1)S(1)} %get-tuple-element.49), channel_id=1, source_target_pairs={{0,1},{2,3},{4,5},{6,7},{8,9},{10,11},{12,13},{14,15},{16,17},{18,... | collective-permute-start | bytes 1928 | tf_op jit(solution)/shard_map/ppermute | solution.py:16
  35.5 1.6 %fusion.27 = (bf16[66,512]{1,0:T(8,128)(2,1)S(1)}, f32[66,512]{1,0:T(8,128)}) fusion(pred[66]{0:T(512)(128)(4,1)} %compare_and_fusion, f32[512]{0:T(512)} %param.17, bf16[66,560]{1,0:T(8,128)(2,1)S(1)} %concatenate.68, bf16[560,512]{1,0:T(8,128)(2,1)S(1)} %copy-done), kind=kOutput, calls=%fused_computation.60 | convolution fusion | flops 38049792 | bytes 852226 | tf_op jit(solution)/shard_map/dot_general | solution.py:64
  39.6 1.1 %constant_dynamic-update-slice_fusion.2 = bf16[256,2048]{1,0:T(8,128)(2,1)S(1)} fusion(bf16[256,2048]{1,0:T(8,128)(2,1)S(1)} %constant_dynamic-update-slice_fusion.3, bf16[128,2048]{1,0:T(8,128)(2,1)} %collective-permute-done.4), kind=kLoop, calls=%fused_computation.71 | loop fusion | bytes 1048576 | tf_op jit(solution)/shard_map/concatenate | solution.py:238
  41.6 1.2 %copy-done.1 = bf16[256,4096]{1,0:T(8,128)(2,1)S(1)} copy-done((bf16[256,4096]{1,0:T(8,128)(2,1)S(1)}, bf16[256,4096]{1,0:T(8,128)(2,1)}, u32[]{:S(2)}) %copy-start.1) | copy-done | bytes 2097176
  50.1 2.6 %collective-permute-done.8 = f32[1920,128]{1,0:T(8,128)} collective-permute-done((f32[1920,128]{1,0:T(8,128)S(1)}, f32[1920,128]{1,0:T(8,128)}, u32[]{:S(2)}, u32[]{:S(2)}) %collective-permute-start.8) | collective-permute-done | bytes 983072 | tf_op jit(solution)/shard_map/ppermute | solution.py:188
  52.7 1.3 %dynamic-slice_add_fusion = f32[1920,128]{1,0:T(8,128)S(1)} fusion(f32[1920,128]{1,0:T(8,128)} %collective-permute-done.8, f32[3840,128]{1,0:T(8,128)S(1)} %fusion, s32[]{:T(128)S(6)} %select_n.365), kind=kLoop, calls=%fused_computation.23 | loop fusion | flops 245760 | bytes 2949124 | tf_op jit(solution)/shard_map/add | solution.py:188
  54.0 2.3 %collective-permute-start.9 = (f32[480,128]{1,0:T(8,128)S(1)}, f32[480,128]{1,0:T(8,128)S(1)}, u32[]{:S(2)}, u32[]{:S(2)}) collective-permute-start(f32[480,128]{1,0:T(8,128)S(1)} %get-tuple-element.26), channel_id=1, source_target_pairs={{0,1},{1,0},{2,10},{3,11},{4,5},{5,4},{6,14},{7,15},{8,9},{9,8},{1... | collective-permute-start | bytes 737288 | tf_op jit(solution)/shard_map/ppermute | solution.py:196
  56.4 1.5 %collective-permute-start.10 = (f32[480,128]{1,0:T(8,128)S(1)}, f32[480,128]{1,0:T(8,128)S(1)}, u32[]{:S(2)}, u32[]{:S(2)}) collective-permute-start(f32[480,128]{1,0:T(8,128)S(1)} %get-tuple-element.28), channel_id=1, source_target_pairs={{0,4},{1,5},{2,18},{3,19},{4,0},{5,1},{6,22},{7,23},{8,12},{9,13},... | collective-permute-start | bytes 737288 | tf_op jit(solution)/shard_map/ppermute | solution.py:196
  57.9 4.8 %collective-permute-done.9 = f32[480,128]{1,0:T(8,128)S(1)} collective-permute-done((f32[480,128]{1,0:T(8,128)S(1)}, f32[480,128]{1,0:T(8,128)S(1)}, u32[]{:S(2)}, u32[]{:S(2)}) %collective-permute-start.9) | collective-permute-done | bytes 245792 | tf_op jit(solution)/shard_map/ppermute | solution.py:196
  63.5 1.3 %collective-permute-done.10 = f32[480,128]{1,0:T(8,128)S(1)} collective-permute-done((f32[480,128]{1,0:T(8,128)S(1)}, f32[480,128]{1,0:T(8,128)S(1)}, u32[]{:S(2)}, u32[]{:S(2)}) %collective-permute-start.10) | collective-permute-done | bytes 245792 | tf_op jit(solution)/shard_map/ppermute | solution.py:196
  65.3 1.5 %collective-permute-start.14 = (f32[120,128]{1,0:T(8,128)S(1)}, f32[120,128]{1,0:T(8,128)S(1)}, u32[]{:S(2)}, u32[]{:S(2)}) collective-permute-start(f32[120,128]{1,0:T(8,128)S(1)} %get-tuple-element.39), channel_id=1, source_target_pairs={{0,24},{1,25},{2,7},{3,6},{4,28},{5,29},{6,3},{7,2},{8,16},{9,17},... | collective-permute-start | bytes 184328 | tf_op jit(solution)/shard_map/ppermute | solution.py:196
  66.8 1.6 %collective-permute-start.13 = (f32[120,128]{1,0:T(8,128)S(1)}, f32[120,128]{1,0:T(8,128)S(1)}, u32[]{:S(2)}, u32[]{:S(2)}) collective-permute-start(f32[120,128]{1,0:T(8,128)S(1)} %get-tuple-element.40), channel_id=1, source_target_pairs={{0,16},{1,17},{2,6},{3,7},{4,20},{5,21},{6,2},{7,3},{8,24},{9,25},... | collective-permute-start | bytes 184328 | tf_op jit(solution)/shard_map/ppermute | solution.py:196
  69.2 2.1 %collective-permute-done.14 = f32[120,128]{1,0:T(8,128)S(1)} collective-permute-done((f32[120,128]{1,0:T(8,128)S(1)}, f32[120,128]{1,0:T(8,128)S(1)}, u32[]{:S(2)}, u32[]{:S(2)}) %collective-permute-start.14) | collective-permute-done | bytes 61472 | tf_op jit(solution)/shard_map/ppermute | solution.py:196
  71.3 1.3 %collective-permute-done.13 = f32[120,128]{1,0:T(8,128)S(1)} collective-permute-done((f32[120,128]{1,0:T(8,128)S(1)}, f32[120,128]{1,0:T(8,128)S(1)}, u32[]{:S(2)}, u32[]{:S(2)}) %collective-permute-start.13) | collective-permute-done | bytes 61472 | tf_op jit(solution)/shard_map/ppermute | solution.py:196
  72.7 2.3 %collective-permute-start.17 = (f32[120,128]{1,0:T(8,128)S(1)}, f32[120,128]{1,0:T(8,128)S(1)}, u32[]{:S(2)}, u32[]{:S(2)}) collective-permute-start(f32[120,128]{1,0:T(8,128)S(1)} %add_add_fusion.1), channel_id=1, source_target_pairs={{0,24},{1,25},{2,7},{3,6},{4,28},{5,29},{6,3},{7,2},{8,16},{9,17},... | collective-permute-start | bytes 184328 | tf_op jit(solution)/shard_map/ppermute | solution.py:201
  75.0 2.1 %collective-permute-start.15 = (f32[120,128]{1,0:T(8,128)S(1)}, f32[120,128]{1,0:T(8,128)S(1)}, u32[]{:S(2)}, u32[]{:S(2)}) collective-permute-start(f32[120,128]{1,0:T(8,128)S(1)} %add_add_fusion.1), channel_id=1, source_target_pairs={{0,8},{1,9},{2,3},{3,2},{4,12},{5,13},{6,7},{7,6},{8,0},{9,1},{10,... | collective-permute-start | bytes 184328 | tf_op jit(solution)/shard_map/ppermute | solution.py:201
  77.1 1.6 %collective-permute-done.17 = f32[120,128]{1,0:T(8,128)S(1)} collective-permute-done((f32[120,128]{1,0:T(8,128)S(1)}, f32[120,128]{1,0:T(8,128)S(1)}, u32[]{:S(2)}, u32[]{:S(2)}) %collective-permute-start.17) | collective-permute-done | bytes 61472 | tf_op jit(solution)/shard_map/ppermute | solution.py:201
  78.8 1.4 %collective-permute-done.16 = f32[120,128]{1,0:T(8,128)S(1)} collective-permute-done((f32[120,128]{1,0:T(8,128)S(1)}, f32[120,128]{1,0:T(8,128)S(1)}, u32[]{:S(2)}, u32[]{:S(2)}) %collective-permute-start.16) | collective-permute-done | bytes 61472 | tf_op jit(solution)/shard_map/ppermute | solution.py:201
  80.2 2.3 %collective-permute-start.20 = (f32[480,128]{1,0:T(8,128)S(1)}, f32[480,128]{1,0:T(8,128)S(1)}, u32[]{:S(2)}, u32[]{:S(2)}) collective-permute-start(f32[480,128]{1,0:T(8,128)S(1)} %pad_maximum_fusion.3), channel_id=1, source_target_pairs={{0,5},{1,4},{2,26},{3,27},{4,1},{5,0},{6,30},{7,31},{8,13},{9,12},... | collective-permute-start | bytes 737288 | tf_op jit(solution)/shard_map/ppermute | solution.py:201
  82.5 1.7 %collective-permute-start.19 = (f32[480,128]{1,0:T(8,128)S(1)}, f32[480,128]{1,0:T(8,128)S(1)}, u32[]{:S(2)}, u32[]{:S(2)}) collective-permute-start(f32[480,128]{1,0:T(8,128)S(1)} %pad_maximum_fusion.3), channel_id=1, source_target_pairs={{0,4},{1,5},{2,18},{3,19},{4,0},{5,1},{6,22},{7,23},{8,12},{9,13},... | collective-permute-start | bytes 737288 | tf_op jit(solution)/shard_map/ppermute | solution.py:201
  84.2 3.2 %collective-permute-done.20 = f32[480,128]{1,0:T(8,128)S(1)} collective-permute-done((f32[480,128]{1,0:T(8,128)S(1)}, f32[480,128]{1,0:T(8,128)S(1)}, u32[]{:S(2)}, u32[]{:S(2)}) %collective-permute-start.20) | collective-permute-done | bytes 245792 | tf_op jit(solution)/shard_map/ppermute | solution.py:201
  87.4 3.7 %collective-permute-done.19 = f32[480,128]{1,0:T(8,128)S(1)} collective-permute-done((f32[480,128]{1,0:T(8,128)S(1)}, f32[480,128]{1,0:T(8,128)S(1)}, u32[]{:S(2)}, u32[]{:S(2)}) %collective-permute-start.19) | collective-permute-done | bytes 245792 | tf_op jit(solution)/shard_map/ppermute | solution.py:201
  91.5 1.4 %collective-permute-start.21 = (f32[1920,128]{1,0:T(8,128)S(1)}, f32[1920,128]{1,0:T(8,128)S(1)}, u32[]{:S(2)}, u32[]{:S(2)}) collective-permute-start(f32[1920,128]{1,0:T(8,128)S(1)} %pad_maximum_fusion), channel_id=1, source_target_pairs={{0,2},{1,3},{2,0},{3,1},{4,6},{5,7},{6,4},{7,5},{8,10},{9,11},{10,... | collective-permute-start | bytes 2949128 | tf_op jit(solution)/shard_map/ppermute | solution.py:210
  92.9 1.1 %fusion.3 = bf16[1,512,256]{2,1,0:T(8,128)(2,1)} fusion(bf16[768,256]{1,0:T(8,128)(2,1)S(1)} %copy-done.16, f32[518,256]{1,0:T(8,128)S(1)} %copy-done.4, bf16[512,256]{1,0:T(8,128)(2,1)S(1)} %copy-done.11, bf16[512,256]{1,0:T(8,128)(2,1)S(1)} %copy-done.13, bf16[512,256]{1,0:T(8,128)(2,1)S(1)} %copy-done.9, f32[256]{0:T(256)S(1)} %copy-done.22), kind=kOutput, calls=%fused_computation.9 | convolution fusion | flops 204079104 | bytes 1967104 | tf_op jit(solution)/shard_map/dot_general | solution.py:92
  94.0 1.1 %collective-permute-done.21 = f32[1920,128]{1,0:T(8,128)S(1)} collective-permute-done((f32[1920,128]{1,0:T(8,128)S(1)}, f32[1920,128]{1,0:T(8,128)S(1)}, u32[]{:S(2)}, u32[]{:S(2)}) %collective-permute-start.21) | collective-permute-done | bytes 983072 | tf_op jit(solution)/shard_map/ppermute | solution.py:210
  97.6 1.1 %slice.165 = f32[2240,128]{1,0:T(8,128)} slice(f32[3840,128]{1,0:T(8,128)S(1)} %broadcast_select_fusion.2), slice={[0:2240], [0:128]} | slice | bytes 2293760 | tf_op jit(solution)/shard_map/slice | solution.py:214
  (151 shorter events, 26.3 us)
Async XLA Ops:
  0.6 34.9 %copy-start = (bf16[560,512]{1,0:T(8,128)(2,1)S(1)}, bf16[560,512]{1,0:T(8,128)(2,1)}, u32[]{:S(2)}) copy-start(bf16[560,512]{1,0:T(8,128)(2,1)} %param.16) | copy-start | bytes 1720324
  0.7 8.5 %copy-start.23 = (s32[1,8]{1,0:T(1,128)S(1)}, s32[1,8]{1,0:T(1,128)}, u32[]{:S(2)}) copy-start(s32[1,8]{1,0:T(1,128)} %param.13) | copy-start | bytes 100
  0.7 8.5 %copy-start.24 = (s32[1,8]{1,0:T(1,128)S(1)}, s32[1,8]{1,0:T(1,128)}, u32[]{:S(2)}) copy-start(s32[1,8]{1,0:T(1,128)} %param.14) | copy-start | bytes 100
  0.7 9.2 %copy-start.17 = (bf16[1,8,640]{2,1,0:T(8,128)(2,1)S(1)}, bf16[1,8,640]{2,1,0:T(8,128)(2,1)}, u32[]{:S(2)}) copy-start(bf16[1,8,640]{2,1,0:T(8,128)(2,1)} %param.11) | copy-start | bytes 30724
  0.7 9.2 %copy-start.21 = (s32[1,8]{1,0:T(1,128)S(1)}, s32[1,8]{1,0:T(1,128)}, u32[]{:S(2)}) copy-start(s32[1,8]{1,0:T(1,128)} %param.12) | copy-start | bytes 100
  2.4 22.8 %copy-start.2 = (bf16[1,512,256]{2,1,0:T(8,128)(2,1)S(1)}, bf16[1,512,256]{2,1,0:T(8,128)(2,1)}, u32[]{:S(2)}) copy-start(bf16[1,512,256]{2,1,0:T(8,128)(2,1)} %param.15) | copy-start | bytes 786436
  2.4 25.7 %copy-start.15 = (bf16[768,256]{1,0:T(8,128)(2,1)S(1)}, bf16[768,256]{1,0:T(8,128)(2,1)}, u32[]{:S(2)}) copy-start(bf16[768,256]{1,0:T(8,128)(2,1)} %param.20) | copy-start | bytes 1179652
  2.4 7.5 %collective-permute-start = (bf16[16,2048]{1,0:T(8,128)(2,1)S(1)}, bf16[16,2048]{1,0:T(8,128)(2,1)}, u32[]{:S(2)}, u32[]{:S(2)}) collective-permute-start(bf16[16,2048]{1,0:T(8,128)(2,1)S(1)} %slice.138), channel_id=1, source_target_pairs={{0,1},{1,0},{2,3},{3,2},{4,5},{5,4},{6,7},{7,6},{8,9},{9,8},{10,11... | collective-permute-start | bytes 196616 | tf_op jit(solution)/shard_map/ppermute | solution.py:234
  6.3 31.7 %collective-permute-start.3 = (bf16[112,2048]{1,0:T(8,128)(2,1)}, bf16[112,2048]{1,0:T(8,128)(2,1)}, u32[]{:S(2)}, u32[]{:S(2)}) collective-permute-start(bf16[112,2048]{1,0:T(8,128)(2,1)} %slice.150), channel_id=1, source_target_pairs={{0,1},{1,0},{2,3},{3,2},{4,5},{5,4},{6,7},{7,6},{8,9},{9,8},{10,11... | collective-permute-start | bytes 1376264 | tf_op jit(solution)/shard_map/ppermute | solution.py:234
  7.2 30.9 %collective-permute-start.4 = (bf16[128,2048]{1,0:T(8,128)(2,1)}, bf16[128,2048]{1,0:T(8,128)(2,1)}, u32[]{:S(2)}, u32[]{:S(2)}) collective-permute-start(bf16[128,2048]{1,0:T(8,128)(2,1)} %slice.151), channel_id=1, source_target_pairs={{0,1},{1,0},{2,3},{3,2},{4,5},{5,4},{6,7},{7,6},{8,9},{9,8},{10,11... | collective-permute-start | bytes 1572872 | tf_op jit(solution)/shard_map/ppermute | solution.py:234
  12.0 12.5 %all-to-all-start = ((bf16[16,2,321]{2,1,0:T(2,128)(2,1)}), bf16[16,2,321]{2,1,0:T(2,128)(2,1)S(1)}, u32[]{:S(2)}, u32[]{:S(2)}) async-start(bf16[16,2,321]{2,1,0:T(2,128)(2,1)} %reshape.119), calls=%async_computation | async-start | bytes 49152 | tf_op jit(solution)/shard_map/all_to_all | solution.py:281
  17.9 19.2 %collective-permute-start.5 = (bf16[16,2048]{1,0:T(8,128)(2,1)}, bf16[16,2048]{1,0:T(8,128)(2,1)}, u32[]{:S(2)}, u32[]{:S(2)}) collective-permute-start(bf16[16,2048]{1,0:T(8,128)(2,1)} %collective-permute-done), channel_id=1, source_target_pairs={{0,2},{2,0},{4,6},{6,4},{8,10},{10,8},{12,14},{14,12},{16,18},{18,... | collective-permute-start | bytes 196616 | tf_op jit(solution)/shard_map/ppermute | solution.py:237
  26.9 8.1 %collective-permute-start.2 = (bf16[4,80]{1,0:T(4,128)(2,1)S(1)}, bf16[4,80]{1,0:T(4,128)(2,1)S(1)}, u32[]{:S(2)}, u32[]{:S(2)}) collective-permute-start(bf16[4,80]{1,0:T(4,128)(2,1)S(1)} %get-tuple-element.48), channel_id=1, source_target_pairs={{1,0},{3,2},{5,4},{7,6},{9,8},{11,10},{13,12},{15,14},{17,16},{19,... | collective-permute-start | bytes 1928 | tf_op jit(solution)/shard_map/ppermute | solution.py:19
  28.6 5.5 %copy-start.7 = (bf16[256,512]{0,1:T(8,128)(2,1)S(1)}, bf16[256,512]{0,1:T(8,128)(2,1)}, u32[]{:S(2)}) copy-start(bf16[256,512]{0,1:T(8,128)(2,1)} %get-tuple-element.32) | copy-start | bytes 786436
  29.5 5.8 %collective-permute-start.1 = (bf16[4,80]{1,0:T(4,128)(2,1)S(1)}, bf16[4,80]{1,0:T(4,128)(2,1)S(1)}, u32[]{:S(2)}, u32[]{:S(2)}) collective-permute-start(bf16[4,80]{1,0:T(4,128)(2,1)S(1)} %get-tuple-element.49), channel_id=1, source_target_pairs={{0,1},{2,3},{4,5},{6,7},{8,9},{10,11},{12,13},{14,15},{16,17},{18,... | collective-permute-start | bytes 1928 | tf_op jit(solution)/shard_map/ppermute | solution.py:16
  38.0 2.7 %collective-permute-start.6 = (bf16[112,2048]{1,0:T(8,128)(2,1)}, bf16[112,2048]{1,0:T(8,128)(2,1)S(1)}, u32[]{:S(2)}, u32[]{:S(2)}) collective-permute-start(bf16[112,2048]{1,0:T(8,128)(2,1)} %collective-permute-done.3), channel_id=1, source_target_pairs={{0,2},{2,0},{4,6},{6,4},{8,10},{10,8},{12,14},{14,12},{16,18},{18,... | collective-permute-start | bytes 1376264 | tf_op jit(solution)/shard_map/ppermute | solution.py:237
  38.0 2.8 %collective-permute-start.7 = (bf16[128,2048]{1,0:T(8,128)(2,1)}, bf16[128,2048]{1,0:T(8,128)(2,1)S(1)}, u32[]{:S(2)}, u32[]{:S(2)}) collective-permute-start(bf16[128,2048]{1,0:T(8,128)(2,1)} %collective-permute-done.4), channel_id=1, source_target_pairs={{0,2},{2,0},{4,6},{6,4},{8,10},{10,8},{12,14},{14,12},{16,18},{18,... | collective-permute-start | bytes 1572872 | tf_op jit(solution)/shard_map/ppermute | solution.py:237
  45.0 1.6 %copy-start.3 = (f32[518,256]{1,0:T(8,128)}, f32[518,256]{1,0:T(8,128)S(1)}, u32[]{:S(2)}) copy-start(f32[518,256]{1,0:T(8,128)S(1)} %get-tuple-element.20) | copy-start | bytes 1591300
  49.9 2.8 %collective-permute-start.8 = (f32[1920,128]{1,0:T(8,128)S(1)}, f32[1920,128]{1,0:T(8,128)}, u32[]{:S(2)}, u32[]{:S(2)}) collective-permute-start(f32[1920,128]{1,0:T(8,128)S(1)} %constant_dynamic-slice_fusion.6), channel_id=1, source_target_pairs={{0,2},{1,3},{2,0},{3,1},{4,6},{5,7},{6,4},{7,5},{8,10},{9,11},{10,... | collective-permute-start | bytes 2949128 | tf_op jit(solution)/shard_map/ppermute | solution.py:188
  54.0 8.7 %collective-permute-start.9 = (f32[480,128]{1,0:T(8,128)S(1)}, f32[480,128]{1,0:T(8,128)S(1)}, u32[]{:S(2)}, u32[]{:S(2)}) collective-permute-start(f32[480,128]{1,0:T(8,128)S(1)} %get-tuple-element.26), channel_id=1, source_target_pairs={{0,1},{1,0},{2,10},{3,11},{4,5},{5,4},{6,14},{7,15},{8,9},{9,8},{1... | collective-permute-start | bytes 737288 | tf_op jit(solution)/shard_map/ppermute | solution.py:196
  56.4 7.1 %collective-permute-start.11 = (f32[480,128]{1,0:T(8,128)S(1)}, f32[480,128]{1,0:T(8,128)S(1)}, u32[]{:S(2)}, u32[]{:S(2)}) collective-permute-start(f32[480,128]{1,0:T(8,128)S(1)} %get-tuple-element.27), channel_id=1, source_target_pairs={{0,5},{1,4},{2,26},{3,27},{4,1},{5,0},{6,30},{7,31},{8,13},{9,12},... | collective-permute-start | bytes 737288 | tf_op jit(solution)/shard_map/ppermute | solution.py:196
  56.4 8.4 %collective-permute-start.10 = (f32[480,128]{1,0:T(8,128)S(1)}, f32[480,128]{1,0:T(8,128)S(1)}, u32[]{:S(2)}, u32[]{:S(2)}) collective-permute-start(f32[480,128]{1,0:T(8,128)S(1)} %get-tuple-element.28), channel_id=1, source_target_pairs={{0,4},{1,5},{2,18},{3,19},{4,0},{5,1},{6,22},{7,23},{8,12},{9,13},... | collective-permute-start | bytes 737288 | tf_op jit(solution)/shard_map/ppermute | solution.py:196
  64.9 4.4 %collective-permute-start.12 = (f32[120,128]{1,0:T(8,128)S(1)}, f32[120,128]{1,0:T(8,128)S(1)}, u32[]{:S(2)}, u32[]{:S(2)}) collective-permute-start(f32[120,128]{1,0:T(8,128)S(1)} %get-tuple-element.38), channel_id=1, source_target_pairs={{0,8},{1,9},{2,3},{3,2},{4,12},{5,13},{6,7},{7,6},{8,0},{9,1},{10,... | collective-permute-start | bytes 184328 | tf_op jit(solution)/shard_map/ppermute | solution.py:196
  65.3 6.0 %collective-permute-start.14 = (f32[120,128]{1,0:T(8,128)S(1)}, f32[120,128]{1,0:T(8,128)S(1)}, u32[]{:S(2)}, u32[]{:S(2)}) collective-permute-start(f32[120,128]{1,0:T(8,128)S(1)} %get-tuple-element.39), channel_id=1, source_target_pairs={{0,24},{1,25},{2,7},{3,6},{4,28},{5,29},{6,3},{7,2},{8,16},{9,17},... | collective-permute-start | bytes 184328 | tf_op jit(solution)/shard_map/ppermute | solution.py:196
  66.8 5.8 %collective-permute-start.13 = (f32[120,128]{1,0:T(8,128)S(1)}, f32[120,128]{1,0:T(8,128)S(1)}, u32[]{:S(2)}, u32[]{:S(2)}) collective-permute-start(f32[120,128]{1,0:T(8,128)S(1)} %get-tuple-element.40), channel_id=1, source_target_pairs={{0,16},{1,17},{2,6},{3,7},{4,20},{5,21},{6,2},{7,3},{8,24},{9,25},... | collective-permute-start | bytes 184328 | tf_op jit(solution)/shard_map/ppermute | solution.py:196
  72.7 6.1 %collective-permute-start.17 = (f32[120,128]{1,0:T(8,128)S(1)}, f32[120,128]{1,0:T(8,128)S(1)}, u32[]{:S(2)}, u32[]{:S(2)}) collective-permute-start(f32[120,128]{1,0:T(8,128)S(1)} %add_add_fusion.1), channel_id=1, source_target_pairs={{0,24},{1,25},{2,7},{3,6},{4,28},{5,29},{6,3},{7,2},{8,16},{9,17},... | collective-permute-start | bytes 184328 | tf_op jit(solution)/shard_map/ppermute | solution.py:201
  75.0 5.1 %collective-permute-start.16 = (f32[120,128]{1,0:T(8,128)S(1)}, f32[120,128]{1,0:T(8,128)S(1)}, u32[]{:S(2)}, u32[]{:S(2)}) collective-permute-start(f32[120,128]{1,0:T(8,128)S(1)} %add_add_fusion.1), channel_id=1, source_target_pairs={{0,16},{1,17},{2,6},{3,7},{4,20},{5,21},{6,2},{7,3},{8,24},{9,25},... | collective-permute-start | bytes 184328 | tf_op jit(solution)/shard_map/ppermute | solution.py:201
  75.0 5.1 %collective-permute-start.15 = (f32[120,128]{1,0:T(8,128)S(1)}, f32[120,128]{1,0:T(8,128)S(1)}, u32[]{:S(2)}, u32[]{:S(2)}) collective-permute-start(f32[120,128]{1,0:T(8,128)S(1)} %add_add_fusion.1), channel_id=1, source_target_pairs={{0,8},{1,9},{2,3},{3,2},{4,12},{5,13},{6,7},{7,6},{8,0},{9,1},{10,... | collective-permute-start | bytes 184328 | tf_op jit(solution)/shard_map/ppermute | solution.py:201
  80.2 7.2 %collective-permute-start.20 = (f32[480,128]{1,0:T(8,128)S(1)}, f32[480,128]{1,0:T(8,128)S(1)}, u32[]{:S(2)}, u32[]{:S(2)}) collective-permute-start(f32[480,128]{1,0:T(8,128)S(1)} %pad_maximum_fusion.3), channel_id=1, source_target_pairs={{0,5},{1,4},{2,26},{3,27},{4,1},{5,0},{6,30},{7,31},{8,13},{9,12},... | collective-permute-start | bytes 737288 | tf_op jit(solution)/shard_map/ppermute | solution.py:201
  82.5 8.5 %collective-permute-start.19 = (f32[480,128]{1,0:T(8,128)S(1)}, f32[480,128]{1,0:T(8,128)S(1)}, u32[]{:S(2)}, u32[]{:S(2)}) collective-permute-start(f32[480,128]{1,0:T(8,128)S(1)} %pad_maximum_fusion.3), channel_id=1, source_target_pairs={{0,4},{1,5},{2,18},{3,19},{4,0},{5,1},{6,22},{7,23},{8,12},{9,13},... | collective-permute-start | bytes 737288 | tf_op jit(solution)/shard_map/ppermute | solution.py:201
  84.2 6.8 %collective-permute-start.18 = (f32[480,128]{1,0:T(8,128)S(1)}, f32[480,128]{1,0:T(8,128)S(1)}, u32[]{:S(2)}, u32[]{:S(2)}) collective-permute-start(f32[480,128]{1,0:T(8,128)S(1)} %pad_maximum_fusion.3), channel_id=1, source_target_pairs={{0,1},{1,0},{2,10},{3,11},{4,5},{5,4},{6,14},{7,15},{8,9},{9,8},{1... | collective-permute-start | bytes 737288 | tf_op jit(solution)/shard_map/ppermute | solution.py:201
  91.5 3.6 %collective-permute-start.21 = (f32[1920,128]{1,0:T(8,128)S(1)}, f32[1920,128]{1,0:T(8,128)S(1)}, u32[]{:S(2)}, u32[]{:S(2)}) collective-permute-start(f32[1920,128]{1,0:T(8,128)S(1)} %pad_maximum_fusion), channel_id=1, source_target_pairs={{0,2},{1,3},{2,0},{3,1},{4,6},{5,7},{6,4},{7,5},{8,10},{9,11},{10,... | collective-permute-start | bytes 2949128 | tf_op jit(solution)/shard_map/ppermute | solution.py:210
  (16 other events, 20.1 us)

commit v12 on v11

--- a/solution.py
+++ b/solution.py
@@ -228,16 +228,20 @@
     cols = width // 2
     core = lax.axis_index("dp") % 2
     tm = lax.axis_index("tm")
-    mine = jnp.where(core == 0, w_ups[:, :cols], w_ups[:, cols:])
     bounds = [0, 16, rows // 2, rows] if rows % 32 == 0 and rows > 32 else [0, rows]
-    got_parts = [
-        lax.ppermute(mine[lo:hi], "tm", [(0, 1), (1, 0)]) for lo, hi in zip(bounds, bounds[1:])
-    ]
     swap = [(i, i ^ 1) for i in range(dp_size)]
-    partner = jnp.concatenate([lax.ppermute(part, "dp", swap) for part in got_parts])
-    got = jnp.concatenate(got_parts)
-    low = jnp.where(core == 0, got, partner)
-    high = jnp.where(core == 0, partner, got)
+    got_parts, partner_parts = [], []
+    for lo, hi in zip(bounds, bounds[1:]):
+        block = w_ups[lo:hi]
+        mine = jnp.where(core == 0, block[:, :cols], block[:, cols:])
+        got_parts.append(lax.ppermute(mine, "tm", [(0, 1), (1, 0)]))
+        partner_parts.append(lax.ppermute(got_parts[-1], "dp", swap))
+    low = jnp.concatenate(
+        [jnp.where(core == 0, g, p) for g, p in zip(got_parts, partner_parts)]
+    )
+    high = jnp.concatenate(
+        [jnp.where(core == 0, p, g) for g, p in zip(got_parts, partner_parts)]
+    )
 
     def forward(act):
         own_act = lax.dynamic_slice_in_dim(act, tm * rows, rows, axis=1)

time: 99.3 us -> 97.8 us (0.985)
  local copies, waits for them, and re-layouts: 17.1 us -> 10.2 us
  other arithmetic: 7.56 us -> 13 us
  matrix products: 7.05 us -> 5.62 us
    select_n x1 -> x6, other arithmetic: 1.7 us -> 8.1 us  [the longest x3 5.05 us: ups_functions(): mine = jnp.where(core == 0, block[:, :cols], block[:, cols:])]
    unnamed x65 -> x51, local copies, waits for them, and re-layouts: 7.62 us -> 4.34 us
    slice x3 -> x0, local copies, waits for them, and re-layouts: 1.67 us -> none  [ups_functions(): mine[lo:hi]]
    dot_general x1, matrix products: 1.61 us -> 0.25 us  [local_pass(): pre = jnp.dot(patches, w_pre, preferred_element_type=jnp.float32) + b_pre]
    concatenate x2 -> x0, local copies, waits for them, and re-layouts: 1.12 us -> none  [the longest x1 1.08 us: ups_functions(): got = jnp.concatenate(got_parts)]
  transfers between devices with their start and end apart: 23 -> 23, of which waited for: 15 -> 15; matrix products, arithmetic and copies ran while one was open for 16% -> 13% of each run, Pallas kernels for 0% -> 0%
where the time goes in v12:
time: 97.8 us; the launch traced here: 97.3 us
  starting transfers between devices  36 us (37%)
  waiting for transfers between devices  31.1 us (32%)
  other arithmetic  13 us (13%)
  local copies, waits for them, and re-layouts  10.2 us (10%)
  matrix products  5.62 us (6%)
  between operations  1.3 us (1%)
    ppermute x6, waiting for transfers between devices, butterfly_psum(): total = total + lax.ppermute(send, axes, perm_of(step, offset))  11.1 us
    ppermute x6, waiting for transfers between devices, butterfly_psum(): lax.ppermute(x, axes, perm_of(step, o))  9.85 us
    ppermute x6, starting transfers between devices, butterfly_psum(): lax.ppermute(x, axes, perm_of(step, o))  8.46 us
    ppermute x6, starting transfers between devices, butterfly_psum(): total = total + lax.ppermute(send, axes, perm_of(step, offset))  7.54 us
    all_to_all x1, waiting for transfers between devices, on_device(): lax.all_to_all(outgoing, 'dp', split_axis=0, concat_axis=0, tiled=True)  6.07 us
    all_to_all x1, starting transfers between devices, on_device(): lax.all_to_all(outgoing, 'dp', split_axis=0, concat_axis=0, tiled=True)  5.91 us
    ppermute x1, starting transfers between devices, with_halo(): lax.ppermute(lax.slice_in_dim(block, block.shape[dim] - width, None, axis...  5.13 us
    select_n x3, other arithmetic, ups_functions(): mine = jnp.where(core == 0, block[:, :cols], block[:, cols:])  5.05 us
  transfers between devices with their start and end apart: 23, of which 15 were waited for; matrix products, arithmetic and copies ran while one was open for 13% of the time, Pallas kernels for 0%

profile of v12, /device:TPU:0, one launch (start us, length us, event | category | flops | bytes accessed | tf_op | source)
XLA Modules:
  0.0 97.3 jit_solution(16897344883074619460)
XLA Ops:
  1.7 3.0 %collective-permute-start = (bf16[16,2048]{1,0:T(8,128)(2,1)S(1)}, bf16[16,2048]{1,0:T(8,128)(2,1)S(1)}, u32[]{:S(2)}, u32[]{:S(2)}) collective-permute-start(bf16[16,2048]{1,0:T(8,128)(2,1)S(1)} %slice_select_fusion.2), channel_id=1, source_target_pairs={{0,1},{1,0},{2,3},{3,2},{4,5},{5,4},{6,7},{7,6},{8,9},{9,8},{10,11... | collective-permute-start | bytes 196616 | tf_op jit(solution)/shard_map/ppermute | solution.py:237
  4.7 2.0 %slice_select_fusion.1 = bf16[112,2048]{1,0:T(8,128)(2,1)} fusion(bf16[256,4096]{1,0:T(8,128)(2,1)} %param.18, pred[]{:T(512)S(6)} %eq.144), kind=kLoop, calls=%fused_computation.42 | loop fusion | flops 229376 | bytes 1376257 | tf_op jit(solution)/shard_map/jit(_where)/select_n | solution.py:236
  6.7 2.1 %slice_select_fusion = bf16[128,2048]{1,0:T(8,128)(2,1)} fusion(bf16[256,4096]{1,0:T(8,128)(2,1)} %param.18, pred[]{:T(512)S(6)} %eq.144), kind=kLoop, calls=%fused_computation.39 | loop fusion | flops 262144 | bytes 1572865 | tf_op jit(solution)/shard_map/jit(_where)/select_n | solution.py:236
  8.8 2.0 %collective-permute-start.6 = (bf16[128,2048]{1,0:T(8,128)(2,1)}, bf16[128,2048]{1,0:T(8,128)(2,1)}, u32[]{:S(2)}, u32[]{:S(2)}) collective-permute-start(bf16[128,2048]{1,0:T(8,128)(2,1)} %slice_select_fusion), channel_id=1, source_target_pairs={{0,1},{1,0},{2,3},{3,2},{4,5},{5,4},{6,7},{7,6},{8,9},{9,8},{10,11... | collective-permute-start | bytes 1572872 | tf_op jit(solution)/shard_map/ppermute | solution.py:237
  13.1 5.9 %all-to-all-start = ((bf16[16,2,321]{2,1,0:T(2,128)(2,1)}), bf16[16,2,321]{2,1,0:T(2,128)(2,1)S(1)}, u32[]{:S(2)}, u32[]{:S(2)}) async-start(bf16[16,2,321]{2,1,0:T(2,128)(2,1)} %reshape.119), calls=%async_computation | async-start | bytes 49152 | tf_op jit(solution)/shard_map/all_to_all | solution.py:285
  19.5 6.1 %all-to-all-done = bf16[16,2,321]{2,1,0:T(2,128)(2,1)S(1)} async-done(((bf16[16,2,321]{2,1,0:T(2,128)(2,1)}), bf16[16,2,321]{2,1,0:T(2,128)(2,1)S(1)}, u32[]{:S(2)}, u32[]{:S(2)}) %all-to-all-start) | async-done | bytes 20576 | tf_op jit(solution)/shard_map/all_to_all | solution.py:285
  27.3 1.3 %collective-permute-start.2 = (bf16[4,80]{1,0:T(4,128)(2,1)}, bf16[4,80]{1,0:T(4,128)(2,1)S(1)}, u32[]{:S(2)}, u32[]{:S(2)}) collective-permute-start(bf16[4,80]{1,0:T(4,128)(2,1)} %get-tuple-element.54), channel_id=1, source_target_pairs={{1,0},{3,2},{5,4},{7,6},{9,8},{11,10},{13,12},{15,14},{17,16},{19,... | collective-permute-start | bytes 1928 | tf_op jit(solution)/shard_map/ppermute | solution.py:19
  28.6 5.1 %collective-permute-start.1 = (bf16[4,80]{1,0:T(4,128)(2,1)}, bf16[4,80]{1,0:T(4,128)(2,1)}, u32[]{:S(2)}, u32[]{:S(2)}) collective-permute-start(bf16[4,80]{1,0:T(4,128)(2,1)} %get-tuple-element.55), channel_id=1, source_target_pairs={{0,1},{2,3},{4,5},{6,7},{8,9},{10,11},{12,13},{14,15},{16,17},{18,... | collective-permute-start | bytes 1928 | tf_op jit(solution)/shard_map/ppermute | solution.py:16
  37.7 1.1 %broadcast_select_fusion.4 = (bf16[112,2048]{1,0:T(8,128)(2,1)S(1)}, bf16[112,2048]{1,0:T(8,128)(2,1)S(1)}) fusion(bf16[112,2048]{1,0:T(8,128)(2,1)} %collective-permute-done.4, bf16[112,2048]{1,0:T(8,128)(2,1)S(1)} %collective-permute-done.5, pred[]{:T(512)S(6)} %eq.144), kind=kLoop, calls=%fused_computation.44 | loop fusion | flops 458752 | bytes 1835009 | tf_op jit(solution)/shard_map/jit(_where)/select_n | solution.py:240
  38.8 1.1 %broadcast_select_fusion.2 = (bf16[128,2048]{1,0:T(8,128)(2,1)S(1)}, bf16[128,2048]{1,0:T(8,128)(2,1)S(1)}) fusion(bf16[128,2048]{1,0:T(8,128)(2,1)} %collective-permute-done.6, bf16[128,2048]{1,0:T(8,128)(2,1)S(1)} %collective-permute-done.7, pred[]{:T(512)S(6)} %eq.144), kind=kLoop, calls=%fused_computation.41 | loop fusion | flops 524288 | bytes 2097153 | tf_op jit(solution)/shard_map/jit(_where)/select_n | solution.py:240
  40.6 1.3 %copy-done.1 = bf16[256,4096]{1,0:T(8,128)(2,1)S(1)} copy-done((bf16[256,4096]{1,0:T(8,128)(2,1)S(1)}, bf16[256,4096]{1,0:T(8,128)(2,1)}, u32[]{:S(2)}) %copy-start.1) | copy-done | bytes 2097176
  48.6 2.6 %collective-permute-done.8 = f32[1920,128]{1,0:T(8,128)} collective-permute-done((f32[1920,128]{1,0:T(8,128)S(1)}, f32[1920,128]{1,0:T(8,128)}, u32[]{:S(2)}, u32[]{:S(2)}) %collective-permute-start.8) | collective-permute-done | bytes 983072 | tf_op jit(solution)/shard_map/ppermute | solution.py:188
  51.1 1.3 %dynamic-slice_add_fusion = f32[1920,128]{1,0:T(8,128)S(1)} fusion(f32[1920,128]{1,0:T(8,128)} %collective-permute-done.8, f32[3840,128]{1,0:T(8,128)S(1)} %fusion, s32[]{:T(128)S(6)} %select_n.405), kind=kLoop, calls=%fused_computation.22 | loop fusion | flops 245760 | bytes 2949124 | tf_op jit(solution)/shard_map/add | solution.py:188
  52.5 2.4 %collective-permute-start.9 = (f32[480,128]{1,0:T(8,128)S(1)}, f32[480,128]{1,0:T(8,128)S(1)}, u32[]{:S(2)}, u32[]{:S(2)}) collective-permute-start(f32[480,128]{1,0:T(8,128)S(1)} %get-tuple-element.28), channel_id=1, source_target_pairs={{0,1},{1,0},{2,10},{3,11},{4,5},{5,4},{6,14},{7,15},{8,9},{9,8},{1... | collective-permute-start | bytes 737288 | tf_op jit(solution)/shard_map/ppermute | solution.py:196
  55.0 1.5 %collective-permute-start.10 = (f32[480,128]{1,0:T(8,128)S(1)}, f32[480,128]{1,0:T(8,128)S(1)}, u32[]{:S(2)}, u32[]{:S(2)}) collective-permute-start(f32[480,128]{1,0:T(8,128)S(1)} %get-tuple-element.30), channel_id=1, source_target_pairs={{0,4},{1,5},{2,18},{3,19},{4,0},{5,1},{6,22},{7,23},{8,12},{9,13},... | collective-permute-start | bytes 737288 | tf_op jit(solution)/shard_map/ppermute | solution.py:196
  56.5 4.8 %collective-permute-done.9 = f32[480,128]{1,0:T(8,128)S(1)} collective-permute-done((f32[480,128]{1,0:T(8,128)S(1)}, f32[480,128]{1,0:T(8,128)S(1)}, u32[]{:S(2)}, u32[]{:S(2)}) %collective-permute-start.9) | collective-permute-done | bytes 245792 | tf_op jit(solution)/shard_map/ppermute | solution.py:196
  62.1 1.3 %collective-permute-done.10 = f32[480,128]{1,0:T(8,128)S(1)} collective-permute-done((f32[480,128]{1,0:T(8,128)S(1)}, f32[480,128]{1,0:T(8,128)S(1)}, u32[]{:S(2)}, u32[]{:S(2)}) %collective-permute-start.10) | collective-permute-done | bytes 245792 | tf_op jit(solution)/shard_map/ppermute | solution.py:196
  63.9 1.5 %collective-permute-start.14 = (f32[120,128]{1,0:T(8,128)S(1)}, f32[120,128]{1,0:T(8,128)S(1)}, u32[]{:S(2)}, u32[]{:S(2)}) collective-permute-start(f32[120,128]{1,0:T(8,128)S(1)} %get-tuple-element.43), channel_id=1, source_target_pairs={{0,24},{1,25},{2,7},{3,6},{4,28},{5,29},{6,3},{7,2},{8,16},{9,17},... | collective-permute-start | bytes 184328 | tf_op jit(solution)/shard_map/ppermute | solution.py:196
  65.4 1.6 %collective-permute-start.13 = (f32[120,128]{1,0:T(8,128)S(1)}, f32[120,128]{1,0:T(8,128)S(1)}, u32[]{:S(2)}, u32[]{:S(2)}) collective-permute-start(f32[120,128]{1,0:T(8,128)S(1)} %get-tuple-element.44), channel_id=1, source_target_pairs={{0,16},{1,17},{2,6},{3,7},{4,20},{5,21},{6,2},{7,3},{8,24},{9,25},... | collective-permute-start | bytes 184328 | tf_op jit(solution)/shard_map/ppermute | solution.py:196
  67.7 2.2 %collective-permute-done.14 = f32[120,128]{1,0:T(8,128)S(1)} collective-permute-done((f32[120,128]{1,0:T(8,128)S(1)}, f32[120,128]{1,0:T(8,128)S(1)}, u32[]{:S(2)}, u32[]{:S(2)}) %collective-permute-start.14) | collective-permute-done | bytes 61472 | tf_op jit(solution)/shard_map/ppermute | solution.py:196
  69.9 1.3 %collective-permute-done.13 = f32[120,128]{1,0:T(8,128)S(1)} collective-permute-done((f32[120,128]{1,0:T(8,128)S(1)}, f32[120,128]{1,0:T(8,128)S(1)}, u32[]{:S(2)}, u32[]{:S(2)}) %collective-permute-start.13) | collective-permute-done | bytes 61472 | tf_op jit(solution)/shard_map/ppermute | solution.py:196
  71.3 2.3 %collective-permute-start.17 = (f32[120,128]{1,0:T(8,128)S(1)}, f32[120,128]{1,0:T(8,128)S(1)}, u32[]{:S(2)}, u32[]{:S(2)}) collective-permute-start(f32[120,128]{1,0:T(8,128)S(1)} %add_add_fusion.1), channel_id=1, source_target_pairs={{0,24},{1,25},{2,7},{3,6},{4,28},{5,29},{6,3},{7,2},{8,16},{9,17},... | collective-permute-start | bytes 184328 | tf_op jit(solution)/shard_map/ppermute | solution.py:201
  73.6 2.1 %collective-permute-start.15 = (f32[120,128]{1,0:T(8,128)S(1)}, f32[120,128]{1,0:T(8,128)S(1)}, u32[]{:S(2)}, u32[]{:S(2)}) collective-permute-start(f32[120,128]{1,0:T(8,128)S(1)} %add_add_fusion.1), channel_id=1, source_target_pairs={{0,8},{1,9},{2,3},{3,2},{4,12},{5,13},{6,7},{7,6},{8,0},{9,1},{10,... | collective-permute-start | bytes 184328 | tf_op jit(solution)/shard_map/ppermute | solution.py:201
  75.7 1.6 %collective-permute-done.17 = f32[120,128]{1,0:T(8,128)S(1)} collective-permute-done((f32[120,128]{1,0:T(8,128)S(1)}, f32[120,128]{1,0:T(8,128)S(1)}, u32[]{:S(2)}, u32[]{:S(2)}) %collective-permute-start.17) | collective-permute-done | bytes 61472 | tf_op jit(solution)/shard_map/ppermute | solution.py:201
  77.3 1.4 %collective-permute-done.16 = f32[120,128]{1,0:T(8,128)S(1)} collective-permute-done((f32[120,128]{1,0:T(8,128)S(1)}, f32[120,128]{1,0:T(8,128)S(1)}, u32[]{:S(2)}, u32[]{:S(2)}) %collective-permute-start.16) | collective-permute-done | bytes 61472 | tf_op jit(solution)/shard_map/ppermute | solution.py:201
  78.8 2.3 %collective-permute-start.20 = (f32[480,128]{1,0:T(8,128)S(1)}, f32[480,128]{1,0:T(8,128)S(1)}, u32[]{:S(2)}, u32[]{:S(2)}) collective-permute-start(f32[480,128]{1,0:T(8,128)S(1)} %pad_maximum_fusion.9), channel_id=1, source_target_pairs={{0,5},{1,4},{2,26},{3,27},{4,1},{5,0},{6,30},{7,31},{8,13},{9,12},... | collective-permute-start | bytes 737288 | tf_op jit(solution)/shard_map/ppermute | solution.py:201
  81.1 1.7 %collective-permute-start.19 = (f32[480,128]{1,0:T(8,128)S(1)}, f32[480,128]{1,0:T(8,128)S(1)}, u32[]{:S(2)}, u32[]{:S(2)}) collective-permute-start(f32[480,128]{1,0:T(8,128)S(1)} %pad_maximum_fusion.9), channel_id=1, source_target_pairs={{0,4},{1,5},{2,18},{3,19},{4,0},{5,1},{6,22},{7,23},{8,12},{9,13},... | collective-permute-start | bytes 737288 | tf_op jit(solution)/shard_map/ppermute | solution.py:201
  82.8 3.2 %collective-permute-done.20 = f32[480,128]{1,0:T(8,128)S(1)} collective-permute-done((f32[480,128]{1,0:T(8,128)S(1)}, f32[480,128]{1,0:T(8,128)S(1)}, u32[]{:S(2)}, u32[]{:S(2)}) %collective-permute-start.20) | collective-permute-done | bytes 245792 | tf_op jit(solution)/shard_map/ppermute | solution.py:201
  85.9 3.7 %collective-permute-done.19 = f32[480,128]{1,0:T(8,128)S(1)} collective-permute-done((f32[480,128]{1,0:T(8,128)S(1)}, f32[480,128]{1,0:T(8,128)S(1)}, u32[]{:S(2)}, u32[]{:S(2)}) %collective-permute-start.19) | collective-permute-done | bytes 245792 | tf_op jit(solution)/shard_map/ppermute | solution.py:201
  90.1 1.4 %collective-permute-start.21 = (f32[1920,128]{1,0:T(8,128)S(1)}, f32[1920,128]{1,0:T(8,128)S(1)}, u32[]{:S(2)}, u32[]{:S(2)}) collective-permute-start(f32[1920,128]{1,0:T(8,128)S(1)} %pad_maximum_fusion.2), channel_id=1, source_target_pairs={{0,2},{1,3},{2,0},{3,1},{4,6},{5,7},{6,4},{7,5},{8,10},{9,11},{10,... | collective-permute-start | bytes 2949128 | tf_op jit(solution)/shard_map/ppermute | solution.py:210
  91.5 1.1 %fusion.3 = bf16[1,512,256]{2,1,0:T(8,128)(2,1)} fusion(bf16[768,256]{1,0:T(8,128)(2,1)S(1)} %copy-done.12, f32[518,256]{1,0:T(8,128)S(1)} %copy-done.4, bf16[512,256]{1,0:T(8,128)(2,1)S(1)} %copy-done.8, bf16[512,256]{1,0:T(8,128)(2,1)S(1)} %copy-done.10, bf16[512,256]{1,0:T(8,128)(2,1)S(1)} %copy-done.6, f32[256]{0:T(256)S(1)} %copy-done.17), kind=kOutput, calls=%fused_computation.9 | convolution fusion | flops 204079104 | bytes 1967104 | tf_op jit(solution)/shard_map/dot_general | solution.py:92
  96.2 1.1 %slice.175 = f32[2240,128]{1,0:T(8,128)} slice(f32[3840,128]{1,0:T(8,128)S(1)} %broadcast_select_fusion), slice={[0:2240], [0:128]} | slice | bytes 2293760 | tf_op jit(solution)/shard_map/slice | solution.py:214
  (137 shorter events, 22.6 us)
Async XLA Ops:
  0.6 35.1 %copy-start = (bf16[560,512]{1,0:T(8,128)(2,1)S(1)}, bf16[560,512]{1,0:T(8,128)(2,1)}, u32[]{:S(2)}) copy-start(bf16[560,512]{1,0:T(8,128)(2,1)} %param.16) | copy-start | bytes 1720324
  0.6 10.1 %copy-start.18 = (s32[1,8]{1,0:T(1,128)S(1)}, s32[1,8]{1,0:T(1,128)}, u32[]{:S(2)}) copy-start(s32[1,8]{1,0:T(1,128)} %param.13) | copy-start | bytes 100
  0.7 10.1 %copy-start.19 = (s32[1,8]{1,0:T(1,128)S(1)}, s32[1,8]{1,0:T(1,128)}, u32[]{:S(2)}) copy-start(s32[1,8]{1,0:T(1,128)} %param.14) | copy-start | bytes 100
  0.7 10.3 %copy-start.13 = (bf16[1,8,640]{2,1,0:T(8,128)(2,1)S(1)}, bf16[1,8,640]{2,1,0:T(8,128)(2,1)}, u32[]{:S(2)}) copy-start(bf16[1,8,640]{2,1,0:T(8,128)(2,1)} %param.11) | copy-start | bytes 30724
  0.7 10.3 %copy-start.16 = (s32[1,8]{1,0:T(1,128)S(1)}, s32[1,8]{1,0:T(1,128)}, u32[]{:S(2)}) copy-start(s32[1,8]{1,0:T(1,128)} %param.12) | copy-start | bytes 100
  0.7 25.6 %copy-start.2 = (bf16[1,512,256]{2,1,0:T(8,128)(2,1)S(1)}, bf16[1,512,256]{2,1,0:T(8,128)(2,1)}, u32[]{:S(2)}) copy-start(bf16[1,512,256]{2,1,0:T(8,128)(2,1)} %param.15) | copy-start | bytes 786436
  1.7 9.3 %collective-permute-start = (bf16[16,2048]{1,0:T(8,128)(2,1)S(1)}, bf16[16,2048]{1,0:T(8,128)(2,1)S(1)}, u32[]{:S(2)}, u32[]{:S(2)}) collective-permute-start(bf16[16,2048]{1,0:T(8,128)(2,1)S(1)} %slice_select_fusion.2), channel_id=1, source_target_pairs={{0,1},{1,0},{2,3},{3,2},{4,5},{5,4},{6,7},{7,6},{8,9},{9,8},{10,11... | collective-permute-start | bytes 196616 | tf_op jit(solution)/shard_map/ppermute | solution.py:237
  6.7 27.0 %copy-start.11 = (bf16[768,256]{1,0:T(8,128)(2,1)S(1)}, bf16[768,256]{1,0:T(8,128)(2,1)}, u32[]{:S(2)}) copy-start(bf16[768,256]{1,0:T(8,128)(2,1)} %param.20) | copy-start | bytes 1179652
  6.7 28.9 %collective-permute-start.4 = (bf16[112,2048]{1,0:T(8,128)(2,1)}, bf16[112,2048]{1,0:T(8,128)(2,1)}, u32[]{:S(2)}, u32[]{:S(2)}) collective-permute-start(bf16[112,2048]{1,0:T(8,128)(2,1)} %slice_select_fusion.1), channel_id=1, source_target_pairs={{0,1},{1,0},{2,3},{3,2},{4,5},{5,4},{6,7},{7,6},{8,9},{9,8},{10,11... | collective-permute-start | bytes 1376264 | tf_op jit(solution)/shard_map/ppermute | solution.py:237
  8.8 27.2 %collective-permute-start.6 = (bf16[128,2048]{1,0:T(8,128)(2,1)}, bf16[128,2048]{1,0:T(8,128)(2,1)}, u32[]{:S(2)}, u32[]{:S(2)}) collective-permute-start(bf16[128,2048]{1,0:T(8,128)(2,1)} %slice_select_fusion), channel_id=1, source_target_pairs={{0,1},{1,0},{2,3},{3,2},{4,5},{5,4},{6,7},{7,6},{8,9},{9,8},{10,11... | collective-permute-start | bytes 1572872 | tf_op jit(solution)/shard_map/ppermute | solution.py:237
  13.1 12.5 %all-to-all-start = ((bf16[16,2,321]{2,1,0:T(2,128)(2,1)}), bf16[16,2,321]{2,1,0:T(2,128)(2,1)S(1)}, u32[]{:S(2)}, u32[]{:S(2)}) async-start(bf16[16,2,321]{2,1,0:T(2,128)(2,1)} %reshape.119), calls=%async_computation | async-start | bytes 49152 | tf_op jit(solution)/shard_map/all_to_all | solution.py:285
  19.1 17.5 %collective-permute-start.3 = (bf16[16,2048]{1,0:T(8,128)(2,1)S(1)}, bf16[16,2048]{1,0:T(8,128)(2,1)}, u32[]{:S(2)}, u32[]{:S(2)}) collective-permute-start(bf16[16,2048]{1,0:T(8,128)(2,1)S(1)} %collective-permute-done), channel_id=1, source_target_pairs={{0,2},{2,0},{4,6},{6,4},{8,10},{10,8},{12,14},{14,12},{16,18},{18,... | collective-permute-start | bytes 196616 | tf_op jit(solution)/shard_map/ppermute | solution.py:238
  27.3 7.2 %collective-permute-start.2 = (bf16[4,80]{1,0:T(4,128)(2,1)}, bf16[4,80]{1,0:T(4,128)(2,1)S(1)}, u32[]{:S(2)}, u32[]{:S(2)}) collective-permute-start(bf16[4,80]{1,0:T(4,128)(2,1)} %get-tuple-element.54), channel_id=1, source_target_pairs={{1,0},{3,2},{5,4},{7,6},{9,8},{11,10},{13,12},{15,14},{17,16},{19,... | collective-permute-start | bytes 1928 | tf_op jit(solution)/shard_map/ppermute | solution.py:19
  28.6 6.0 %collective-permute-start.1 = (bf16[4,80]{1,0:T(4,128)(2,1)}, bf16[4,80]{1,0:T(4,128)(2,1)}, u32[]{:S(2)}, u32[]{:S(2)}) collective-permute-start(bf16[4,80]{1,0:T(4,128)(2,1)} %get-tuple-element.55), channel_id=1, source_target_pairs={{0,1},{2,3},{4,5},{6,7},{8,9},{10,11},{12,13},{14,15},{16,17},{18,... | collective-permute-start | bytes 1928 | tf_op jit(solution)/shard_map/ppermute | solution.py:16
  35.6 2.1 %collective-permute-start.5 = (bf16[112,2048]{1,0:T(8,128)(2,1)}, bf16[112,2048]{1,0:T(8,128)(2,1)S(1)}, u32[]{:S(2)}, u32[]{:S(2)}) collective-permute-start(bf16[112,2048]{1,0:T(8,128)(2,1)} %collective-permute-done.4), channel_id=1, source_target_pairs={{0,2},{2,0},{4,6},{6,4},{8,10},{10,8},{12,14},{14,12},{16,18},{18,... | collective-permute-start | bytes 1376264 | tf_op jit(solution)/shard_map/ppermute | solution.py:238
  36.0 2.8 %collective-permute-start.7 = (bf16[128,2048]{1,0:T(8,128)(2,1)}, bf16[128,2048]{1,0:T(8,128)(2,1)S(1)}, u32[]{:S(2)}, u32[]{:S(2)}) collective-permute-start(bf16[128,2048]{1,0:T(8,128)(2,1)} %collective-permute-done.6), channel_id=1, source_target_pairs={{0,2},{2,0},{4,6},{6,4},{8,10},{10,8},{12,14},{14,12},{16,18},{18,... | collective-permute-start | bytes 1572872 | tf_op jit(solution)/shard_map/ppermute | solution.py:238
  43.7 1.6 %copy-start.3 = (f32[518,256]{1,0:T(8,128)}, f32[518,256]{1,0:T(8,128)S(1)}, u32[]{:S(2)}) copy-start(f32[518,256]{1,0:T(8,128)S(1)} %get-tuple-element.20) | copy-start | bytes 1591300
  48.4 2.8 %collective-permute-start.8 = (f32[1920,128]{1,0:T(8,128)S(1)}, f32[1920,128]{1,0:T(8,128)}, u32[]{:S(2)}, u32[]{:S(2)}) collective-permute-start(f32[1920,128]{1,0:T(8,128)S(1)} %constant_dynamic-slice_fusion.6), channel_id=1, source_target_pairs={{0,2},{1,3},{2,0},{3,1},{4,6},{5,7},{6,4},{7,5},{8,10},{9,11},{10,... | collective-permute-start | bytes 2949128 | tf_op jit(solution)/shard_map/ppermute | solution.py:188
  52.5 8.8 %collective-permute-start.9 = (f32[480,128]{1,0:T(8,128)S(1)}, f32[480,128]{1,0:T(8,128)S(1)}, u32[]{:S(2)}, u32[]{:S(2)}) collective-permute-start(f32[480,128]{1,0:T(8,128)S(1)} %get-tuple-element.28), channel_id=1, source_target_pairs={{0,1},{1,0},{2,10},{3,11},{4,5},{5,4},{6,14},{7,15},{8,9},{9,8},{1... | collective-permute-start | bytes 737288 | tf_op jit(solution)/shard_map/ppermute | solution.py:196
  55.0 7.1 %collective-permute-start.11 = (f32[480,128]{1,0:T(8,128)S(1)}, f32[480,128]{1,0:T(8,128)S(1)}, u32[]{:S(2)}, u32[]{:S(2)}) collective-permute-start(f32[480,128]{1,0:T(8,128)S(1)} %get-tuple-element.29), channel_id=1, source_target_pairs={{0,5},{1,4},{2,26},{3,27},{4,1},{5,0},{6,30},{7,31},{8,13},{9,12},... | collective-permute-start | bytes 737288 | tf_op jit(solution)/shard_map/ppermute | solution.py:196
  55.0 8.4 %collective-permute-start.10 = (f32[480,128]{1,0:T(8,128)S(1)}, f32[480,128]{1,0:T(8,128)S(1)}, u32[]{:S(2)}, u32[]{:S(2)}) collective-permute-start(f32[480,128]{1,0:T(8,128)S(1)} %get-tuple-element.30), channel_id=1, source_target_pairs={{0,4},{1,5},{2,18},{3,19},{4,0},{5,1},{6,22},{7,23},{8,12},{9,13},... | collective-permute-start | bytes 737288 | tf_op jit(solution)/shard_map/ppermute | solution.py:196
  63.4 4.3 %collective-permute-start.12 = (f32[120,128]{1,0:T(8,128)S(1)}, f32[120,128]{1,0:T(8,128)S(1)}, u32[]{:S(2)}, u32[]{:S(2)}) collective-permute-start(f32[120,128]{1,0:T(8,128)S(1)} %get-tuple-element.42), channel_id=1, source_target_pairs={{0,8},{1,9},{2,3},{3,2},{4,12},{5,13},{6,7},{7,6},{8,0},{9,1},{10,... | collective-permute-start | bytes 184328 | tf_op jit(solution)/shard_map/ppermute | solution.py:196
  63.9 6.0 %collective-permute-start.14 = (f32[120,128]{1,0:T(8,128)S(1)}, f32[120,128]{1,0:T(8,128)S(1)}, u32[]{:S(2)}, u32[]{:S(2)}) collective-permute-start(f32[120,128]{1,0:T(8,128)S(1)} %get-tuple-element.43), channel_id=1, source_target_pairs={{0,24},{1,25},{2,7},{3,6},{4,28},{5,29},{6,3},{7,2},{8,16},{9,17},... | collective-permute-start | bytes 184328 | tf_op jit(solution)/shard_map/ppermute | solution.py:196
  65.4 5.8 %collective-permute-start.13 = (f32[120,128]{1,0:T(8,128)S(1)}, f32[120,128]{1,0:T(8,128)S(1)}, u32[]{:S(2)}, u32[]{:S(2)}) collective-permute-start(f32[120,128]{1,0:T(8,128)S(1)} %get-tuple-element.44), channel_id=1, source_target_pairs={{0,16},{1,17},{2,6},{3,7},{4,20},{5,21},{6,2},{7,3},{8,24},{9,25},... | collective-permute-start | bytes 184328 | tf_op jit(solution)/shard_map/ppermute | solution.py:196
  71.3 6.1 %collective-permute-start.17 = (f32[120,128]{1,0:T(8,128)S(1)}, f32[120,128]{1,0:T(8,128)S(1)}, u32[]{:S(2)}, u32[]{:S(2)}) collective-permute-start(f32[120,128]{1,0:T(8,128)S(1)} %add_add_fusion.1), channel_id=1, source_target_pairs={{0,24},{1,25},{2,7},{3,6},{4,28},{5,29},{6,3},{7,2},{8,16},{9,17},... | collective-permute-start | bytes 184328 | tf_op jit(solution)/shard_map/ppermute | solution.py:201
  73.6 5.1 %collective-permute-start.16 = (f32[120,128]{1,0:T(8,128)S(1)}, f32[120,128]{1,0:T(8,128)S(1)}, u32[]{:S(2)}, u32[]{:S(2)}) collective-permute-start(f32[120,128]{1,0:T(8,128)S(1)} %add_add_fusion.1), channel_id=1, source_target_pairs={{0,16},{1,17},{2,6},{3,7},{4,20},{5,21},{6,2},{7,3},{8,24},{9,25},... | collective-permute-start | bytes 184328 | tf_op jit(solution)/shard_map/ppermute | solution.py:201
  73.6 5.1 %collective-permute-start.15 = (f32[120,128]{1,0:T(8,128)S(1)}, f32[120,128]{1,0:T(8,128)S(1)}, u32[]{:S(2)}, u32[]{:S(2)}) collective-permute-start(f32[120,128]{1,0:T(8,128)S(1)} %add_add_fusion.1), channel_id=1, source_target_pairs={{0,8},{1,9},{2,3},{3,2},{4,12},{5,13},{6,7},{7,6},{8,0},{9,1},{10,... | collective-permute-start | bytes 184328 | tf_op jit(solution)/shard_map/ppermute | solution.py:201
  78.8 7.2 %collective-permute-start.20 = (f32[480,128]{1,0:T(8,128)S(1)}, f32[480,128]{1,0:T(8,128)S(1)}, u32[]{:S(2)}, u32[]{:S(2)}) collective-permute-start(f32[480,128]{1,0:T(8,128)S(1)} %pad_maximum_fusion.9), channel_id=1, source_target_pairs={{0,5},{1,4},{2,26},{3,27},{4,1},{5,0},{6,30},{7,31},{8,13},{9,12},... | collective-permute-start | bytes 737288 | tf_op jit(solution)/shard_map/ppermute | solution.py:201
  81.1 8.5 %collective-permute-start.19 = (f32[480,128]{1,0:T(8,128)S(1)}, f32[480,128]{1,0:T(8,128)S(1)}, u32[]{:S(2)}, u32[]{:S(2)}) collective-permute-start(f32[480,128]{1,0:T(8,128)S(1)} %pad_maximum_fusion.9), channel_id=1, source_target_pairs={{0,4},{1,5},{2,18},{3,19},{4,0},{5,1},{6,22},{7,23},{8,12},{9,13},... | collective-permute-start | bytes 737288 | tf_op jit(solution)/shard_map/ppermute | solution.py:201
  82.8 6.8 %collective-permute-start.18 = (f32[480,128]{1,0:T(8,128)S(1)}, f32[480,128]{1,0:T(8,128)S(1)}, u32[]{:S(2)}, u32[]{:S(2)}) collective-permute-start(f32[480,128]{1,0:T(8,128)S(1)} %pad_maximum_fusion.9), channel_id=1, source_target_pairs={{0,1},{1,0},{2,10},{3,11},{4,5},{5,4},{6,14},{7,15},{8,9},{9,8},{1... | collective-permute-start | bytes 737288 | tf_op jit(solution)/shard_map/ppermute | solution.py:201
  89.8 1.6 %copy-start.4 = (f32[518,256]{1,0:T(8,128)S(1)}, f32[518,256]{1,0:T(8,128)}, u32[]{:S(2)}) copy-start(f32[518,256]{1,0:T(8,128)} %copy-done.3) | copy-start | bytes 1591300
  90.1 3.6 %collective-permute-start.21 = (f32[1920,128]{1,0:T(8,128)S(1)}, f32[1920,128]{1,0:T(8,128)S(1)}, u32[]{:S(2)}, u32[]{:S(2)}) collective-permute-start(f32[1920,128]{1,0:T(8,128)S(1)} %pad_maximum_fusion.2), channel_id=1, source_target_pairs={{0,2},{1,3},{2,0},{3,1},{4,6},{5,7},{6,4},{7,5},{8,10},{9,11},{10,... | collective-permute-start | bytes 2949128 | tf_op jit(solution)/shard_map/ppermute | solution.py:210
  (11 other events, 14.2 us)

commit v13 on v12

--- a/solution.py
+++ b/solution.py
@@ -195,6 +195,7 @@
             send = lax.dynamic_slice_in_dim(x, (slot ^ offset) * piece, piece)
             total = total + lax.ppermute(send, axes, perm_of(step, offset))
         x = total
+    x = x.astype(jnp.bfloat16)
     for step in reversed(range(len(groups))):
         radix = 1 << len(groups[step])
         slot = slot_of(step)
@@ -209,6 +210,7 @@
         x = jnp.concatenate(pieces)
     recv = lax.ppermute(x, axes, core_perm)
     x = jnp.where(core == 0, jnp.concatenate([x, recv]), jnp.concatenate([recv, x]))
+    x = x.astype(jnp.float32)
     out, at = [], 0
     for p, t in zip(parts, tiles):
         out.append(untile_rows(x[at : at + t.shape[0]], p.shape))

time: 97.8 us -> 97.9 us (level)
  starting transfers between devices: 36 us -> 32.6 us
  waiting for transfers between devices: 31.1 us -> 32.9 us
  matrix products: 5.62 us -> 6.64 us
    ppermute x1, waiting for transfers between devices: 0.01 us -> 3.62 us  [with_halo(): lax.ppermute(lax.slice_in_dim(block, 0, width, axis=dim), axis, backward)]
    ppermute x1, starting transfers between devices: 5.13 us -> 2.98 us  [with_halo(): lax.ppermute(lax.slice_in_dim(block, block.shape[dim] - width, None, axis...]
    ppermute x1, starting transfers between devices: 1.41 us -> 0.07 us  [butterfly_psum(): recv = lax.ppermute(x, axes, core_perm)]
    ppermute x6, waiting for transfers between devices: 11.1 us -> 9.76 us  [butterfly_psum(): total = total + lax.ppermute(send, axes, perm_of(step, offset))]
    dot_general x3, matrix products: 0.85 us -> 1.87 us  [contract_rows(): lax.dot_general(left, right, (((0,), (0,)), ((), ())), preferred_element_...]
    unnamed x51 -> x53, local copies, waits for them, and re-layouts: 4.34 us -> 5.15 us
where the time goes in v13:
time: 97.9 us; the launch traced here: 97.4 us
  waiting for transfers between devices  32.9 us (34%)
  starting transfers between devices  32.6 us (33%)
  other arithmetic  13 us (13%)
  local copies, waits for them, and re-layouts  11 us (11%)
  matrix products  6.64 us (7%)
  between operations  1.31 us (1%)
    ppermute x6, waiting for transfers between devices, butterfly_psum(): lax.ppermute(x, axes, perm_of(step, o))  9.86 us
    ppermute x6, waiting for transfers between devices, butterfly_psum(): total = total + lax.ppermute(send, axes, perm_of(step, offset))  9.76 us
    ppermute x6, starting transfers between devices, butterfly_psum(): total = total + lax.ppermute(send, axes, perm_of(step, offset))  8.01 us
    ppermute x6, starting transfers between devices, butterfly_psum(): lax.ppermute(x, axes, perm_of(step, o))  8.01 us
    all_to_all x1, waiting for transfers between devices, on_device(): lax.all_to_all(outgoing, 'dp', split_axis=0, concat_axis=0, tiled=True)  6.07 us
    all_to_all x1, starting transfers between devices, on_device(): lax.all_to_all(outgoing, 'dp', split_axis=0, concat_axis=0, tiled=True)  5.91 us
    unnamed x53, local copies, waits for them, and re-layouts  5.15 us
    select_n x3, other arithmetic, ups_functions(): mine = jnp.where(core == 0, block[:, :cols], block[:, cols:])  5.05 us
  transfers between devices with their start and end apart: 23, of which 15 were waited for; matrix products, arithmetic and copies ran while one was open for 13% of the time, Pallas kernels for 0%

profile of v13, /device:TPU:0, one launch (start us, length us, event | category | flops | bytes accessed | tf_op | source)
XLA Modules:
  0.0 97.4 jit_solution(3340667861469158340)
XLA Ops:
  1.7 3.0 %collective-permute-start = (bf16[16,2048]{1,0:T(8,128)(2,1)S(1)}, bf16[16,2048]{1,0:T(8,128)(2,1)S(1)}, u32[]{:S(2)}, u32[]{:S(2)}) collective-permute-start(bf16[16,2048]{1,0:T(8,128)(2,1)S(1)} %slice_select_fusion.2), channel_id=1, source_target_pairs={{0,1},{1,0},{2,3},{3,2},{4,5},{5,4},{6,7},{7,6},{8,9},{9,8},{10,11... | collective-permute-start | bytes 196616 | tf_op jit(solution)/shard_map/ppermute | solution.py:239
  4.7 2.0 %slice_select_fusion = bf16[128,2048]{1,0:T(8,128)(2,1)} fusion(bf16[256,4096]{1,0:T(8,128)(2,1)} %param.18, pred[]{:T(512)S(6)} %eq.144), kind=kLoop, calls=%fused_computation.38 | loop fusion | flops 262144 | bytes 1572865 | tf_op jit(solution)/shard_map/jit(_where)/select_n | solution.py:238
  6.8 2.0 %slice_select_fusion.1 = bf16[112,2048]{1,0:T(8,128)(2,1)} fusion(bf16[256,4096]{1,0:T(8,128)(2,1)} %param.18, pred[]{:T(512)S(6)} %eq.144), kind=kLoop, calls=%fused_computation.42 | loop fusion | flops 229376 | bytes 1376257 | tf_op jit(solution)/shard_map/jit(_where)/select_n | solution.py:238
  8.8 2.0 %collective-permute-start.4 = (bf16[112,2048]{1,0:T(8,128)(2,1)}, bf16[112,2048]{1,0:T(8,128)(2,1)}, u32[]{:S(2)}, u32[]{:S(2)}) collective-permute-start(bf16[112,2048]{1,0:T(8,128)(2,1)} %slice_select_fusion.1), channel_id=1, source_target_pairs={{0,1},{1,0},{2,3},{3,2},{4,5},{5,4},{6,7},{7,6},{8,9},{9,8},{10,11... | collective-permute-start | bytes 1376264 | tf_op jit(solution)/shard_map/ppermute | solution.py:239
  13.1 5.9 %all-to-all-start = ((bf16[16,2,321]{2,1,0:T(2,128)(2,1)}), bf16[16,2,321]{2,1,0:T(2,128)(2,1)S(1)}, u32[]{:S(2)}, u32[]{:S(2)}) async-start(bf16[16,2,321]{2,1,0:T(2,128)(2,1)} %reshape.119), calls=%async_computation | async-start | bytes 49152 | tf_op jit(solution)/shard_map/all_to_all | solution.py:287
  19.5 6.1 %all-to-all-done = bf16[16,2,321]{2,1,0:T(2,128)(2,1)S(1)} async-done(((bf16[16,2,321]{2,1,0:T(2,128)(2,1)}), bf16[16,2,321]{2,1,0:T(2,128)(2,1)S(1)}, u32[]{:S(2)}, u32[]{:S(2)}) %all-to-all-start) | async-done | bytes 20576 | tf_op jit(solution)/shard_map/all_to_all | solution.py:287
  27.3 3.0 %collective-permute-start.1 = (bf16[4,80]{1,0:T(4,128)(2,1)}, bf16[4,80]{1,0:T(4,128)(2,1)}, u32[]{:S(2)}, u32[]{:S(2)}) collective-permute-start(bf16[4,80]{1,0:T(4,128)(2,1)} %get-tuple-element.55), channel_id=1, source_target_pairs={{0,1},{2,3},{4,5},{6,7},{8,9},{10,11},{12,13},{14,15},{16,17},{18,... | collective-permute-start | bytes 1928 | tf_op jit(solution)/shard_map/ppermute | solution.py:16
  30.3 1.3 %collective-permute-start.2 = (bf16[4,80]{1,0:T(4,128)(2,1)}, bf16[4,80]{1,0:T(4,128)(2,1)S(1)}, u32[]{:S(2)}, u32[]{:S(2)}) collective-permute-start(bf16[4,80]{1,0:T(4,128)(2,1)} %get-tuple-element.54), channel_id=1, source_target_pairs={{1,0},{3,2},{5,4},{7,6},{9,8},{11,10},{13,12},{15,14},{17,16},{19,... | collective-permute-start | bytes 1928 | tf_op jit(solution)/shard_map/ppermute | solution.py:19
  32.3 3.6 %collective-permute-done.2 = bf16[4,80]{1,0:T(4,128)(2,1)S(1)} collective-permute-done((bf16[4,80]{1,0:T(4,128)(2,1)}, bf16[4,80]{1,0:T(4,128)(2,1)S(1)}, u32[]{:S(2)}, u32[]{:S(2)}) %collective-permute-start.2) | collective-permute-done | bytes 672 | tf_op jit(solution)/shard_map/ppermute | solution.py:19
  39.0 1.1 %broadcast_select_fusion.3 = (bf16[112,2048]{1,0:T(8,128)(2,1)S(1)}, bf16[112,2048]{1,0:T(8,128)(2,1)S(1)}) fusion(bf16[112,2048]{1,0:T(8,128)(2,1)} %collective-permute-done.4, bf16[112,2048]{1,0:T(8,128)(2,1)S(1)} %collective-permute-done.5, pred[]{:T(512)S(6)} %eq.144), kind=kLoop, calls=%fused_computation.44 | loop fusion | flops 458752 | bytes 1835009 | tf_op jit(solution)/shard_map/jit(_where)/select_n | solution.py:242
  40.1 1.1 %broadcast_select_fusion.1 = (bf16[128,2048]{1,0:T(8,128)(2,1)S(1)}, bf16[128,2048]{1,0:T(8,128)(2,1)S(1)}) fusion(bf16[128,2048]{1,0:T(8,128)(2,1)} %collective-permute-done.6, bf16[128,2048]{1,0:T(8,128)(2,1)S(1)} %collective-permute-done.7, pred[]{:T(512)S(6)} %eq.144), kind=kLoop, calls=%fused_computation.40 | loop fusion | flops 524288 | bytes 2097153 | tf_op jit(solution)/shard_map/jit(_where)/select_n | solution.py:242
  41.9 1.3 %copy-done.1 = bf16[256,4096]{1,0:T(8,128)(2,1)S(1)} copy-done((bf16[256,4096]{1,0:T(8,128)(2,1)S(1)}, bf16[256,4096]{1,0:T(8,128)(2,1)}, u32[]{:S(2)}) %copy-start.1) | copy-done | bytes 2097176
  47.2 1.3 %fusion.62 = f32[560,512]{1,0:T(8,128)} fusion(bf16[66,560]{1,0:T(8,128)(2,1)S(1)} %concatenate.68, bf16[66,512]{1,0:T(8,128)(2,1)S(1)} %get-tuple-element.18), kind=kOutput, calls=%fused_computation.147 | convolution fusion | flops 37847040 | bytes 1288384 | tf_op jit(solution)/shard_map/dot_general | solution.py:33
  51.7 2.6 %collective-permute-done.8 = f32[1920,128]{1,0:T(8,128)} collective-permute-done((f32[1920,128]{1,0:T(8,128)S(1)}, f32[1920,128]{1,0:T(8,128)}, u32[]{:S(2)}, u32[]{:S(2)}) %collective-permute-start.8) | collective-permute-done | bytes 983072 | tf_op jit(solution)/shard_map/ppermute | solution.py:188
  54.3 1.3 %dynamic-slice_add_fusion = f32[1920,128]{1,0:T(8,128)S(1)} fusion(f32[1920,128]{1,0:T(8,128)} %collective-permute-done.8, f32[3840,128]{1,0:T(8,128)S(1)} %fusion, s32[]{:T(128)S(6)} %select_n.405), kind=kLoop, calls=%fused_computation.22 | loop fusion | flops 245760 | bytes 2949124 | tf_op jit(solution)/shard_map/add | solution.py:188
  57.0 2.3 %collective-permute-start.9 = (f32[480,128]{1,0:T(8,128)S(1)}, f32[480,128]{1,0:T(8,128)S(1)}, u32[]{:S(2)}, u32[]{:S(2)}) collective-permute-start(f32[480,128]{1,0:T(8,128)S(1)} %get-tuple-element.26), channel_id=1, source_target_pairs={{0,1},{1,0},{2,10},{3,11},{4,5},{5,4},{6,14},{7,15},{8,9},{9,8},{1... | collective-permute-start | bytes 737288 | tf_op jit(solution)/shard_map/ppermute | solution.py:196
  59.2 2.7 %collective-permute-done.10 = f32[480,128]{1,0:T(8,128)S(1)} collective-permute-done((f32[480,128]{1,0:T(8,128)S(1)}, f32[480,128]{1,0:T(8,128)S(1)}, u32[]{:S(2)}, u32[]{:S(2)}) %collective-permute-start.10) | collective-permute-done | bytes 245792 | tf_op jit(solution)/shard_map/ppermute | solution.py:196
  61.9 1.9 %collective-permute-done.11 = f32[480,128]{1,0:T(8,128)S(1)} collective-permute-done((f32[480,128]{1,0:T(8,128)S(1)}, f32[480,128]{1,0:T(8,128)S(1)}, u32[]{:S(2)}, u32[]{:S(2)}) %collective-permute-start.11) | collective-permute-done | bytes 245792 | tf_op jit(solution)/shard_map/ppermute | solution.py:196
  63.9 2.2 %collective-permute-done.9 = f32[480,128]{1,0:T(8,128)S(1)} collective-permute-done((f32[480,128]{1,0:T(8,128)S(1)}, f32[480,128]{1,0:T(8,128)S(1)}, u32[]{:S(2)}, u32[]{:S(2)}) %collective-permute-start.9) | collective-permute-done | bytes 245792 | tf_op jit(solution)/shard_map/ppermute | solution.py:196
  67.2 3.3 %collective-permute-start.14 = (f32[120,128]{1,0:T(8,128)S(1)}, f32[120,128]{1,0:T(8,128)S(1)}, u32[]{:S(2)}, u32[]{:S(2)}) collective-permute-start(f32[120,128]{1,0:T(8,128)S(1)} %get-tuple-element.39), channel_id=1, source_target_pairs={{0,24},{1,25},{2,7},{3,6},{4,28},{5,29},{6,3},{7,2},{8,16},{9,17},... | collective-permute-start | bytes 184328 | tf_op jit(solution)/shard_map/ppermute | solution.py:196
  70.6 1.1 %collective-permute-done.13 = f32[120,128]{1,0:T(8,128)S(1)} collective-permute-done((f32[120,128]{1,0:T(8,128)S(1)}, f32[120,128]{1,0:T(8,128)S(1)}, u32[]{:S(2)}, u32[]{:S(2)}) %collective-permute-start.13) | collective-permute-done | bytes 61472 | tf_op jit(solution)/shard_map/ppermute | solution.py:196
  71.7 1.8 %collective-permute-done.14 = f32[120,128]{1,0:T(8,128)S(1)} collective-permute-done((f32[120,128]{1,0:T(8,128)S(1)}, f32[120,128]{1,0:T(8,128)S(1)}, u32[]{:S(2)}, u32[]{:S(2)}) %collective-permute-start.14) | collective-permute-done | bytes 61472 | tf_op jit(solution)/shard_map/ppermute | solution.py:196
  74.3 2.9 %collective-permute-start.16 = (bf16[120,128]{1,0:T(8,128)(2,1)S(1)}, bf16[120,128]{1,0:T(8,128)(2,1)S(1)}, u32[]{:S(2)}, u32[]{:S(2)}) collective-permute-start(bf16[120,128]{1,0:T(8,128)(2,1)S(1)} %add_convert_fusion), channel_id=1, source_target_pairs={{0,16},{1,17},{2,6},{3,7},{4,20},{5,21},{6,2},{7,3},{8,24},{9,25},... | collective-permute-start | bytes 92168 | tf_op jit(solution)/shard_map/ppermute | solution.py:202
  78.0 1.1 %collective-permute-done.16 = bf16[120,128]{1,0:T(8,128)(2,1)S(1)} collective-permute-done((bf16[120,128]{1,0:T(8,128)(2,1)S(1)}, bf16[120,128]{1,0:T(8,128)(2,1)S(1)}, u32[]{:S(2)}, u32[]{:S(2)}) %collective-permute-start.16) | collective-permute-done | bytes 30752 | tf_op jit(solution)/shard_map/ppermute | solution.py:202
  79.1 4.1 %collective-permute-done.17 = bf16[120,128]{1,0:T(8,128)(2,1)S(1)} collective-permute-done((bf16[120,128]{1,0:T(8,128)(2,1)S(1)}, bf16[120,128]{1,0:T(8,128)(2,1)S(1)}, u32[]{:S(2)}, u32[]{:S(2)}) %collective-permute-start.17) | collective-permute-done | bytes 30752 | tf_op jit(solution)/shard_map/ppermute | solution.py:202
  83.3 2.0 %collective-permute-start.18 = (bf16[480,128]{1,0:T(8,128)(2,1)S(1)}, bf16[480,128]{1,0:T(8,128)(2,1)S(1)}, u32[]{:S(2)}, u32[]{:S(2)}) collective-permute-start(bf16[480,128]{1,0:T(8,128)(2,1)S(1)} %pad_maximum_fusion.9), channel_id=1, source_target_pairs={{0,1},{1,0},{2,10},{3,11},{4,5},{5,4},{6,14},{7,15},{8,9},{9,8},{1... | collective-permute-start | bytes 368648 | tf_op jit(solution)/shard_map/ppermute | solution.py:202
  85.7 1.1 %collective-permute-start.20 = (bf16[480,128]{1,0:T(8,128)(2,1)S(1)}, bf16[480,128]{1,0:T(8,128)(2,1)S(1)}, u32[]{:S(2)}, u32[]{:S(2)}) collective-permute-start(bf16[480,128]{1,0:T(8,128)(2,1)S(1)} %pad_maximum_fusion.9), channel_id=1, source_target_pairs={{0,5},{1,4},{2,26},{3,27},{4,1},{5,0},{6,30},{7,31},{8,13},{9,12},... | collective-permute-start | bytes 368648 | tf_op jit(solution)/shard_map/ppermute | solution.py:202
  86.9 1.4 %collective-permute-done.18 = bf16[480,128]{1,0:T(8,128)(2,1)S(1)} collective-permute-done((bf16[480,128]{1,0:T(8,128)(2,1)S(1)}, bf16[480,128]{1,0:T(8,128)(2,1)S(1)}, u32[]{:S(2)}, u32[]{:S(2)}) %collective-permute-start.18) | collective-permute-done | bytes 122912 | tf_op jit(solution)/shard_map/ppermute | solution.py:202
  88.3 1.9 %collective-permute-done.19 = bf16[480,128]{1,0:T(8,128)(2,1)S(1)} collective-permute-done((bf16[480,128]{1,0:T(8,128)(2,1)S(1)}, bf16[480,128]{1,0:T(8,128)(2,1)S(1)}, u32[]{:S(2)}, u32[]{:S(2)}) %collective-permute-start.19) | collective-permute-done | bytes 122912 | tf_op jit(solution)/shard_map/ppermute | solution.py:202
  90.2 1.3 %collective-permute-done.20 = bf16[480,128]{1,0:T(8,128)(2,1)S(1)} collective-permute-done((bf16[480,128]{1,0:T(8,128)(2,1)S(1)}, bf16[480,128]{1,0:T(8,128)(2,1)S(1)}, u32[]{:S(2)}, u32[]{:S(2)}) %collective-permute-start.20) | collective-permute-done | bytes 122912 | tf_op jit(solution)/shard_map/ppermute | solution.py:202
  92.1 1.1 %fusion.3 = bf16[1,512,256]{2,1,0:T(8,128)(2,1)} fusion(bf16[768,256]{1,0:T(8,128)(2,1)S(1)} %copy-done.13, f32[518,256]{1,0:T(8,128)S(1)} %copy-done.5, bf16[512,256]{1,0:T(8,128)(2,1)S(1)} %copy-done.9, bf16[512,256]{1,0:T(8,128)(2,1)S(1)} %copy-done.11, bf16[512,256]{1,0:T(8,128)(2,1)S(1)} %copy-done.7, f32[256]{0:T(256)S(1)} %copy-done.18), kind=kOutput, calls=%fused_computation.9 | convolution fusion | flops 204079104 | bytes 1967104 | tf_op jit(solution)/shard_map/dot_general | solution.py:92
  94.2 1.1 %slice.175 = f32[2240,128]{1,0:T(8,128)} slice(f32[3840,128]{1,0:T(8,128)S(1)} %select_convert_fusion), slice={[0:2240], [0:128]} | slice | bytes 2293760 | tf_op jit(solution)/shard_map/slice | solution.py:216
  (139 shorter events, 25.1 us)
Async XLA Ops:
  0.6 36.4 %copy-start = (bf16[560,512]{1,0:T(8,128)(2,1)S(1)}, bf16[560,512]{1,0:T(8,128)(2,1)}, u32[]{:S(2)}) copy-start(bf16[560,512]{1,0:T(8,128)(2,1)} %param.16) | copy-start | bytes 1720324
  0.6 10.1 %copy-start.19 = (s32[1,8]{1,0:T(1,128)S(1)}, s32[1,8]{1,0:T(1,128)}, u32[]{:S(2)}) copy-start(s32[1,8]{1,0:T(1,128)} %param.13) | copy-start | bytes 100
  0.7 10.2 %copy-start.20 = (s32[1,8]{1,0:T(1,128)S(1)}, s32[1,8]{1,0:T(1,128)}, u32[]{:S(2)}) copy-start(s32[1,8]{1,0:T(1,128)} %param.14) | copy-start | bytes 100
  0.7 10.3 %copy-start.14 = (bf16[1,8,640]{2,1,0:T(8,128)(2,1)S(1)}, bf16[1,8,640]{2,1,0:T(8,128)(2,1)}, u32[]{:S(2)}) copy-start(bf16[1,8,640]{2,1,0:T(8,128)(2,1)} %param.11) | copy-start | bytes 30724
  0.7 10.3 %copy-start.17 = (s32[1,8]{1,0:T(1,128)S(1)}, s32[1,8]{1,0:T(1,128)}, u32[]{:S(2)}) copy-start(s32[1,8]{1,0:T(1,128)} %param.12) | copy-start | bytes 100
  0.7 25.6 %copy-start.3 = (bf16[1,512,256]{2,1,0:T(8,128)(2,1)S(1)}, bf16[1,512,256]{2,1,0:T(8,128)(2,1)}, u32[]{:S(2)}) copy-start(bf16[1,512,256]{2,1,0:T(8,128)(2,1)} %param.15) | copy-start | bytes 786436
  1.7 9.3 %collective-permute-start = (bf16[16,2048]{1,0:T(8,128)(2,1)S(1)}, bf16[16,2048]{1,0:T(8,128)(2,1)S(1)}, u32[]{:S(2)}, u32[]{:S(2)}) collective-permute-start(bf16[16,2048]{1,0:T(8,128)(2,1)S(1)} %slice_select_fusion.2), channel_id=1, source_target_pairs={{0,1},{1,0},{2,3},{3,2},{4,5},{5,4},{6,7},{7,6},{8,9},{9,8},{10,11... | collective-permute-start | bytes 196616 | tf_op jit(solution)/shard_map/ppermute | solution.py:239
  6.8 24.8 %copy-start.12 = (bf16[768,256]{1,0:T(8,128)(2,1)S(1)}, bf16[768,256]{1,0:T(8,128)(2,1)}, u32[]{:S(2)}) copy-start(bf16[768,256]{1,0:T(8,128)(2,1)} %param.20) | copy-start | bytes 1179652
  6.8 30.5 %collective-permute-start.6 = (bf16[128,2048]{1,0:T(8,128)(2,1)}, bf16[128,2048]{1,0:T(8,128)(2,1)}, u32[]{:S(2)}, u32[]{:S(2)}) collective-permute-start(bf16[128,2048]{1,0:T(8,128)(2,1)} %slice_select_fusion), channel_id=1, source_target_pairs={{0,1},{1,0},{2,3},{3,2},{4,5},{5,4},{6,7},{7,6},{8,9},{9,8},{10,11... | collective-permute-start | bytes 1572872 | tf_op jit(solution)/shard_map/ppermute | solution.py:239
  8.8 28.1 %collective-permute-start.4 = (bf16[112,2048]{1,0:T(8,128)(2,1)}, bf16[112,2048]{1,0:T(8,128)(2,1)}, u32[]{:S(2)}, u32[]{:S(2)}) collective-permute-start(bf16[112,2048]{1,0:T(8,128)(2,1)} %slice_select_fusion.1), channel_id=1, source_target_pairs={{0,1},{1,0},{2,3},{3,2},{4,5},{5,4},{6,7},{7,6},{8,9},{9,8},{10,11... | collective-permute-start | bytes 1376264 | tf_op jit(solution)/shard_map/ppermute | solution.py:239
  13.1 12.5 %all-to-all-start = ((bf16[16,2,321]{2,1,0:T(2,128)(2,1)}), bf16[16,2,321]{2,1,0:T(2,128)(2,1)S(1)}, u32[]{:S(2)}, u32[]{:S(2)}) async-start(bf16[16,2,321]{2,1,0:T(2,128)(2,1)} %reshape.119), calls=%async_computation | async-start | bytes 49152 | tf_op jit(solution)/shard_map/all_to_all | solution.py:287
  19.1 18.8 %collective-permute-start.3 = (bf16[16,2048]{1,0:T(8,128)(2,1)S(1)}, bf16[16,2048]{1,0:T(8,128)(2,1)}, u32[]{:S(2)}, u32[]{:S(2)}) collective-permute-start(bf16[16,2048]{1,0:T(8,128)(2,1)S(1)} %collective-permute-done), channel_id=1, source_target_pairs={{0,2},{2,0},{4,6},{6,4},{8,10},{10,8},{12,14},{14,12},{16,18},{18,... | collective-permute-start | bytes 196616 | tf_op jit(solution)/shard_map/ppermute | solution.py:240
  27.3 5.0 %collective-permute-start.1 = (bf16[4,80]{1,0:T(4,128)(2,1)}, bf16[4,80]{1,0:T(4,128)(2,1)}, u32[]{:S(2)}, u32[]{:S(2)}) collective-permute-start(bf16[4,80]{1,0:T(4,128)(2,1)} %get-tuple-element.55), channel_id=1, source_target_pairs={{0,1},{2,3},{4,5},{6,7},{8,9},{10,11},{12,13},{14,15},{16,17},{18,... | collective-permute-start | bytes 1928 | tf_op jit(solution)/shard_map/ppermute | solution.py:16
  30.3 5.7 %collective-permute-start.2 = (bf16[4,80]{1,0:T(4,128)(2,1)}, bf16[4,80]{1,0:T(4,128)(2,1)S(1)}, u32[]{:S(2)}, u32[]{:S(2)}) collective-permute-start(bf16[4,80]{1,0:T(4,128)(2,1)} %get-tuple-element.54), channel_id=1, source_target_pairs={{1,0},{3,2},{5,4},{7,6},{9,8},{11,10},{13,12},{15,14},{17,16},{19,... | collective-permute-start | bytes 1928 | tf_op jit(solution)/shard_map/ppermute | solution.py:19
  36.9 2.1 %collective-permute-start.5 = (bf16[112,2048]{1,0:T(8,128)(2,1)}, bf16[112,2048]{1,0:T(8,128)(2,1)S(1)}, u32[]{:S(2)}, u32[]{:S(2)}) collective-permute-start(bf16[112,2048]{1,0:T(8,128)(2,1)} %collective-permute-done.4), channel_id=1, source_target_pairs={{0,2},{2,0},{4,6},{6,4},{8,10},{10,8},{12,14},{14,12},{16,18},{18,... | collective-permute-start | bytes 1376264 | tf_op jit(solution)/shard_map/ppermute | solution.py:240
  37.3 2.8 %collective-permute-start.7 = (bf16[128,2048]{1,0:T(8,128)(2,1)}, bf16[128,2048]{1,0:T(8,128)(2,1)S(1)}, u32[]{:S(2)}, u32[]{:S(2)}) collective-permute-start(bf16[128,2048]{1,0:T(8,128)(2,1)} %collective-permute-done.6), channel_id=1, source_target_pairs={{0,2},{2,0},{4,6},{6,4},{8,10},{10,8},{12,14},{14,12},{16,18},{18,... | collective-permute-start | bytes 1572872 | tf_op jit(solution)/shard_map/ppermute | solution.py:240
  51.5 2.8 %collective-permute-start.8 = (f32[1920,128]{1,0:T(8,128)S(1)}, f32[1920,128]{1,0:T(8,128)}, u32[]{:S(2)}, u32[]{:S(2)}) collective-permute-start(f32[1920,128]{1,0:T(8,128)S(1)} %constant_dynamic-slice_fusion.6), channel_id=1, source_target_pairs={{0,2},{1,3},{2,0},{3,1},{4,6},{5,7},{6,4},{7,5},{8,10},{9,11},{10,... | collective-permute-start | bytes 2949128 | tf_op jit(solution)/shard_map/ppermute | solution.py:188
  55.7 6.3 %collective-permute-start.10 = (f32[480,128]{1,0:T(8,128)S(1)}, f32[480,128]{1,0:T(8,128)S(1)}, u32[]{:S(2)}, u32[]{:S(2)}) collective-permute-start(f32[480,128]{1,0:T(8,128)S(1)} %get-tuple-element.28), channel_id=1, source_target_pairs={{0,4},{1,5},{2,18},{3,19},{4,0},{5,1},{6,22},{7,23},{8,12},{9,13},... | collective-permute-start | bytes 737288 | tf_op jit(solution)/shard_map/ppermute | solution.py:196
  56.1 7.7 %collective-permute-start.11 = (f32[480,128]{1,0:T(8,128)S(1)}, f32[480,128]{1,0:T(8,128)S(1)}, u32[]{:S(2)}, u32[]{:S(2)}) collective-permute-start(f32[480,128]{1,0:T(8,128)S(1)} %get-tuple-element.27), channel_id=1, source_target_pairs={{0,5},{1,4},{2,26},{3,27},{4,1},{5,0},{6,30},{7,31},{8,13},{9,12},... | collective-permute-start | bytes 737288 | tf_op jit(solution)/shard_map/ppermute | solution.py:196
  57.0 9.1 %collective-permute-start.9 = (f32[480,128]{1,0:T(8,128)S(1)}, f32[480,128]{1,0:T(8,128)S(1)}, u32[]{:S(2)}, u32[]{:S(2)}) collective-permute-start(f32[480,128]{1,0:T(8,128)S(1)} %get-tuple-element.26), channel_id=1, source_target_pairs={{0,1},{1,0},{2,10},{3,11},{4,5},{5,4},{6,14},{7,15},{8,9},{9,8},{1... | collective-permute-start | bytes 737288 | tf_op jit(solution)/shard_map/ppermute | solution.py:196
  66.1 4.5 %collective-permute-start.12 = (f32[120,128]{1,0:T(8,128)S(1)}, f32[120,128]{1,0:T(8,128)S(1)}, u32[]{:S(2)}, u32[]{:S(2)}) collective-permute-start(f32[120,128]{1,0:T(8,128)S(1)} %get-tuple-element.38), channel_id=1, source_target_pairs={{0,8},{1,9},{2,3},{3,2},{4,12},{5,13},{6,7},{7,6},{8,0},{9,1},{10,... | collective-permute-start | bytes 184328 | tf_op jit(solution)/shard_map/ppermute | solution.py:196
  66.6 5.1 %collective-permute-start.13 = (f32[120,128]{1,0:T(8,128)S(1)}, f32[120,128]{1,0:T(8,128)S(1)}, u32[]{:S(2)}, u32[]{:S(2)}) collective-permute-start(f32[120,128]{1,0:T(8,128)S(1)} %get-tuple-element.40), channel_id=1, source_target_pairs={{0,16},{1,17},{2,6},{3,7},{4,20},{5,21},{6,2},{7,3},{8,24},{9,25},... | collective-permute-start | bytes 184328 | tf_op jit(solution)/shard_map/ppermute | solution.py:196
  67.2 6.3 %collective-permute-start.14 = (f32[120,128]{1,0:T(8,128)S(1)}, f32[120,128]{1,0:T(8,128)S(1)}, u32[]{:S(2)}, u32[]{:S(2)}) collective-permute-start(f32[120,128]{1,0:T(8,128)S(1)} %get-tuple-element.39), channel_id=1, source_target_pairs={{0,24},{1,25},{2,7},{3,6},{4,28},{5,29},{6,3},{7,2},{8,16},{9,17},... | collective-permute-start | bytes 184328 | tf_op jit(solution)/shard_map/ppermute | solution.py:196
  73.6 4.5 %collective-permute-start.15 = (bf16[120,128]{1,0:T(8,128)(2,1)S(1)}, bf16[120,128]{1,0:T(8,128)(2,1)S(1)}, u32[]{:S(2)}, u32[]{:S(2)}) collective-permute-start(bf16[120,128]{1,0:T(8,128)(2,1)S(1)} %add_convert_fusion), channel_id=1, source_target_pairs={{0,8},{1,9},{2,3},{3,2},{4,12},{5,13},{6,7},{7,6},{8,0},{9,1},{10,... | collective-permute-start | bytes 92168 | tf_op jit(solution)/shard_map/ppermute | solution.py:202
  74.3 4.8 %collective-permute-start.16 = (bf16[120,128]{1,0:T(8,128)(2,1)S(1)}, bf16[120,128]{1,0:T(8,128)(2,1)S(1)}, u32[]{:S(2)}, u32[]{:S(2)}) collective-permute-start(bf16[120,128]{1,0:T(8,128)(2,1)S(1)} %add_convert_fusion), channel_id=1, source_target_pairs={{0,16},{1,17},{2,6},{3,7},{4,20},{5,21},{6,2},{7,3},{8,24},{9,25},... | collective-permute-start | bytes 92168 | tf_op jit(solution)/shard_map/ppermute | solution.py:202
  77.2 6.0 %collective-permute-start.17 = (bf16[120,128]{1,0:T(8,128)(2,1)S(1)}, bf16[120,128]{1,0:T(8,128)(2,1)S(1)}, u32[]{:S(2)}, u32[]{:S(2)}) collective-permute-start(bf16[120,128]{1,0:T(8,128)(2,1)S(1)} %add_convert_fusion), channel_id=1, source_target_pairs={{0,24},{1,25},{2,7},{3,6},{4,28},{5,29},{6,3},{7,2},{8,16},{9,17},... | collective-permute-start | bytes 92168 | tf_op jit(solution)/shard_map/ppermute | solution.py:202
  83.3 4.9 %collective-permute-start.18 = (bf16[480,128]{1,0:T(8,128)(2,1)S(1)}, bf16[480,128]{1,0:T(8,128)(2,1)S(1)}, u32[]{:S(2)}, u32[]{:S(2)}) collective-permute-start(bf16[480,128]{1,0:T(8,128)(2,1)S(1)} %pad_maximum_fusion.9), channel_id=1, source_target_pairs={{0,1},{1,0},{2,10},{3,11},{4,5},{5,4},{6,14},{7,15},{8,9},{9,8},{1... | collective-permute-start | bytes 368648 | tf_op jit(solution)/shard_map/ppermute | solution.py:202
  85.3 4.9 %collective-permute-start.19 = (bf16[480,128]{1,0:T(8,128)(2,1)S(1)}, bf16[480,128]{1,0:T(8,128)(2,1)S(1)}, u32[]{:S(2)}, u32[]{:S(2)}) collective-permute-start(bf16[480,128]{1,0:T(8,128)(2,1)S(1)} %pad_maximum_fusion.9), channel_id=1, source_target_pairs={{0,4},{1,5},{2,18},{3,19},{4,0},{5,1},{6,22},{7,23},{8,12},{9,13},... | collective-permute-start | bytes 368648 | tf_op jit(solution)/shard_map/ppermute | solution.py:202
  85.7 5.8 %collective-permute-start.20 = (bf16[480,128]{1,0:T(8,128)(2,1)S(1)}, bf16[480,128]{1,0:T(8,128)(2,1)S(1)}, u32[]{:S(2)}, u32[]{:S(2)}) collective-permute-start(bf16[480,128]{1,0:T(8,128)(2,1)S(1)} %pad_maximum_fusion.9), channel_id=1, source_target_pairs={{0,5},{1,4},{2,26},{3,27},{4,1},{5,0},{6,30},{7,31},{8,13},{9,12},... | collective-permute-start | bytes 368648 | tf_op jit(solution)/shard_map/ppermute | solution.py:202
  86.9 5.2 %copy-start.13 = (bf16[768,256]{1,0:T(8,128)(2,1)S(1)}, bf16[768,256]{1,0:T(8,128)(2,1)}, u32[]{:S(2)}) copy-start(bf16[768,256]{1,0:T(8,128)(2,1)} %param.20) | copy-start | bytes 1179652
  86.9 5.2 %copy-start.18 = (f32[256]{0:T(256)S(1)}, f32[256]{0:T(256)}, u32[]{:S(2)}) copy-start(f32[256]{0:T(256)} %param.21) | copy-start | bytes 3076
  91.9 1.9 %collective-permute-start.21 = (bf16[1920,128]{1,0:T(8,128)(2,1)S(1)}, bf16[1920,128]{1,0:T(8,128)(2,1)S(1)}, u32[]{:S(2)}, u32[]{:S(2)}) collective-permute-start(bf16[1920,128]{1,0:T(8,128)(2,1)S(1)} %pad_maximum_fusion.3), channel_id=1, source_target_pairs={{0,2},{1,3},{2,0},{3,1},{4,6},{5,7},{6,4},{7,5},{8,10},{9,11},{10,... | collective-permute-start | bytes 1474568 | tf_op jit(solution)/shard_map/ppermute | solution.py:211
  (12 other events, 35.1 us)

commit v14 on v12

--- a/solution.py
+++ b/solution.py
@@ -154,7 +154,7 @@
     levels = [("tm", 1 << k) for k in range(tm_size.bit_length() - 1)]
     levels += [("dp", 1 << k) for k in range(1, dp_size.bit_length() - 1)]
     groups = [levels[i : i + 2] for i in range(0, len(levels), 2)]
-    orders = (groups, groups[::-1])
+    orders = (groups, groups)
     count = dp_size * tm_size
 
     def perm_of(step, offset):

time: 97.8 us -> 103 us (1.053)
  waiting for transfers between devices: 31.1 us -> 37.4 us
  starting transfers between devices: 36 us -> 34.2 us
  local copies, waits for them, and re-layouts: 10.2 us -> 11.3 us
    ppermute x6, waiting for transfers between devices: 11.1 us -> 16.7 us  [butterfly_psum(): total = total + lax.ppermute(send, axes, perm_of(step, offset))]
    ppermute x6, waiting for transfers between devices: 9.85 us -> 11.3 us  [butterfly_psum(): lax.ppermute(x, axes, perm_of(step, o))]
    ppermute x1, starting transfers between devices: 1.41 us -> 0.07 us  [butterfly_psum(): recv = lax.ppermute(x, axes, core_perm)]
    unnamed x51, local copies, waits for them, and re-layouts: 4.34 us -> 5.44 us
  transfers between devices with their start and end apart: 23 -> 23, of which waited for: 15 -> 14; matrix products, arithmetic and copies ran while one was open for 13% -> 13% of each run, Pallas kernels for 0% -> 0%
where the time goes in v14:
time: 103 us
  waiting for transfers between devices  37.4 us (36%)
  starting transfers between devices  34.2 us (33%)
  other arithmetic  13 us (13%)
  local copies, waits for them, and re-layouts  11.3 us (11%)
  matrix products  5.62 us (5%)
  between operations  1.29 us (1%)
    ppermute x6, waiting for transfers between devices, butterfly_psum(): total = total + lax.ppermute(send, axes, perm_of(step, offset))  16.7 us
    ppermute x6, waiting for transfers between devices, butterfly_psum(): lax.ppermute(x, axes, perm_of(step, o))  11.3 us
    ppermute x6, starting transfers between devices, butterfly_psum(): lax.ppermute(x, axes, perm_of(step, o))  8.01 us
    ppermute x6, starting transfers between devices, butterfly_psum(): total = total + lax.ppermute(send, axes, perm_of(step, offset))  7.54 us
    all_to_all x1, waiting for transfers between devices, on_device(): lax.all_to_all(outgoing, 'dp', split_axis=0, concat_axis=0, tiled=True)  6.07 us
    all_to_all x1, starting transfers between devices, on_device(): lax.all_to_all(outgoing, 'dp', split_axis=0, concat_axis=0, tiled=True)  5.91 us
    unnamed x51, local copies, waits for them, and re-layouts  5.44 us
    ppermute x1, starting transfers between devices, with_halo(): lax.ppermute(lax.slice_in_dim(block, block.shape[dim] - width, None, axis...  5.13 us
  transfers between devices with their start and end apart: 23, of which 14 were waited for; matrix products, arithmetic and copies ran while one was open for 13% of the time, Pallas kernels for 0%

profile of v14, /device:TPU:0, one launch (start us, length us, event | category | flops | bytes accessed | tf_op | source)
XLA Modules:
  0.0 102.8 jit_solution(13127153412250404032)
XLA Ops:
  1.7 3.0 %collective-permute-start = (bf16[16,2048]{1,0:T(8,128)(2,1)S(1)}, bf16[16,2048]{1,0:T(8,128)(2,1)S(1)}, u32[]{:S(2)}, u32[]{:S(2)}) collective-permute-start(bf16[16,2048]{1,0:T(8,128)(2,1)S(1)} %slice_select_fusion.2), channel_id=1, source_target_pairs={{0,1},{1,0},{2,3},{3,2},{4,5},{5,4},{6,7},{7,6},{8,9},{9,8},{10,11... | collective-permute-start | bytes 196616 | tf_op jit(solution)/shard_map/ppermute | solution.py:237
  4.7 2.0 %slice_select_fusion.1 = bf16[112,2048]{1,0:T(8,128)(2,1)} fusion(bf16[256,4096]{1,0:T(8,128)(2,1)} %param.18, pred[]{:T(512)S(6)} %eq.144), kind=kLoop, calls=%fused_computation.42 | loop fusion | flops 229376 | bytes 1376257 | tf_op jit(solution)/shard_map/jit(_where)/select_n | solution.py:236
  6.7 2.1 %slice_select_fusion = bf16[128,2048]{1,0:T(8,128)(2,1)} fusion(bf16[256,4096]{1,0:T(8,128)(2,1)} %param.18, pred[]{:T(512)S(6)} %eq.144), kind=kLoop, calls=%fused_computation.39 | loop fusion | flops 262144 | bytes 1572865 | tf_op jit(solution)/shard_map/jit(_where)/select_n | solution.py:236
  8.8 2.0 %collective-permute-start.6 = (bf16[128,2048]{1,0:T(8,128)(2,1)}, bf16[128,2048]{1,0:T(8,128)(2,1)}, u32[]{:S(2)}, u32[]{:S(2)}) collective-permute-start(bf16[128,2048]{1,0:T(8,128)(2,1)} %slice_select_fusion), channel_id=1, source_target_pairs={{0,1},{1,0},{2,3},{3,2},{4,5},{5,4},{6,7},{7,6},{8,9},{9,8},{10,11... | collective-permute-start | bytes 1572872 | tf_op jit(solution)/shard_map/ppermute | solution.py:237
  13.1 5.9 %all-to-all-start = ((bf16[16,2,321]{2,1,0:T(2,128)(2,1)}), bf16[16,2,321]{2,1,0:T(2,128)(2,1)S(1)}, u32[]{:S(2)}, u32[]{:S(2)}) async-start(bf16[16,2,321]{2,1,0:T(2,128)(2,1)} %reshape.119), calls=%async_computation | async-start | bytes 49152 | tf_op jit(solution)/shard_map/all_to_all | solution.py:285
  19.5 6.1 %all-to-all-done = bf16[16,2,321]{2,1,0:T(2,128)(2,1)S(1)} async-done(((bf16[16,2,321]{2,1,0:T(2,128)(2,1)}), bf16[16,2,321]{2,1,0:T(2,128)(2,1)S(1)}, u32[]{:S(2)}, u32[]{:S(2)}) %all-to-all-start) | async-done | bytes 20576 | tf_op jit(solution)/shard_map/all_to_all | solution.py:285
  27.3 1.3 %collective-permute-start.2 = (bf16[4,80]{1,0:T(4,128)(2,1)}, bf16[4,80]{1,0:T(4,128)(2,1)S(1)}, u32[]{:S(2)}, u32[]{:S(2)}) collective-permute-start(bf16[4,80]{1,0:T(4,128)(2,1)} %get-tuple-element.54), channel_id=1, source_target_pairs={{1,0},{3,2},{5,4},{7,6},{9,8},{11,10},{13,12},{15,14},{17,16},{19,... | collective-permute-start | bytes 1928 | tf_op jit(solution)/shard_map/ppermute | solution.py:19
  28.6 5.1 %collective-permute-start.1 = (bf16[4,80]{1,0:T(4,128)(2,1)}, bf16[4,80]{1,0:T(4,128)(2,1)}, u32[]{:S(2)}, u32[]{:S(2)}) collective-permute-start(bf16[4,80]{1,0:T(4,128)(2,1)} %get-tuple-element.55), channel_id=1, source_target_pairs={{0,1},{2,3},{4,5},{6,7},{8,9},{10,11},{12,13},{14,15},{16,17},{18,... | collective-permute-start | bytes 1928 | tf_op jit(solution)/shard_map/ppermute | solution.py:16
  37.7 1.1 %broadcast_select_fusion.4 = (bf16[112,2048]{1,0:T(8,128)(2,1)S(1)}, bf16[112,2048]{1,0:T(8,128)(2,1)S(1)}) fusion(bf16[112,2048]{1,0:T(8,128)(2,1)} %collective-permute-done.4, bf16[112,2048]{1,0:T(8,128)(2,1)S(1)} %collective-permute-done.5, pred[]{:T(512)S(6)} %eq.144), kind=kLoop, calls=%fused_computation.44 | loop fusion | flops 458752 | bytes 1835009 | tf_op jit(solution)/shard_map/jit(_where)/select_n | solution.py:240
  38.8 1.1 %broadcast_select_fusion.2 = (bf16[128,2048]{1,0:T(8,128)(2,1)S(1)}, bf16[128,2048]{1,0:T(8,128)(2,1)S(1)}) fusion(bf16[128,2048]{1,0:T(8,128)(2,1)} %collective-permute-done.6, bf16[128,2048]{1,0:T(8,128)(2,1)S(1)} %collective-permute-done.7, pred[]{:T(512)S(6)} %eq.144), kind=kLoop, calls=%fused_computation.41 | loop fusion | flops 524288 | bytes 2097153 | tf_op jit(solution)/shard_map/jit(_where)/select_n | solution.py:240
  40.6 1.3 %copy-done.1 = bf16[256,4096]{1,0:T(8,128)(2,1)S(1)} copy-done((bf16[256,4096]{1,0:T(8,128)(2,1)S(1)}, bf16[256,4096]{1,0:T(8,128)(2,1)}, u32[]{:S(2)}) %copy-start.1) | copy-done | bytes 2097176
  48.6 2.6 %collective-permute-done.8 = f32[1920,128]{1,0:T(8,128)} collective-permute-done((f32[1920,128]{1,0:T(8,128)S(1)}, f32[1920,128]{1,0:T(8,128)}, u32[]{:S(2)}, u32[]{:S(2)}) %collective-permute-start.8) | collective-permute-done | bytes 983072 | tf_op jit(solution)/shard_map/ppermute | solution.py:188
  51.1 1.3 %dynamic-slice_add_fusion = f32[1920,128]{1,0:T(8,128)S(1)} fusion(f32[1920,128]{1,0:T(8,128)} %collective-permute-done.8, f32[3840,128]{1,0:T(8,128)S(1)} %fusion, s32[]{:T(128)S(6)} %select_n.399), kind=kLoop, calls=%fused_computation.22 | loop fusion | flops 245760 | bytes 2949124 | tf_op jit(solution)/shard_map/add | solution.py:188
  52.5 2.4 %collective-permute-start.9 = (f32[480,128]{1,0:T(8,128)S(1)}, f32[480,128]{1,0:T(8,128)S(1)}, u32[]{:S(2)}, u32[]{:S(2)}) collective-permute-start(f32[480,128]{1,0:T(8,128)S(1)} %get-tuple-element.28), channel_id=1, source_target_pairs={{0,1},{1,0},{2,3},{3,2},{4,5},{5,4},{6,7},{7,6},{8,9},{9,8},{10,11... | collective-permute-start | bytes 737288 | tf_op jit(solution)/shard_map/ppermute | solution.py:196
  55.0 1.5 %collective-permute-start.10 = (f32[480,128]{1,0:T(8,128)S(1)}, f32[480,128]{1,0:T(8,128)S(1)}, u32[]{:S(2)}, u32[]{:S(2)}) collective-permute-start(f32[480,128]{1,0:T(8,128)S(1)} %get-tuple-element.30), channel_id=1, source_target_pairs={{0,4},{1,5},{2,6},{3,7},{4,0},{5,1},{6,2},{7,3},{8,12},{9,13},{10,... | collective-permute-start | bytes 737288 | tf_op jit(solution)/shard_map/ppermute | solution.py:196
  56.5 10.0 %collective-permute-done.9 = f32[480,128]{1,0:T(8,128)S(1)} collective-permute-done((f32[480,128]{1,0:T(8,128)S(1)}, f32[480,128]{1,0:T(8,128)S(1)}, u32[]{:S(2)}, u32[]{:S(2)}) %collective-permute-start.9) | collective-permute-done | bytes 245792 | tf_op jit(solution)/shard_map/ppermute | solution.py:196
  66.5 1.3 %collective-permute-done.10 = f32[480,128]{1,0:T(8,128)S(1)} collective-permute-done((f32[480,128]{1,0:T(8,128)S(1)}, f32[480,128]{1,0:T(8,128)S(1)}, u32[]{:S(2)}, u32[]{:S(2)}) %collective-permute-start.10) | collective-permute-done | bytes 245792 | tf_op jit(solution)/shard_map/ppermute | solution.py:196
  68.3 1.5 %collective-permute-start.14 = (f32[120,128]{1,0:T(8,128)S(1)}, f32[120,128]{1,0:T(8,128)S(1)}, u32[]{:S(2)}, u32[]{:S(2)}) collective-permute-start(f32[120,128]{1,0:T(8,128)S(1)} %get-tuple-element.43), channel_id=1, source_target_pairs={{0,24},{1,25},{2,26},{3,27},{4,28},{5,29},{6,30},{7,31},{8,16},{9,... | collective-permute-start | bytes 184328 | tf_op jit(solution)/shard_map/ppermute | solution.py:196
  69.8 1.6 %collective-permute-start.13 = (f32[120,128]{1,0:T(8,128)S(1)}, f32[120,128]{1,0:T(8,128)S(1)}, u32[]{:S(2)}, u32[]{:S(2)}) collective-permute-start(f32[120,128]{1,0:T(8,128)S(1)} %get-tuple-element.44), channel_id=1, source_target_pairs={{0,16},{1,17},{2,18},{3,19},{4,20},{5,21},{6,22},{7,23},{8,24},{9,... | collective-permute-start | bytes 184328 | tf_op jit(solution)/shard_map/ppermute | solution.py:196
  71.4 1.6 %collective-permute-done.12 = f32[120,128]{1,0:T(8,128)S(1)} collective-permute-done((f32[120,128]{1,0:T(8,128)S(1)}, f32[120,128]{1,0:T(8,128)S(1)}, u32[]{:S(2)}, u32[]{:S(2)}) %collective-permute-start.12) | collective-permute-done | bytes 61472 | tf_op jit(solution)/shard_map/ppermute | solution.py:196
  73.1 1.3 %collective-permute-done.14 = f32[120,128]{1,0:T(8,128)S(1)} collective-permute-done((f32[120,128]{1,0:T(8,128)S(1)}, f32[120,128]{1,0:T(8,128)S(1)}, u32[]{:S(2)}, u32[]{:S(2)}) %collective-permute-start.14) | collective-permute-done | bytes 61472 | tf_op jit(solution)/shard_map/ppermute | solution.py:196
  74.4 2.4 %collective-permute-done.13 = f32[120,128]{1,0:T(8,128)S(1)} collective-permute-done((f32[120,128]{1,0:T(8,128)S(1)}, f32[120,128]{1,0:T(8,128)S(1)}, u32[]{:S(2)}, u32[]{:S(2)}) %collective-permute-start.13) | collective-permute-done | bytes 61472 | tf_op jit(solution)/shard_map/ppermute | solution.py:196
  76.8 1.2 %collective-permute-start.17 = (f32[120,128]{1,0:T(8,128)S(1)}, f32[120,128]{1,0:T(8,128)S(1)}, u32[]{:S(2)}, u32[]{:S(2)}) collective-permute-start(f32[120,128]{1,0:T(8,128)S(1)} %add_add_fusion.1), channel_id=1, source_target_pairs={{0,24},{1,25},{2,26},{3,27},{4,28},{5,29},{6,30},{7,31},{8,16},{9,... | collective-permute-start | bytes 184328 | tf_op jit(solution)/shard_map/ppermute | solution.py:201
  78.1 3.2 %collective-permute-start.15 = (f32[120,128]{1,0:T(8,128)S(1)}, f32[120,128]{1,0:T(8,128)S(1)}, u32[]{:S(2)}, u32[]{:S(2)}) collective-permute-start(f32[120,128]{1,0:T(8,128)S(1)} %add_add_fusion.1), channel_id=1, source_target_pairs={{0,8},{1,9},{2,10},{3,11},{4,12},{5,13},{6,14},{7,15},{8,0},{9,1},... | collective-permute-start | bytes 184328 | tf_op jit(solution)/shard_map/ppermute | solution.py:201
  81.3 1.7 %collective-permute-done.17 = f32[120,128]{1,0:T(8,128)S(1)} collective-permute-done((f32[120,128]{1,0:T(8,128)S(1)}, f32[120,128]{1,0:T(8,128)S(1)}, u32[]{:S(2)}, u32[]{:S(2)}) %collective-permute-start.17) | collective-permute-done | bytes 61472 | tf_op jit(solution)/shard_map/ppermute | solution.py:201
  83.0 1.3 %collective-permute-done.16 = f32[120,128]{1,0:T(8,128)S(1)} collective-permute-done((f32[120,128]{1,0:T(8,128)S(1)}, f32[120,128]{1,0:T(8,128)S(1)}, u32[]{:S(2)}, u32[]{:S(2)}) %collective-permute-start.16) | collective-permute-done | bytes 61472 | tf_op jit(solution)/shard_map/ppermute | solution.py:201
  84.3 1.5 %collective-permute-start.20 = (f32[480,128]{1,0:T(8,128)S(1)}, f32[480,128]{1,0:T(8,128)S(1)}, u32[]{:S(2)}, u32[]{:S(2)}) collective-permute-start(f32[480,128]{1,0:T(8,128)S(1)} %pad_maximum_fusion.9), channel_id=1, source_target_pairs={{0,5},{1,4},{2,7},{3,6},{4,1},{5,0},{6,3},{7,2},{8,13},{9,12},{10,... | collective-permute-start | bytes 737288 | tf_op jit(solution)/shard_map/ppermute | solution.py:201
  85.8 1.4 %collective-permute-start.19 = (f32[480,128]{1,0:T(8,128)S(1)}, f32[480,128]{1,0:T(8,128)S(1)}, u32[]{:S(2)}, u32[]{:S(2)}) collective-permute-start(f32[480,128]{1,0:T(8,128)S(1)} %pad_maximum_fusion.9), channel_id=1, source_target_pairs={{0,4},{1,5},{2,6},{3,7},{4,0},{5,1},{6,2},{7,3},{8,12},{9,13},{10,... | collective-permute-start | bytes 737288 | tf_op jit(solution)/shard_map/ppermute | solution.py:201
  87.8 5.7 %collective-permute-done.20 = f32[480,128]{1,0:T(8,128)S(1)} collective-permute-done((f32[480,128]{1,0:T(8,128)S(1)}, f32[480,128]{1,0:T(8,128)S(1)}, u32[]{:S(2)}, u32[]{:S(2)}) %collective-permute-start.20) | collective-permute-done | bytes 245792 | tf_op jit(solution)/shard_map/ppermute | solution.py:201
  93.6 2.6 %collective-permute-done.19 = f32[480,128]{1,0:T(8,128)S(1)} collective-permute-done((f32[480,128]{1,0:T(8,128)S(1)}, f32[480,128]{1,0:T(8,128)S(1)}, u32[]{:S(2)}, u32[]{:S(2)}) %collective-permute-start.19) | collective-permute-done | bytes 245792 | tf_op jit(solution)/shard_map/ppermute | solution.py:201
  97.8 1.1 %fusion.3 = bf16[1,512,256]{2,1,0:T(8,128)(2,1)} fusion(bf16[768,256]{1,0:T(8,128)(2,1)S(1)} %copy-done.12, f32[518,256]{1,0:T(8,128)S(1)} %copy-done.4, bf16[512,256]{1,0:T(8,128)(2,1)S(1)} %copy-done.8, bf16[512,256]{1,0:T(8,128)(2,1)S(1)} %copy-done.10, bf16[512,256]{1,0:T(8,128)(2,1)S(1)} %copy-done.6, f32[256]{0:T(256)S(1)} %copy-done.17), kind=kOutput, calls=%fused_computation.9 | convolution fusion | flops 204079104 | bytes 1967104 | tf_op jit(solution)/shard_map/dot_general | solution.py:92
  101.7 1.1 %slice.175 = f32[2240,128]{1,0:T(8,128)} slice(f32[3840,128]{1,0:T(8,128)S(1)} %broadcast_select_fusion), slice={[0:2240], [0:128]} | slice | bytes 2293760 | tf_op jit(solution)/shard_map/slice | solution.py:214
  (137 shorter events, 22.2 us)
Async XLA Ops:
  0.6 35.1 %copy-start = (bf16[560,512]{1,0:T(8,128)(2,1)S(1)}, bf16[560,512]{1,0:T(8,128)(2,1)}, u32[]{:S(2)}) copy-start(bf16[560,512]{1,0:T(8,128)(2,1)} %param.16) | copy-start | bytes 1720324
  0.6 10.1 %copy-start.18 = (s32[1,8]{1,0:T(1,128)S(1)}, s32[1,8]{1,0:T(1,128)}, u32[]{:S(2)}) copy-start(s32[1,8]{1,0:T(1,128)} %param.13) | copy-start | bytes 100
  0.7 10.1 %copy-start.19 = (s32[1,8]{1,0:T(1,128)S(1)}, s32[1,8]{1,0:T(1,128)}, u32[]{:S(2)}) copy-start(s32[1,8]{1,0:T(1,128)} %param.14) | copy-start | bytes 100
  0.7 10.3 %copy-start.13 = (bf16[1,8,640]{2,1,0:T(8,128)(2,1)S(1)}, bf16[1,8,640]{2,1,0:T(8,128)(2,1)}, u32[]{:S(2)}) copy-start(bf16[1,8,640]{2,1,0:T(8,128)(2,1)} %param.11) | copy-start | bytes 30724
  0.7 10.3 %copy-start.16 = (s32[1,8]{1,0:T(1,128)S(1)}, s32[1,8]{1,0:T(1,128)}, u32[]{:S(2)}) copy-start(s32[1,8]{1,0:T(1,128)} %param.12) | copy-start | bytes 100
  0.7 25.6 %copy-start.2 = (bf16[1,512,256]{2,1,0:T(8,128)(2,1)S(1)}, bf16[1,512,256]{2,1,0:T(8,128)(2,1)}, u32[]{:S(2)}) copy-start(bf16[1,512,256]{2,1,0:T(8,128)(2,1)} %param.15) | copy-start | bytes 786436
  1.7 9.3 %collective-permute-start = (bf16[16,2048]{1,0:T(8,128)(2,1)S(1)}, bf16[16,2048]{1,0:T(8,128)(2,1)S(1)}, u32[]{:S(2)}, u32[]{:S(2)}) collective-permute-start(bf16[16,2048]{1,0:T(8,128)(2,1)S(1)} %slice_select_fusion.2), channel_id=1, source_target_pairs={{0,1},{1,0},{2,3},{3,2},{4,5},{5,4},{6,7},{7,6},{8,9},{9,8},{10,11... | collective-permute-start | bytes 196616 | tf_op jit(solution)/shard_map/ppermute | solution.py:237
  6.7 27.0 %copy-start.11 = (bf16[768,256]{1,0:T(8,128)(2,1)S(1)}, bf16[768,256]{1,0:T(8,128)(2,1)}, u32[]{:S(2)}) copy-start(bf16[768,256]{1,0:T(8,128)(2,1)} %param.20) | copy-start | bytes 1179652
  6.7 28.9 %collective-permute-start.4 = (bf16[112,2048]{1,0:T(8,128)(2,1)}, bf16[112,2048]{1,0:T(8,128)(2,1)}, u32[]{:S(2)}, u32[]{:S(2)}) collective-permute-start(bf16[112,2048]{1,0:T(8,128)(2,1)} %slice_select_fusion.1), channel_id=1, source_target_pairs={{0,1},{1,0},{2,3},{3,2},{4,5},{5,4},{6,7},{7,6},{8,9},{9,8},{10,11... | collective-permute-start | bytes 1376264 | tf_op jit(solution)/shard_map/ppermute | solution.py:237
  8.8 27.2 %collective-permute-start.6 = (bf16[128,2048]{1,0:T(8,128)(2,1)}, bf16[128,2048]{1,0:T(8,128)(2,1)}, u32[]{:S(2)}, u32[]{:S(2)}) collective-permute-start(bf16[128,2048]{1,0:T(8,128)(2,1)} %slice_select_fusion), channel_id=1, source_target_pairs={{0,1},{1,0},{2,3},{3,2},{4,5},{5,4},{6,7},{7,6},{8,9},{9,8},{10,11... | collective-permute-start | bytes 1572872 | tf_op jit(solution)/shard_map/ppermute | solution.py:237
  13.1 12.5 %all-to-all-start = ((bf16[16,2,321]{2,1,0:T(2,128)(2,1)}), bf16[16,2,321]{2,1,0:T(2,128)(2,1)S(1)}, u32[]{:S(2)}, u32[]{:S(2)}) async-start(bf16[16,2,321]{2,1,0:T(2,128)(2,1)} %reshape.119), calls=%async_computation | async-start | bytes 49152 | tf_op jit(solution)/shard_map/all_to_all | solution.py:285
  19.1 17.5 %collective-permute-start.3 = (bf16[16,2048]{1,0:T(8,128)(2,1)S(1)}, bf16[16,2048]{1,0:T(8,128)(2,1)}, u32[]{:S(2)}, u32[]{:S(2)}) collective-permute-start(bf16[16,2048]{1,0:T(8,128)(2,1)S(1)} %collective-permute-done), channel_id=1, source_target_pairs={{0,2},{2,0},{4,6},{6,4},{8,10},{10,8},{12,14},{14,12},{16,18},{18,... | collective-permute-start | bytes 196616 | tf_op jit(solution)/shard_map/ppermute | solution.py:238
  27.3 7.2 %collective-permute-start.2 = (bf16[4,80]{1,0:T(4,128)(2,1)}, bf16[4,80]{1,0:T(4,128)(2,1)S(1)}, u32[]{:S(2)}, u32[]{:S(2)}) collective-permute-start(bf16[4,80]{1,0:T(4,128)(2,1)} %get-tuple-element.54), channel_id=1, source_target_pairs={{1,0},{3,2},{5,4},{7,6},{9,8},{11,10},{13,12},{15,14},{17,16},{19,... | collective-permute-start | bytes 1928 | tf_op jit(solution)/shard_map/ppermute | solution.py:19
  28.6 6.0 %collective-permute-start.1 = (bf16[4,80]{1,0:T(4,128)(2,1)}, bf16[4,80]{1,0:T(4,128)(2,1)}, u32[]{:S(2)}, u32[]{:S(2)}) collective-permute-start(bf16[4,80]{1,0:T(4,128)(2,1)} %get-tuple-element.55), channel_id=1, source_target_pairs={{0,1},{2,3},{4,5},{6,7},{8,9},{10,11},{12,13},{14,15},{16,17},{18,... | collective-permute-start | bytes 1928 | tf_op jit(solution)/shard_map/ppermute | solution.py:16
  34.1 1.6 %copy-start.14 = (f32[512]{0:T(512)S(1)}, f32[512]{0:T(512)}, u32[]{:S(2)}) copy-start(f32[512]{0:T(512)} %param.17) | copy-start | bytes 6148
  35.6 2.1 %collective-permute-start.5 = (bf16[112,2048]{1,0:T(8,128)(2,1)}, bf16[112,2048]{1,0:T(8,128)(2,1)S(1)}, u32[]{:S(2)}, u32[]{:S(2)}) collective-permute-start(bf16[112,2048]{1,0:T(8,128)(2,1)} %collective-permute-done.4), channel_id=1, source_target_pairs={{0,2},{2,0},{4,6},{6,4},{8,10},{10,8},{12,14},{14,12},{16,18},{18,... | collective-permute-start | bytes 1376264 | tf_op jit(solution)/shard_map/ppermute | solution.py:238
  36.0 2.8 %collective-permute-start.7 = (bf16[128,2048]{1,0:T(8,128)(2,1)}, bf16[128,2048]{1,0:T(8,128)(2,1)S(1)}, u32[]{:S(2)}, u32[]{:S(2)}) collective-permute-start(bf16[128,2048]{1,0:T(8,128)(2,1)} %collective-permute-done.6), channel_id=1, source_target_pairs={{0,2},{2,0},{4,6},{6,4},{8,10},{10,8},{12,14},{14,12},{16,18},{18,... | collective-permute-start | bytes 1572872 | tf_op jit(solution)/shard_map/ppermute | solution.py:238
  43.7 1.6 %copy-start.3 = (f32[518,256]{1,0:T(8,128)}, f32[518,256]{1,0:T(8,128)S(1)}, u32[]{:S(2)}) copy-start(f32[518,256]{1,0:T(8,128)S(1)} %get-tuple-element.20) | copy-start | bytes 1591300
  48.4 2.8 %collective-permute-start.8 = (f32[1920,128]{1,0:T(8,128)S(1)}, f32[1920,128]{1,0:T(8,128)}, u32[]{:S(2)}, u32[]{:S(2)}) collective-permute-start(f32[1920,128]{1,0:T(8,128)S(1)} %constant_dynamic-slice_fusion.6), channel_id=1, source_target_pairs={{0,2},{1,3},{2,0},{3,1},{4,6},{5,7},{6,4},{7,5},{8,10},{9,11},{10,... | collective-permute-start | bytes 2949128 | tf_op jit(solution)/shard_map/ppermute | solution.py:188
  52.5 14.0 %collective-permute-start.9 = (f32[480,128]{1,0:T(8,128)S(1)}, f32[480,128]{1,0:T(8,128)S(1)}, u32[]{:S(2)}, u32[]{:S(2)}) collective-permute-start(f32[480,128]{1,0:T(8,128)S(1)} %get-tuple-element.28), channel_id=1, source_target_pairs={{0,1},{1,0},{2,3},{3,2},{4,5},{5,4},{6,7},{7,6},{8,9},{9,8},{10,11... | collective-permute-start | bytes 737288 | tf_op jit(solution)/shard_map/ppermute | solution.py:196
  55.0 11.5 %collective-permute-start.11 = (f32[480,128]{1,0:T(8,128)S(1)}, f32[480,128]{1,0:T(8,128)S(1)}, u32[]{:S(2)}, u32[]{:S(2)}) collective-permute-start(f32[480,128]{1,0:T(8,128)S(1)} %get-tuple-element.29), channel_id=1, source_target_pairs={{0,5},{1,4},{2,7},{3,6},{4,1},{5,0},{6,3},{7,2},{8,13},{9,12},{10,... | collective-permute-start | bytes 737288 | tf_op jit(solution)/shard_map/ppermute | solution.py:196
  55.0 12.8 %collective-permute-start.10 = (f32[480,128]{1,0:T(8,128)S(1)}, f32[480,128]{1,0:T(8,128)S(1)}, u32[]{:S(2)}, u32[]{:S(2)}) collective-permute-start(f32[480,128]{1,0:T(8,128)S(1)} %get-tuple-element.30), channel_id=1, source_target_pairs={{0,4},{1,5},{2,6},{3,7},{4,0},{5,1},{6,2},{7,3},{8,12},{9,13},{10,... | collective-permute-start | bytes 737288 | tf_op jit(solution)/shard_map/ppermute | solution.py:196
  67.9 5.2 %collective-permute-start.12 = (f32[120,128]{1,0:T(8,128)S(1)}, f32[120,128]{1,0:T(8,128)S(1)}, u32[]{:S(2)}, u32[]{:S(2)}) collective-permute-start(f32[120,128]{1,0:T(8,128)S(1)} %get-tuple-element.42), channel_id=1, source_target_pairs={{0,8},{1,9},{2,10},{3,11},{4,12},{5,13},{6,14},{7,15},{8,0},{9,1},... | collective-permute-start | bytes 184328 | tf_op jit(solution)/shard_map/ppermute | solution.py:196
  68.3 6.0 %collective-permute-start.14 = (f32[120,128]{1,0:T(8,128)S(1)}, f32[120,128]{1,0:T(8,128)S(1)}, u32[]{:S(2)}, u32[]{:S(2)}) collective-permute-start(f32[120,128]{1,0:T(8,128)S(1)} %get-tuple-element.43), channel_id=1, source_target_pairs={{0,24},{1,25},{2,26},{3,27},{4,28},{5,29},{6,30},{7,31},{8,16},{9,... | collective-permute-start | bytes 184328 | tf_op jit(solution)/shard_map/ppermute | solution.py:196
  69.8 7.0 %collective-permute-start.13 = (f32[120,128]{1,0:T(8,128)S(1)}, f32[120,128]{1,0:T(8,128)S(1)}, u32[]{:S(2)}, u32[]{:S(2)}) collective-permute-start(f32[120,128]{1,0:T(8,128)S(1)} %get-tuple-element.44), channel_id=1, source_target_pairs={{0,16},{1,17},{2,18},{3,19},{4,20},{5,21},{6,22},{7,23},{8,24},{9,... | collective-permute-start | bytes 184328 | tf_op jit(solution)/shard_map/ppermute | solution.py:196
  76.8 6.1 %collective-permute-start.17 = (f32[120,128]{1,0:T(8,128)S(1)}, f32[120,128]{1,0:T(8,128)S(1)}, u32[]{:S(2)}, u32[]{:S(2)}) collective-permute-start(f32[120,128]{1,0:T(8,128)S(1)} %add_add_fusion.1), channel_id=1, source_target_pairs={{0,24},{1,25},{2,26},{3,27},{4,28},{5,29},{6,30},{7,31},{8,16},{9,... | collective-permute-start | bytes 184328 | tf_op jit(solution)/shard_map/ppermute | solution.py:201
  78.1 6.2 %collective-permute-start.16 = (f32[120,128]{1,0:T(8,128)S(1)}, f32[120,128]{1,0:T(8,128)S(1)}, u32[]{:S(2)}, u32[]{:S(2)}) collective-permute-start(f32[120,128]{1,0:T(8,128)S(1)} %add_add_fusion.1), channel_id=1, source_target_pairs={{0,16},{1,17},{2,18},{3,19},{4,20},{5,21},{6,22},{7,23},{8,24},{9,... | collective-permute-start | bytes 184328 | tf_op jit(solution)/shard_map/ppermute | solution.py:201
  78.1 6.2 %collective-permute-start.15 = (f32[120,128]{1,0:T(8,128)S(1)}, f32[120,128]{1,0:T(8,128)S(1)}, u32[]{:S(2)}, u32[]{:S(2)}) collective-permute-start(f32[120,128]{1,0:T(8,128)S(1)} %add_add_fusion.1), channel_id=1, source_target_pairs={{0,8},{1,9},{2,10},{3,11},{4,12},{5,13},{6,14},{7,15},{8,0},{9,1},... | collective-permute-start | bytes 184328 | tf_op jit(solution)/shard_map/ppermute | solution.py:201
  84.3 9.3 %collective-permute-start.20 = (f32[480,128]{1,0:T(8,128)S(1)}, f32[480,128]{1,0:T(8,128)S(1)}, u32[]{:S(2)}, u32[]{:S(2)}) collective-permute-start(f32[480,128]{1,0:T(8,128)S(1)} %pad_maximum_fusion.9), channel_id=1, source_target_pairs={{0,5},{1,4},{2,7},{3,6},{4,1},{5,0},{6,3},{7,2},{8,13},{9,12},{10,... | collective-permute-start | bytes 737288 | tf_op jit(solution)/shard_map/ppermute | solution.py:201
  85.8 10.4 %collective-permute-start.19 = (f32[480,128]{1,0:T(8,128)S(1)}, f32[480,128]{1,0:T(8,128)S(1)}, u32[]{:S(2)}, u32[]{:S(2)}) collective-permute-start(f32[480,128]{1,0:T(8,128)S(1)} %pad_maximum_fusion.9), channel_id=1, source_target_pairs={{0,4},{1,5},{2,6},{3,7},{4,0},{5,1},{6,2},{7,3},{8,12},{9,13},{10,... | collective-permute-start | bytes 737288 | tf_op jit(solution)/shard_map/ppermute | solution.py:201
  87.2 8.9 %collective-permute-start.18 = (f32[480,128]{1,0:T(8,128)S(1)}, f32[480,128]{1,0:T(8,128)S(1)}, u32[]{:S(2)}, u32[]{:S(2)}) collective-permute-start(f32[480,128]{1,0:T(8,128)S(1)} %pad_maximum_fusion.9), channel_id=1, source_target_pairs={{0,1},{1,0},{2,3},{3,2},{4,5},{5,4},{6,7},{7,6},{8,9},{9,8},{10,11... | collective-permute-start | bytes 737288 | tf_op jit(solution)/shard_map/ppermute | solution.py:201
  96.6 2.6 %collective-permute-start.21 = (f32[1920,128]{1,0:T(8,128)S(1)}, f32[1920,128]{1,0:T(8,128)S(1)}, u32[]{:S(2)}, u32[]{:S(2)}) collective-permute-start(f32[1920,128]{1,0:T(8,128)S(1)} %pad_maximum_fusion.2), channel_id=1, source_target_pairs={{0,2},{1,3},{2,0},{3,1},{4,6},{5,7},{6,4},{7,5},{8,10},{9,11},{10,... | collective-permute-start | bytes 2949128 | tf_op jit(solution)/shard_map/ppermute | solution.py:210
  (11 other events, 11.9 us)

commit v15 on v12

--- a/solution.py
+++ b/solution.py
@@ -225,15 +225,14 @@
             whole,
         )
     rows, width = w_ups.shape
-    cols = width // 2
     core = lax.axis_index("dp") % 2
     tm = lax.axis_index("tm")
-    bounds = [0, 16, rows // 2, rows] if rows % 32 == 0 and rows > 32 else [0, rows]
+    half = rows // 2
+    bounds = [0, 16, half // 2, half] if half % 32 == 0 and half > 32 else [0, half]
     swap = [(i, i ^ 1) for i in range(dp_size)]
     got_parts, partner_parts = [], []
     for lo, hi in zip(bounds, bounds[1:]):
-        block = w_ups[lo:hi]
-        mine = jnp.where(core == 0, block[:, :cols], block[:, cols:])
+        mine = lax.dynamic_slice_in_dim(w_ups, core * half + lo, hi - lo, axis=0)
         got_parts.append(lax.ppermute(mine, "tm", [(0, 1), (1, 0)]))
         partner_parts.append(lax.ppermute(got_parts[-1], "dp", swap))
     low = jnp.concatenate(
@@ -247,18 +246,14 @@
         own_act = lax.dynamic_slice_in_dim(act, tm * rows, rows, axis=1)
         other_act = lax.dynamic_slice_in_dim(act, (1 - tm) * rows, rows, axis=1)
         own = jnp.dot(own_act, w_ups, preferred_element_type=jnp.float32)
-        other = jnp.concatenate(
-            [
-                jnp.dot(other_act, low, preferred_element_type=jnp.float32),
-                jnp.dot(other_act, high, preferred_element_type=jnp.float32),
-            ],
-            axis=1,
-        )
+        other = jnp.dot(
+            other_act[:, :half], low, preferred_element_type=jnp.float32
+        ) + jnp.dot(other_act[:, half:], high, preferred_element_type=jnp.float32)
         return own + other
 
     def backward(d_taps):
         own = contract_cols(d_taps, w_ups)
-        other = contract_cols(d_taps[:, :cols], low) + contract_cols(d_taps[:, cols:], high)
+        other = jnp.concatenate([contract_cols(d_taps, low), contract_cols(d_taps, high)], axis=1)
         return jnp.where(
             tm == 0, jnp.concatenate([own, other], axis=1), jnp.concatenate([other, own], axis=1)
         )

time: 97.8 us -> 109 us (1.11)
  local copies, waits for them, and re-layouts: 10.2 us -> 17.6 us
  matrix products: 5.62 us -> 8.72 us
    select_n x3 -> x0, other arithmetic: 5.05 us -> none  [ups_functions(): mine = jnp.where(core == 0, block[:, :cols], block[:, cols:])]
    unnamed x51 -> x57, local copies, waits for them, and re-layouts: 4.34 us -> 7.01 us
    add x2, other arithmetic: 0.06 us -> 2.08 us  [butterfly_psum(): total = total + lax.ppermute(send, axes, perm_of(step, offset))]
    dot_general x2, local copies, waits for them, and re-layouts: 0.42 us -> 2.31 us  [contract_rows(): lax.dot_general(left, right, (((0,), (0,)), ((), ())), preferred_element_...]
    dot_general x1, matrix products: 0.25 us -> 1.98 us  [local_pass(): pre = jnp.dot(patches, w_pre, preferred_element_type=jnp.float32) + b_pre]
    dynamic_slice x0 -> x3, local copies, waits for them, and re-layouts: none -> 1.64 us  [ups_functions(): mine = lax.dynamic_slice_in_dim(w_ups, core * half + lo, hi - lo, axis=0)]
    dot_general x2, other arithmetic: 0.19 us -> 1.77 us  [contract_rows(): lax.dot_general(left, right, (((0,), (0,)), ((), ())), preferred_element_...]
    dot_general x4, matrix products: 2.12 us -> 3.45 us  [contract_cols(): lax.dot_general(left, right, (((1,), (1,)), ((), ())), preferred_element_...]
  transfers between devices with their start and end apart: 23 -> 23, of which waited for: 15 -> 16; matrix products, arithmetic and copies ran while one was open for 13% -> 13% of each run, Pallas kernels for 0% -> 0%
where the time goes in v15:
time: 109 us; the launch traced here: 108 us
  starting transfers between devices  36.1 us (33%)
  waiting for transfers between devices  32 us (29%)
  local copies, waits for them, and re-layouts  17.6 us (16%)
  other arithmetic  12.8 us (12%)
  matrix products  8.72 us (8%)
  between operations  1.26 us (1%)
    ppermute x6, waiting for transfers between devices, butterfly_psum(): total = total + lax.ppermute(send, axes, perm_of(step, offset))  11.4 us
    ppermute x6, waiting for transfers between devices, butterfly_psum(): lax.ppermute(x, axes, perm_of(step, o))  10 us
    ppermute x6, starting transfers between devices, butterfly_psum(): lax.ppermute(x, axes, perm_of(step, o))  7.94 us
    ppermute x6, starting transfers between devices, butterfly_psum(): total = total + lax.ppermute(send, axes, perm_of(step, offset))  7.29 us
    unnamed x57, local copies, waits for them, and re-layouts  7.01 us
    all_to_all x1, starting transfers between devices, on_device(): lax.all_to_all(outgoing, 'dp', split_axis=0, concat_axis=0, tiled=True)  6.39 us
    all_to_all x1, waiting for transfers between devices, on_device(): lax.all_to_all(outgoing, 'dp', split_axis=0, concat_axis=0, tiled=True)  6.06 us
    ppermute x3, starting transfers between devices, ups_functions(): got_parts.append(lax.ppermute(mine, 'tm', [(0, 1), (1, 0)]))  5.06 us
  transfers between devices with their start and end apart: 23, of which 16 were waited for; matrix products, arithmetic and copies ran while one was open for 13% of the time, Pallas kernels for 0%

profile of v15, /device:TPU:0, one launch (start us, length us, event | category | flops | bytes accessed | tf_op | source)
XLA Modules:
  0.0 108.5 jit_solution(12273685745173411739)
XLA Ops:
  0.7 1.5 %copy-done = bf16[256,4096]{1,0:T(8,128)(2,1)S(1)} copy-done((bf16[256,4096]{1,0:T(8,128)(2,1)S(1)}, bf16[256,4096]{1,0:T(8,128)(2,1)}, u32[]{:S(2)}) %copy-start) | copy-done | bytes 2097176
  2.2 3.0 %collective-permute-start = (bf16[16,4096]{1,0:T(8,128)(2,1)S(1)}, bf16[16,4096]{1,0:T(8,128)(2,1)}, u32[]{:S(2)}, u32[]{:S(2)}) collective-permute-start(bf16[16,4096]{1,0:T(8,128)(2,1)S(1)} %constant_dynamic-slice_fusion.9), channel_id=1, source_target_pairs={{0,1},{1,0},{2,3},{3,2},{4,5},{5,4},{6,7},{7,6},{8,9},{9,8},{10,11... | collective-permute-start | bytes 393224 | tf_op jit(solution)/shard_map/ppermute | solution.py:236
  6.9 2.0 %collective-permute-start.6 = (bf16[64,4096]{1,0:T(8,128)(2,1)}, bf16[64,4096]{1,0:T(8,128)(2,1)}, u32[]{:S(2)}, u32[]{:S(2)}) collective-permute-start(bf16[64,4096]{1,0:T(8,128)(2,1)} %constant_dynamic-slice_fusion.7), channel_id=1, source_target_pairs={{0,1},{1,0},{2,3},{3,2},{4,5},{5,4},{6,7},{7,6},{8,9},{9,8},{10,11... | collective-permute-start | bytes 1572872 | tf_op jit(solution)/shard_map/ppermute | solution.py:236
  11.3 6.4 %all-to-all-start = ((bf16[16,2,321]{2,1,0:T(2,128)(2,1)}), bf16[16,2,321]{2,1,0:T(2,128)(2,1)S(1)}, u32[]{:S(2)}, u32[]{:S(2)}) async-start(bf16[16,2,321]{2,1,0:T(2,128)(2,1)} %reshape.119), calls=%async_computation | async-start | bytes 49152 | tf_op jit(solution)/shard_map/all_to_all | solution.py:280
  18.2 6.1 %all-to-all-done = bf16[16,2,321]{2,1,0:T(2,128)(2,1)S(1)} async-done(((bf16[16,2,321]{2,1,0:T(2,128)(2,1)}), bf16[16,2,321]{2,1,0:T(2,128)(2,1)S(1)}, u32[]{:S(2)}, u32[]{:S(2)}) %all-to-all-start) | async-done | bytes 20576 | tf_op jit(solution)/shard_map/all_to_all | solution.py:280
  26.0 1.3 %collective-permute-start.2 = (bf16[4,80]{1,0:T(4,128)(2,1)S(1)}, bf16[4,80]{1,0:T(4,128)(2,1)S(1)}, u32[]{:S(2)}, u32[]{:S(2)}) collective-permute-start(bf16[4,80]{1,0:T(4,128)(2,1)S(1)} %get-tuple-element.54), channel_id=1, source_target_pairs={{1,0},{3,2},{5,4},{7,6},{9,8},{11,10},{13,12},{15,14},{17,16},{19,... | collective-permute-start | bytes 1928 | tf_op jit(solution)/shard_map/ppermute | solution.py:19
  28.9 4.5 %collective-permute-start.1 = (bf16[4,80]{1,0:T(4,128)(2,1)S(1)}, bf16[4,80]{1,0:T(4,128)(2,1)S(1)}, u32[]{:S(2)}, u32[]{:S(2)}) collective-permute-start(bf16[4,80]{1,0:T(4,128)(2,1)S(1)} %get-tuple-element.55), channel_id=1, source_target_pairs={{0,1},{2,3},{4,5},{6,7},{8,9},{10,11},{12,13},{14,15},{16,17},{18,... | collective-permute-start | bytes 1928 | tf_op jit(solution)/shard_map/ppermute | solution.py:16
  34.9 2.0 %fusion.26 = (bf16[66,512]{1,0:T(8,128)(2,1)S(1)}, f32[66,512]{1,0:T(8,128)}) fusion(pred[66]{0:T(512)(128)(4,1)S(1)} %compare_and_fusion, f32[512]{0:T(512)S(1)} %copy-done.17, bf16[66,560]{1,0:T(8,128)(2,1)S(1)} %concatenate.68, bf16[560,512]{1,0:T(8,128)(2,1)} %param.16), kind=kOutput, calls=%fused_computation.61 | convolution fusion | flops 38049792 | bytes 852226 | tf_op jit(solution)/shard_map/dot_general | solution.py:64
  45.4 1.1 %fusion.20 = f32[66,128]{1,0:T(8,128)} fusion(bf16[66,4096]{1,0:T(8,128)(2,1)S(1)} %bitcast.88, bf16[64,4096]{1,0:T(8,128)(2,1)S(1)} %get-tuple-element.24, bf16[48,4096]{1,0:T(8,128)(2,1)S(1)} %get-tuple-element.31, bf16[16,4096]{1,0:T(8,128)(2,1)S(1)} %get-tuple-element.38), kind=kOutput, calls=%fused_computation.43 | convolution fusion | flops 72351744 | bytes 1623040 | tf_op jit(solution)/shard_map/dot_general | solution.py:39
  46.5 1.4 %fusion.61 = f32[66,256]{1,0:T(8,128)} fusion(bf16[66,4096]{1,0:T(8,128)(2,1)S(1)} %bitcast.89, bf16[256,4096]{1,0:T(8,128)(2,1)S(1)} %copy-done), kind=kOutput, calls=%fused_computation.145 | convolution fusion | flops 138412032 | bytes 2705408 | tf_op jit(solution)/shard_map/dot_general | solution.py:39
  49.9 1.5 %copy.37 = bf16[768,512]{1,0:T(8,128)(2,1)S(1)} copy(bf16[768,512]{0,1:T(8,128)(2,1)} %fusion.21) | data formatting | bytes 1572864 | tf_op jit(solution)/shard_map/dot_general | solution.py:33
  53.4 1.3 %copy-done.1 = f32[3840,128]{1,0:T(8,128)} copy-done((f32[3840,128]{1,0:T(8,128)}, f32[3840,128]{1,0:T(8,128)S(1)}, u32[]{:S(2)}) %copy-start.1) | copy-done | bytes 1966104
  55.2 2.3 %collective-permute-done.8 = f32[1920,128]{1,0:T(8,128)} collective-permute-done((f32[1920,128]{1,0:T(8,128)S(1)}, f32[1920,128]{1,0:T(8,128)}, u32[]{:S(2)}, u32[]{:S(2)}) %collective-permute-start.8) | collective-permute-done | bytes 983072 | tf_op jit(solution)/shard_map/ppermute | solution.py:188
  57.5 1.6 %dynamic-slice_add_fusion = f32[1920,128]{1,0:T(8,128)S(1)} fusion(f32[1920,128]{1,0:T(8,128)} %collective-permute-done.8, f32[3840,128]{1,0:T(8,128)} %copy-done.1, s32[]{:T(128)S(6)} %select_n.402), kind=kLoop, calls=%fused_computation.22 | loop fusion | flops 245760 | bytes 2949124 | tf_op jit(solution)/shard_map/add | solution.py:188
  60.0 2.3 %collective-permute-start.9 = (f32[480,128]{1,0:T(8,128)}, f32[480,128]{1,0:T(8,128)}, u32[]{:S(2)}, u32[]{:S(2)}) collective-permute-start(f32[480,128]{1,0:T(8,128)} %get-tuple-element.28), channel_id=1, source_target_pairs={{0,1},{1,0},{2,10},{3,11},{4,5},{5,4},{6,14},{7,15},{8,9},{9,8},{1... | collective-permute-start | bytes 737288 | tf_op jit(solution)/shard_map/ppermute | solution.py:196
  62.3 1.5 %collective-permute-start.10 = (f32[480,128]{1,0:T(8,128)}, f32[480,128]{1,0:T(8,128)}, u32[]{:S(2)}, u32[]{:S(2)}) collective-permute-start(f32[480,128]{1,0:T(8,128)} %get-tuple-element.30), channel_id=1, source_target_pairs={{0,4},{1,5},{2,18},{3,19},{4,0},{5,1},{6,22},{7,23},{8,12},{9,13},... | collective-permute-start | bytes 737288 | tf_op jit(solution)/shard_map/ppermute | solution.py:196
  63.8 5.2 %collective-permute-done.9 = f32[480,128]{1,0:T(8,128)} collective-permute-done((f32[480,128]{1,0:T(8,128)}, f32[480,128]{1,0:T(8,128)}, u32[]{:S(2)}, u32[]{:S(2)}) %collective-permute-start.9) | collective-permute-done | bytes 245792 | tf_op jit(solution)/shard_map/ppermute | solution.py:196
  69.7 1.2 %collective-permute-done.10 = f32[480,128]{1,0:T(8,128)} collective-permute-done((f32[480,128]{1,0:T(8,128)}, f32[480,128]{1,0:T(8,128)}, u32[]{:S(2)}, u32[]{:S(2)}) %collective-permute-start.10) | collective-permute-done | bytes 245792 | tf_op jit(solution)/shard_map/ppermute | solution.py:196
  70.9 1.2 %add_add_fusion = f32[480,128]{1,0:T(8,128)S(1)} fusion(f32[480,128]{1,0:T(8,128)} %collective-permute-done.11, f32[480,128]{1,0:T(8,128)} %collective-permute-done.10, f32[480,128]{1,0:T(8,128)} %collective-permute-done.9, f32[1920,128]{1,0:T(8,128)S(1)} %dynamic-slice_add_fusion, s32[]{:T(128)S(6)} %select_n.404), kind=kLoop, calls=%fused_computation.54 | loop fusion | flops 184320 | bytes 1228804 | tf_op jit(solution)/shard_map/add | solution.py:196
  73.3 1.5 %collective-permute-start.14 = (f32[120,128]{1,0:T(8,128)S(1)}, f32[120,128]{1,0:T(8,128)S(1)}, u32[]{:S(2)}, u32[]{:S(2)}) collective-permute-start(f32[120,128]{1,0:T(8,128)S(1)} %get-tuple-element.45), channel_id=1, source_target_pairs={{0,24},{1,25},{2,7},{3,6},{4,28},{5,29},{6,3},{7,2},{8,16},{9,17},... | collective-permute-start | bytes 184328 | tf_op jit(solution)/shard_map/ppermute | solution.py:196
  74.8 1.6 %collective-permute-start.13 = (f32[120,128]{1,0:T(8,128)S(1)}, f32[120,128]{1,0:T(8,128)S(1)}, u32[]{:S(2)}, u32[]{:S(2)}) collective-permute-start(f32[120,128]{1,0:T(8,128)S(1)} %get-tuple-element.46), channel_id=1, source_target_pairs={{0,16},{1,17},{2,6},{3,7},{4,20},{5,21},{6,2},{7,3},{8,24},{9,25},... | collective-permute-start | bytes 184328 | tf_op jit(solution)/shard_map/ppermute | solution.py:196
  77.1 2.2 %collective-permute-done.14 = f32[120,128]{1,0:T(8,128)S(1)} collective-permute-done((f32[120,128]{1,0:T(8,128)S(1)}, f32[120,128]{1,0:T(8,128)S(1)}, u32[]{:S(2)}, u32[]{:S(2)}) %collective-permute-start.14) | collective-permute-done | bytes 61472 | tf_op jit(solution)/shard_map/ppermute | solution.py:196
  79.3 1.3 %collective-permute-done.13 = f32[120,128]{1,0:T(8,128)S(1)} collective-permute-done((f32[120,128]{1,0:T(8,128)S(1)}, f32[120,128]{1,0:T(8,128)S(1)}, u32[]{:S(2)}, u32[]{:S(2)}) %collective-permute-start.13) | collective-permute-done | bytes 61472 | tf_op jit(solution)/shard_map/ppermute | solution.py:196
  81.5 2.3 %collective-permute-start.17 = (f32[120,128]{1,0:T(8,128)S(1)}, f32[120,128]{1,0:T(8,128)S(1)}, u32[]{:S(2)}, u32[]{:S(2)}) collective-permute-start(f32[120,128]{1,0:T(8,128)S(1)} %add_add_fusion.1), channel_id=1, source_target_pairs={{0,24},{1,25},{2,7},{3,6},{4,28},{5,29},{6,3},{7,2},{8,16},{9,17},... | collective-permute-start | bytes 184328 | tf_op jit(solution)/shard_map/ppermute | solution.py:201
  83.8 2.1 %collective-permute-start.15 = (f32[120,128]{1,0:T(8,128)S(1)}, f32[120,128]{1,0:T(8,128)S(1)}, u32[]{:S(2)}, u32[]{:S(2)}) collective-permute-start(f32[120,128]{1,0:T(8,128)S(1)} %add_add_fusion.1), channel_id=1, source_target_pairs={{0,8},{1,9},{2,3},{3,2},{4,12},{5,13},{6,7},{7,6},{8,0},{9,1},{10,... | collective-permute-start | bytes 184328 | tf_op jit(solution)/shard_map/ppermute | solution.py:201
  86.0 1.6 %collective-permute-done.17 = f32[120,128]{1,0:T(8,128)S(1)} collective-permute-done((f32[120,128]{1,0:T(8,128)S(1)}, f32[120,128]{1,0:T(8,128)S(1)}, u32[]{:S(2)}, u32[]{:S(2)}) %collective-permute-start.17) | collective-permute-done | bytes 61472 | tf_op jit(solution)/shard_map/ppermute | solution.py:201
  87.6 1.4 %collective-permute-done.16 = f32[120,128]{1,0:T(8,128)S(1)} collective-permute-done((f32[120,128]{1,0:T(8,128)S(1)}, f32[120,128]{1,0:T(8,128)S(1)}, u32[]{:S(2)}, u32[]{:S(2)}) %collective-permute-start.16) | collective-permute-done | bytes 61472 | tf_op jit(solution)/shard_map/ppermute | solution.py:201
  89.7 2.0 %collective-permute-start.20 = (f32[480,128]{1,0:T(8,128)}, f32[480,128]{1,0:T(8,128)S(1)}, u32[]{:S(2)}, u32[]{:S(2)}) collective-permute-start(f32[480,128]{1,0:T(8,128)} %pad_maximum_fusion.9), channel_id=1, source_target_pairs={{0,5},{1,4},{2,26},{3,27},{4,1},{5,0},{6,30},{7,31},{8,13},{9,12},... | collective-permute-start | bytes 737288 | tf_op jit(solution)/shard_map/ppermute | solution.py:201
  91.7 1.5 %collective-permute-start.19 = (f32[480,128]{1,0:T(8,128)}, f32[480,128]{1,0:T(8,128)S(1)}, u32[]{:S(2)}, u32[]{:S(2)}) collective-permute-start(f32[480,128]{1,0:T(8,128)} %pad_maximum_fusion.9), channel_id=1, source_target_pairs={{0,4},{1,5},{2,18},{3,19},{4,0},{5,1},{6,22},{7,23},{8,12},{9,13},... | collective-permute-start | bytes 737288 | tf_op jit(solution)/shard_map/ppermute | solution.py:201
  93.2 3.8 %collective-permute-done.20 = f32[480,128]{1,0:T(8,128)S(1)} collective-permute-done((f32[480,128]{1,0:T(8,128)}, f32[480,128]{1,0:T(8,128)S(1)}, u32[]{:S(2)}, u32[]{:S(2)}) %collective-permute-start.20) | collective-permute-done | bytes 245792 | tf_op jit(solution)/shard_map/ppermute | solution.py:201
  97.0 3.2 %collective-permute-done.19 = f32[480,128]{1,0:T(8,128)S(1)} collective-permute-done((f32[480,128]{1,0:T(8,128)}, f32[480,128]{1,0:T(8,128)S(1)}, u32[]{:S(2)}, u32[]{:S(2)}) %collective-permute-start.19) | collective-permute-done | bytes 245792 | tf_op jit(solution)/shard_map/ppermute | solution.py:201
  100.6 2.0 %collective-permute-start.21 = (f32[1920,128]{1,0:T(8,128)S(1)}, f32[1920,128]{1,0:T(8,128)S(1)}, u32[]{:S(2)}, u32[]{:S(2)}) collective-permute-start(f32[1920,128]{1,0:T(8,128)S(1)} %pad_maximum_fusion.2), channel_id=1, source_target_pairs={{0,2},{1,3},{2,0},{3,1},{4,6},{5,7},{6,4},{7,5},{8,10},{9,11},{10,... | collective-permute-start | bytes 2949128 | tf_op jit(solution)/shard_map/ppermute | solution.py:210
  (143 shorter events, 33.3 us)
Async XLA Ops:
  0.6 8.3 %copy-start.21 = (s32[1,8]{1,0:T(1,128)S(1)}, s32[1,8]{1,0:T(1,128)}, u32[]{:S(2)}) copy-start(s32[1,8]{1,0:T(1,128)} %param.13) | copy-start | bytes 100
  0.7 8.3 %copy-start.22 = (s32[1,8]{1,0:T(1,128)S(1)}, s32[1,8]{1,0:T(1,128)}, u32[]{:S(2)}) copy-start(s32[1,8]{1,0:T(1,128)} %param.14) | copy-start | bytes 100
  0.7 8.5 %copy-start.16 = (bf16[1,8,640]{2,1,0:T(8,128)(2,1)S(1)}, bf16[1,8,640]{2,1,0:T(8,128)(2,1)}, u32[]{:S(2)}) copy-start(bf16[1,8,640]{2,1,0:T(8,128)(2,1)} %param.11) | copy-start | bytes 30724
  0.7 8.5 %copy-start.19 = (s32[1,8]{1,0:T(1,128)S(1)}, s32[1,8]{1,0:T(1,128)}, u32[]{:S(2)}) copy-start(s32[1,8]{1,0:T(1,128)} %param.12) | copy-start | bytes 100
  0.7 24.3 %copy-start.2 = (bf16[1,512,256]{2,1,0:T(8,128)(2,1)S(1)}, bf16[1,512,256]{2,1,0:T(8,128)(2,1)}, u32[]{:S(2)}) copy-start(bf16[1,512,256]{2,1,0:T(8,128)(2,1)} %param.15) | copy-start | bytes 786436
  0.7 26.6 %copy-start.14 = (bf16[768,256]{1,0:T(8,128)(2,1)S(1)}, bf16[768,256]{1,0:T(8,128)(2,1)}, u32[]{:S(2)}) copy-start(bf16[768,256]{1,0:T(8,128)(2,1)} %param.20) | copy-start | bytes 1179652
  2.2 6.9 %collective-permute-start = (bf16[16,4096]{1,0:T(8,128)(2,1)S(1)}, bf16[16,4096]{1,0:T(8,128)(2,1)}, u32[]{:S(2)}, u32[]{:S(2)}) collective-permute-start(bf16[16,4096]{1,0:T(8,128)(2,1)S(1)} %constant_dynamic-slice_fusion.9), channel_id=1, source_target_pairs={{0,1},{1,0},{2,3},{3,2},{4,5},{5,4},{6,7},{7,6},{8,9},{9,8},{10,11... | collective-permute-start | bytes 393224 | tf_op jit(solution)/shard_map/ppermute | solution.py:236
  6.1 31.3 %collective-permute-start.4 = (bf16[48,4096]{1,0:T(8,128)(2,1)}, bf16[48,4096]{1,0:T(8,128)(2,1)}, u32[]{:S(2)}, u32[]{:S(2)}) collective-permute-start(bf16[48,4096]{1,0:T(8,128)(2,1)} %constant_dynamic-slice_fusion.8), channel_id=1, source_target_pairs={{0,1},{1,0},{2,3},{3,2},{4,5},{5,4},{6,7},{7,6},{8,9},{9,8},{10,11... | collective-permute-start | bytes 1179656 | tf_op jit(solution)/shard_map/ppermute | solution.py:236
  6.9 31.5 %collective-permute-start.6 = (bf16[64,4096]{1,0:T(8,128)(2,1)}, bf16[64,4096]{1,0:T(8,128)(2,1)}, u32[]{:S(2)}, u32[]{:S(2)}) collective-permute-start(bf16[64,4096]{1,0:T(8,128)(2,1)} %constant_dynamic-slice_fusion.7), channel_id=1, source_target_pairs={{0,1},{1,0},{2,3},{3,2},{4,5},{5,4},{6,7},{7,6},{8,9},{9,8},{10,11... | collective-permute-start | bytes 1572872 | tf_op jit(solution)/shard_map/ppermute | solution.py:236
  11.3 13.0 %all-to-all-start = ((bf16[16,2,321]{2,1,0:T(2,128)(2,1)}), bf16[16,2,321]{2,1,0:T(2,128)(2,1)S(1)}, u32[]{:S(2)}, u32[]{:S(2)}) async-start(bf16[16,2,321]{2,1,0:T(2,128)(2,1)} %reshape.119), calls=%async_computation | async-start | bytes 49152 | tf_op jit(solution)/shard_map/all_to_all | solution.py:280
  17.7 19.8 %collective-permute-start.3 = (bf16[16,4096]{1,0:T(8,128)(2,1)}, bf16[16,4096]{1,0:T(8,128)(2,1)}, u32[]{:S(2)}, u32[]{:S(2)}) collective-permute-start(bf16[16,4096]{1,0:T(8,128)(2,1)} %collective-permute-done), channel_id=1, source_target_pairs={{0,2},{2,0},{4,6},{6,4},{8,10},{10,8},{12,14},{14,12},{16,18},{18,... | collective-permute-start | bytes 393224 | tf_op jit(solution)/shard_map/ppermute | solution.py:237
  26.0 8.3 %collective-permute-start.2 = (bf16[4,80]{1,0:T(4,128)(2,1)S(1)}, bf16[4,80]{1,0:T(4,128)(2,1)S(1)}, u32[]{:S(2)}, u32[]{:S(2)}) collective-permute-start(bf16[4,80]{1,0:T(4,128)(2,1)S(1)} %get-tuple-element.54), channel_id=1, source_target_pairs={{1,0},{3,2},{5,4},{7,6},{9,8},{11,10},{13,12},{15,14},{17,16},{19,... | collective-permute-start | bytes 1928 | tf_op jit(solution)/shard_map/ppermute | solution.py:19
  27.8 5.7 %copy-start.8 = (bf16[256,512]{0,1:T(8,128)(2,1)S(1)}, bf16[256,512]{0,1:T(8,128)(2,1)}, u32[]{:S(2)}) copy-start(bf16[256,512]{0,1:T(8,128)(2,1)} %get-tuple-element.36) | copy-start | bytes 786436
  27.8 7.1 %copy-start.17 = (f32[512]{0:T(512)S(1)}, f32[512]{0:T(512)}, u32[]{:S(2)}) copy-start(f32[512]{0:T(512)} %param.17) | copy-start | bytes 6148
  28.9 5.8 %collective-permute-start.1 = (bf16[4,80]{1,0:T(4,128)(2,1)S(1)}, bf16[4,80]{1,0:T(4,128)(2,1)S(1)}, u32[]{:S(2)}, u32[]{:S(2)}) collective-permute-start(bf16[4,80]{1,0:T(4,128)(2,1)S(1)} %get-tuple-element.55), channel_id=1, source_target_pairs={{0,1},{2,3},{4,5},{6,7},{8,9},{10,11},{12,13},{14,15},{16,17},{18,... | collective-permute-start | bytes 1928 | tf_op jit(solution)/shard_map/ppermute | solution.py:16
  37.4 2.0 %collective-permute-start.5 = (bf16[48,4096]{1,0:T(8,128)(2,1)}, bf16[48,4096]{1,0:T(8,128)(2,1)S(1)}, u32[]{:S(2)}, u32[]{:S(2)}) collective-permute-start(bf16[48,4096]{1,0:T(8,128)(2,1)} %collective-permute-done.4), channel_id=1, source_target_pairs={{0,2},{2,0},{4,6},{6,4},{8,10},{10,8},{12,14},{14,12},{16,18},{18,... | collective-permute-start | bytes 1179656 | tf_op jit(solution)/shard_map/ppermute | solution.py:237
  38.5 2.3 %collective-permute-start.7 = (bf16[64,4096]{1,0:T(8,128)(2,1)}, bf16[64,4096]{1,0:T(8,128)(2,1)S(1)}, u32[]{:S(2)}, u32[]{:S(2)}) collective-permute-start(bf16[64,4096]{1,0:T(8,128)(2,1)} %collective-permute-done.6), channel_id=1, source_target_pairs={{0,2},{2,0},{4,6},{6,4},{8,10},{10,8},{12,14},{14,12},{16,18},{18,... | collective-permute-start | bytes 1572872 | tf_op jit(solution)/shard_map/ppermute | solution.py:237
  44.5 3.4 %copy-start.3 = (f32[518,256]{1,0:T(8,128)}, f32[518,256]{1,0:T(8,128)S(1)}, u32[]{:S(2)}) copy-start(f32[518,256]{1,0:T(8,128)S(1)} %get-tuple-element.20) | copy-start | bytes 1591300
  54.8 2.8 %collective-permute-start.8 = (f32[1920,128]{1,0:T(8,128)S(1)}, f32[1920,128]{1,0:T(8,128)}, u32[]{:S(2)}, u32[]{:S(2)}) collective-permute-start(f32[1920,128]{1,0:T(8,128)S(1)} %constant_dynamic-slice_fusion.6), channel_id=1, source_target_pairs={{0,2},{1,3},{2,0},{3,1},{4,6},{5,7},{6,4},{7,5},{8,10},{9,11},{10,... | collective-permute-start | bytes 2949128 | tf_op jit(solution)/shard_map/ppermute | solution.py:188
  60.0 8.9 %collective-permute-start.9 = (f32[480,128]{1,0:T(8,128)}, f32[480,128]{1,0:T(8,128)}, u32[]{:S(2)}, u32[]{:S(2)}) collective-permute-start(f32[480,128]{1,0:T(8,128)} %get-tuple-element.28), channel_id=1, source_target_pairs={{0,1},{1,0},{2,10},{3,11},{4,5},{5,4},{6,14},{7,15},{8,9},{9,8},{1... | collective-permute-start | bytes 737288 | tf_op jit(solution)/shard_map/ppermute | solution.py:196
  62.3 7.4 %collective-permute-start.11 = (f32[480,128]{1,0:T(8,128)}, f32[480,128]{1,0:T(8,128)}, u32[]{:S(2)}, u32[]{:S(2)}) collective-permute-start(f32[480,128]{1,0:T(8,128)} %get-tuple-element.29), channel_id=1, source_target_pairs={{0,5},{1,4},{2,26},{3,27},{4,1},{5,0},{6,30},{7,31},{8,13},{9,12},... | collective-permute-start | bytes 737288 | tf_op jit(solution)/shard_map/ppermute | solution.py:196
  62.3 8.6 %collective-permute-start.10 = (f32[480,128]{1,0:T(8,128)}, f32[480,128]{1,0:T(8,128)}, u32[]{:S(2)}, u32[]{:S(2)}) collective-permute-start(f32[480,128]{1,0:T(8,128)} %get-tuple-element.30), channel_id=1, source_target_pairs={{0,4},{1,5},{2,18},{3,19},{4,0},{5,1},{6,22},{7,23},{8,12},{9,13},... | collective-permute-start | bytes 737288 | tf_op jit(solution)/shard_map/ppermute | solution.py:196
  72.9 4.3 %collective-permute-start.12 = (f32[120,128]{1,0:T(8,128)S(1)}, f32[120,128]{1,0:T(8,128)S(1)}, u32[]{:S(2)}, u32[]{:S(2)}) collective-permute-start(f32[120,128]{1,0:T(8,128)S(1)} %get-tuple-element.44), channel_id=1, source_target_pairs={{0,8},{1,9},{2,3},{3,2},{4,12},{5,13},{6,7},{7,6},{8,0},{9,1},{10,... | collective-permute-start | bytes 184328 | tf_op jit(solution)/shard_map/ppermute | solution.py:196
  73.3 6.0 %collective-permute-start.14 = (f32[120,128]{1,0:T(8,128)S(1)}, f32[120,128]{1,0:T(8,128)S(1)}, u32[]{:S(2)}, u32[]{:S(2)}) collective-permute-start(f32[120,128]{1,0:T(8,128)S(1)} %get-tuple-element.45), channel_id=1, source_target_pairs={{0,24},{1,25},{2,7},{3,6},{4,28},{5,29},{6,3},{7,2},{8,16},{9,17},... | collective-permute-start | bytes 184328 | tf_op jit(solution)/shard_map/ppermute | solution.py:196
  74.8 5.8 %collective-permute-start.13 = (f32[120,128]{1,0:T(8,128)S(1)}, f32[120,128]{1,0:T(8,128)S(1)}, u32[]{:S(2)}, u32[]{:S(2)}) collective-permute-start(f32[120,128]{1,0:T(8,128)S(1)} %get-tuple-element.46), channel_id=1, source_target_pairs={{0,16},{1,17},{2,6},{3,7},{4,20},{5,21},{6,2},{7,3},{8,24},{9,25},... | collective-permute-start | bytes 184328 | tf_op jit(solution)/shard_map/ppermute | solution.py:196
  81.5 6.1 %collective-permute-start.17 = (f32[120,128]{1,0:T(8,128)S(1)}, f32[120,128]{1,0:T(8,128)S(1)}, u32[]{:S(2)}, u32[]{:S(2)}) collective-permute-start(f32[120,128]{1,0:T(8,128)S(1)} %add_add_fusion.1), channel_id=1, source_target_pairs={{0,24},{1,25},{2,7},{3,6},{4,28},{5,29},{6,3},{7,2},{8,16},{9,17},... | collective-permute-start | bytes 184328 | tf_op jit(solution)/shard_map/ppermute | solution.py:201
  83.8 5.1 %collective-permute-start.16 = (f32[120,128]{1,0:T(8,128)S(1)}, f32[120,128]{1,0:T(8,128)S(1)}, u32[]{:S(2)}, u32[]{:S(2)}) collective-permute-start(f32[120,128]{1,0:T(8,128)S(1)} %add_add_fusion.1), channel_id=1, source_target_pairs={{0,16},{1,17},{2,6},{3,7},{4,20},{5,21},{6,2},{7,3},{8,24},{9,25},... | collective-permute-start | bytes 184328 | tf_op jit(solution)/shard_map/ppermute | solution.py:201
  83.8 5.1 %collective-permute-start.15 = (f32[120,128]{1,0:T(8,128)S(1)}, f32[120,128]{1,0:T(8,128)S(1)}, u32[]{:S(2)}, u32[]{:S(2)}) collective-permute-start(f32[120,128]{1,0:T(8,128)S(1)} %add_add_fusion.1), channel_id=1, source_target_pairs={{0,8},{1,9},{2,3},{3,2},{4,12},{5,13},{6,7},{7,6},{8,0},{9,1},{10,... | collective-permute-start | bytes 184328 | tf_op jit(solution)/shard_map/ppermute | solution.py:201
  89.7 7.3 %collective-permute-start.20 = (f32[480,128]{1,0:T(8,128)}, f32[480,128]{1,0:T(8,128)S(1)}, u32[]{:S(2)}, u32[]{:S(2)}) collective-permute-start(f32[480,128]{1,0:T(8,128)} %pad_maximum_fusion.9), channel_id=1, source_target_pairs={{0,5},{1,4},{2,26},{3,27},{4,1},{5,0},{6,30},{7,31},{8,13},{9,12},... | collective-permute-start | bytes 737288 | tf_op jit(solution)/shard_map/ppermute | solution.py:201
  91.7 8.5 %collective-permute-start.19 = (f32[480,128]{1,0:T(8,128)}, f32[480,128]{1,0:T(8,128)S(1)}, u32[]{:S(2)}, u32[]{:S(2)}) collective-permute-start(f32[480,128]{1,0:T(8,128)} %pad_maximum_fusion.9), channel_id=1, source_target_pairs={{0,4},{1,5},{2,18},{3,19},{4,0},{5,1},{6,22},{7,23},{8,12},{9,13},... | collective-permute-start | bytes 737288 | tf_op jit(solution)/shard_map/ppermute | solution.py:201
  93.2 7.1 %collective-permute-start.18 = (f32[480,128]{1,0:T(8,128)}, f32[480,128]{1,0:T(8,128)S(1)}, u32[]{:S(2)}, u32[]{:S(2)}) collective-permute-start(f32[480,128]{1,0:T(8,128)} %pad_maximum_fusion.9), channel_id=1, source_target_pairs={{0,1},{1,0},{2,10},{3,11},{4,5},{5,4},{6,14},{7,15},{8,9},{9,8},{1... | collective-permute-start | bytes 737288 | tf_op jit(solution)/shard_map/ppermute | solution.py:201
  100.6 4.2 %collective-permute-start.21 = (f32[1920,128]{1,0:T(8,128)S(1)}, f32[1920,128]{1,0:T(8,128)S(1)}, u32[]{:S(2)}, u32[]{:S(2)}) collective-permute-start(f32[1920,128]{1,0:T(8,128)S(1)} %pad_maximum_fusion.2), channel_id=1, source_target_pairs={{0,2},{1,3},{2,0},{3,1},{4,6},{5,7},{6,4},{7,5},{8,10},{9,11},{10,... | collective-permute-start | bytes 2949128 | tf_op jit(solution)/shard_map/ppermute | solution.py:210
  (14 other events, 22.6 us)

commit v16 on v12

--- a/solution.py
+++ b/solution.py
@@ -231,10 +231,9 @@
     bounds = [0, 16, rows // 2, rows] if rows % 32 == 0 and rows > 32 else [0, rows]
     swap = [(i, i ^ 1) for i in range(dp_size)]
     got_parts, partner_parts = [], []
+    mine = jnp.where(core == 0, w_ups[:, :cols], w_ups[:, cols:])
     for lo, hi in zip(bounds, bounds[1:]):
-        block = w_ups[lo:hi]
-        mine = jnp.where(core == 0, block[:, :cols], block[:, cols:])
-        got_parts.append(lax.ppermute(mine, "tm", [(0, 1), (1, 0)]))
+        got_parts.append(lax.ppermute(mine[lo:hi], "tm", [(0, 1), (1, 0)]))
         partner_parts.append(lax.ppermute(got_parts[-1], "dp", swap))
     low = jnp.concatenate(
         [jnp.where(core == 0, g, p) for g, p in zip(got_parts, partner_parts)]

time: 97.8 us -> 96.1 us (0.983)
  other arithmetic: 13 us -> 9.66 us
  local copies, waits for them, and re-layouts: 10.2 us -> 11.8 us
    select_n x3 -> x1, other arithmetic: 5.05 us -> 1.7 us  [ups_functions(): mine = jnp.where(core == 0, w_ups[:, :cols], w_ups[:, cols:])]
    slice x0 -> x3, local copies, waits for them, and re-layouts: none -> 1.63 us  [ups_functions(): got_parts.append(lax.ppermute(mine[lo:hi], 'tm', [(0, 1), (1, 0)]))]
  transfers between devices with their start and end apart: 23 -> 23, of which waited for: 15 -> 15; matrix products, arithmetic and copies ran while one was open for 13% -> 11% of each run, Pallas kernels for 0% -> 0%
where the time goes in v16:
time: 96.1 us; the launch traced here: 95.6 us
  starting transfers between devices  36.1 us (38%)
  waiting for transfers between devices  31.1 us (32%)
  local copies, waits for them, and re-layouts  11.8 us (12%)
  other arithmetic  9.66 us (10%)
  matrix products  5.63 us (6%)
  between operations  1.32 us (1%)
    ppermute x6, waiting for transfers between devices, butterfly_psum(): total = total + lax.ppermute(send, axes, perm_of(step, offset))  11.1 us
    ppermute x6, waiting for transfers between devices, butterfly_psum(): lax.ppermute(x, axes, perm_of(step, o))  9.85 us
    ppermute x6, starting transfers between devices, butterfly_psum(): lax.ppermute(x, axes, perm_of(step, o))  8.46 us
    ppermute x6, starting transfers between devices, butterfly_psum(): total = total + lax.ppermute(send, axes, perm_of(step, offset))  7.54 us
    all_to_all x1, waiting for transfers between devices, on_device(): lax.all_to_all(outgoing, 'dp', split_axis=0, concat_axis=0, tiled=True)  6.07 us
    all_to_all x1, starting transfers between devices, on_device(): lax.all_to_all(outgoing, 'dp', split_axis=0, concat_axis=0, tiled=True)  5.91 us
    ppermute x1, starting transfers between devices, with_halo(): lax.ppermute(lax.slice_in_dim(block, block.shape[dim] - width, None, axis...  5.13 us
    ppermute x3, starting transfers between devices, ups_functions(): got_parts.append(lax.ppermute(mine[lo:hi], 'tm', [(0, 1), (1, 0)]))  5.06 us
  transfers between devices with their start and end apart: 23, of which 15 were waited for; matrix products, arithmetic and copies ran while one was open for 11% of the time, Pallas kernels for 0%

profile of v16, /device:TPU:0, one launch (start us, length us, event | category | flops | bytes accessed | tf_op | source)
XLA Modules:
  0.0 95.6 jit_solution(2598546562765946421)
XLA Ops:
  0.7 1.7 %slice_select_fusion = bf16[256,2048]{1,0:T(8,128)(2,1)S(1)} fusion(bf16[256,4096]{1,0:T(8,128)(2,1)} %param.18, pred[]{:T(512)S(6)} %eq.142), kind=kLoop, calls=%fused_computation.21 | loop fusion | flops 524288 | bytes 3145729 | tf_op jit(solution)/shard_map/jit(_where)/select_n | solution.py:234
  2.4 3.0 %collective-permute-start = (bf16[16,2048]{1,0:T(8,128)(2,1)S(1)}, bf16[16,2048]{1,0:T(8,128)(2,1)S(1)}, u32[]{:S(2)}, u32[]{:S(2)}) collective-permute-start(bf16[16,2048]{1,0:T(8,128)(2,1)S(1)} %slice.138), channel_id=1, source_target_pairs={{0,1},{1,0},{2,3},{3,2},{4,5},{5,4},{6,7},{7,6},{8,9},{9,8},{10,11... | collective-permute-start | bytes 196616 | tf_op jit(solution)/shard_map/ppermute | solution.py:236
  7.1 2.0 %collective-permute-start.6 = (bf16[128,2048]{1,0:T(8,128)(2,1)}, bf16[128,2048]{1,0:T(8,128)(2,1)}, u32[]{:S(2)}, u32[]{:S(2)}) collective-permute-start(bf16[128,2048]{1,0:T(8,128)(2,1)} %slice.151), channel_id=1, source_target_pairs={{0,1},{1,0},{2,3},{3,2},{4,5},{5,4},{6,7},{7,6},{8,9},{9,8},{10,11... | collective-permute-start | bytes 1572872 | tf_op jit(solution)/shard_map/ppermute | solution.py:236
  11.5 5.9 %all-to-all-start = ((bf16[16,2,321]{2,1,0:T(2,128)(2,1)}), bf16[16,2,321]{2,1,0:T(2,128)(2,1)S(1)}, u32[]{:S(2)}, u32[]{:S(2)}) async-start(bf16[16,2,321]{2,1,0:T(2,128)(2,1)} %reshape.119), calls=%async_computation | async-start | bytes 49152 | tf_op jit(solution)/shard_map/all_to_all | solution.py:284
  17.9 6.1 %all-to-all-done = bf16[16,2,321]{2,1,0:T(2,128)(2,1)S(1)} async-done(((bf16[16,2,321]{2,1,0:T(2,128)(2,1)}), bf16[16,2,321]{2,1,0:T(2,128)(2,1)S(1)}, u32[]{:S(2)}, u32[]{:S(2)}) %all-to-all-start) | async-done | bytes 20576 | tf_op jit(solution)/shard_map/all_to_all | solution.py:284
  25.6 1.3 %collective-permute-start.2 = (bf16[4,80]{1,0:T(4,128)(2,1)}, bf16[4,80]{1,0:T(4,128)(2,1)S(1)}, u32[]{:S(2)}, u32[]{:S(2)}) collective-permute-start(bf16[4,80]{1,0:T(4,128)(2,1)} %get-tuple-element.54), channel_id=1, source_target_pairs={{1,0},{3,2},{5,4},{7,6},{9,8},{11,10},{13,12},{15,14},{17,16},{19,... | collective-permute-start | bytes 1928 | tf_op jit(solution)/shard_map/ppermute | solution.py:19
  26.9 5.1 %collective-permute-start.1 = (bf16[4,80]{1,0:T(4,128)(2,1)}, bf16[4,80]{1,0:T(4,128)(2,1)}, u32[]{:S(2)}, u32[]{:S(2)}) collective-permute-start(bf16[4,80]{1,0:T(4,128)(2,1)} %get-tuple-element.55), channel_id=1, source_target_pairs={{0,1},{2,3},{4,5},{6,7},{8,9},{10,11},{12,13},{14,15},{16,17},{18,... | collective-permute-start | bytes 1928 | tf_op jit(solution)/shard_map/ppermute | solution.py:16
  36.1 1.1 %broadcast_select_fusion.4 = (bf16[112,2048]{1,0:T(8,128)(2,1)S(1)}, bf16[112,2048]{1,0:T(8,128)(2,1)S(1)}) fusion(bf16[112,2048]{1,0:T(8,128)(2,1)} %collective-permute-done.4, bf16[112,2048]{1,0:T(8,128)(2,1)S(1)} %collective-permute-done.5, pred[]{:T(512)S(6)} %eq.142), kind=kLoop, calls=%fused_computation.43 | loop fusion | flops 458752 | bytes 1835009 | tf_op jit(solution)/shard_map/jit(_where)/select_n | solution.py:239
  37.2 1.1 %broadcast_select_fusion.2 = (bf16[128,2048]{1,0:T(8,128)(2,1)S(1)}, bf16[128,2048]{1,0:T(8,128)(2,1)S(1)}) fusion(bf16[128,2048]{1,0:T(8,128)(2,1)} %collective-permute-done.6, bf16[128,2048]{1,0:T(8,128)(2,1)S(1)} %collective-permute-done.7, pred[]{:T(512)S(6)} %eq.142), kind=kLoop, calls=%fused_computation.41 | loop fusion | flops 524288 | bytes 2097153 | tf_op jit(solution)/shard_map/jit(_where)/select_n | solution.py:239
  38.9 1.3 %copy-done.1 = bf16[256,4096]{1,0:T(8,128)(2,1)S(1)} copy-done((bf16[256,4096]{1,0:T(8,128)(2,1)S(1)}, bf16[256,4096]{1,0:T(8,128)(2,1)}, u32[]{:S(2)}) %copy-start.1) | copy-done | bytes 2097176
  46.9 2.6 %collective-permute-done.8 = f32[1920,128]{1,0:T(8,128)} collective-permute-done((f32[1920,128]{1,0:T(8,128)S(1)}, f32[1920,128]{1,0:T(8,128)}, u32[]{:S(2)}, u32[]{:S(2)}) %collective-permute-start.8) | collective-permute-done | bytes 983072 | tf_op jit(solution)/shard_map/ppermute | solution.py:188
  49.5 1.3 %dynamic-slice_add_fusion = f32[1920,128]{1,0:T(8,128)S(1)} fusion(f32[1920,128]{1,0:T(8,128)} %collective-permute-done.8, f32[3840,128]{1,0:T(8,128)S(1)} %fusion, s32[]{:T(128)S(6)} %select_n.400), kind=kLoop, calls=%fused_computation.23 | loop fusion | flops 245760 | bytes 2949124 | tf_op jit(solution)/shard_map/add | solution.py:188
  50.9 2.4 %collective-permute-start.9 = (f32[480,128]{1,0:T(8,128)S(1)}, f32[480,128]{1,0:T(8,128)S(1)}, u32[]{:S(2)}, u32[]{:S(2)}) collective-permute-start(f32[480,128]{1,0:T(8,128)S(1)} %get-tuple-element.28), channel_id=1, source_target_pairs={{0,1},{1,0},{2,10},{3,11},{4,5},{5,4},{6,14},{7,15},{8,9},{9,8},{1... | collective-permute-start | bytes 737288 | tf_op jit(solution)/shard_map/ppermute | solution.py:196
  53.3 1.5 %collective-permute-start.10 = (f32[480,128]{1,0:T(8,128)S(1)}, f32[480,128]{1,0:T(8,128)S(1)}, u32[]{:S(2)}, u32[]{:S(2)}) collective-permute-start(f32[480,128]{1,0:T(8,128)S(1)} %get-tuple-element.30), channel_id=1, source_target_pairs={{0,4},{1,5},{2,18},{3,19},{4,0},{5,1},{6,22},{7,23},{8,12},{9,13},... | collective-permute-start | bytes 737288 | tf_op jit(solution)/shard_map/ppermute | solution.py:196
  54.9 4.8 %collective-permute-done.9 = f32[480,128]{1,0:T(8,128)S(1)} collective-permute-done((f32[480,128]{1,0:T(8,128)S(1)}, f32[480,128]{1,0:T(8,128)S(1)}, u32[]{:S(2)}, u32[]{:S(2)}) %collective-permute-start.9) | collective-permute-done | bytes 245792 | tf_op jit(solution)/shard_map/ppermute | solution.py:196
  60.4 1.3 %collective-permute-done.10 = f32[480,128]{1,0:T(8,128)S(1)} collective-permute-done((f32[480,128]{1,0:T(8,128)S(1)}, f32[480,128]{1,0:T(8,128)S(1)}, u32[]{:S(2)}, u32[]{:S(2)}) %collective-permute-start.10) | collective-permute-done | bytes 245792 | tf_op jit(solution)/shard_map/ppermute | solution.py:196
  62.2 1.5 %collective-permute-start.14 = (f32[120,128]{1,0:T(8,128)S(1)}, f32[120,128]{1,0:T(8,128)S(1)}, u32[]{:S(2)}, u32[]{:S(2)}) collective-permute-start(f32[120,128]{1,0:T(8,128)S(1)} %get-tuple-element.43), channel_id=1, source_target_pairs={{0,24},{1,25},{2,7},{3,6},{4,28},{5,29},{6,3},{7,2},{8,16},{9,17},... | collective-permute-start | bytes 184328 | tf_op jit(solution)/shard_map/ppermute | solution.py:196
  63.7 1.6 %collective-permute-start.13 = (f32[120,128]{1,0:T(8,128)S(1)}, f32[120,128]{1,0:T(8,128)S(1)}, u32[]{:S(2)}, u32[]{:S(2)}) collective-permute-start(f32[120,128]{1,0:T(8,128)S(1)} %get-tuple-element.44), channel_id=1, source_target_pairs={{0,16},{1,17},{2,6},{3,7},{4,20},{5,21},{6,2},{7,3},{8,24},{9,25},... | collective-permute-start | bytes 184328 | tf_op jit(solution)/shard_map/ppermute | solution.py:196
  66.1 2.2 %collective-permute-done.14 = f32[120,128]{1,0:T(8,128)S(1)} collective-permute-done((f32[120,128]{1,0:T(8,128)S(1)}, f32[120,128]{1,0:T(8,128)S(1)}, u32[]{:S(2)}, u32[]{:S(2)}) %collective-permute-start.14) | collective-permute-done | bytes 61472 | tf_op jit(solution)/shard_map/ppermute | solution.py:196
  68.3 1.3 %collective-permute-done.13 = f32[120,128]{1,0:T(8,128)S(1)} collective-permute-done((f32[120,128]{1,0:T(8,128)S(1)}, f32[120,128]{1,0:T(8,128)S(1)}, u32[]{:S(2)}, u32[]{:S(2)}) %collective-permute-start.13) | collective-permute-done | bytes 61472 | tf_op jit(solution)/shard_map/ppermute | solution.py:196
  69.6 2.3 %collective-permute-start.17 = (f32[120,128]{1,0:T(8,128)S(1)}, f32[120,128]{1,0:T(8,128)S(1)}, u32[]{:S(2)}, u32[]{:S(2)}) collective-permute-start(f32[120,128]{1,0:T(8,128)S(1)} %add_add_fusion.1), channel_id=1, source_target_pairs={{0,24},{1,25},{2,7},{3,6},{4,28},{5,29},{6,3},{7,2},{8,16},{9,17},... | collective-permute-start | bytes 184328 | tf_op jit(solution)/shard_map/ppermute | solution.py:201
  71.9 2.1 %collective-permute-start.15 = (f32[120,128]{1,0:T(8,128)S(1)}, f32[120,128]{1,0:T(8,128)S(1)}, u32[]{:S(2)}, u32[]{:S(2)}) collective-permute-start(f32[120,128]{1,0:T(8,128)S(1)} %add_add_fusion.1), channel_id=1, source_target_pairs={{0,8},{1,9},{2,3},{3,2},{4,12},{5,13},{6,7},{7,6},{8,0},{9,1},{10,... | collective-permute-start | bytes 184328 | tf_op jit(solution)/shard_map/ppermute | solution.py:201
  74.1 1.6 %collective-permute-done.17 = f32[120,128]{1,0:T(8,128)S(1)} collective-permute-done((f32[120,128]{1,0:T(8,128)S(1)}, f32[120,128]{1,0:T(8,128)S(1)}, u32[]{:S(2)}, u32[]{:S(2)}) %collective-permute-start.17) | collective-permute-done | bytes 61472 | tf_op jit(solution)/shard_map/ppermute | solution.py:201
  75.7 1.4 %collective-permute-done.16 = f32[120,128]{1,0:T(8,128)S(1)} collective-permute-done((f32[120,128]{1,0:T(8,128)S(1)}, f32[120,128]{1,0:T(8,128)S(1)}, u32[]{:S(2)}, u32[]{:S(2)}) %collective-permute-start.16) | collective-permute-done | bytes 61472 | tf_op jit(solution)/shard_map/ppermute | solution.py:201
  77.1 2.3 %collective-permute-start.20 = (f32[480,128]{1,0:T(8,128)S(1)}, f32[480,128]{1,0:T(8,128)S(1)}, u32[]{:S(2)}, u32[]{:S(2)}) collective-permute-start(f32[480,128]{1,0:T(8,128)S(1)} %pad_maximum_fusion.9), channel_id=1, source_target_pairs={{0,5},{1,4},{2,26},{3,27},{4,1},{5,0},{6,30},{7,31},{8,13},{9,12},... | collective-permute-start | bytes 737288 | tf_op jit(solution)/shard_map/ppermute | solution.py:201
  79.4 1.7 %collective-permute-start.19 = (f32[480,128]{1,0:T(8,128)S(1)}, f32[480,128]{1,0:T(8,128)S(1)}, u32[]{:S(2)}, u32[]{:S(2)}) collective-permute-start(f32[480,128]{1,0:T(8,128)S(1)} %pad_maximum_fusion.9), channel_id=1, source_target_pairs={{0,4},{1,5},{2,18},{3,19},{4,0},{5,1},{6,22},{7,23},{8,12},{9,13},... | collective-permute-start | bytes 737288 | tf_op jit(solution)/shard_map/ppermute | solution.py:201
  81.1 3.2 %collective-permute-done.20 = f32[480,128]{1,0:T(8,128)S(1)} collective-permute-done((f32[480,128]{1,0:T(8,128)S(1)}, f32[480,128]{1,0:T(8,128)S(1)}, u32[]{:S(2)}, u32[]{:S(2)}) %collective-permute-start.20) | collective-permute-done | bytes 245792 | tf_op jit(solution)/shard_map/ppermute | solution.py:201
  84.3 3.7 %collective-permute-done.19 = f32[480,128]{1,0:T(8,128)S(1)} collective-permute-done((f32[480,128]{1,0:T(8,128)S(1)}, f32[480,128]{1,0:T(8,128)S(1)}, u32[]{:S(2)}, u32[]{:S(2)}) %collective-permute-start.19) | collective-permute-done | bytes 245792 | tf_op jit(solution)/shard_map/ppermute | solution.py:201
  88.4 1.4 %collective-permute-start.21 = (f32[1920,128]{1,0:T(8,128)S(1)}, f32[1920,128]{1,0:T(8,128)S(1)}, u32[]{:S(2)}, u32[]{:S(2)}) collective-permute-start(f32[1920,128]{1,0:T(8,128)S(1)} %pad_maximum_fusion.2), channel_id=1, source_target_pairs={{0,2},{1,3},{2,0},{3,1},{4,6},{5,7},{6,4},{7,5},{8,10},{9,11},{10,... | collective-permute-start | bytes 2949128 | tf_op jit(solution)/shard_map/ppermute | solution.py:210
  89.8 1.1 %fusion.3 = bf16[1,512,256]{2,1,0:T(8,128)(2,1)} fusion(bf16[768,256]{1,0:T(8,128)(2,1)S(1)} %copy-done.12, f32[518,256]{1,0:T(8,128)S(1)} %copy-done.4, bf16[512,256]{1,0:T(8,128)(2,1)S(1)} %copy-done.8, bf16[512,256]{1,0:T(8,128)(2,1)S(1)} %copy-done.10, bf16[512,256]{1,0:T(8,128)(2,1)S(1)} %copy-done.6, f32[256]{0:T(256)S(1)} %copy-done.17), kind=kOutput, calls=%fused_computation.9 | convolution fusion | flops 204079104 | bytes 1967104 | tf_op jit(solution)/shard_map/dot_general | solution.py:92
  90.9 1.1 %collective-permute-done.21 = f32[1920,128]{1,0:T(8,128)S(1)} collective-permute-done((f32[1920,128]{1,0:T(8,128)S(1)}, f32[1920,128]{1,0:T(8,128)S(1)}, u32[]{:S(2)}, u32[]{:S(2)}) %collective-permute-start.21) | collective-permute-done | bytes 983072 | tf_op jit(solution)/shard_map/ppermute | solution.py:210
  94.5 1.1 %slice.165 = f32[2240,128]{1,0:T(8,128)} slice(f32[3840,128]{1,0:T(8,128)S(1)} %broadcast_select_fusion), slice={[0:2240], [0:128]} | slice | bytes 2293760 | tf_op jit(solution)/shard_map/slice | solution.py:214
  (138 shorter events, 22.2 us)
Async XLA Ops:
  0.6 33.4 %copy-start = (bf16[560,512]{1,0:T(8,128)(2,1)S(1)}, bf16[560,512]{1,0:T(8,128)(2,1)}, u32[]{:S(2)}) copy-start(bf16[560,512]{1,0:T(8,128)(2,1)} %param.16) | copy-start | bytes 1720324
  0.7 8.5 %copy-start.18 = (s32[1,8]{1,0:T(1,128)S(1)}, s32[1,8]{1,0:T(1,128)}, u32[]{:S(2)}) copy-start(s32[1,8]{1,0:T(1,128)} %param.13) | copy-start | bytes 100
  0.7 8.5 %copy-start.19 = (s32[1,8]{1,0:T(1,128)S(1)}, s32[1,8]{1,0:T(1,128)}, u32[]{:S(2)}) copy-start(s32[1,8]{1,0:T(1,128)} %param.14) | copy-start | bytes 100
  0.7 8.7 %copy-start.13 = (bf16[1,8,640]{2,1,0:T(8,128)(2,1)S(1)}, bf16[1,8,640]{2,1,0:T(8,128)(2,1)}, u32[]{:S(2)}) copy-start(bf16[1,8,640]{2,1,0:T(8,128)(2,1)} %param.11) | copy-start | bytes 30724
  0.7 8.7 %copy-start.16 = (s32[1,8]{1,0:T(1,128)S(1)}, s32[1,8]{1,0:T(1,128)}, u32[]{:S(2)}) copy-start(s32[1,8]{1,0:T(1,128)} %param.12) | copy-start | bytes 100
  2.4 22.2 %copy-start.2 = (bf16[1,512,256]{2,1,0:T(8,128)(2,1)S(1)}, bf16[1,512,256]{2,1,0:T(8,128)(2,1)}, u32[]{:S(2)}) copy-start(bf16[1,512,256]{2,1,0:T(8,128)(2,1)} %param.15) | copy-start | bytes 786436
  2.4 29.6 %copy-start.11 = (bf16[768,256]{1,0:T(8,128)(2,1)S(1)}, bf16[768,256]{1,0:T(8,128)(2,1)}, u32[]{:S(2)}) copy-start(bf16[768,256]{1,0:T(8,128)(2,1)} %param.20) | copy-start | bytes 1179652
  2.4 6.9 %collective-permute-start = (bf16[16,2048]{1,0:T(8,128)(2,1)S(1)}, bf16[16,2048]{1,0:T(8,128)(2,1)S(1)}, u32[]{:S(2)}, u32[]{:S(2)}) collective-permute-start(bf16[16,2048]{1,0:T(8,128)(2,1)S(1)} %slice.138), channel_id=1, source_target_pairs={{0,1},{1,0},{2,3},{3,2},{4,5},{5,4},{6,7},{7,6},{8,9},{9,8},{10,11... | collective-permute-start | bytes 196616 | tf_op jit(solution)/shard_map/ppermute | solution.py:236
  6.3 27.7 %collective-permute-start.4 = (bf16[112,2048]{1,0:T(8,128)(2,1)}, bf16[112,2048]{1,0:T(8,128)(2,1)}, u32[]{:S(2)}, u32[]{:S(2)}) collective-permute-start(bf16[112,2048]{1,0:T(8,128)(2,1)} %slice.150), channel_id=1, source_target_pairs={{0,1},{1,0},{2,3},{3,2},{4,5},{5,4},{6,7},{7,6},{8,9},{9,8},{10,11... | collective-permute-start | bytes 1376264 | tf_op jit(solution)/shard_map/ppermute | solution.py:236
  7.1 27.2 %collective-permute-start.6 = (bf16[128,2048]{1,0:T(8,128)(2,1)}, bf16[128,2048]{1,0:T(8,128)(2,1)}, u32[]{:S(2)}, u32[]{:S(2)}) collective-permute-start(bf16[128,2048]{1,0:T(8,128)(2,1)} %slice.151), channel_id=1, source_target_pairs={{0,1},{1,0},{2,3},{3,2},{4,5},{5,4},{6,7},{7,6},{8,9},{9,8},{10,11... | collective-permute-start | bytes 1572872 | tf_op jit(solution)/shard_map/ppermute | solution.py:236
  11.5 12.5 %all-to-all-start = ((bf16[16,2,321]{2,1,0:T(2,128)(2,1)}), bf16[16,2,321]{2,1,0:T(2,128)(2,1)S(1)}, u32[]{:S(2)}, u32[]{:S(2)}) async-start(bf16[16,2,321]{2,1,0:T(2,128)(2,1)} %reshape.119), calls=%async_computation | async-start | bytes 49152 | tf_op jit(solution)/shard_map/all_to_all | solution.py:284
  17.4 17.5 %collective-permute-start.3 = (bf16[16,2048]{1,0:T(8,128)(2,1)S(1)}, bf16[16,2048]{1,0:T(8,128)(2,1)}, u32[]{:S(2)}, u32[]{:S(2)}) collective-permute-start(bf16[16,2048]{1,0:T(8,128)(2,1)S(1)} %collective-permute-done), channel_id=1, source_target_pairs={{0,2},{2,0},{4,6},{6,4},{8,10},{10,8},{12,14},{14,12},{16,18},{18,... | collective-permute-start | bytes 196616 | tf_op jit(solution)/shard_map/ppermute | solution.py:237
  25.6 7.2 %collective-permute-start.2 = (bf16[4,80]{1,0:T(4,128)(2,1)}, bf16[4,80]{1,0:T(4,128)(2,1)S(1)}, u32[]{:S(2)}, u32[]{:S(2)}) collective-permute-start(bf16[4,80]{1,0:T(4,128)(2,1)} %get-tuple-element.54), channel_id=1, source_target_pairs={{1,0},{3,2},{5,4},{7,6},{9,8},{11,10},{13,12},{15,14},{17,16},{19,... | collective-permute-start | bytes 1928 | tf_op jit(solution)/shard_map/ppermute | solution.py:19
  26.9 6.0 %collective-permute-start.1 = (bf16[4,80]{1,0:T(4,128)(2,1)}, bf16[4,80]{1,0:T(4,128)(2,1)}, u32[]{:S(2)}, u32[]{:S(2)}) collective-permute-start(bf16[4,80]{1,0:T(4,128)(2,1)} %get-tuple-element.55), channel_id=1, source_target_pairs={{0,1},{2,3},{4,5},{6,7},{8,9},{10,11},{12,13},{14,15},{16,17},{18,... | collective-permute-start | bytes 1928 | tf_op jit(solution)/shard_map/ppermute | solution.py:16
  34.0 2.1 %collective-permute-start.5 = (bf16[112,2048]{1,0:T(8,128)(2,1)}, bf16[112,2048]{1,0:T(8,128)(2,1)S(1)}, u32[]{:S(2)}, u32[]{:S(2)}) collective-permute-start(bf16[112,2048]{1,0:T(8,128)(2,1)} %collective-permute-done.4), channel_id=1, source_target_pairs={{0,2},{2,0},{4,6},{6,4},{8,10},{10,8},{12,14},{14,12},{16,18},{18,... | collective-permute-start | bytes 1376264 | tf_op jit(solution)/shard_map/ppermute | solution.py:237
  34.4 2.8 %collective-permute-start.7 = (bf16[128,2048]{1,0:T(8,128)(2,1)}, bf16[128,2048]{1,0:T(8,128)(2,1)S(1)}, u32[]{:S(2)}, u32[]{:S(2)}) collective-permute-start(bf16[128,2048]{1,0:T(8,128)(2,1)} %collective-permute-done.6), channel_id=1, source_target_pairs={{0,2},{2,0},{4,6},{6,4},{8,10},{10,8},{12,14},{14,12},{16,18},{18,... | collective-permute-start | bytes 1572872 | tf_op jit(solution)/shard_map/ppermute | solution.py:237
  42.1 1.6 %copy-start.3 = (f32[518,256]{1,0:T(8,128)}, f32[518,256]{1,0:T(8,128)S(1)}, u32[]{:S(2)}) copy-start(f32[518,256]{1,0:T(8,128)S(1)} %get-tuple-element.20) | copy-start | bytes 1591300
  46.7 2.8 %collective-permute-start.8 = (f32[1920,128]{1,0:T(8,128)S(1)}, f32[1920,128]{1,0:T(8,128)}, u32[]{:S(2)}, u32[]{:S(2)}) collective-permute-start(f32[1920,128]{1,0:T(8,128)S(1)} %constant_dynamic-slice_fusion.6), channel_id=1, source_target_pairs={{0,2},{1,3},{2,0},{3,1},{4,6},{5,7},{6,4},{7,5},{8,10},{9,11},{10,... | collective-permute-start | bytes 2949128 | tf_op jit(solution)/shard_map/ppermute | solution.py:188
  50.9 8.8 %collective-permute-start.9 = (f32[480,128]{1,0:T(8,128)S(1)}, f32[480,128]{1,0:T(8,128)S(1)}, u32[]{:S(2)}, u32[]{:S(2)}) collective-permute-start(f32[480,128]{1,0:T(8,128)S(1)} %get-tuple-element.28), channel_id=1, source_target_pairs={{0,1},{1,0},{2,10},{3,11},{4,5},{5,4},{6,14},{7,15},{8,9},{9,8},{1... | collective-permute-start | bytes 737288 | tf_op jit(solution)/shard_map/ppermute | solution.py:196
  53.3 7.1 %collective-permute-start.11 = (f32[480,128]{1,0:T(8,128)S(1)}, f32[480,128]{1,0:T(8,128)S(1)}, u32[]{:S(2)}, u32[]{:S(2)}) collective-permute-start(f32[480,128]{1,0:T(8,128)S(1)} %get-tuple-element.29), channel_id=1, source_target_pairs={{0,5},{1,4},{2,26},{3,27},{4,1},{5,0},{6,30},{7,31},{8,13},{9,12},... | collective-permute-start | bytes 737288 | tf_op jit(solution)/shard_map/ppermute | solution.py:196
  53.3 8.4 %collective-permute-start.10 = (f32[480,128]{1,0:T(8,128)S(1)}, f32[480,128]{1,0:T(8,128)S(1)}, u32[]{:S(2)}, u32[]{:S(2)}) collective-permute-start(f32[480,128]{1,0:T(8,128)S(1)} %get-tuple-element.30), channel_id=1, source_target_pairs={{0,4},{1,5},{2,18},{3,19},{4,0},{5,1},{6,22},{7,23},{8,12},{9,13},... | collective-permute-start | bytes 737288 | tf_op jit(solution)/shard_map/ppermute | solution.py:196
  61.8 4.3 %collective-permute-start.12 = (f32[120,128]{1,0:T(8,128)S(1)}, f32[120,128]{1,0:T(8,128)S(1)}, u32[]{:S(2)}, u32[]{:S(2)}) collective-permute-start(f32[120,128]{1,0:T(8,128)S(1)} %get-tuple-element.42), channel_id=1, source_target_pairs={{0,8},{1,9},{2,3},{3,2},{4,12},{5,13},{6,7},{7,6},{8,0},{9,1},{10,... | collective-permute-start | bytes 184328 | tf_op jit(solution)/shard_map/ppermute | solution.py:196
  62.2 6.0 %collective-permute-start.14 = (f32[120,128]{1,0:T(8,128)S(1)}, f32[120,128]{1,0:T(8,128)S(1)}, u32[]{:S(2)}, u32[]{:S(2)}) collective-permute-start(f32[120,128]{1,0:T(8,128)S(1)} %get-tuple-element.43), channel_id=1, source_target_pairs={{0,24},{1,25},{2,7},{3,6},{4,28},{5,29},{6,3},{7,2},{8,16},{9,17},... | collective-permute-start | bytes 184328 | tf_op jit(solution)/shard_map/ppermute | solution.py:196
  63.7 5.8 %collective-permute-start.13 = (f32[120,128]{1,0:T(8,128)S(1)}, f32[120,128]{1,0:T(8,128)S(1)}, u32[]{:S(2)}, u32[]{:S(2)}) collective-permute-start(f32[120,128]{1,0:T(8,128)S(1)} %get-tuple-element.44), channel_id=1, source_target_pairs={{0,16},{1,17},{2,6},{3,7},{4,20},{5,21},{6,2},{7,3},{8,24},{9,25},... | collective-permute-start | bytes 184328 | tf_op jit(solution)/shard_map/ppermute | solution.py:196
  69.6 6.1 %collective-permute-start.17 = (f32[120,128]{1,0:T(8,128)S(1)}, f32[120,128]{1,0:T(8,128)S(1)}, u32[]{:S(2)}, u32[]{:S(2)}) collective-permute-start(f32[120,128]{1,0:T(8,128)S(1)} %add_add_fusion.1), channel_id=1, source_target_pairs={{0,24},{1,25},{2,7},{3,6},{4,28},{5,29},{6,3},{7,2},{8,16},{9,17},... | collective-permute-start | bytes 184328 | tf_op jit(solution)/shard_map/ppermute | solution.py:201
  71.9 5.1 %collective-permute-start.16 = (f32[120,128]{1,0:T(8,128)S(1)}, f32[120,128]{1,0:T(8,128)S(1)}, u32[]{:S(2)}, u32[]{:S(2)}) collective-permute-start(f32[120,128]{1,0:T(8,128)S(1)} %add_add_fusion.1), channel_id=1, source_target_pairs={{0,16},{1,17},{2,6},{3,7},{4,20},{5,21},{6,2},{7,3},{8,24},{9,25},... | collective-permute-start | bytes 184328 | tf_op jit(solution)/shard_map/ppermute | solution.py:201
  71.9 5.1 %collective-permute-start.15 = (f32[120,128]{1,0:T(8,128)S(1)}, f32[120,128]{1,0:T(8,128)S(1)}, u32[]{:S(2)}, u32[]{:S(2)}) collective-permute-start(f32[120,128]{1,0:T(8,128)S(1)} %add_add_fusion.1), channel_id=1, source_target_pairs={{0,8},{1,9},{2,3},{3,2},{4,12},{5,13},{6,7},{7,6},{8,0},{9,1},{10,... | collective-permute-start | bytes 184328 | tf_op jit(solution)/shard_map/ppermute | solution.py:201
  77.1 7.2 %collective-permute-start.20 = (f32[480,128]{1,0:T(8,128)S(1)}, f32[480,128]{1,0:T(8,128)S(1)}, u32[]{:S(2)}, u32[]{:S(2)}) collective-permute-start(f32[480,128]{1,0:T(8,128)S(1)} %pad_maximum_fusion.9), channel_id=1, source_target_pairs={{0,5},{1,4},{2,26},{3,27},{4,1},{5,0},{6,30},{7,31},{8,13},{9,12},... | collective-permute-start | bytes 737288 | tf_op jit(solution)/shard_map/ppermute | solution.py:201
  79.4 8.5 %collective-permute-start.19 = (f32[480,128]{1,0:T(8,128)S(1)}, f32[480,128]{1,0:T(8,128)S(1)}, u32[]{:S(2)}, u32[]{:S(2)}) collective-permute-start(f32[480,128]{1,0:T(8,128)S(1)} %pad_maximum_fusion.9), channel_id=1, source_target_pairs={{0,4},{1,5},{2,18},{3,19},{4,0},{5,1},{6,22},{7,23},{8,12},{9,13},... | collective-permute-start | bytes 737288 | tf_op jit(solution)/shard_map/ppermute | solution.py:201
  81.1 6.8 %collective-permute-start.18 = (f32[480,128]{1,0:T(8,128)S(1)}, f32[480,128]{1,0:T(8,128)S(1)}, u32[]{:S(2)}, u32[]{:S(2)}) collective-permute-start(f32[480,128]{1,0:T(8,128)S(1)} %pad_maximum_fusion.9), channel_id=1, source_target_pairs={{0,1},{1,0},{2,10},{3,11},{4,5},{5,4},{6,14},{7,15},{8,9},{9,8},{1... | collective-permute-start | bytes 737288 | tf_op jit(solution)/shard_map/ppermute | solution.py:201
  88.2 1.6 %copy-start.4 = (f32[518,256]{1,0:T(8,128)S(1)}, f32[518,256]{1,0:T(8,128)}, u32[]{:S(2)}) copy-start(f32[518,256]{1,0:T(8,128)} %copy-done.3) | copy-start | bytes 1591300
  88.4 3.6 %collective-permute-start.21 = (f32[1920,128]{1,0:T(8,128)S(1)}, f32[1920,128]{1,0:T(8,128)S(1)}, u32[]{:S(2)}, u32[]{:S(2)}) collective-permute-start(f32[1920,128]{1,0:T(8,128)S(1)} %pad_maximum_fusion.2), channel_id=1, source_target_pairs={{0,2},{1,3},{2,0},{3,1},{4,6},{5,7},{6,4},{7,5},{8,10},{9,11},{10,... | collective-permute-start | bytes 2949128 | tf_op jit(solution)/shard_map/ppermute | solution.py:210
  (11 other events, 14.2 us)

commit v17 on v16

--- a/solution.py
+++ b/solution.py
@@ -233,7 +233,10 @@
     got_parts, partner_parts = [], []
     mine = jnp.where(core == 0, w_ups[:, :cols], w_ups[:, cols:])
     for lo, hi in zip(bounds, bounds[1:]):
-        got_parts.append(lax.ppermute(mine[lo:hi], "tm", [(0, 1), (1, 0)]))
+        piece = mine[lo:hi]
+        if len(got_parts) > 1:
+            piece, _ = lax.optimization_barrier((piece, got_parts[-1]))
+        got_parts.append(lax.ppermute(piece, "tm", [(0, 1), (1, 0)]))
         partner_parts.append(lax.ppermute(got_parts[-1], "dp", swap))
     low = jnp.concatenate(
         [jnp.where(core == 0, g, p) for g, p in zip(got_parts, partner_parts)]

time: 96.1 us -> 104 us (1.082)
  waiting for transfers between devices: 31.1 us -> 43 us
  starting transfers between devices: 36.1 us -> 34.4 us
  other arithmetic: 9.66 us -> 7.99 us
    ppermute x3, waiting for transfers between devices: 0.01 us -> 11.7 us  [ups_functions(): got_parts.append(lax.ppermute(piece, 'tm', [(0, 1), (1, 0)]))]
  transfers between devices with their start and end apart: 23 -> 23, of which waited for: 15 -> 16; matrix products, arithmetic and copies ran while one was open for 11% -> 8% of each run, Pallas kernels for 0% -> 0%
where the time goes in v17:
time: 104 us
  waiting for transfers between devices  43 us (41%)
  starting transfers between devices  34.4 us (33%)
  local copies, waits for them, and re-layouts  11.5 us (11%)
  other arithmetic  7.99 us (8%)
  matrix products  5.64 us (5%)
  between operations  1.29 us (1%)
    ppermute x3, waiting for transfers between devices, ups_functions(): got_parts.append(lax.ppermute(piece, 'tm', [(0, 1), (1, 0)]))  11.7 us
    ppermute x6, waiting for transfers between devices, butterfly_psum(): total = total + lax.ppermute(send, axes, perm_of(step, offset))  11.5 us
    ppermute x6, waiting for transfers between devices, butterfly_psum(): lax.ppermute(x, axes, perm_of(step, o))  9.79 us
    ppermute x6, starting transfers between devices, butterfly_psum(): lax.ppermute(x, axes, perm_of(step, o))  8.27 us
    ppermute x6, starting transfers between devices, butterfly_psum(): total = total + lax.ppermute(send, axes, perm_of(step, offset))  7.11 us
    all_to_all x1, starting transfers between devices, on_device(): lax.all_to_all(outgoing, 'dp', split_axis=0, concat_axis=0, tiled=True)  6.17 us
    ppermute x3, starting transfers between devices, ups_functions(): got_parts.append(lax.ppermute(piece, 'tm', [(0, 1), (1, 0)]))  5.38 us
    all_to_all x1, waiting for transfers between devices, on_device(): lax.all_to_all(outgoing, 'dp', split_axis=0, concat_axis=0, tiled=True)  5.31 us
  transfers between devices with their start and end apart: 23, of which 16 were waited for; matrix products, arithmetic and copies ran while one was open for 8% of the time, Pallas kernels for 0%

profile of v17, /device:TPU:0, one launch (start us, length us, event | category | flops | bytes accessed | tf_op | source)
XLA Modules:
  0.0 103.8 jit_solution(16758746886540363081)
XLA Ops:
  0.7 1.7 %slice_select_fusion = bf16[256,2048]{1,0:T(8,128)(2,1)S(1)} fusion(bf16[256,4096]{1,0:T(8,128)(2,1)} %param.18, pred[]{:T(512)S(6)} %eq.142), kind=kLoop, calls=%fused_computation.21 | loop fusion | flops 524288 | bytes 3145729 | tf_op jit(solution)/shard_map/jit(_where)/select_n | solution.py:234
  2.4 3.0 %collective-permute-start = (bf16[16,2048]{1,0:T(8,128)(2,1)S(1)}, bf16[16,2048]{1,0:T(8,128)(2,1)S(1)}, u32[]{:S(2)}, u32[]{:S(2)}) collective-permute-start(bf16[16,2048]{1,0:T(8,128)(2,1)S(1)} %slice.138), channel_id=1, source_target_pairs={{0,1},{1,0},{2,3},{3,2},{4,5},{5,4},{6,7},{7,6},{8,9},{9,8},{10,11... | collective-permute-start | bytes 196616 | tf_op jit(solution)/shard_map/ppermute | solution.py:239
  6.5 1.4 %collective-permute-done = bf16[16,2048]{1,0:T(8,128)(2,1)S(1)} collective-permute-done((bf16[16,2048]{1,0:T(8,128)(2,1)S(1)}, bf16[16,2048]{1,0:T(8,128)(2,1)S(1)}, u32[]{:S(2)}, u32[]{:S(2)}) %collective-permute-start) | collective-permute-done | bytes 65568 | tf_op jit(solution)/shard_map/ppermute | solution.py:239
  10.0 6.2 %all-to-all-start = ((bf16[16,2,321]{2,1,0:T(2,128)(2,1)}), bf16[16,2,321]{2,1,0:T(2,128)(2,1)S(1)}, u32[]{:S(2)}, u32[]{:S(2)}) async-start(bf16[16,2,321]{2,1,0:T(2,128)(2,1)} %reshape.119), calls=%async_computation | async-start | bytes 49152 | tf_op jit(solution)/shard_map/all_to_all | solution.py:287
  17.5 5.3 %all-to-all-done = bf16[16,2,321]{2,1,0:T(2,128)(2,1)S(1)} async-done(((bf16[16,2,321]{2,1,0:T(2,128)(2,1)}), bf16[16,2,321]{2,1,0:T(2,128)(2,1)S(1)}, u32[]{:S(2)}, u32[]{:S(2)}) %all-to-all-start) | async-done | bytes 20576 | tf_op jit(solution)/shard_map/all_to_all | solution.py:287
  23.6 1.3 %collective-permute-start.2 = (bf16[4,80]{1,0:T(4,128)(2,1)S(1)}, bf16[4,80]{1,0:T(4,128)(2,1)S(1)}, u32[]{:S(2)}, u32[]{:S(2)}) collective-permute-start(bf16[4,80]{1,0:T(4,128)(2,1)S(1)} %get-tuple-element.56), channel_id=1, source_target_pairs={{1,0},{3,2},{5,4},{7,6},{9,8},{11,10},{13,12},{15,14},{17,16},{19,... | collective-permute-start | bytes 1928 | tf_op jit(solution)/shard_map/ppermute | solution.py:19
  24.9 4.5 %collective-permute-start.1 = (bf16[4,80]{1,0:T(4,128)(2,1)S(1)}, bf16[4,80]{1,0:T(4,128)(2,1)S(1)}, u32[]{:S(2)}, u32[]{:S(2)}) collective-permute-start(bf16[4,80]{1,0:T(4,128)(2,1)S(1)} %get-tuple-element.57), channel_id=1, source_target_pairs={{0,1},{2,3},{4,5},{6,7},{8,9},{10,11},{12,13},{14,15},{16,17},{18,... | collective-permute-start | bytes 1928 | tf_op jit(solution)/shard_map/ppermute | solution.py:16
  30.8 2.3 %collective-permute-start.6 = (bf16[128,2048]{1,0:T(8,128)(2,1)}, bf16[128,2048]{1,0:T(8,128)(2,1)}, u32[]{:S(2)}, u32[]{:S(2)}) collective-permute-start(bf16[128,2048]{1,0:T(8,128)(2,1)} %slice.151), channel_id=1, source_target_pairs={{0,1},{1,0},{2,3},{3,2},{4,5},{5,4},{6,7},{7,6},{8,9},{9,8},{10,11... | collective-permute-start | bytes 1572872 | tf_op jit(solution)/shard_map/ppermute | solution.py:239
  33.6 10.3 %collective-permute-done.6 = bf16[128,2048]{1,0:T(8,128)(2,1)} collective-permute-done((bf16[128,2048]{1,0:T(8,128)(2,1)}, bf16[128,2048]{1,0:T(8,128)(2,1)}, u32[]{:S(2)}, u32[]{:S(2)}) %collective-permute-start.6) | collective-permute-done | bytes 524320 | tf_op jit(solution)/shard_map/ppermute | solution.py:239
  44.0 1.1 %broadcast_select_fusion.4 = (bf16[112,2048]{1,0:T(8,128)(2,1)S(1)}, bf16[112,2048]{1,0:T(8,128)(2,1)S(1)}) fusion(bf16[112,2048]{1,0:T(8,128)(2,1)} %collective-permute-done.4, bf16[112,2048]{1,0:T(8,128)(2,1)S(1)} %collective-permute-done.5, pred[]{:T(512)S(6)} %eq.142), kind=kLoop, calls=%fused_computation.43 | loop fusion | flops 458752 | bytes 1835009 | tf_op jit(solution)/shard_map/jit(_where)/select_n | solution.py:242
  46.1 1.1 %broadcast_select_fusion.2 = (bf16[128,2048]{1,0:T(8,128)(2,1)S(1)}, bf16[128,2048]{1,0:T(8,128)(2,1)S(1)}) fusion(bf16[128,2048]{1,0:T(8,128)(2,1)} %collective-permute-done.6, bf16[128,2048]{1,0:T(8,128)(2,1)S(1)} %collective-permute-done.7, pred[]{:T(512)S(6)} %eq.142), kind=kLoop, calls=%fused_computation.41 | loop fusion | flops 524288 | bytes 2097153 | tf_op jit(solution)/shard_map/jit(_where)/select_n | solution.py:242
  47.8 1.3 %copy-done.1 = bf16[256,4096]{1,0:T(8,128)(2,1)S(1)} copy-done((bf16[256,4096]{1,0:T(8,128)(2,1)S(1)}, bf16[256,4096]{1,0:T(8,128)(2,1)}, u32[]{:S(2)}) %copy-start.1) | copy-done | bytes 2097176
  55.8 2.6 %collective-permute-done.8 = f32[1920,128]{1,0:T(8,128)} collective-permute-done((f32[1920,128]{1,0:T(8,128)S(1)}, f32[1920,128]{1,0:T(8,128)}, u32[]{:S(2)}, u32[]{:S(2)}) %collective-permute-start.8) | collective-permute-done | bytes 983072 | tf_op jit(solution)/shard_map/ppermute | solution.py:188
  58.4 1.3 %dynamic-slice_add_fusion = f32[1920,128]{1,0:T(8,128)S(1)} fusion(f32[1920,128]{1,0:T(8,128)} %collective-permute-done.8, f32[3840,128]{1,0:T(8,128)S(1)} %fusion, s32[]{:T(128)S(6)} %select_n.400), kind=kLoop, calls=%fused_computation.23 | loop fusion | flops 245760 | bytes 2949124 | tf_op jit(solution)/shard_map/add | solution.py:188
  59.8 1.7 %collective-permute-start.9 = (f32[480,128]{1,0:T(8,128)S(1)}, f32[480,128]{1,0:T(8,128)S(1)}, u32[]{:S(2)}, u32[]{:S(2)}) collective-permute-start(f32[480,128]{1,0:T(8,128)S(1)} %get-tuple-element.30), channel_id=1, source_target_pairs={{0,1},{1,0},{2,10},{3,11},{4,5},{5,4},{6,14},{7,15},{8,9},{9,8},{1... | collective-permute-start | bytes 737288 | tf_op jit(solution)/shard_map/ppermute | solution.py:196
  62.1 1.2 %collective-permute-start.10 = (f32[480,128]{1,0:T(8,128)S(1)}, f32[480,128]{1,0:T(8,128)S(1)}, u32[]{:S(2)}, u32[]{:S(2)}) collective-permute-start(f32[480,128]{1,0:T(8,128)S(1)} %get-tuple-element.32), channel_id=1, source_target_pairs={{0,4},{1,5},{2,18},{3,19},{4,0},{5,1},{6,22},{7,23},{8,12},{9,13},... | collective-permute-start | bytes 737288 | tf_op jit(solution)/shard_map/ppermute | solution.py:196
  63.3 5.3 %collective-permute-done.9 = f32[480,128]{1,0:T(8,128)S(1)} collective-permute-done((f32[480,128]{1,0:T(8,128)S(1)}, f32[480,128]{1,0:T(8,128)S(1)}, u32[]{:S(2)}, u32[]{:S(2)}) %collective-permute-start.9) | collective-permute-done | bytes 245792 | tf_op jit(solution)/shard_map/ppermute | solution.py:196
  68.7 1.5 %collective-permute-done.10 = f32[480,128]{1,0:T(8,128)S(1)} collective-permute-done((f32[480,128]{1,0:T(8,128)S(1)}, f32[480,128]{1,0:T(8,128)S(1)}, u32[]{:S(2)}, u32[]{:S(2)}) %collective-permute-start.10) | collective-permute-done | bytes 245792 | tf_op jit(solution)/shard_map/ppermute | solution.py:196
  71.1 1.5 %collective-permute-start.14 = (f32[120,128]{1,0:T(8,128)S(1)}, f32[120,128]{1,0:T(8,128)S(1)}, u32[]{:S(2)}, u32[]{:S(2)}) collective-permute-start(f32[120,128]{1,0:T(8,128)S(1)} %get-tuple-element.45), channel_id=1, source_target_pairs={{0,24},{1,25},{2,7},{3,6},{4,28},{5,29},{6,3},{7,2},{8,16},{9,17},... | collective-permute-start | bytes 184328 | tf_op jit(solution)/shard_map/ppermute | solution.py:196
  72.6 1.2 %collective-permute-start.13 = (f32[120,128]{1,0:T(8,128)S(1)}, f32[120,128]{1,0:T(8,128)S(1)}, u32[]{:S(2)}, u32[]{:S(2)}) collective-permute-start(f32[120,128]{1,0:T(8,128)S(1)} %get-tuple-element.46), channel_id=1, source_target_pairs={{0,16},{1,17},{2,6},{3,7},{4,20},{5,21},{6,2},{7,3},{8,24},{9,25},... | collective-permute-start | bytes 184328 | tf_op jit(solution)/shard_map/ppermute | solution.py:196
  73.8 1.1 %collective-permute-done.12 = f32[120,128]{1,0:T(8,128)S(1)} collective-permute-done((f32[120,128]{1,0:T(8,128)S(1)}, f32[120,128]{1,0:T(8,128)S(1)}, u32[]{:S(2)}, u32[]{:S(2)}) %collective-permute-start.12) | collective-permute-done | bytes 61472 | tf_op jit(solution)/shard_map/ppermute | solution.py:196
  74.9 2.2 %collective-permute-done.14 = f32[120,128]{1,0:T(8,128)S(1)} collective-permute-done((f32[120,128]{1,0:T(8,128)S(1)}, f32[120,128]{1,0:T(8,128)S(1)}, u32[]{:S(2)}, u32[]{:S(2)}) %collective-permute-start.14) | collective-permute-done | bytes 61472 | tf_op jit(solution)/shard_map/ppermute | solution.py:196
  77.1 1.3 %collective-permute-done.13 = f32[120,128]{1,0:T(8,128)S(1)} collective-permute-done((f32[120,128]{1,0:T(8,128)S(1)}, f32[120,128]{1,0:T(8,128)S(1)}, u32[]{:S(2)}, u32[]{:S(2)}) %collective-permute-start.13) | collective-permute-done | bytes 61472 | tf_op jit(solution)/shard_map/ppermute | solution.py:196
  78.5 2.1 %collective-permute-start.17 = (f32[120,128]{1,0:T(8,128)S(1)}, f32[120,128]{1,0:T(8,128)S(1)}, u32[]{:S(2)}, u32[]{:S(2)}) collective-permute-start(f32[120,128]{1,0:T(8,128)S(1)} %add_add_fusion.1), channel_id=1, source_target_pairs={{0,24},{1,25},{2,7},{3,6},{4,28},{5,29},{6,3},{7,2},{8,16},{9,17},... | collective-permute-start | bytes 184328 | tf_op jit(solution)/shard_map/ppermute | solution.py:201
  80.6 2.3 %collective-permute-start.15 = (f32[120,128]{1,0:T(8,128)S(1)}, f32[120,128]{1,0:T(8,128)S(1)}, u32[]{:S(2)}, u32[]{:S(2)}) collective-permute-start(f32[120,128]{1,0:T(8,128)S(1)} %add_add_fusion.1), channel_id=1, source_target_pairs={{0,8},{1,9},{2,3},{3,2},{4,12},{5,13},{6,7},{7,6},{8,0},{9,1},{10,... | collective-permute-start | bytes 184328 | tf_op jit(solution)/shard_map/ppermute | solution.py:201
  82.9 1.6 %collective-permute-done.17 = f32[120,128]{1,0:T(8,128)S(1)} collective-permute-done((f32[120,128]{1,0:T(8,128)S(1)}, f32[120,128]{1,0:T(8,128)S(1)}, u32[]{:S(2)}, u32[]{:S(2)}) %collective-permute-start.17) | collective-permute-done | bytes 61472 | tf_op jit(solution)/shard_map/ppermute | solution.py:201
  84.6 1.3 %collective-permute-done.16 = f32[120,128]{1,0:T(8,128)S(1)} collective-permute-done((f32[120,128]{1,0:T(8,128)S(1)}, f32[120,128]{1,0:T(8,128)S(1)}, u32[]{:S(2)}, u32[]{:S(2)}) %collective-permute-start.16) | collective-permute-done | bytes 61472 | tf_op jit(solution)/shard_map/ppermute | solution.py:201
  85.9 2.3 %collective-permute-start.20 = (f32[480,128]{1,0:T(8,128)S(1)}, f32[480,128]{1,0:T(8,128)S(1)}, u32[]{:S(2)}, u32[]{:S(2)}) collective-permute-start(f32[480,128]{1,0:T(8,128)S(1)} %pad_maximum_fusion.9), channel_id=1, source_target_pairs={{0,5},{1,4},{2,26},{3,27},{4,1},{5,0},{6,30},{7,31},{8,13},{9,12},... | collective-permute-start | bytes 737288 | tf_op jit(solution)/shard_map/ppermute | solution.py:201
  88.2 1.5 %collective-permute-start.19 = (f32[480,128]{1,0:T(8,128)S(1)}, f32[480,128]{1,0:T(8,128)S(1)}, u32[]{:S(2)}, u32[]{:S(2)}) collective-permute-start(f32[480,128]{1,0:T(8,128)S(1)} %pad_maximum_fusion.9), channel_id=1, source_target_pairs={{0,4},{1,5},{2,18},{3,19},{4,0},{5,1},{6,22},{7,23},{8,12},{9,13},... | collective-permute-start | bytes 737288 | tf_op jit(solution)/shard_map/ppermute | solution.py:201
  89.8 3.3 %collective-permute-done.20 = f32[480,128]{1,0:T(8,128)S(1)} collective-permute-done((f32[480,128]{1,0:T(8,128)S(1)}, f32[480,128]{1,0:T(8,128)S(1)}, u32[]{:S(2)}, u32[]{:S(2)}) %collective-permute-start.20) | collective-permute-done | bytes 245792 | tf_op jit(solution)/shard_map/ppermute | solution.py:201
  93.1 3.5 %collective-permute-done.19 = f32[480,128]{1,0:T(8,128)S(1)} collective-permute-done((f32[480,128]{1,0:T(8,128)S(1)}, f32[480,128]{1,0:T(8,128)S(1)}, u32[]{:S(2)}, u32[]{:S(2)}) %collective-permute-start.19) | collective-permute-done | bytes 245792 | tf_op jit(solution)/shard_map/ppermute | solution.py:201
  98.2 1.1 %fusion.3 = bf16[1,512,256]{2,1,0:T(8,128)(2,1)} fusion(bf16[768,256]{1,0:T(8,128)(2,1)S(1)} %copy-done.12, f32[518,256]{1,0:T(8,128)S(1)} %copy-done.4, bf16[512,256]{1,0:T(8,128)(2,1)S(1)} %copy-done.8, bf16[512,256]{1,0:T(8,128)(2,1)S(1)} %copy-done.10, bf16[512,256]{1,0:T(8,128)(2,1)S(1)} %copy-done.6, f32[256]{0:T(256)S(1)} %copy-done.17), kind=kOutput, calls=%fused_computation.9 | convolution fusion | flops 204079104 | bytes 1967104 | tf_op jit(solution)/shard_map/dot_general | solution.py:92
  (138 shorter events, 22.8 us)
Async XLA Ops:
  0.6 32.7 %copy-start = (bf16[560,512]{1,0:T(8,128)(2,1)S(1)}, bf16[560,512]{1,0:T(8,128)(2,1)}, u32[]{:S(2)}) copy-start(bf16[560,512]{1,0:T(8,128)(2,1)} %param.16) | copy-start | bytes 1720324
  0.7 5.6 %copy-start.18 = (s32[1,8]{1,0:T(1,128)S(1)}, s32[1,8]{1,0:T(1,128)}, u32[]{:S(2)}) copy-start(s32[1,8]{1,0:T(1,128)} %param.13) | copy-start | bytes 100
  0.7 5.6 %copy-start.19 = (s32[1,8]{1,0:T(1,128)S(1)}, s32[1,8]{1,0:T(1,128)}, u32[]{:S(2)}) copy-start(s32[1,8]{1,0:T(1,128)} %param.14) | copy-start | bytes 100
  0.7 7.3 %copy-start.13 = (bf16[1,8,640]{2,1,0:T(8,128)(2,1)S(1)}, bf16[1,8,640]{2,1,0:T(8,128)(2,1)}, u32[]{:S(2)}) copy-start(bf16[1,8,640]{2,1,0:T(8,128)(2,1)} %param.11) | copy-start | bytes 30724
  0.7 7.3 %copy-start.16 = (s32[1,8]{1,0:T(1,128)S(1)}, s32[1,8]{1,0:T(1,128)}, u32[]{:S(2)}) copy-start(s32[1,8]{1,0:T(1,128)} %param.12) | copy-start | bytes 100
  2.4 27.1 %copy-start.2 = (bf16[1,512,256]{2,1,0:T(8,128)(2,1)S(1)}, bf16[1,512,256]{2,1,0:T(8,128)(2,1)}, u32[]{:S(2)}) copy-start(bf16[1,512,256]{2,1,0:T(8,128)(2,1)} %param.15) | copy-start | bytes 786436
  2.4 27.2 %copy-start.11 = (bf16[768,256]{1,0:T(8,128)(2,1)S(1)}, bf16[768,256]{1,0:T(8,128)(2,1)}, u32[]{:S(2)}) copy-start(bf16[768,256]{1,0:T(8,128)(2,1)} %param.20) | copy-start | bytes 1179652
  2.4 5.5 %collective-permute-start = (bf16[16,2048]{1,0:T(8,128)(2,1)S(1)}, bf16[16,2048]{1,0:T(8,128)(2,1)S(1)}, u32[]{:S(2)}, u32[]{:S(2)}) collective-permute-start(bf16[16,2048]{1,0:T(8,128)(2,1)S(1)} %slice.138), channel_id=1, source_target_pairs={{0,1},{1,0},{2,3},{3,2},{4,5},{5,4},{6,7},{7,6},{8,9},{9,8},{10,11... | collective-permute-start | bytes 196616 | tf_op jit(solution)/shard_map/ppermute | solution.py:239
  6.3 24.5 %collective-permute-start.4 = (bf16[112,2048]{1,0:T(8,128)(2,1)}, bf16[112,2048]{1,0:T(8,128)(2,1)}, u32[]{:S(2)}, u32[]{:S(2)}) collective-permute-start(bf16[112,2048]{1,0:T(8,128)(2,1)} %slice.150), channel_id=1, source_target_pairs={{0,1},{1,0},{2,3},{3,2},{4,5},{5,4},{6,7},{7,6},{8,9},{9,8},{10,11... | collective-permute-start | bytes 1376264 | tf_op jit(solution)/shard_map/ppermute | solution.py:239
  10.0 12.7 %all-to-all-start = ((bf16[16,2,321]{2,1,0:T(2,128)(2,1)}), bf16[16,2,321]{2,1,0:T(2,128)(2,1)S(1)}, u32[]{:S(2)}, u32[]{:S(2)}) async-start(bf16[16,2,321]{2,1,0:T(2,128)(2,1)} %reshape.119), calls=%async_computation | async-start | bytes 49152 | tf_op jit(solution)/shard_map/all_to_all | solution.py:287
  17.1 26.9 %collective-permute-start.3 = (bf16[16,2048]{1,0:T(8,128)(2,1)S(1)}, bf16[16,2048]{1,0:T(8,128)(2,1)S(1)}, u32[]{:S(2)}, u32[]{:S(2)}) collective-permute-start(bf16[16,2048]{1,0:T(8,128)(2,1)S(1)} %collective-permute-done), channel_id=1, source_target_pairs={{0,2},{2,0},{4,6},{6,4},{8,10},{10,8},{12,14},{14,12},{16,18},{18,... | collective-permute-start | bytes 196616 | tf_op jit(solution)/shard_map/ppermute | solution.py:240
  23.6 6.9 %collective-permute-start.2 = (bf16[4,80]{1,0:T(4,128)(2,1)S(1)}, bf16[4,80]{1,0:T(4,128)(2,1)S(1)}, u32[]{:S(2)}, u32[]{:S(2)}) collective-permute-start(bf16[4,80]{1,0:T(4,128)(2,1)S(1)} %get-tuple-element.56), channel_id=1, source_target_pairs={{1,0},{3,2},{5,4},{7,6},{9,8},{11,10},{13,12},{15,14},{17,16},{19,... | collective-permute-start | bytes 1928 | tf_op jit(solution)/shard_map/ppermute | solution.py:19
  24.9 5.8 %collective-permute-start.1 = (bf16[4,80]{1,0:T(4,128)(2,1)S(1)}, bf16[4,80]{1,0:T(4,128)(2,1)S(1)}, u32[]{:S(2)}, u32[]{:S(2)}) collective-permute-start(bf16[4,80]{1,0:T(4,128)(2,1)S(1)} %get-tuple-element.57), channel_id=1, source_target_pairs={{0,1},{2,3},{4,5},{6,7},{8,9},{10,11},{12,13},{14,15},{16,17},{18,... | collective-permute-start | bytes 1928 | tf_op jit(solution)/shard_map/ppermute | solution.py:16
  30.0 3.3 %copy-start.14 = (f32[512]{0:T(512)S(1)}, f32[512]{0:T(512)}, u32[]{:S(2)}) copy-start(f32[512]{0:T(512)} %param.17) | copy-start | bytes 6148
  30.8 13.1 %collective-permute-start.6 = (bf16[128,2048]{1,0:T(8,128)(2,1)}, bf16[128,2048]{1,0:T(8,128)(2,1)}, u32[]{:S(2)}, u32[]{:S(2)}) collective-permute-start(bf16[128,2048]{1,0:T(8,128)(2,1)} %slice.151), channel_id=1, source_target_pairs={{0,1},{1,0},{2,3},{3,2},{4,5},{5,4},{6,7},{7,6},{8,9},{9,8},{10,11... | collective-permute-start | bytes 1572872 | tf_op jit(solution)/shard_map/ppermute | solution.py:239
  33.3 10.7 %collective-permute-start.5 = (bf16[112,2048]{1,0:T(8,128)(2,1)}, bf16[112,2048]{1,0:T(8,128)(2,1)S(1)}, u32[]{:S(2)}, u32[]{:S(2)}) collective-permute-start(bf16[112,2048]{1,0:T(8,128)(2,1)} %collective-permute-done.4), channel_id=1, source_target_pairs={{0,2},{2,0},{4,6},{6,4},{8,10},{10,8},{12,14},{14,12},{16,18},{18,... | collective-permute-start | bytes 1376264 | tf_op jit(solution)/shard_map/ppermute | solution.py:240
  43.9 2.1 %collective-permute-start.7 = (bf16[128,2048]{1,0:T(8,128)(2,1)}, bf16[128,2048]{1,0:T(8,128)(2,1)S(1)}, u32[]{:S(2)}, u32[]{:S(2)}) collective-permute-start(bf16[128,2048]{1,0:T(8,128)(2,1)} %collective-permute-done.6), channel_id=1, source_target_pairs={{0,2},{2,0},{4,6},{6,4},{8,10},{10,8},{12,14},{14,12},{16,18},{18,... | collective-permute-start | bytes 1572872 | tf_op jit(solution)/shard_map/ppermute | solution.py:240
  51.0 1.6 %copy-start.3 = (f32[518,256]{1,0:T(8,128)}, f32[518,256]{1,0:T(8,128)S(1)}, u32[]{:S(2)}) copy-start(f32[518,256]{1,0:T(8,128)S(1)} %get-tuple-element.22) | copy-start | bytes 1591300
  55.6 2.8 %collective-permute-start.8 = (f32[1920,128]{1,0:T(8,128)S(1)}, f32[1920,128]{1,0:T(8,128)}, u32[]{:S(2)}, u32[]{:S(2)}) collective-permute-start(f32[1920,128]{1,0:T(8,128)S(1)} %constant_dynamic-slice_fusion.6), channel_id=1, source_target_pairs={{0,2},{1,3},{2,0},{3,1},{4,6},{5,7},{6,4},{7,5},{8,10},{9,11},{10,... | collective-permute-start | bytes 2949128 | tf_op jit(solution)/shard_map/ppermute | solution.py:188
  59.8 8.9 %collective-permute-start.9 = (f32[480,128]{1,0:T(8,128)S(1)}, f32[480,128]{1,0:T(8,128)S(1)}, u32[]{:S(2)}, u32[]{:S(2)}) collective-permute-start(f32[480,128]{1,0:T(8,128)S(1)} %get-tuple-element.30), channel_id=1, source_target_pairs={{0,1},{1,0},{2,10},{3,11},{4,5},{5,4},{6,14},{7,15},{8,9},{9,8},{1... | collective-permute-start | bytes 737288 | tf_op jit(solution)/shard_map/ppermute | solution.py:196
  61.5 7.2 %collective-permute-start.11 = (f32[480,128]{1,0:T(8,128)S(1)}, f32[480,128]{1,0:T(8,128)S(1)}, u32[]{:S(2)}, u32[]{:S(2)}) collective-permute-start(f32[480,128]{1,0:T(8,128)S(1)} %get-tuple-element.31), channel_id=1, source_target_pairs={{0,5},{1,4},{2,26},{3,27},{4,1},{5,0},{6,30},{7,31},{8,13},{9,12},... | collective-permute-start | bytes 737288 | tf_op jit(solution)/shard_map/ppermute | solution.py:196
  62.1 8.1 %collective-permute-start.10 = (f32[480,128]{1,0:T(8,128)S(1)}, f32[480,128]{1,0:T(8,128)S(1)}, u32[]{:S(2)}, u32[]{:S(2)}) collective-permute-start(f32[480,128]{1,0:T(8,128)S(1)} %get-tuple-element.32), channel_id=1, source_target_pairs={{0,4},{1,5},{2,18},{3,19},{4,0},{5,1},{6,22},{7,23},{8,12},{9,13},... | collective-permute-start | bytes 737288 | tf_op jit(solution)/shard_map/ppermute | solution.py:196
  70.3 4.7 %collective-permute-start.12 = (f32[120,128]{1,0:T(8,128)S(1)}, f32[120,128]{1,0:T(8,128)S(1)}, u32[]{:S(2)}, u32[]{:S(2)}) collective-permute-start(f32[120,128]{1,0:T(8,128)S(1)} %get-tuple-element.44), channel_id=1, source_target_pairs={{0,8},{1,9},{2,3},{3,2},{4,12},{5,13},{6,7},{7,6},{8,0},{9,1},{10,... | collective-permute-start | bytes 184328 | tf_op jit(solution)/shard_map/ppermute | solution.py:196
  71.1 6.0 %collective-permute-start.14 = (f32[120,128]{1,0:T(8,128)S(1)}, f32[120,128]{1,0:T(8,128)S(1)}, u32[]{:S(2)}, u32[]{:S(2)}) collective-permute-start(f32[120,128]{1,0:T(8,128)S(1)} %get-tuple-element.45), channel_id=1, source_target_pairs={{0,24},{1,25},{2,7},{3,6},{4,28},{5,29},{6,3},{7,2},{8,16},{9,17},... | collective-permute-start | bytes 184328 | tf_op jit(solution)/shard_map/ppermute | solution.py:196
  72.6 5.8 %collective-permute-start.13 = (f32[120,128]{1,0:T(8,128)S(1)}, f32[120,128]{1,0:T(8,128)S(1)}, u32[]{:S(2)}, u32[]{:S(2)}) collective-permute-start(f32[120,128]{1,0:T(8,128)S(1)} %get-tuple-element.46), channel_id=1, source_target_pairs={{0,16},{1,17},{2,6},{3,7},{4,20},{5,21},{6,2},{7,3},{8,24},{9,25},... | collective-permute-start | bytes 184328 | tf_op jit(solution)/shard_map/ppermute | solution.py:196
  78.5 6.1 %collective-permute-start.17 = (f32[120,128]{1,0:T(8,128)S(1)}, f32[120,128]{1,0:T(8,128)S(1)}, u32[]{:S(2)}, u32[]{:S(2)}) collective-permute-start(f32[120,128]{1,0:T(8,128)S(1)} %add_add_fusion.1), channel_id=1, source_target_pairs={{0,24},{1,25},{2,7},{3,6},{4,28},{5,29},{6,3},{7,2},{8,16},{9,17},... | collective-permute-start | bytes 184328 | tf_op jit(solution)/shard_map/ppermute | solution.py:201
  80.6 5.3 %collective-permute-start.16 = (f32[120,128]{1,0:T(8,128)S(1)}, f32[120,128]{1,0:T(8,128)S(1)}, u32[]{:S(2)}, u32[]{:S(2)}) collective-permute-start(f32[120,128]{1,0:T(8,128)S(1)} %add_add_fusion.1), channel_id=1, source_target_pairs={{0,16},{1,17},{2,6},{3,7},{4,20},{5,21},{6,2},{7,3},{8,24},{9,25},... | collective-permute-start | bytes 184328 | tf_op jit(solution)/shard_map/ppermute | solution.py:201
  80.6 5.3 %collective-permute-start.15 = (f32[120,128]{1,0:T(8,128)S(1)}, f32[120,128]{1,0:T(8,128)S(1)}, u32[]{:S(2)}, u32[]{:S(2)}) collective-permute-start(f32[120,128]{1,0:T(8,128)S(1)} %add_add_fusion.1), channel_id=1, source_target_pairs={{0,8},{1,9},{2,3},{3,2},{4,12},{5,13},{6,7},{7,6},{8,0},{9,1},{10,... | collective-permute-start | bytes 184328 | tf_op jit(solution)/shard_map/ppermute | solution.py:201
  85.9 7.2 %collective-permute-start.20 = (f32[480,128]{1,0:T(8,128)S(1)}, f32[480,128]{1,0:T(8,128)S(1)}, u32[]{:S(2)}, u32[]{:S(2)}) collective-permute-start(f32[480,128]{1,0:T(8,128)S(1)} %pad_maximum_fusion.9), channel_id=1, source_target_pairs={{0,5},{1,4},{2,26},{3,27},{4,1},{5,0},{6,30},{7,31},{8,13},{9,12},... | collective-permute-start | bytes 737288 | tf_op jit(solution)/shard_map/ppermute | solution.py:201
  88.2 8.4 %collective-permute-start.19 = (f32[480,128]{1,0:T(8,128)S(1)}, f32[480,128]{1,0:T(8,128)S(1)}, u32[]{:S(2)}, u32[]{:S(2)}) collective-permute-start(f32[480,128]{1,0:T(8,128)S(1)} %pad_maximum_fusion.9), channel_id=1, source_target_pairs={{0,4},{1,5},{2,18},{3,19},{4,0},{5,1},{6,22},{7,23},{8,12},{9,13},... | collective-permute-start | bytes 737288 | tf_op jit(solution)/shard_map/ppermute | solution.py:201
  89.8 6.8 %collective-permute-start.18 = (f32[480,128]{1,0:T(8,128)S(1)}, f32[480,128]{1,0:T(8,128)S(1)}, u32[]{:S(2)}, u32[]{:S(2)}) collective-permute-start(f32[480,128]{1,0:T(8,128)S(1)} %pad_maximum_fusion.9), channel_id=1, source_target_pairs={{0,1},{1,0},{2,10},{3,11},{4,5},{5,4},{6,14},{7,15},{8,9},{9,8},{1... | collective-permute-start | bytes 737288 | tf_op jit(solution)/shard_map/ppermute | solution.py:201
  97.0 3.1 %collective-permute-start.21 = (f32[1920,128]{1,0:T(8,128)S(1)}, f32[1920,128]{1,0:T(8,128)S(1)}, u32[]{:S(2)}, u32[]{:S(2)}) collective-permute-start(f32[1920,128]{1,0:T(8,128)S(1)} %pad_maximum_fusion.2), channel_id=1, source_target_pairs={{0,2},{1,3},{2,0},{3,1},{4,6},{5,7},{6,4},{7,5},{8,10},{9,11},{10,... | collective-permute-start | bytes 2949128 | tf_op jit(solution)/shard_map/ppermute | solution.py:210
  (11 other events, 12.0 us)

commit v18 on v16

--- a/solution.py
+++ b/solution.py
@@ -186,7 +186,7 @@
     half = x.shape[0] // 2
     send = lax.dynamic_slice_in_dim(x, (1 - core) * half, half)
     x = lax.dynamic_slice_in_dim(x, core * half, half) + lax.ppermute(send, axes, core_perm)
-    for step in range(len(groups)):
+    for step in range(len(groups) - 1):
         radix = 1 << len(groups[step])
         piece = x.shape[0] // radix
         slot = slot_of(step)
@@ -195,7 +195,22 @@
             send = lax.dynamic_slice_in_dim(x, (slot ^ offset) * piece, piece)
             total = total + lax.ppermute(send, axes, perm_of(step, offset))
         x = total
-    for step in reversed(range(len(groups))):
+    if groups:
+        last = len(groups) - 1
+        radix = 1 << len(groups[last])
+        slot = slot_of(last)
+        got = [x] + [lax.ppermute(x, axes, perm_of(last, o)) for o in range(1, radix)]
+        pieces = []
+        for q in range(radix):
+            source = slot ^ q
+            chosen = got[radix - 1]
+            for o in range(radix - 2, -1, -1):
+                chosen = jnp.where(source == o, got[o], chosen)
+            pieces.append(chosen)
+        while len(pieces) > 1:
+            pieces = [pieces[i] + pieces[i + 1] for i in range(0, len(pieces), 2)]
+        x = pieces[0]
+    for step in reversed(range(len(groups) - 1)):
         radix = 1 << len(groups[step])
         slot = slot_of(step)
         got = [x] + [lax.ppermute(x, axes, perm_of(step, o)) for o in range(1, radix)]

time: 96.1 us -> 94.5 us (0.983)
  starting transfers between devices: 36.1 us -> 32 us
  waiting for transfers between devices: 31.1 us -> 33.3 us
    ppermute x0 -> x3, waiting for transfers between devices: none -> 9.7 us  [butterfly_psum(): lax.ppermute(x, axes, perm_of(last, o))]
    ppermute x0 -> x3, starting transfers between devices: none -> 4.45 us  [butterfly_psum(): lax.ppermute(x, axes, perm_of(last, o))]
    ppermute x6 -> x3, starting transfers between devices: 8.46 us -> 4.1 us  [butterfly_psum(): lax.ppermute(x, axes, perm_of(step, o))]
    ppermute x6 -> x3, waiting for transfers between devices: 11.1 us -> 6.85 us  [butterfly_psum(): total = total + lax.ppermute(send, axes, perm_of(step, offset))]
    ppermute x6 -> x3, starting transfers between devices: 7.54 us -> 3.99 us  [butterfly_psum(): total = total + lax.ppermute(send, axes, perm_of(step, offset))]
    ppermute x6 -> x3, waiting for transfers between devices: 9.85 us -> 6.85 us  [butterfly_psum(): lax.ppermute(x, axes, perm_of(step, o))]
  transfers between devices with their start and end apart: 23 -> 20, of which waited for: 15 -> 12; matrix products, arithmetic and copies ran while one was open for 11% -> 11% of each run, Pallas kernels for 0% -> 0%
where the time goes in v18:
time: 94.5 us; the launch traced here: 94 us
  waiting for transfers between devices  33.3 us (35%)
  starting transfers between devices  32 us (34%)
  local copies, waits for them, and re-layouts  12.1 us (13%)
  other arithmetic  9.66 us (10%)
  matrix products  5.62 us (6%)
  between operations  1.29 us (1%)
    ppermute x3, waiting for transfers between devices, butterfly_psum(): lax.ppermute(x, axes, perm_of(last, o))  9.7 us
    ppermute x3, waiting for transfers between devices, butterfly_psum(): total = total + lax.ppermute(send, axes, perm_of(step, offset))  6.85 us
    ppermute x3, waiting for transfers between devices, butterfly_psum(): lax.ppermute(x, axes, perm_of(step, o))  6.85 us
    all_to_all x1, waiting for transfers between devices, on_device(): lax.all_to_all(outgoing, 'dp', split_axis=0, concat_axis=0, tiled=True)  6.07 us
    all_to_all x1, starting transfers between devices, on_device(): lax.all_to_all(outgoing, 'dp', split_axis=0, concat_axis=0, tiled=True)  5.91 us
    ppermute x1, starting transfers between devices, with_halo(): lax.ppermute(lax.slice_in_dim(block, block.shape[dim] - width, None, axis...  5.12 us
    ppermute x3, starting transfers between devices, ups_functions(): got_parts.append(lax.ppermute(mine[lo:hi], 'tm', [(0, 1), (1, 0)]))  5.06 us
    unnamed x51, local copies, waits for them, and re-layouts  4.69 us
  transfers between devices with their start and end apart: 20, of which 12 were waited for; matrix products, arithmetic and copies ran while one was open for 11% of the time, Pallas kernels for 0%

profile of v18, /device:TPU:0, one launch (start us, length us, event | category | flops | bytes accessed | tf_op | source)
XLA Modules:
  0.0 94.0 jit_solution(15045688542414748274)
XLA Ops:
  0.7 1.7 %slice_select_fusion = bf16[256,2048]{1,0:T(8,128)(2,1)S(1)} fusion(bf16[256,4096]{1,0:T(8,128)(2,1)} %param.18, pred[]{:T(512)S(6)} %eq.137), kind=kLoop, calls=%fused_computation.21 | loop fusion | flops 524288 | bytes 3145729 | tf_op jit(solution)/shard_map/jit(_where)/select_n | solution.py:249
  2.4 3.0 %collective-permute-start = (bf16[16,2048]{1,0:T(8,128)(2,1)S(1)}, bf16[16,2048]{1,0:T(8,128)(2,1)S(1)}, u32[]{:S(2)}, u32[]{:S(2)}) collective-permute-start(bf16[16,2048]{1,0:T(8,128)(2,1)S(1)} %slice.138), channel_id=1, source_target_pairs={{0,1},{1,0},{2,3},{3,2},{4,5},{5,4},{6,7},{7,6},{8,9},{9,8},{10,11... | collective-permute-start | bytes 196616 | tf_op jit(solution)/shard_map/ppermute | solution.py:251
  5.5 0.8 slice.150
  6.3 0.8 slice.151
  7.1 2.0 %collective-permute-start.6 = (bf16[128,2048]{1,0:T(8,128)(2,1)}, bf16[128,2048]{1,0:T(8,128)(2,1)}, u32[]{:S(2)}, u32[]{:S(2)}) collective-permute-start(bf16[128,2048]{1,0:T(8,128)(2,1)} %slice.151), channel_id=1, source_target_pairs={{0,1},{1,0},{2,3},{3,2},{4,5},{5,4},{6,7},{7,6},{8,9},{9,8},{10,11... | collective-permute-start | bytes 1572872 | tf_op jit(solution)/shard_map/ppermute | solution.py:251
  11.5 5.9 %all-to-all-start = ((bf16[16,2,321]{2,1,0:T(2,128)(2,1)}), bf16[16,2,321]{2,1,0:T(2,128)(2,1)S(1)}, u32[]{:S(2)}, u32[]{:S(2)}) async-start(bf16[16,2,321]{2,1,0:T(2,128)(2,1)} %reshape.119), calls=%async_computation | async-start | bytes 49152 | tf_op jit(solution)/shard_map/all_to_all | solution.py:299
  17.9 6.1 %all-to-all-done = bf16[16,2,321]{2,1,0:T(2,128)(2,1)S(1)} async-done(((bf16[16,2,321]{2,1,0:T(2,128)(2,1)}), bf16[16,2,321]{2,1,0:T(2,128)(2,1)S(1)}, u32[]{:S(2)}, u32[]{:S(2)}) %all-to-all-start) | async-done | bytes 20576 | tf_op jit(solution)/shard_map/all_to_all | solution.py:299
  25.6 1.3 %collective-permute-start.2 = (bf16[4,80]{1,0:T(4,128)(2,1)}, bf16[4,80]{1,0:T(4,128)(2,1)S(1)}, u32[]{:S(2)}, u32[]{:S(2)}) collective-permute-start(bf16[4,80]{1,0:T(4,128)(2,1)} %get-tuple-element.47), channel_id=1, source_target_pairs={{1,0},{3,2},{5,4},{7,6},{9,8},{11,10},{13,12},{15,14},{17,16},{19,... | collective-permute-start | bytes 1928 | tf_op jit(solution)/shard_map/ppermute | solution.py:19
  26.9 5.1 %collective-permute-start.1 = (bf16[4,80]{1,0:T(4,128)(2,1)}, bf16[4,80]{1,0:T(4,128)(2,1)}, u32[]{:S(2)}, u32[]{:S(2)}) collective-permute-start(bf16[4,80]{1,0:T(4,128)(2,1)} %get-tuple-element.48), channel_id=1, source_target_pairs={{0,1},{2,3},{4,5},{6,7},{8,9},{10,11},{12,13},{14,15},{16,17},{18,... | collective-permute-start | bytes 1928 | tf_op jit(solution)/shard_map/ppermute | solution.py:16
  33.0 0.8 pad_maximum_fusion.9
  34.9 0.9 broadcast_select_fusion.6
  36.1 1.1 %broadcast_select_fusion.4 = (bf16[112,2048]{1,0:T(8,128)(2,1)S(1)}, bf16[112,2048]{1,0:T(8,128)(2,1)S(1)}) fusion(bf16[112,2048]{1,0:T(8,128)(2,1)} %collective-permute-done.4, bf16[112,2048]{1,0:T(8,128)(2,1)S(1)} %collective-permute-done.5, pred[]{:T(512)S(6)} %eq.137), kind=kLoop, calls=%fused_computation.43 | loop fusion | flops 458752 | bytes 1835009 | tf_op jit(solution)/shard_map/jit(_where)/select_n | solution.py:254
  37.2 1.1 %broadcast_select_fusion.2 = (bf16[128,2048]{1,0:T(8,128)(2,1)S(1)}, bf16[128,2048]{1,0:T(8,128)(2,1)S(1)}) fusion(bf16[128,2048]{1,0:T(8,128)(2,1)} %collective-permute-done.6, bf16[128,2048]{1,0:T(8,128)(2,1)S(1)} %collective-permute-done.7, pred[]{:T(512)S(6)} %eq.137), kind=kLoop, calls=%fused_computation.41 | loop fusion | flops 524288 | bytes 2097153 | tf_op jit(solution)/shard_map/jit(_where)/select_n | solution.py:254
  38.9 1.3 %copy-done.1 = bf16[256,4096]{1,0:T(8,128)(2,1)S(1)} copy-done((bf16[256,4096]{1,0:T(8,128)(2,1)S(1)}, bf16[256,4096]{1,0:T(8,128)(2,1)}, u32[]{:S(2)}) %copy-start.1) | copy-done | bytes 2097176
  46.9 2.6 %collective-permute-done.8 = f32[1920,128]{1,0:T(8,128)} collective-permute-done((f32[1920,128]{1,0:T(8,128)S(1)}, f32[1920,128]{1,0:T(8,128)}, u32[]{:S(2)}, u32[]{:S(2)}) %collective-permute-start.8) | collective-permute-done | bytes 983072 | tf_op jit(solution)/shard_map/ppermute | solution.py:188
  49.5 1.3 %dynamic-slice_add_fusion = f32[1920,128]{1,0:T(8,128)S(1)} fusion(f32[1920,128]{1,0:T(8,128)} %collective-permute-done.8, f32[3840,128]{1,0:T(8,128)S(1)} %fusion, s32[]{:T(128)S(6)} %select_n.373), kind=kLoop, calls=%fused_computation.23 | loop fusion | flops 245760 | bytes 2949124 | tf_op jit(solution)/shard_map/add | solution.py:188
  50.9 2.4 %collective-permute-start.9 = (f32[480,128]{1,0:T(8,128)S(1)}, f32[480,128]{1,0:T(8,128)S(1)}, u32[]{:S(2)}, u32[]{:S(2)}) collective-permute-start(f32[480,128]{1,0:T(8,128)S(1)} %get-tuple-element.28), channel_id=1, source_target_pairs={{0,1},{1,0},{2,10},{3,11},{4,5},{5,4},{6,14},{7,15},{8,9},{9,8},{1... | collective-permute-start | bytes 737288 | tf_op jit(solution)/shard_map/ppermute | solution.py:196
  53.3 1.5 %collective-permute-start.10 = (f32[480,128]{1,0:T(8,128)S(1)}, f32[480,128]{1,0:T(8,128)S(1)}, u32[]{:S(2)}, u32[]{:S(2)}) collective-permute-start(f32[480,128]{1,0:T(8,128)S(1)} %get-tuple-element.30), channel_id=1, source_target_pairs={{0,4},{1,5},{2,18},{3,19},{4,0},{5,1},{6,22},{7,23},{8,12},{9,13},... | collective-permute-start | bytes 737288 | tf_op jit(solution)/shard_map/ppermute | solution.py:196
  54.8 4.8 %collective-permute-done.9 = f32[480,128]{1,0:T(8,128)S(1)} collective-permute-done((f32[480,128]{1,0:T(8,128)S(1)}, f32[480,128]{1,0:T(8,128)S(1)}, u32[]{:S(2)}, u32[]{:S(2)}) %collective-permute-start.9) | collective-permute-done | bytes 245792 | tf_op jit(solution)/shard_map/ppermute | solution.py:196
  60.4 1.3 %collective-permute-done.10 = f32[480,128]{1,0:T(8,128)S(1)} collective-permute-done((f32[480,128]{1,0:T(8,128)S(1)}, f32[480,128]{1,0:T(8,128)S(1)}, u32[]{:S(2)}, u32[]{:S(2)}) %collective-permute-start.10) | collective-permute-done | bytes 245792 | tf_op jit(solution)/shard_map/ppermute | solution.py:196
  62.3 1.4 %collective-permute-start.13 = (f32[480,128]{1,0:T(8,128)S(1)}, f32[480,128]{1,0:T(8,128)S(1)}, u32[]{:S(2)}, u32[]{:S(2)}) collective-permute-start(f32[480,128]{1,0:T(8,128)S(1)} %add_add_fusion.1), channel_id=1, source_target_pairs={{0,16},{1,17},{2,6},{3,7},{4,20},{5,21},{6,2},{7,3},{8,24},{9,25},... | collective-permute-start | bytes 737288 | tf_op jit(solution)/shard_map/ppermute | solution.py:202
  63.7 2.5 %collective-permute-start.12 = (f32[480,128]{1,0:T(8,128)S(1)}, f32[480,128]{1,0:T(8,128)S(1)}, u32[]{:S(2)}, u32[]{:S(2)}) collective-permute-start(f32[480,128]{1,0:T(8,128)S(1)} %add_add_fusion.1), channel_id=1, source_target_pairs={{0,8},{1,9},{2,3},{3,2},{4,12},{5,13},{6,7},{7,6},{8,0},{9,1},{10,... | collective-permute-start | bytes 737288 | tf_op jit(solution)/shard_map/ppermute | solution.py:202
  66.2 3.8 %collective-permute-done.14 = f32[480,128]{1,0:T(8,128)S(1)} collective-permute-done((f32[480,128]{1,0:T(8,128)S(1)}, f32[480,128]{1,0:T(8,128)S(1)}, u32[]{:S(2)}, u32[]{:S(2)}) %collective-permute-start.14) | collective-permute-done | bytes 245792 | tf_op jit(solution)/shard_map/ppermute | solution.py:202
  70.0 5.9 %collective-permute-done.13 = f32[480,128]{1,0:T(8,128)S(1)} collective-permute-done((f32[480,128]{1,0:T(8,128)S(1)}, f32[480,128]{1,0:T(8,128)S(1)}, u32[]{:S(2)}, u32[]{:S(2)}) %collective-permute-start.13) | collective-permute-done | bytes 245792 | tf_op jit(solution)/shard_map/ppermute | solution.py:202
  76.0 2.7 %collective-permute-start.17 = (f32[480,128]{1,0:T(8,128)S(1)}, f32[480,128]{1,0:T(8,128)S(1)}, u32[]{:S(2)}, u32[]{:S(2)}) collective-permute-start(f32[480,128]{1,0:T(8,128)S(1)} %add_add_fusion), channel_id=1, source_target_pairs={{0,5},{1,4},{2,26},{3,27},{4,1},{5,0},{6,30},{7,31},{8,13},{9,12},... | collective-permute-start | bytes 737288 | tf_op jit(solution)/shard_map/ppermute | solution.py:216
  78.7 1.4 %collective-permute-start.16 = (f32[480,128]{1,0:T(8,128)S(1)}, f32[480,128]{1,0:T(8,128)S(1)}, u32[]{:S(2)}, u32[]{:S(2)}) collective-permute-start(f32[480,128]{1,0:T(8,128)S(1)} %add_add_fusion), channel_id=1, source_target_pairs={{0,4},{1,5},{2,18},{3,19},{4,0},{5,1},{6,22},{7,23},{8,12},{9,13},... | collective-permute-start | bytes 737288 | tf_op jit(solution)/shard_map/ppermute | solution.py:216
  80.1 3.1 %collective-permute-done.17 = f32[480,128]{1,0:T(8,128)S(1)} collective-permute-done((f32[480,128]{1,0:T(8,128)S(1)}, f32[480,128]{1,0:T(8,128)S(1)}, u32[]{:S(2)}, u32[]{:S(2)}) %collective-permute-start.17) | collective-permute-done | bytes 245792 | tf_op jit(solution)/shard_map/ppermute | solution.py:216
  83.2 3.8 %collective-permute-done.16 = f32[480,128]{1,0:T(8,128)S(1)} collective-permute-done((f32[480,128]{1,0:T(8,128)S(1)}, f32[480,128]{1,0:T(8,128)S(1)}, u32[]{:S(2)}, u32[]{:S(2)}) %collective-permute-start.16) | collective-permute-done | bytes 245792 | tf_op jit(solution)/shard_map/ppermute | solution.py:216
  87.4 0.8 collective-permute-start.18
  88.6 1.1 %fusion.3 = bf16[1,512,256]{2,1,0:T(8,128)(2,1)} fusion(bf16[768,256]{1,0:T(8,128)(2,1)S(1)} %copy-done.12, f32[518,256]{1,0:T(8,128)S(1)} %copy-done.4, bf16[512,256]{1,0:T(8,128)(2,1)S(1)} %copy-done.8, bf16[512,256]{1,0:T(8,128)(2,1)S(1)} %copy-done.10, bf16[512,256]{1,0:T(8,128)(2,1)S(1)} %copy-done.6, f32[256]{0:T(256)S(1)} %copy-done.17), kind=kOutput, calls=%fused_computation.9 | convolution fusion | flops 204079104 | bytes 1967104 | tf_op jit(solution)/shard_map/dot_general | solution.py:92
  92.0 0.9 slice.167
  92.9 1.1 %slice.165 = f32[2240,128]{1,0:T(8,128)} slice(f32[3840,128]{1,0:T(8,128)S(1)} %broadcast_select_fusion), slice={[0:2240], [0:128]} | slice | bytes 2293760 | tf_op jit(solution)/shard_map/slice | solution.py:229
  (129 shorter events, 18.4 us)
Async XLA Ops:
  0.6 33.4 %copy-start = (bf16[560,512]{1,0:T(8,128)(2,1)S(1)}, bf16[560,512]{1,0:T(8,128)(2,1)}, u32[]{:S(2)}) copy-start(bf16[560,512]{1,0:T(8,128)(2,1)} %param.16) | copy-start | bytes 1720324
  0.7 8.5 %copy-start.18 = (s32[1,8]{1,0:T(1,128)S(1)}, s32[1,8]{1,0:T(1,128)}, u32[]{:S(2)}) copy-start(s32[1,8]{1,0:T(1,128)} %param.13) | copy-start | bytes 100
  0.7 8.5 %copy-start.19 = (s32[1,8]{1,0:T(1,128)S(1)}, s32[1,8]{1,0:T(1,128)}, u32[]{:S(2)}) copy-start(s32[1,8]{1,0:T(1,128)} %param.14) | copy-start | bytes 100
  0.7 8.7 %copy-start.13 = (bf16[1,8,640]{2,1,0:T(8,128)(2,1)S(1)}, bf16[1,8,640]{2,1,0:T(8,128)(2,1)}, u32[]{:S(2)}) copy-start(bf16[1,8,640]{2,1,0:T(8,128)(2,1)} %param.11) | copy-start | bytes 30724
  0.7 8.7 %copy-start.16 = (s32[1,8]{1,0:T(1,128)S(1)}, s32[1,8]{1,0:T(1,128)}, u32[]{:S(2)}) copy-start(s32[1,8]{1,0:T(1,128)} %param.12) | copy-start | bytes 100
  2.4 22.2 %copy-start.2 = (bf16[1,512,256]{2,1,0:T(8,128)(2,1)S(1)}, bf16[1,512,256]{2,1,0:T(8,128)(2,1)}, u32[]{:S(2)}) copy-start(bf16[1,512,256]{2,1,0:T(8,128)(2,1)} %param.15) | copy-start | bytes 786436
  2.4 29.6 %copy-start.11 = (bf16[768,256]{1,0:T(8,128)(2,1)S(1)}, bf16[768,256]{1,0:T(8,128)(2,1)}, u32[]{:S(2)}) copy-start(bf16[768,256]{1,0:T(8,128)(2,1)} %param.20) | copy-start | bytes 1179652
  2.4 6.9 %collective-permute-start = (bf16[16,2048]{1,0:T(8,128)(2,1)S(1)}, bf16[16,2048]{1,0:T(8,128)(2,1)S(1)}, u32[]{:S(2)}, u32[]{:S(2)}) collective-permute-start(bf16[16,2048]{1,0:T(8,128)(2,1)S(1)} %slice.138), channel_id=1, source_target_pairs={{0,1},{1,0},{2,3},{3,2},{4,5},{5,4},{6,7},{7,6},{8,9},{9,8},{10,11... | collective-permute-start | bytes 196616 | tf_op jit(solution)/shard_map/ppermute | solution.py:251
  6.3 27.7 %collective-permute-start.4 = (bf16[112,2048]{1,0:T(8,128)(2,1)}, bf16[112,2048]{1,0:T(8,128)(2,1)}, u32[]{:S(2)}, u32[]{:S(2)}) collective-permute-start(bf16[112,2048]{1,0:T(8,128)(2,1)} %slice.150), channel_id=1, source_target_pairs={{0,1},{1,0},{2,3},{3,2},{4,5},{5,4},{6,7},{7,6},{8,9},{9,8},{10,11... | collective-permute-start | bytes 1376264 | tf_op jit(solution)/shard_map/ppermute | solution.py:251
  7.1 27.2 %collective-permute-start.6 = (bf16[128,2048]{1,0:T(8,128)(2,1)}, bf16[128,2048]{1,0:T(8,128)(2,1)}, u32[]{:S(2)}, u32[]{:S(2)}) collective-permute-start(bf16[128,2048]{1,0:T(8,128)(2,1)} %slice.151), channel_id=1, source_target_pairs={{0,1},{1,0},{2,3},{3,2},{4,5},{5,4},{6,7},{7,6},{8,9},{9,8},{10,11... | collective-permute-start | bytes 1572872 | tf_op jit(solution)/shard_map/ppermute | solution.py:251
  11.5 12.5 %all-to-all-start = ((bf16[16,2,321]{2,1,0:T(2,128)(2,1)}), bf16[16,2,321]{2,1,0:T(2,128)(2,1)S(1)}, u32[]{:S(2)}, u32[]{:S(2)}) async-start(bf16[16,2,321]{2,1,0:T(2,128)(2,1)} %reshape.119), calls=%async_computation | async-start | bytes 49152 | tf_op jit(solution)/shard_map/all_to_all | solution.py:299
  17.4 17.5 %collective-permute-start.3 = (bf16[16,2048]{1,0:T(8,128)(2,1)S(1)}, bf16[16,2048]{1,0:T(8,128)(2,1)}, u32[]{:S(2)}, u32[]{:S(2)}) collective-permute-start(bf16[16,2048]{1,0:T(8,128)(2,1)S(1)} %collective-permute-done), channel_id=1, source_target_pairs={{0,2},{2,0},{4,6},{6,4},{8,10},{10,8},{12,14},{14,12},{16,18},{18,... | collective-permute-start | bytes 196616 | tf_op jit(solution)/shard_map/ppermute | solution.py:252
  25.6 7.1 %collective-permute-start.2 = (bf16[4,80]{1,0:T(4,128)(2,1)}, bf16[4,80]{1,0:T(4,128)(2,1)S(1)}, u32[]{:S(2)}, u32[]{:S(2)}) collective-permute-start(bf16[4,80]{1,0:T(4,128)(2,1)} %get-tuple-element.47), channel_id=1, source_target_pairs={{1,0},{3,2},{5,4},{7,6},{9,8},{11,10},{13,12},{15,14},{17,16},{19,... | collective-permute-start | bytes 1928 | tf_op jit(solution)/shard_map/ppermute | solution.py:19
  26.9 6.0 %collective-permute-start.1 = (bf16[4,80]{1,0:T(4,128)(2,1)}, bf16[4,80]{1,0:T(4,128)(2,1)}, u32[]{:S(2)}, u32[]{:S(2)}) collective-permute-start(bf16[4,80]{1,0:T(4,128)(2,1)} %get-tuple-element.48), channel_id=1, source_target_pairs={{0,1},{2,3},{4,5},{6,7},{8,9},{10,11},{12,13},{14,15},{16,17},{18,... | collective-permute-start | bytes 1928 | tf_op jit(solution)/shard_map/ppermute | solution.py:16
  32.5 1.6 %copy-start.14 = (f32[512]{0:T(512)S(1)}, f32[512]{0:T(512)}, u32[]{:S(2)}) copy-start(f32[512]{0:T(512)} %param.17) | copy-start | bytes 6148
  34.0 2.1 %collective-permute-start.5 = (bf16[112,2048]{1,0:T(8,128)(2,1)}, bf16[112,2048]{1,0:T(8,128)(2,1)S(1)}, u32[]{:S(2)}, u32[]{:S(2)}) collective-permute-start(bf16[112,2048]{1,0:T(8,128)(2,1)} %collective-permute-done.4), channel_id=1, source_target_pairs={{0,2},{2,0},{4,6},{6,4},{8,10},{10,8},{12,14},{14,12},{16,18},{18,... | collective-permute-start | bytes 1376264 | tf_op jit(solution)/shard_map/ppermute | solution.py:252
  34.4 2.8 %collective-permute-start.7 = (bf16[128,2048]{1,0:T(8,128)(2,1)}, bf16[128,2048]{1,0:T(8,128)(2,1)S(1)}, u32[]{:S(2)}, u32[]{:S(2)}) collective-permute-start(bf16[128,2048]{1,0:T(8,128)(2,1)} %collective-permute-done.6), channel_id=1, source_target_pairs={{0,2},{2,0},{4,6},{6,4},{8,10},{10,8},{12,14},{14,12},{16,18},{18,... | collective-permute-start | bytes 1572872 | tf_op jit(solution)/shard_map/ppermute | solution.py:252
  38.6 1.6 %copy-start.1 = (bf16[256,4096]{1,0:T(8,128)(2,1)S(1)}, bf16[256,4096]{1,0:T(8,128)(2,1)}, u32[]{:S(2)}) copy-start(bf16[256,4096]{1,0:T(8,128)(2,1)} %param.18) | copy-start | bytes 6291460
  42.1 1.6 %copy-start.3 = (f32[518,256]{1,0:T(8,128)}, f32[518,256]{1,0:T(8,128)S(1)}, u32[]{:S(2)}) copy-start(f32[518,256]{1,0:T(8,128)S(1)} %get-tuple-element.20) | copy-start | bytes 1591300
  46.7 2.8 %collective-permute-start.8 = (f32[1920,128]{1,0:T(8,128)S(1)}, f32[1920,128]{1,0:T(8,128)}, u32[]{:S(2)}, u32[]{:S(2)}) collective-permute-start(f32[1920,128]{1,0:T(8,128)S(1)} %constant_dynamic-slice_fusion.3), channel_id=1, source_target_pairs={{0,2},{1,3},{2,0},{3,1},{4,6},{5,7},{6,4},{7,5},{8,10},{9,11},{10,... | collective-permute-start | bytes 2949128 | tf_op jit(solution)/shard_map/ppermute | solution.py:188
  50.9 8.8 %collective-permute-start.9 = (f32[480,128]{1,0:T(8,128)S(1)}, f32[480,128]{1,0:T(8,128)S(1)}, u32[]{:S(2)}, u32[]{:S(2)}) collective-permute-start(f32[480,128]{1,0:T(8,128)S(1)} %get-tuple-element.28), channel_id=1, source_target_pairs={{0,1},{1,0},{2,10},{3,11},{4,5},{5,4},{6,14},{7,15},{8,9},{9,8},{1... | collective-permute-start | bytes 737288 | tf_op jit(solution)/shard_map/ppermute | solution.py:196
  53.3 7.1 %collective-permute-start.11 = (f32[480,128]{1,0:T(8,128)S(1)}, f32[480,128]{1,0:T(8,128)S(1)}, u32[]{:S(2)}, u32[]{:S(2)}) collective-permute-start(f32[480,128]{1,0:T(8,128)S(1)} %get-tuple-element.29), channel_id=1, source_target_pairs={{0,5},{1,4},{2,26},{3,27},{4,1},{5,0},{6,30},{7,31},{8,13},{9,12},... | collective-permute-start | bytes 737288 | tf_op jit(solution)/shard_map/ppermute | solution.py:196
  53.3 8.4 %collective-permute-start.10 = (f32[480,128]{1,0:T(8,128)S(1)}, f32[480,128]{1,0:T(8,128)S(1)}, u32[]{:S(2)}, u32[]{:S(2)}) collective-permute-start(f32[480,128]{1,0:T(8,128)S(1)} %get-tuple-element.30), channel_id=1, source_target_pairs={{0,4},{1,5},{2,18},{3,19},{4,0},{5,1},{6,22},{7,23},{8,12},{9,13},... | collective-permute-start | bytes 737288 | tf_op jit(solution)/shard_map/ppermute | solution.py:196
  61.7 8.3 %collective-permute-start.14 = (f32[480,128]{1,0:T(8,128)S(1)}, f32[480,128]{1,0:T(8,128)S(1)}, u32[]{:S(2)}, u32[]{:S(2)}) collective-permute-start(f32[480,128]{1,0:T(8,128)S(1)} %add_add_fusion.1), channel_id=1, source_target_pairs={{0,24},{1,25},{2,7},{3,6},{4,28},{5,29},{6,3},{7,2},{8,16},{9,17},... | collective-permute-start | bytes 737288 | tf_op jit(solution)/shard_map/ppermute | solution.py:202
  62.3 13.6 %collective-permute-start.13 = (f32[480,128]{1,0:T(8,128)S(1)}, f32[480,128]{1,0:T(8,128)S(1)}, u32[]{:S(2)}, u32[]{:S(2)}) collective-permute-start(f32[480,128]{1,0:T(8,128)S(1)} %add_add_fusion.1), channel_id=1, source_target_pairs={{0,16},{1,17},{2,6},{3,7},{4,20},{5,21},{6,2},{7,3},{8,24},{9,25},... | collective-permute-start | bytes 737288 | tf_op jit(solution)/shard_map/ppermute | solution.py:202
  63.7 12.2 %collective-permute-start.12 = (f32[480,128]{1,0:T(8,128)S(1)}, f32[480,128]{1,0:T(8,128)S(1)}, u32[]{:S(2)}, u32[]{:S(2)}) collective-permute-start(f32[480,128]{1,0:T(8,128)S(1)} %add_add_fusion.1), channel_id=1, source_target_pairs={{0,8},{1,9},{2,3},{3,2},{4,12},{5,13},{6,7},{7,6},{8,0},{9,1},{10,... | collective-permute-start | bytes 737288 | tf_op jit(solution)/shard_map/ppermute | solution.py:202
  76.0 7.2 %collective-permute-start.17 = (f32[480,128]{1,0:T(8,128)S(1)}, f32[480,128]{1,0:T(8,128)S(1)}, u32[]{:S(2)}, u32[]{:S(2)}) collective-permute-start(f32[480,128]{1,0:T(8,128)S(1)} %add_add_fusion), channel_id=1, source_target_pairs={{0,5},{1,4},{2,26},{3,27},{4,1},{5,0},{6,30},{7,31},{8,13},{9,12},... | collective-permute-start | bytes 737288 | tf_op jit(solution)/shard_map/ppermute | solution.py:216
  78.7 8.3 %collective-permute-start.16 = (f32[480,128]{1,0:T(8,128)S(1)}, f32[480,128]{1,0:T(8,128)S(1)}, u32[]{:S(2)}, u32[]{:S(2)}) collective-permute-start(f32[480,128]{1,0:T(8,128)S(1)} %add_add_fusion), channel_id=1, source_target_pairs={{0,4},{1,5},{2,18},{3,19},{4,0},{5,1},{6,22},{7,23},{8,12},{9,13},... | collective-permute-start | bytes 737288 | tf_op jit(solution)/shard_map/ppermute | solution.py:216
  80.1 6.8 %collective-permute-start.15 = (f32[480,128]{1,0:T(8,128)S(1)}, f32[480,128]{1,0:T(8,128)S(1)}, u32[]{:S(2)}, u32[]{:S(2)}) collective-permute-start(f32[480,128]{1,0:T(8,128)S(1)} %add_add_fusion), channel_id=1, source_target_pairs={{0,1},{1,0},{2,10},{3,11},{4,5},{5,4},{6,14},{7,15},{8,9},{9,8},{1... | collective-permute-start | bytes 737288 | tf_op jit(solution)/shard_map/ppermute | solution.py:216
  87.2 1.4 %copy-start.12 = (bf16[768,256]{1,0:T(8,128)(2,1)S(1)}, bf16[768,256]{1,0:T(8,128)(2,1)}, u32[]{:S(2)}) copy-start(bf16[768,256]{1,0:T(8,128)(2,1)} %param.20) | copy-start | bytes 1179652
  87.2 1.3 %copy-start.17 = (f32[256]{0:T(256)S(1)}, f32[256]{0:T(256)}, u32[]{:S(2)}) copy-start(f32[256]{0:T(256)} %param.21) | copy-start | bytes 3076
  87.4 3.0 %collective-permute-start.18 = (f32[1920,128]{1,0:T(8,128)S(1)}, f32[1920,128]{1,0:T(8,128)S(1)}, u32[]{:S(2)}, u32[]{:S(2)}) collective-permute-start(f32[1920,128]{1,0:T(8,128)S(1)} %pad_maximum_fusion.2), channel_id=1, source_target_pairs={{0,2},{1,3},{2,0},{3,1},{4,6},{5,7},{6,4},{7,5},{8,10},{9,11},{10,... | collective-permute-start | bytes 2949128 | tf_op jit(solution)/shard_map/ppermute | solution.py:225
  (8 other events, 7.6 us)

commit v19 on v18

--- a/solution.py
+++ b/solution.py
@@ -243,7 +243,7 @@
     cols = width // 2
     core = lax.axis_index("dp") % 2
     tm = lax.axis_index("tm")
-    bounds = [0, 16, rows // 2, rows] if rows % 32 == 0 and rows > 32 else [0, rows]
+    bounds = [0, 16, rows] if rows % 32 == 0 and rows > 32 else [0, rows]
     swap = [(i, i ^ 1) for i in range(dp_size)]
     got_parts, partner_parts = [], []
     mine = jnp.where(core == 0, w_ups[:, :cols], w_ups[:, cols:])

time: 94.5 us -> 93 us (0.984)
  waiting for transfers between devices: 33.3 us -> 35.9 us
  starting transfers between devices: 32 us -> 29.7 us
  local copies, waits for them, and re-layouts: 12.1 us -> 11 us
    ppermute x3 -> x2, starting transfers between devices: 5.06 us -> 3.05 us  [ups_functions(): got_parts.append(lax.ppermute(mine[lo:hi], 'tm', [(0, 1), (1, 0)]))]
    ppermute x3 -> x2, waiting for transfers between devices: 0.32 us -> 1.57 us  [ups_functions(): partner_parts.append(lax.ppermute(got_parts[-1], 'dp', swap))]
    ppermute x3 -> x2, waiting for transfers between devices: 0.01 us -> 1.14 us  [ups_functions(): got_parts.append(lax.ppermute(mine[lo:hi], 'tm', [(0, 1), (1, 0)]))]
    select_n x3 -> x2, other arithmetic: 3.05 us -> 2.48 us  [ups_functions(): jnp.where(core == 0, g, p)]
  transfers between devices with their start and end apart: 20 -> 18, of which waited for: 12 -> 12; matrix products, arithmetic and copies ran while one was open for 11% -> 10% of each run, Pallas kernels for 0% -> 0%
where the time goes in v19:
time: 93 us; the launch traced here: 92.6 us
  waiting for transfers between devices  35.9 us (39%)
  starting transfers between devices  29.7 us (32%)
  local copies, waits for them, and re-layouts  11 us (12%)
  other arithmetic  9.11 us (10%)
  matrix products  5.62 us (6%)
  between operations  1.29 us (1%)
    ppermute x3, waiting for transfers between devices, butterfly_psum(): lax.ppermute(x, axes, perm_of(last, o))  9.86 us
    ppermute x3, waiting for transfers between devices, butterfly_psum(): total = total + lax.ppermute(send, axes, perm_of(step, offset))  6.85 us
    ppermute x3, waiting for transfers between devices, butterfly_psum(): lax.ppermute(x, axes, perm_of(step, o))  6.85 us
    all_to_all x1, starting transfers between devices, on_device(): lax.all_to_all(outgoing, 'dp', split_axis=0, concat_axis=0, tiled=True)  6.27 us
    all_to_all x1, waiting for transfers between devices, on_device(): lax.all_to_all(outgoing, 'dp', split_axis=0, concat_axis=0, tiled=True)  6.07 us
    ppermute x1, starting transfers between devices, with_halo(): lax.ppermute(lax.slice_in_dim(block, block.shape[dim] - width, None, axis...  5.12 us
    ppermute x3, starting transfers between devices, butterfly_psum(): lax.ppermute(x, axes, perm_of(last, o))  4.45 us
    unnamed x51, local copies, waits for them, and re-layouts  4.16 us
  transfers between devices with their start and end apart: 18, of which 12 were waited for; matrix products, arithmetic and copies ran while one was open for 10% of the time, Pallas kernels for 0%

profile of v19, /device:TPU:0, one launch (start us, length us, event | category | flops | bytes accessed | tf_op | source)
XLA Modules:
  0.0 92.6 jit_solution(13749202384300931689)
XLA Ops:
  0.7 1.7 %slice_select_fusion = bf16[256,2048]{1,0:T(8,128)(2,1)S(1)} fusion(bf16[256,4096]{1,0:T(8,128)(2,1)} %param.18, pred[]{:T(512)S(6)} %eq.135), kind=kLoop, calls=%fused_computation.21 | loop fusion | flops 524288 | bytes 3145729 | tf_op jit(solution)/shard_map/jit(_where)/select_n | solution.py:249
  2.4 3.0 %collective-permute-start = (bf16[16,2048]{1,0:T(8,128)(2,1)S(1)}, bf16[16,2048]{1,0:T(8,128)(2,1)S(1)}, u32[]{:S(2)}, u32[]{:S(2)}) collective-permute-start(bf16[16,2048]{1,0:T(8,128)(2,1)S(1)} %slice.134), channel_id=1, source_target_pairs={{0,1},{1,0},{2,3},{3,2},{4,5},{5,4},{6,7},{7,6},{8,9},{9,8},{10,11... | collective-permute-start | bytes 196616 | tf_op jit(solution)/shard_map/ppermute | solution.py:251
  5.5 1.0 %slice.146 = bf16[240,2048]{1,0:T(8,128)(2,1)} slice(bf16[256,2048]{1,0:T(8,128)(2,1)S(1)} %slice_select_fusion), slice={[16:256], [0:2048]} | slice | bytes 1966080 | tf_op jit(solution)/shard_map/slice | solution.py:251
  6.7 1.1 %collective-permute-done = bf16[16,2048]{1,0:T(8,128)(2,1)S(1)} collective-permute-done((bf16[16,2048]{1,0:T(8,128)(2,1)S(1)}, bf16[16,2048]{1,0:T(8,128)(2,1)S(1)}, u32[]{:S(2)}, u32[]{:S(2)}) %collective-permute-start) | collective-permute-done | bytes 65568 | tf_op jit(solution)/shard_map/ppermute | solution.py:251
  9.9 6.3 %all-to-all-start = ((bf16[16,2,321]{2,1,0:T(2,128)(2,1)}), bf16[16,2,321]{2,1,0:T(2,128)(2,1)S(1)}, u32[]{:S(2)}, u32[]{:S(2)}) async-start(bf16[16,2,321]{2,1,0:T(2,128)(2,1)} %reshape.119), calls=%async_computation | async-start | bytes 49152 | tf_op jit(solution)/shard_map/all_to_all | solution.py:299
  16.7 6.1 %all-to-all-done = bf16[16,2,321]{2,1,0:T(2,128)(2,1)S(1)} async-done(((bf16[16,2,321]{2,1,0:T(2,128)(2,1)}), bf16[16,2,321]{2,1,0:T(2,128)(2,1)S(1)}, u32[]{:S(2)}, u32[]{:S(2)}) %all-to-all-start) | async-done | bytes 20576 | tf_op jit(solution)/shard_map/all_to_all | solution.py:299
  24.2 1.3 %collective-permute-start.2 = (bf16[4,80]{1,0:T(4,128)(2,1)}, bf16[4,80]{1,0:T(4,128)(2,1)S(1)}, u32[]{:S(2)}, u32[]{:S(2)}) collective-permute-start(bf16[4,80]{1,0:T(4,128)(2,1)} %get-tuple-element.45), channel_id=1, source_target_pairs={{1,0},{3,2},{5,4},{7,6},{9,8},{11,10},{13,12},{15,14},{17,16},{19,... | collective-permute-start | bytes 1928 | tf_op jit(solution)/shard_map/ppermute | solution.py:19
  25.5 5.1 %collective-permute-start.1 = (bf16[4,80]{1,0:T(4,128)(2,1)}, bf16[4,80]{1,0:T(4,128)(2,1)}, u32[]{:S(2)}, u32[]{:S(2)}) collective-permute-start(bf16[4,80]{1,0:T(4,128)(2,1)} %get-tuple-element.46), channel_id=1, source_target_pairs={{0,1},{2,3},{4,5},{6,7},{8,9},{10,11},{12,13},{14,15},{16,17},{18,... | collective-permute-start | bytes 1928 | tf_op jit(solution)/shard_map/ppermute | solution.py:16
  31.6 0.8 pad_maximum_fusion.9
  33.1 0.9 broadcast_select_fusion.4
  33.9 1.6 %collective-permute-done.5 = bf16[240,2048]{1,0:T(8,128)(2,1)} collective-permute-done((bf16[240,2048]{1,0:T(8,128)(2,1)}, bf16[240,2048]{1,0:T(8,128)(2,1)}, u32[]{:S(2)}, u32[]{:S(2)}) %collective-permute-start.5) | collective-permute-done | bytes 983072 | tf_op jit(solution)/shard_map/ppermute | solution.py:252
  35.5 1.6 %broadcast_select_fusion.2 = (bf16[240,2048]{1,0:T(8,128)(2,1)S(1)}, bf16[240,2048]{1,0:T(8,128)(2,1)S(1)}) fusion(bf16[240,2048]{1,0:T(8,128)(2,1)} %collective-permute-done.4, bf16[240,2048]{1,0:T(8,128)(2,1)} %collective-permute-done.5, pred[]{:T(512)S(6)} %eq.135), kind=kLoop, calls=%fused_computation.26 | loop fusion | flops 983040 | bytes 3932161 | tf_op jit(solution)/shard_map/jit(_where)/select_n | solution.py:254
  37.8 0.9 %copy-done.1 = bf16[256,4096]{1,0:T(8,128)(2,1)S(1)} copy-done((bf16[256,4096]{1,0:T(8,128)(2,1)S(1)}, bf16[256,4096]{1,0:T(8,128)(2,1)}, u32[]{:S(2)}) %copy-start.1) | copy-done | bytes 2097176
  45.4 2.6 %collective-permute-done.6 = f32[1920,128]{1,0:T(8,128)} collective-permute-done((f32[1920,128]{1,0:T(8,128)S(1)}, f32[1920,128]{1,0:T(8,128)}, u32[]{:S(2)}, u32[]{:S(2)}) %collective-permute-start.6) | collective-permute-done | bytes 983072 | tf_op jit(solution)/shard_map/ppermute | solution.py:188
  48.0 1.3 %dynamic-slice_add_fusion = f32[1920,128]{1,0:T(8,128)S(1)} fusion(f32[1920,128]{1,0:T(8,128)} %collective-permute-done.6, f32[3840,128]{1,0:T(8,128)S(1)} %fusion, s32[]{:T(128)S(6)} %select_n.358), kind=kLoop, calls=%fused_computation.23 | loop fusion | flops 245760 | bytes 2949124 | tf_op jit(solution)/shard_map/add | solution.py:188
  49.4 2.3 %collective-permute-start.7 = (f32[480,128]{1,0:T(8,128)S(1)}, f32[480,128]{1,0:T(8,128)S(1)}, u32[]{:S(2)}, u32[]{:S(2)}) collective-permute-start(f32[480,128]{1,0:T(8,128)S(1)} %get-tuple-element.28), channel_id=1, source_target_pairs={{0,1},{1,0},{2,10},{3,11},{4,5},{5,4},{6,14},{7,15},{8,9},{9,8},{1... | collective-permute-start | bytes 737288 | tf_op jit(solution)/shard_map/ppermute | solution.py:196
  51.7 1.5 %collective-permute-start.8 = (f32[480,128]{1,0:T(8,128)S(1)}, f32[480,128]{1,0:T(8,128)S(1)}, u32[]{:S(2)}, u32[]{:S(2)}) collective-permute-start(f32[480,128]{1,0:T(8,128)S(1)} %get-tuple-element.30), channel_id=1, source_target_pairs={{0,4},{1,5},{2,18},{3,19},{4,0},{5,1},{6,22},{7,23},{8,12},{9,13},... | collective-permute-start | bytes 737288 | tf_op jit(solution)/shard_map/ppermute | solution.py:196
  53.2 4.8 %collective-permute-done.7 = f32[480,128]{1,0:T(8,128)S(1)} collective-permute-done((f32[480,128]{1,0:T(8,128)S(1)}, f32[480,128]{1,0:T(8,128)S(1)}, u32[]{:S(2)}, u32[]{:S(2)}) %collective-permute-start.7) | collective-permute-done | bytes 245792 | tf_op jit(solution)/shard_map/ppermute | solution.py:196
  58.8 1.3 %collective-permute-done.8 = f32[480,128]{1,0:T(8,128)S(1)} collective-permute-done((f32[480,128]{1,0:T(8,128)S(1)}, f32[480,128]{1,0:T(8,128)S(1)}, u32[]{:S(2)}, u32[]{:S(2)}) %collective-permute-start.8) | collective-permute-done | bytes 245792 | tf_op jit(solution)/shard_map/ppermute | solution.py:196
  60.1 1.8 %collective-permute-start.12 = (f32[480,128]{1,0:T(8,128)S(1)}, f32[480,128]{1,0:T(8,128)S(1)}, u32[]{:S(2)}, u32[]{:S(2)}) collective-permute-start(f32[480,128]{1,0:T(8,128)S(1)} %add_add_fusion.1), channel_id=1, source_target_pairs={{0,24},{1,25},{2,7},{3,6},{4,28},{5,29},{6,3},{7,2},{8,16},{9,17},... | collective-permute-start | bytes 737288 | tf_op jit(solution)/shard_map/ppermute | solution.py:202
  62.0 2.5 %collective-permute-start.10 = (f32[480,128]{1,0:T(8,128)S(1)}, f32[480,128]{1,0:T(8,128)S(1)}, u32[]{:S(2)}, u32[]{:S(2)}) collective-permute-start(f32[480,128]{1,0:T(8,128)S(1)} %add_add_fusion.1), channel_id=1, source_target_pairs={{0,8},{1,9},{2,3},{3,2},{4,12},{5,13},{6,7},{7,6},{8,0},{9,1},{10,... | collective-permute-start | bytes 737288 | tf_op jit(solution)/shard_map/ppermute | solution.py:202
  64.6 3.8 %collective-permute-done.12 = f32[480,128]{1,0:T(8,128)S(1)} collective-permute-done((f32[480,128]{1,0:T(8,128)S(1)}, f32[480,128]{1,0:T(8,128)S(1)}, u32[]{:S(2)}, u32[]{:S(2)}) %collective-permute-start.12) | collective-permute-done | bytes 245792 | tf_op jit(solution)/shard_map/ppermute | solution.py:202
  68.4 6.1 %collective-permute-done.11 = f32[480,128]{1,0:T(8,128)S(1)} collective-permute-done((f32[480,128]{1,0:T(8,128)S(1)}, f32[480,128]{1,0:T(8,128)S(1)}, u32[]{:S(2)}, u32[]{:S(2)}) %collective-permute-start.11) | collective-permute-done | bytes 245792 | tf_op jit(solution)/shard_map/ppermute | solution.py:202
  74.6 2.1 %collective-permute-start.15 = (f32[480,128]{1,0:T(8,128)S(1)}, f32[480,128]{1,0:T(8,128)S(1)}, u32[]{:S(2)}, u32[]{:S(2)}) collective-permute-start(f32[480,128]{1,0:T(8,128)S(1)} %add_add_fusion), channel_id=1, source_target_pairs={{0,5},{1,4},{2,26},{3,27},{4,1},{5,0},{6,30},{7,31},{8,13},{9,12},... | collective-permute-start | bytes 737288 | tf_op jit(solution)/shard_map/ppermute | solution.py:216
  76.7 1.8 %collective-permute-start.14 = (f32[480,128]{1,0:T(8,128)S(1)}, f32[480,128]{1,0:T(8,128)S(1)}, u32[]{:S(2)}, u32[]{:S(2)}) collective-permute-start(f32[480,128]{1,0:T(8,128)S(1)} %add_add_fusion), channel_id=1, source_target_pairs={{0,4},{1,5},{2,18},{3,19},{4,0},{5,1},{6,22},{7,23},{8,12},{9,13},... | collective-permute-start | bytes 737288 | tf_op jit(solution)/shard_map/ppermute | solution.py:216
  78.5 3.2 %collective-permute-done.15 = f32[480,128]{1,0:T(8,128)S(1)} collective-permute-done((f32[480,128]{1,0:T(8,128)S(1)}, f32[480,128]{1,0:T(8,128)S(1)}, u32[]{:S(2)}, u32[]{:S(2)}) %collective-permute-start.15) | collective-permute-done | bytes 245792 | tf_op jit(solution)/shard_map/ppermute | solution.py:216
  81.7 3.6 %collective-permute-done.14 = f32[480,128]{1,0:T(8,128)S(1)} collective-permute-done((f32[480,128]{1,0:T(8,128)S(1)}, f32[480,128]{1,0:T(8,128)S(1)}, u32[]{:S(2)}, u32[]{:S(2)}) %collective-permute-start.14) | collective-permute-done | bytes 245792 | tf_op jit(solution)/shard_map/ppermute | solution.py:216
  85.7 1.0 %collective-permute-start.16 = (f32[1920,128]{1,0:T(8,128)S(1)}, f32[1920,128]{1,0:T(8,128)S(1)}, u32[]{:S(2)}, u32[]{:S(2)}) collective-permute-start(f32[1920,128]{1,0:T(8,128)S(1)} %pad_maximum_fusion.2), channel_id=1, source_target_pairs={{0,2},{1,3},{2,0},{3,1},{4,6},{5,7},{6,4},{7,5},{8,10},{9,11},{10,... | collective-permute-start | bytes 2949128 | tf_op jit(solution)/shard_map/ppermute | solution.py:225
  86.9 1.1 %fusion.3 = bf16[1,512,256]{2,1,0:T(8,128)(2,1)} fusion(bf16[768,256]{1,0:T(8,128)(2,1)S(1)} %copy-done.12, f32[518,256]{1,0:T(8,128)S(1)} %copy-done.4, bf16[512,256]{1,0:T(8,128)(2,1)S(1)} %copy-done.8, bf16[512,256]{1,0:T(8,128)(2,1)S(1)} %copy-done.10, bf16[512,256]{1,0:T(8,128)(2,1)S(1)} %copy-done.6, f32[256]{0:T(256)S(1)} %copy-done.17), kind=kOutput, calls=%fused_computation.9 | convolution fusion | flops 204079104 | bytes 1967104 | tf_op jit(solution)/shard_map/dot_general | solution.py:92
  88.0 1.0 %collective-permute-done.16 = f32[1920,128]{1,0:T(8,128)S(1)} collective-permute-done((f32[1920,128]{1,0:T(8,128)S(1)}, f32[1920,128]{1,0:T(8,128)S(1)}, u32[]{:S(2)}, u32[]{:S(2)}) %collective-permute-start.16) | collective-permute-done | bytes 983072 | tf_op jit(solution)/shard_map/ppermute | solution.py:225
  90.6 0.9 %slice.162 = f32[1536,128]{1,0:T(8,128)} slice(f32[3840,128]{1,0:T(8,128)S(1)} %broadcast_select_fusion), slice={[2244:3780], [0:128]} | slice | bytes 1572864 | tf_op jit(solution)/shard_map/slice | solution.py:229
  91.5 1.1 %slice.160 = f32[2240,128]{1,0:T(8,128)} slice(f32[3840,128]{1,0:T(8,128)S(1)} %broadcast_select_fusion), slice={[0:2240], [0:128]} | slice | bytes 2293760 | tf_op jit(solution)/shard_map/slice | solution.py:229
  (123 shorter events, 16.0 us)
Async XLA Ops:
  0.6 32.1 %copy-start = (bf16[560,512]{1,0:T(8,128)(2,1)S(1)}, bf16[560,512]{1,0:T(8,128)(2,1)}, u32[]{:S(2)}) copy-start(bf16[560,512]{1,0:T(8,128)(2,1)} %param.16) | copy-start | bytes 1720324
  0.7 5.8 %copy-start.18 = (s32[1,8]{1,0:T(1,128)S(1)}, s32[1,8]{1,0:T(1,128)}, u32[]{:S(2)}) copy-start(s32[1,8]{1,0:T(1,128)} %param.13) | copy-start | bytes 100
  0.7 5.8 %copy-start.19 = (s32[1,8]{1,0:T(1,128)S(1)}, s32[1,8]{1,0:T(1,128)}, u32[]{:S(2)}) copy-start(s32[1,8]{1,0:T(1,128)} %param.14) | copy-start | bytes 100
  0.7 7.2 %copy-start.13 = (bf16[1,8,640]{2,1,0:T(8,128)(2,1)S(1)}, bf16[1,8,640]{2,1,0:T(8,128)(2,1)}, u32[]{:S(2)}) copy-start(bf16[1,8,640]{2,1,0:T(8,128)(2,1)} %param.11) | copy-start | bytes 30724
  0.7 7.2 %copy-start.16 = (s32[1,8]{1,0:T(1,128)S(1)}, s32[1,8]{1,0:T(1,128)}, u32[]{:S(2)}) copy-start(s32[1,8]{1,0:T(1,128)} %param.12) | copy-start | bytes 100
  2.4 28.2 %copy-start.2 = (bf16[1,512,256]{2,1,0:T(8,128)(2,1)S(1)}, bf16[1,512,256]{2,1,0:T(8,128)(2,1)}, u32[]{:S(2)}) copy-start(bf16[1,512,256]{2,1,0:T(8,128)(2,1)} %param.15) | copy-start | bytes 786436
  2.4 28.5 %copy-start.11 = (bf16[768,256]{1,0:T(8,128)(2,1)S(1)}, bf16[768,256]{1,0:T(8,128)(2,1)}, u32[]{:S(2)}) copy-start(bf16[768,256]{1,0:T(8,128)(2,1)} %param.20) | copy-start | bytes 1179652
  2.4 5.4 %collective-permute-start = (bf16[16,2048]{1,0:T(8,128)(2,1)S(1)}, bf16[16,2048]{1,0:T(8,128)(2,1)S(1)}, u32[]{:S(2)}, u32[]{:S(2)}) collective-permute-start(bf16[16,2048]{1,0:T(8,128)(2,1)S(1)} %slice.134), channel_id=1, source_target_pairs={{0,1},{1,0},{2,3},{3,2},{4,5},{5,4},{6,7},{7,6},{8,9},{9,8},{10,11... | collective-permute-start | bytes 196616 | tf_op jit(solution)/shard_map/ppermute | solution.py:251
  6.5 26.0 %collective-permute-start.4 = (bf16[240,2048]{1,0:T(8,128)(2,1)}, bf16[240,2048]{1,0:T(8,128)(2,1)}, u32[]{:S(2)}, u32[]{:S(2)}) collective-permute-start(bf16[240,2048]{1,0:T(8,128)(2,1)} %slice.146), channel_id=1, source_target_pairs={{0,1},{1,0},{2,3},{3,2},{4,5},{5,4},{6,7},{7,6},{8,9},{9,8},{10,11... | collective-permute-start | bytes 2949128 | tf_op jit(solution)/shard_map/ppermute | solution.py:251
  9.9 12.8 %all-to-all-start = ((bf16[16,2,321]{2,1,0:T(2,128)(2,1)}), bf16[16,2,321]{2,1,0:T(2,128)(2,1)S(1)}, u32[]{:S(2)}, u32[]{:S(2)}) async-start(bf16[16,2,321]{2,1,0:T(2,128)(2,1)} %reshape.119), calls=%async_computation | async-start | bytes 49152 | tf_op jit(solution)/shard_map/all_to_all | solution.py:299
  16.3 16.8 %collective-permute-start.3 = (bf16[16,2048]{1,0:T(8,128)(2,1)S(1)}, bf16[16,2048]{1,0:T(8,128)(2,1)}, u32[]{:S(2)}, u32[]{:S(2)}) collective-permute-start(bf16[16,2048]{1,0:T(8,128)(2,1)S(1)} %collective-permute-done), channel_id=1, source_target_pairs={{0,2},{2,0},{4,6},{6,4},{8,10},{10,8},{12,14},{14,12},{16,18},{18,... | collective-permute-start | bytes 196616 | tf_op jit(solution)/shard_map/ppermute | solution.py:252
  24.2 7.5 %collective-permute-start.2 = (bf16[4,80]{1,0:T(4,128)(2,1)}, bf16[4,80]{1,0:T(4,128)(2,1)S(1)}, u32[]{:S(2)}, u32[]{:S(2)}) collective-permute-start(bf16[4,80]{1,0:T(4,128)(2,1)} %get-tuple-element.45), channel_id=1, source_target_pairs={{1,0},{3,2},{5,4},{7,6},{9,8},{11,10},{13,12},{15,14},{17,16},{19,... | collective-permute-start | bytes 1928 | tf_op jit(solution)/shard_map/ppermute | solution.py:19
  25.5 6.2 %collective-permute-start.1 = (bf16[4,80]{1,0:T(4,128)(2,1)}, bf16[4,80]{1,0:T(4,128)(2,1)}, u32[]{:S(2)}, u32[]{:S(2)}) collective-permute-start(bf16[4,80]{1,0:T(4,128)(2,1)} %get-tuple-element.46), channel_id=1, source_target_pairs={{0,1},{2,3},{4,5},{6,7},{8,9},{10,11},{12,13},{14,15},{16,17},{18,... | collective-permute-start | bytes 1928 | tf_op jit(solution)/shard_map/ppermute | solution.py:16
  31.3 1.5 %copy-start.14 = (f32[512]{0:T(512)S(1)}, f32[512]{0:T(512)}, u32[]{:S(2)}) copy-start(f32[512]{0:T(512)} %param.17) | copy-start | bytes 6148
  32.5 3.0 %collective-permute-start.5 = (bf16[240,2048]{1,0:T(8,128)(2,1)}, bf16[240,2048]{1,0:T(8,128)(2,1)}, u32[]{:S(2)}, u32[]{:S(2)}) collective-permute-start(bf16[240,2048]{1,0:T(8,128)(2,1)} %collective-permute-done.4), channel_id=1, source_target_pairs={{0,2},{2,0},{4,6},{6,4},{8,10},{10,8},{12,14},{14,12},{16,18},{18,... | collective-permute-start | bytes 2949128 | tf_op jit(solution)/shard_map/ppermute | solution.py:252
  37.1 1.6 %copy-start.1 = (bf16[256,4096]{1,0:T(8,128)(2,1)S(1)}, bf16[256,4096]{1,0:T(8,128)(2,1)}, u32[]{:S(2)}) copy-start(bf16[256,4096]{1,0:T(8,128)(2,1)} %param.18) | copy-start | bytes 6291460
  40.6 1.6 %copy-start.3 = (f32[518,256]{1,0:T(8,128)}, f32[518,256]{1,0:T(8,128)S(1)}, u32[]{:S(2)}) copy-start(f32[518,256]{1,0:T(8,128)S(1)} %get-tuple-element.20) | copy-start | bytes 1591300
  45.2 2.8 %collective-permute-start.6 = (f32[1920,128]{1,0:T(8,128)S(1)}, f32[1920,128]{1,0:T(8,128)}, u32[]{:S(2)}, u32[]{:S(2)}) collective-permute-start(f32[1920,128]{1,0:T(8,128)S(1)} %constant_dynamic-slice_fusion.3), channel_id=1, source_target_pairs={{0,2},{1,3},{2,0},{3,1},{4,6},{5,7},{6,4},{7,5},{8,10},{9,11},{10,... | collective-permute-start | bytes 2949128 | tf_op jit(solution)/shard_map/ppermute | solution.py:188
  49.4 8.6 %collective-permute-start.7 = (f32[480,128]{1,0:T(8,128)S(1)}, f32[480,128]{1,0:T(8,128)S(1)}, u32[]{:S(2)}, u32[]{:S(2)}) collective-permute-start(f32[480,128]{1,0:T(8,128)S(1)} %get-tuple-element.28), channel_id=1, source_target_pairs={{0,1},{1,0},{2,10},{3,11},{4,5},{5,4},{6,14},{7,15},{8,9},{9,8},{1... | collective-permute-start | bytes 737288 | tf_op jit(solution)/shard_map/ppermute | solution.py:196
  51.7 7.1 %collective-permute-start.9 = (f32[480,128]{1,0:T(8,128)S(1)}, f32[480,128]{1,0:T(8,128)S(1)}, u32[]{:S(2)}, u32[]{:S(2)}) collective-permute-start(f32[480,128]{1,0:T(8,128)S(1)} %get-tuple-element.29), channel_id=1, source_target_pairs={{0,5},{1,4},{2,26},{3,27},{4,1},{5,0},{6,30},{7,31},{8,13},{9,12},... | collective-permute-start | bytes 737288 | tf_op jit(solution)/shard_map/ppermute | solution.py:196
  51.7 8.4 %collective-permute-start.8 = (f32[480,128]{1,0:T(8,128)S(1)}, f32[480,128]{1,0:T(8,128)S(1)}, u32[]{:S(2)}, u32[]{:S(2)}) collective-permute-start(f32[480,128]{1,0:T(8,128)S(1)} %get-tuple-element.30), channel_id=1, source_target_pairs={{0,4},{1,5},{2,18},{3,19},{4,0},{5,1},{6,22},{7,23},{8,12},{9,13},... | collective-permute-start | bytes 737288 | tf_op jit(solution)/shard_map/ppermute | solution.py:196
  60.1 8.3 %collective-permute-start.12 = (f32[480,128]{1,0:T(8,128)S(1)}, f32[480,128]{1,0:T(8,128)S(1)}, u32[]{:S(2)}, u32[]{:S(2)}) collective-permute-start(f32[480,128]{1,0:T(8,128)S(1)} %add_add_fusion.1), channel_id=1, source_target_pairs={{0,24},{1,25},{2,7},{3,6},{4,28},{5,29},{6,3},{7,2},{8,16},{9,17},... | collective-permute-start | bytes 737288 | tf_op jit(solution)/shard_map/ppermute | solution.py:202
  61.9 12.5 %collective-permute-start.11 = (f32[480,128]{1,0:T(8,128)S(1)}, f32[480,128]{1,0:T(8,128)S(1)}, u32[]{:S(2)}, u32[]{:S(2)}) collective-permute-start(f32[480,128]{1,0:T(8,128)S(1)} %add_add_fusion.1), channel_id=1, source_target_pairs={{0,16},{1,17},{2,6},{3,7},{4,20},{5,21},{6,2},{7,3},{8,24},{9,25},... | collective-permute-start | bytes 737288 | tf_op jit(solution)/shard_map/ppermute | solution.py:202
  62.0 12.4 %collective-permute-start.10 = (f32[480,128]{1,0:T(8,128)S(1)}, f32[480,128]{1,0:T(8,128)S(1)}, u32[]{:S(2)}, u32[]{:S(2)}) collective-permute-start(f32[480,128]{1,0:T(8,128)S(1)} %add_add_fusion.1), channel_id=1, source_target_pairs={{0,8},{1,9},{2,3},{3,2},{4,12},{5,13},{6,7},{7,6},{8,0},{9,1},{10,... | collective-permute-start | bytes 737288 | tf_op jit(solution)/shard_map/ppermute | solution.py:202
  74.6 7.2 %collective-permute-start.15 = (f32[480,128]{1,0:T(8,128)S(1)}, f32[480,128]{1,0:T(8,128)S(1)}, u32[]{:S(2)}, u32[]{:S(2)}) collective-permute-start(f32[480,128]{1,0:T(8,128)S(1)} %add_add_fusion), channel_id=1, source_target_pairs={{0,5},{1,4},{2,26},{3,27},{4,1},{5,0},{6,30},{7,31},{8,13},{9,12},... | collective-permute-start | bytes 737288 | tf_op jit(solution)/shard_map/ppermute | solution.py:216
  76.7 8.7 %collective-permute-start.14 = (f32[480,128]{1,0:T(8,128)S(1)}, f32[480,128]{1,0:T(8,128)S(1)}, u32[]{:S(2)}, u32[]{:S(2)}) collective-permute-start(f32[480,128]{1,0:T(8,128)S(1)} %add_add_fusion), channel_id=1, source_target_pairs={{0,4},{1,5},{2,18},{3,19},{4,0},{5,1},{6,22},{7,23},{8,12},{9,13},... | collective-permute-start | bytes 737288 | tf_op jit(solution)/shard_map/ppermute | solution.py:216
  78.5 6.8 %collective-permute-start.13 = (f32[480,128]{1,0:T(8,128)S(1)}, f32[480,128]{1,0:T(8,128)S(1)}, u32[]{:S(2)}, u32[]{:S(2)}) collective-permute-start(f32[480,128]{1,0:T(8,128)S(1)} %add_add_fusion), channel_id=1, source_target_pairs={{0,1},{1,0},{2,10},{3,11},{4,5},{5,4},{6,14},{7,15},{8,9},{9,8},{1... | collective-permute-start | bytes 737288 | tf_op jit(solution)/shard_map/ppermute | solution.py:216
  85.5 1.3 %copy-start.4 = (f32[518,256]{1,0:T(8,128)S(1)}, f32[518,256]{1,0:T(8,128)}, u32[]{:S(2)}) copy-start(f32[518,256]{1,0:T(8,128)} %copy-done.3) | copy-start | bytes 1591300
  85.5 1.2 %copy-start.6 = (bf16[512,256]{1,0:T(8,128)(2,1)S(1)}, bf16[512,256]{1,0:T(8,128)(2,1)}, u32[]{:S(2)}) copy-start(bf16[512,256]{1,0:T(8,128)(2,1)} %copy-done.5) | copy-start | bytes 786436
  85.6 1.4 %copy-start.12 = (bf16[768,256]{1,0:T(8,128)(2,1)S(1)}, bf16[768,256]{1,0:T(8,128)(2,1)}, u32[]{:S(2)}) copy-start(bf16[768,256]{1,0:T(8,128)(2,1)} %param.20) | copy-start | bytes 1179652
  85.6 1.3 %copy-start.17 = (f32[256]{0:T(256)S(1)}, f32[256]{0:T(256)}, u32[]{:S(2)}) copy-start(f32[256]{0:T(256)} %param.21) | copy-start | bytes 3076
  85.7 3.2 %collective-permute-start.16 = (f32[1920,128]{1,0:T(8,128)S(1)}, f32[1920,128]{1,0:T(8,128)S(1)}, u32[]{:S(2)}, u32[]{:S(2)}) collective-permute-start(f32[1920,128]{1,0:T(8,128)S(1)} %pad_maximum_fusion.2), channel_id=1, source_target_pairs={{0,2},{1,3},{2,0},{3,1},{4,6},{5,7},{6,4},{7,5},{8,10},{9,11},{10,... | collective-permute-start | bytes 2949128 | tf_op jit(solution)/shard_map/ppermute | solution.py:225
  (6 other events, 5.5 us)

commit v20 on v19

--- a/solution.py
+++ b/solution.py
@@ -243,19 +243,19 @@
     cols = width // 2
     core = lax.axis_index("dp") % 2
     tm = lax.axis_index("tm")
-    bounds = [0, 16, rows] if rows % 32 == 0 and rows > 32 else [0, rows]
+    head = 16 if rows % 32 == 0 and rows > 32 else 0
     swap = [(i, i ^ 1) for i in range(dp_size)]
-    got_parts, partner_parts = [], []
-    mine = jnp.where(core == 0, w_ups[:, :cols], w_ups[:, cols:])
-    for lo, hi in zip(bounds, bounds[1:]):
-        got_parts.append(lax.ppermute(mine[lo:hi], "tm", [(0, 1), (1, 0)]))
-        partner_parts.append(lax.ppermute(got_parts[-1], "dp", swap))
-    low = jnp.concatenate(
-        [jnp.where(core == 0, g, p) for g, p in zip(got_parts, partner_parts)]
-    )
-    high = jnp.concatenate(
-        [jnp.where(core == 0, p, g) for g, p in zip(got_parts, partner_parts)]
-    )
+    mine = jnp.where(core == 0, w_ups[head:, :cols], w_ups[head:, cols:])
+    got = lax.ppermute(mine, "tm", [(0, 1), (1, 0)])
+    partner = lax.ppermute(got, "dp", swap)
+    low = jnp.where(core == 0, got, partner)
+    high = jnp.where(core == 0, partner, got)
+    got_parts = [got]
+    if head:
+        first = lax.ppermute(w_ups[:head], "tm", [(0, 1), (1, 0)])
+        got_parts = [first]
+        low = jnp.concatenate([first[:, :cols], low])
+        high = jnp.concatenate([first[:, cols:], high])
 
     def forward(act):
         own_act = lax.dynamic_slice_in_dim(act, tm * rows, rows, axis=1)

time: 93 us -> 94.9 us (1.020)
  waiting for transfers between devices: 35.9 us -> 40 us
  starting transfers between devices: 29.7 us -> 27.4 us
  other arithmetic: 9.11 us -> 7.98 us
    ppermute x4 -> x3, waiting for transfers between devices: 2.71 us -> 4.77 us  [the longest x1 3.49 us: ups_functions(): got = lax.ppermute(mine, 'tm', [(0, 1), (1, 0)])]
    ppermute x1, starting transfers between devices: 5.12 us -> 3.26 us  [with_halo(): lax.ppermute(lax.slice_in_dim(block, block.shape[dim] - width, None, axis...]
    ppermute x1, waiting for transfers between devices: 0.01 us -> 1.32 us  [with_halo(): lax.ppermute(lax.slice_in_dim(block, block.shape[dim] - width, None, axis...]
    select_n x3 -> x2, other arithmetic: 4.19 us -> 3.31 us  [the longest x1 1.66 us: ups_functions(): low = jnp.where(core == 0, got, partner)]
    ppermute x4 -> x3, starting transfers between devices: 3.59 us -> 3.14 us  [the longest x1 3.03 us: ups_functions(): first = lax.ppermute(w_ups[:head], 'tm', [(0, 1), (1, 0)])]
    unnamed x51 -> x55, local copies, waits for them, and re-layouts: 4.16 us -> 4.01 us
  transfers between devices with their start and end apart: 18 -> 17, of which waited for: 12 -> 13; matrix products, arithmetic and copies ran while one was open for 10% -> 10% of each run, Pallas kernels for 0% -> 0%
where the time goes in v20:
time: 94.9 us; the launch traced here: 94.5 us
  waiting for transfers between devices  40 us (42%)
  starting transfers between devices  27.4 us (29%)
  local copies, waits for them, and re-layouts  11.4 us (12%)
  other arithmetic  7.98 us (8%)
  matrix products  6.29 us (7%)
  between operations  1.4 us (1%)
    ppermute x3, waiting for transfers between devices, butterfly_psum(): lax.ppermute(x, axes, perm_of(last, o))  10.8 us
    ppermute x3, waiting for transfers between devices, butterfly_psum(): total = total + lax.ppermute(send, axes, perm_of(step, offset))  6.85 us
    ppermute x3, waiting for transfers between devices, butterfly_psum(): lax.ppermute(x, axes, perm_of(step, o))  6.74 us
    all_to_all x1, waiting for transfers between devices, on_device(): lax.all_to_all(outgoing, 'dp', split_axis=0, concat_axis=0, tiled=True)  5.93 us
    all_to_all x1, starting transfers between devices, on_device(): lax.all_to_all(outgoing, 'dp', split_axis=0, concat_axis=0, tiled=True)  5.77 us
    ppermute x3, starting transfers between devices, butterfly_psum(): lax.ppermute(x, axes, perm_of(last, o))  4.45 us
    unnamed x55, local copies, waits for them, and re-layouts  4.01 us
    ppermute x3, starting transfers between devices, butterfly_psum(): lax.ppermute(x, axes, perm_of(step, o))  3.9 us
  transfers between devices with their start and end apart: 17, of which 13 were waited for; matrix products, arithmetic and copies ran while one was open for 10% of the time, Pallas kernels for 0%

profile of v20, /device:TPU:0, one launch (start us, length us, event | category | flops | bytes accessed | tf_op | source)
XLA Modules:
  0.0 94.5 jit_solution(7447715292933521163)
XLA Ops:
  0.7 1.0 %slice.105 = bf16[16,4096]{1,0:T(8,128)(2,1)S(1)} slice(bf16[256,4096]{1,0:T(8,128)(2,1)} %param.18), slice={[0:16], [0:4096]} | slice | bytes 262144 | tf_op jit(solution)/shard_map/slice | solution.py:255
  1.7 3.0 %collective-permute-start = (bf16[16,4096]{1,0:T(8,128)(2,1)S(1)}, bf16[16,4096]{1,0:T(8,128)(2,1)S(1)}, u32[]{:S(2)}, u32[]{:S(2)}) collective-permute-start(bf16[16,4096]{1,0:T(8,128)(2,1)S(1)} %slice.105), channel_id=1, source_target_pairs={{0,1},{1,0},{2,3},{3,2},{4,5},{5,4},{6,7},{7,6},{8,9},{9,8},{10,11... | collective-permute-start | bytes 393224 | tf_op jit(solution)/shard_map/ppermute | solution.py:255
  4.7 1.7 %slice_select_fusion = bf16[240,2048]{1,0:T(8,128)(2,1)S(1)} fusion(bf16[256,4096]{1,0:T(8,128)(2,1)} %param.18, pred[]{:T(512)S(6)} %eq.137), kind=kLoop, calls=%fused_computation.23 | loop fusion | flops 491520 | bytes 2949121 | tf_op jit(solution)/shard_map/jit(_where)/select_n | solution.py:248
  7.3 1.3 %collective-permute-done = bf16[16,4096]{1,0:T(8,128)(2,1)S(1)} collective-permute-done((bf16[16,4096]{1,0:T(8,128)(2,1)S(1)}, bf16[16,4096]{1,0:T(8,128)(2,1)S(1)}, u32[]{:S(2)}, u32[]{:S(2)}) %collective-permute-start) | collective-permute-done | bytes 131104 | tf_op jit(solution)/shard_map/ppermute | solution.py:255
  10.7 5.8 %all-to-all-start = ((bf16[16,2,321]{2,1,0:T(2,128)(2,1)}), bf16[16,2,321]{2,1,0:T(2,128)(2,1)S(1)}, u32[]{:S(2)}, u32[]{:S(2)}) async-start(bf16[16,2,321]{2,1,0:T(2,128)(2,1)} %reshape.119), calls=%async_computation | async-start | bytes 49152 | tf_op jit(solution)/shard_map/all_to_all | solution.py:299
  17.1 5.9 %all-to-all-done = bf16[16,2,321]{2,1,0:T(2,128)(2,1)S(1)} async-done(((bf16[16,2,321]{2,1,0:T(2,128)(2,1)}), bf16[16,2,321]{2,1,0:T(2,128)(2,1)S(1)}, u32[]{:S(2)}, u32[]{:S(2)}) %all-to-all-start) | async-done | bytes 20576 | tf_op jit(solution)/shard_map/all_to_all | solution.py:299
  24.4 1.3 %collective-permute-start.2 = (bf16[4,80]{1,0:T(4,128)(2,1)}, bf16[4,80]{1,0:T(4,128)(2,1)S(1)}, u32[]{:S(2)}, u32[]{:S(2)}) collective-permute-start(bf16[4,80]{1,0:T(4,128)(2,1)} %get-tuple-element.45), channel_id=1, source_target_pairs={{1,0},{3,2},{5,4},{7,6},{9,8},{11,10},{13,12},{15,14},{17,16},{19,... | collective-permute-start | bytes 1928 | tf_op jit(solution)/shard_map/ppermute | solution.py:19
  26.3 3.5 %collective-permute-done.3 = bf16[240,2048]{1,0:T(8,128)(2,1)} collective-permute-done((bf16[240,2048]{1,0:T(8,128)(2,1)S(1)}, bf16[240,2048]{1,0:T(8,128)(2,1)}, u32[]{:S(2)}, u32[]{:S(2)}) %collective-permute-start.3) | collective-permute-done | bytes 983072 | tf_op jit(solution)/shard_map/ppermute | solution.py:249
  30.1 3.3 %collective-permute-start.1 = (bf16[4,80]{1,0:T(4,128)(2,1)}, bf16[4,80]{1,0:T(4,128)(2,1)S(1)}, u32[]{:S(2)}, u32[]{:S(2)}) collective-permute-start(bf16[4,80]{1,0:T(4,128)(2,1)} %get-tuple-element.46), channel_id=1, source_target_pairs={{0,1},{2,3},{4,5},{6,7},{8,9},{10,11},{12,13},{14,15},{16,17},{18,... | collective-permute-start | bytes 1928 | tf_op jit(solution)/shard_map/ppermute | solution.py:16
  33.5 1.3 %collective-permute-done.1 = bf16[4,80]{1,0:T(4,128)(2,1)S(1)} collective-permute-done((bf16[4,80]{1,0:T(4,128)(2,1)}, bf16[4,80]{1,0:T(4,128)(2,1)S(1)}, u32[]{:S(2)}, u32[]{:S(2)}) %collective-permute-start.1) | collective-permute-done | bytes 672 | tf_op jit(solution)/shard_map/ppermute | solution.py:16
  35.1 0.9 fusion.27
  36.0 1.7 %broadcast_select_fusion.2 = (bf16[240,2048]{1,0:T(8,128)(2,1)S(1)}, bf16[240,2048]{1,0:T(8,128)(2,1)S(1)}) fusion(bf16[240,2048]{1,0:T(8,128)(2,1)} %collective-permute-done.3, bf16[240,2048]{1,0:T(8,128)(2,1)} %collective-permute-done.4, pred[]{:T(512)S(6)} %eq.137), kind=kLoop, calls=%fused_computation.26 | loop fusion | flops 983040 | bytes 3932161 | tf_op jit(solution)/shard_map/jit(_where)/select_n | solution.py:251
  38.3 0.9 copy-done.1
  42.0 0.8 fusion.62
  46.0 2.6 %collective-permute-done.5 = f32[1920,128]{1,0:T(8,128)} collective-permute-done((f32[1920,128]{1,0:T(8,128)S(1)}, f32[1920,128]{1,0:T(8,128)}, u32[]{:S(2)}, u32[]{:S(2)}) %collective-permute-start.5) | collective-permute-done | bytes 983072 | tf_op jit(solution)/shard_map/ppermute | solution.py:188
  48.6 1.3 %dynamic-slice_add_fusion = f32[1920,128]{1,0:T(8,128)S(1)} fusion(f32[1920,128]{1,0:T(8,128)} %collective-permute-done.5, f32[3840,128]{1,0:T(8,128)S(1)} %fusion, s32[]{:T(128)S(6)} %select_n.338), kind=kLoop, calls=%fused_computation.22 | loop fusion | flops 245760 | bytes 2949124 | tf_op jit(solution)/shard_map/add | solution.py:188
  49.9 2.3 %collective-permute-start.6 = (f32[480,128]{1,0:T(8,128)S(1)}, f32[480,128]{1,0:T(8,128)S(1)}, u32[]{:S(2)}, u32[]{:S(2)}) collective-permute-start(f32[480,128]{1,0:T(8,128)S(1)} %get-tuple-element.28), channel_id=1, source_target_pairs={{0,1},{1,0},{2,10},{3,11},{4,5},{5,4},{6,14},{7,15},{8,9},{9,8},{1... | collective-permute-start | bytes 737288 | tf_op jit(solution)/shard_map/ppermute | solution.py:196
  52.3 1.0 %collective-permute-start.8 = (f32[480,128]{1,0:T(8,128)S(1)}, f32[480,128]{1,0:T(8,128)S(1)}, u32[]{:S(2)}, u32[]{:S(2)}) collective-permute-start(f32[480,128]{1,0:T(8,128)S(1)} %get-tuple-element.29), channel_id=1, source_target_pairs={{0,5},{1,4},{2,26},{3,27},{4,1},{5,0},{6,30},{7,31},{8,13},{9,12},... | collective-permute-start | bytes 737288 | tf_op jit(solution)/shard_map/ppermute | solution.py:196
  53.8 4.8 %collective-permute-done.6 = f32[480,128]{1,0:T(8,128)S(1)} collective-permute-done((f32[480,128]{1,0:T(8,128)S(1)}, f32[480,128]{1,0:T(8,128)S(1)}, u32[]{:S(2)}, u32[]{:S(2)}) %collective-permute-start.6) | collective-permute-done | bytes 245792 | tf_op jit(solution)/shard_map/ppermute | solution.py:196
  59.4 1.3 %collective-permute-done.7 = f32[480,128]{1,0:T(8,128)S(1)} collective-permute-done((f32[480,128]{1,0:T(8,128)S(1)}, f32[480,128]{1,0:T(8,128)S(1)}, u32[]{:S(2)}, u32[]{:S(2)}) %collective-permute-start.7) | collective-permute-done | bytes 245792 | tf_op jit(solution)/shard_map/ppermute | solution.py:196
  60.7 3.7 %collective-permute-start.11 = (f32[480,128]{1,0:T(8,128)S(1)}, f32[480,128]{1,0:T(8,128)S(1)}, u32[]{:S(2)}, u32[]{:S(2)}) collective-permute-start(f32[480,128]{1,0:T(8,128)S(1)} %add_add_fusion.1), channel_id=1, source_target_pairs={{0,24},{1,25},{2,7},{3,6},{4,28},{5,29},{6,3},{7,2},{8,16},{9,17},... | collective-permute-start | bytes 737288 | tf_op jit(solution)/shard_map/ppermute | solution.py:202
  64.4 0.8 collective-permute-start.9
  65.2 3.8 %collective-permute-done.11 = f32[480,128]{1,0:T(8,128)S(1)} collective-permute-done((f32[480,128]{1,0:T(8,128)S(1)}, f32[480,128]{1,0:T(8,128)S(1)}, u32[]{:S(2)}, u32[]{:S(2)}) %collective-permute-start.11) | collective-permute-done | bytes 245792 | tf_op jit(solution)/shard_map/ppermute | solution.py:202
  69.0 7.0 %collective-permute-done.10 = f32[480,128]{1,0:T(8,128)S(1)} collective-permute-done((f32[480,128]{1,0:T(8,128)S(1)}, f32[480,128]{1,0:T(8,128)S(1)}, u32[]{:S(2)}, u32[]{:S(2)}) %collective-permute-start.10) | collective-permute-done | bytes 245792 | tf_op jit(solution)/shard_map/ppermute | solution.py:202
  76.1 3.3 %collective-permute-start.14 = (f32[480,128]{1,0:T(8,128)S(1)}, f32[480,128]{1,0:T(8,128)S(1)}, u32[]{:S(2)}, u32[]{:S(2)}) collective-permute-start(f32[480,128]{1,0:T(8,128)S(1)} %add_add_fusion), channel_id=1, source_target_pairs={{0,5},{1,4},{2,26},{3,27},{4,1},{5,0},{6,30},{7,31},{8,13},{9,12},... | collective-permute-start | bytes 737288 | tf_op jit(solution)/shard_map/ppermute | solution.py:216
  80.0 3.5 %collective-permute-done.14 = f32[480,128]{1,0:T(8,128)S(1)} collective-permute-done((f32[480,128]{1,0:T(8,128)S(1)}, f32[480,128]{1,0:T(8,128)S(1)}, u32[]{:S(2)}, u32[]{:S(2)}) %collective-permute-start.14) | collective-permute-done | bytes 245792 | tf_op jit(solution)/shard_map/ppermute | solution.py:216
  83.5 3.2 %collective-permute-done.13 = f32[480,128]{1,0:T(8,128)S(1)} collective-permute-done((f32[480,128]{1,0:T(8,128)S(1)}, f32[480,128]{1,0:T(8,128)S(1)}, u32[]{:S(2)}, u32[]{:S(2)}) %collective-permute-start.13) | collective-permute-done | bytes 245792 | tf_op jit(solution)/shard_map/ppermute | solution.py:216
  87.1 1.6 %collective-permute-start.15 = (f32[1920,128]{1,0:T(8,128)S(1)}, f32[1920,128]{1,0:T(8,128)S(1)}, u32[]{:S(2)}, u32[]{:S(2)}) collective-permute-start(f32[1920,128]{1,0:T(8,128)S(1)} %pad_maximum_fusion.2), channel_id=1, source_target_pairs={{0,2},{1,3},{2,0},{3,1},{4,6},{5,7},{6,4},{7,5},{8,10},{9,11},{10,... | collective-permute-start | bytes 2949128 | tf_op jit(solution)/shard_map/ppermute | solution.py:225
  88.8 1.1 %fusion.3 = bf16[1,512,256]{2,1,0:T(8,128)(2,1)} fusion(bf16[768,256]{1,0:T(8,128)(2,1)S(1)} %copy-done.12, f32[518,256]{1,0:T(8,128)S(1)} %copy-done.4, bf16[512,256]{1,0:T(8,128)(2,1)S(1)} %copy-done.8, bf16[512,256]{1,0:T(8,128)(2,1)S(1)} %copy-done.10, bf16[512,256]{1,0:T(8,128)(2,1)S(1)} %copy-done.6, f32[256]{0:T(256)S(1)} %copy-done.19), kind=kOutput, calls=%fused_computation.9 | convolution fusion | flops 204079104 | bytes 1967104 | tf_op jit(solution)/shard_map/dot_general | solution.py:92
  89.9 1.1 %collective-permute-done.15 = f32[1920,128]{1,0:T(8,128)S(1)} collective-permute-done((f32[1920,128]{1,0:T(8,128)S(1)}, f32[1920,128]{1,0:T(8,128)S(1)}, u32[]{:S(2)}, u32[]{:S(2)}) %collective-permute-start.15) | collective-permute-done | bytes 983072 | tf_op jit(solution)/shard_map/ppermute | solution.py:225
  92.5 0.9 slice.166
  93.5 1.1 %slice.164 = f32[2240,128]{1,0:T(8,128)} slice(f32[3840,128]{1,0:T(8,128)S(1)} %broadcast_select_fusion), slice={[0:2240], [0:128]} | slice | bytes 2293760 | tf_op jit(solution)/shard_map/slice | solution.py:229
  (124 shorter events, 16.5 us)
Async XLA Ops:
  0.6 34.4 %copy-start = (bf16[560,512]{1,0:T(8,128)(2,1)S(1)}, bf16[560,512]{1,0:T(8,128)(2,1)}, u32[]{:S(2)}) copy-start(bf16[560,512]{1,0:T(8,128)(2,1)} %param.16) | copy-start | bytes 1720324
  0.6 5.8 %copy-start.20 = (s32[1,8]{1,0:T(1,128)S(1)}, s32[1,8]{1,0:T(1,128)}, u32[]{:S(2)}) copy-start(s32[1,8]{1,0:T(1,128)} %param.13) | copy-start | bytes 100
  0.7 5.8 %copy-start.21 = (s32[1,8]{1,0:T(1,128)S(1)}, s32[1,8]{1,0:T(1,128)}, u32[]{:S(2)}) copy-start(s32[1,8]{1,0:T(1,128)} %param.14) | copy-start | bytes 100
  0.7 7.9 %copy-start.14 = (bf16[1,8,640]{2,1,0:T(8,128)(2,1)S(1)}, bf16[1,8,640]{2,1,0:T(8,128)(2,1)}, u32[]{:S(2)}) copy-start(bf16[1,8,640]{2,1,0:T(8,128)(2,1)} %param.11) | copy-start | bytes 30724
  0.7 7.9 %copy-start.18 = (s32[1,8]{1,0:T(1,128)S(1)}, s32[1,8]{1,0:T(1,128)}, u32[]{:S(2)}) copy-start(s32[1,8]{1,0:T(1,128)} %param.12) | copy-start | bytes 100
  0.7 25.0 %copy-start.2 = (bf16[1,512,256]{2,1,0:T(8,128)(2,1)S(1)}, bf16[1,512,256]{2,1,0:T(8,128)(2,1)}, u32[]{:S(2)}) copy-start(bf16[1,512,256]{2,1,0:T(8,128)(2,1)} %param.15) | copy-start | bytes 786436
  1.7 6.9 %collective-permute-start = (bf16[16,4096]{1,0:T(8,128)(2,1)S(1)}, bf16[16,4096]{1,0:T(8,128)(2,1)S(1)}, u32[]{:S(2)}, u32[]{:S(2)}) collective-permute-start(bf16[16,4096]{1,0:T(8,128)(2,1)S(1)} %slice.105), channel_id=1, source_target_pairs={{0,1},{1,0},{2,3},{3,2},{4,5},{5,4},{6,7},{7,6},{8,9},{9,8},{10,11... | collective-permute-start | bytes 393224 | tf_op jit(solution)/shard_map/ppermute | solution.py:255
  4.7 21.1 %copy-start.11 = (bf16[768,256]{1,0:T(8,128)(2,1)S(1)}, bf16[768,256]{1,0:T(8,128)(2,1)}, u32[]{:S(2)}) copy-start(bf16[768,256]{1,0:T(8,128)(2,1)} %param.20) | copy-start | bytes 1179652
  6.4 23.4 %collective-permute-start.3 = (bf16[240,2048]{1,0:T(8,128)(2,1)S(1)}, bf16[240,2048]{1,0:T(8,128)(2,1)}, u32[]{:S(2)}, u32[]{:S(2)}) collective-permute-start(bf16[240,2048]{1,0:T(8,128)(2,1)S(1)} %slice_select_fusion), channel_id=1, source_target_pairs={{0,1},{1,0},{2,3},{3,2},{4,5},{5,4},{6,7},{7,6},{8,9},{9,8},{10,11... | collective-permute-start | bytes 2949128 | tf_op jit(solution)/shard_map/ppermute | solution.py:249
  10.7 12.3 %all-to-all-start = ((bf16[16,2,321]{2,1,0:T(2,128)(2,1)}), bf16[16,2,321]{2,1,0:T(2,128)(2,1)S(1)}, u32[]{:S(2)}, u32[]{:S(2)}) async-start(bf16[16,2,321]{2,1,0:T(2,128)(2,1)} %reshape.119), calls=%async_computation | async-start | bytes 49152 | tf_op jit(solution)/shard_map/all_to_all | solution.py:299
  24.4 9.1 %collective-permute-start.2 = (bf16[4,80]{1,0:T(4,128)(2,1)}, bf16[4,80]{1,0:T(4,128)(2,1)S(1)}, u32[]{:S(2)}, u32[]{:S(2)}) collective-permute-start(bf16[4,80]{1,0:T(4,128)(2,1)} %get-tuple-element.45), channel_id=1, source_target_pairs={{1,0},{3,2},{5,4},{7,6},{9,8},{11,10},{13,12},{15,14},{17,16},{19,... | collective-permute-start | bytes 1928 | tf_op jit(solution)/shard_map/ppermute | solution.py:19
  26.3 8.8 %copy-start.15 = (f32[512]{0:T(512)S(1)}, f32[512]{0:T(512)}, u32[]{:S(2)}) copy-start(f32[512]{0:T(512)} %param.17) | copy-start | bytes 6148
  29.8 6.2 %collective-permute-start.4 = (bf16[240,2048]{1,0:T(8,128)(2,1)}, bf16[240,2048]{1,0:T(8,128)(2,1)}, u32[]{:S(2)}, u32[]{:S(2)}) collective-permute-start(bf16[240,2048]{1,0:T(8,128)(2,1)} %collective-permute-done.3), channel_id=1, source_target_pairs={{0,2},{2,0},{4,6},{6,4},{8,10},{10,8},{12,14},{14,12},{16,18},{18,... | collective-permute-start | bytes 2949128 | tf_op jit(solution)/shard_map/ppermute | solution.py:250
  30.1 4.8 %collective-permute-start.1 = (bf16[4,80]{1,0:T(4,128)(2,1)}, bf16[4,80]{1,0:T(4,128)(2,1)S(1)}, u32[]{:S(2)}, u32[]{:S(2)}) collective-permute-start(bf16[4,80]{1,0:T(4,128)(2,1)} %get-tuple-element.46), channel_id=1, source_target_pairs={{0,1},{2,3},{4,5},{6,7},{8,9},{10,11},{12,13},{14,15},{16,17},{18,... | collective-permute-start | bytes 1928 | tf_op jit(solution)/shard_map/ppermute | solution.py:16
  36.0 2.0 %copy-start.13 = (bf16[16,2048]{1,0:T(8,128)(2,1)S(1)}, bf16[16,2048]{1,0:T(8,128)(2,1)}, u32[]{:S(2)}) copy-start(bf16[16,2048]{1,0:T(8,128)(2,1)} %get-tuple-element.37) | copy-start | bytes 196612
  45.8 2.8 %collective-permute-start.5 = (f32[1920,128]{1,0:T(8,128)S(1)}, f32[1920,128]{1,0:T(8,128)}, u32[]{:S(2)}, u32[]{:S(2)}) collective-permute-start(f32[1920,128]{1,0:T(8,128)S(1)} %constant_dynamic-slice_fusion.3), channel_id=1, source_target_pairs={{0,2},{1,3},{2,0},{3,1},{4,6},{5,7},{6,4},{7,5},{8,10},{9,11},{10,... | collective-permute-start | bytes 2949128 | tf_op jit(solution)/shard_map/ppermute | solution.py:188
  49.9 8.7 %collective-permute-start.6 = (f32[480,128]{1,0:T(8,128)S(1)}, f32[480,128]{1,0:T(8,128)S(1)}, u32[]{:S(2)}, u32[]{:S(2)}) collective-permute-start(f32[480,128]{1,0:T(8,128)S(1)} %get-tuple-element.28), channel_id=1, source_target_pairs={{0,1},{1,0},{2,10},{3,11},{4,5},{5,4},{6,14},{7,15},{8,9},{9,8},{1... | collective-permute-start | bytes 737288 | tf_op jit(solution)/shard_map/ppermute | solution.py:196
  52.3 7.1 %collective-permute-start.8 = (f32[480,128]{1,0:T(8,128)S(1)}, f32[480,128]{1,0:T(8,128)S(1)}, u32[]{:S(2)}, u32[]{:S(2)}) collective-permute-start(f32[480,128]{1,0:T(8,128)S(1)} %get-tuple-element.29), channel_id=1, source_target_pairs={{0,5},{1,4},{2,26},{3,27},{4,1},{5,0},{6,30},{7,31},{8,13},{9,12},... | collective-permute-start | bytes 737288 | tf_op jit(solution)/shard_map/ppermute | solution.py:196
  53.3 7.4 %collective-permute-start.7 = (f32[480,128]{1,0:T(8,128)S(1)}, f32[480,128]{1,0:T(8,128)S(1)}, u32[]{:S(2)}, u32[]{:S(2)}) collective-permute-start(f32[480,128]{1,0:T(8,128)S(1)} %get-tuple-element.30), channel_id=1, source_target_pairs={{0,4},{1,5},{2,18},{3,19},{4,0},{5,1},{6,22},{7,23},{8,12},{9,13},... | collective-permute-start | bytes 737288 | tf_op jit(solution)/shard_map/ppermute | solution.py:196
  60.7 8.3 %collective-permute-start.11 = (f32[480,128]{1,0:T(8,128)S(1)}, f32[480,128]{1,0:T(8,128)S(1)}, u32[]{:S(2)}, u32[]{:S(2)}) collective-permute-start(f32[480,128]{1,0:T(8,128)S(1)} %add_add_fusion.1), channel_id=1, source_target_pairs={{0,24},{1,25},{2,7},{3,6},{4,28},{5,29},{6,3},{7,2},{8,16},{9,17},... | collective-permute-start | bytes 737288 | tf_op jit(solution)/shard_map/ppermute | solution.py:202
  64.4 11.6 %collective-permute-start.10 = (f32[480,128]{1,0:T(8,128)S(1)}, f32[480,128]{1,0:T(8,128)S(1)}, u32[]{:S(2)}, u32[]{:S(2)}) collective-permute-start(f32[480,128]{1,0:T(8,128)S(1)} %add_add_fusion.1), channel_id=1, source_target_pairs={{0,16},{1,17},{2,6},{3,7},{4,20},{5,21},{6,2},{7,3},{8,24},{9,25},... | collective-permute-start | bytes 737288 | tf_op jit(solution)/shard_map/ppermute | solution.py:202
  64.4 11.6 %collective-permute-start.9 = (f32[480,128]{1,0:T(8,128)S(1)}, f32[480,128]{1,0:T(8,128)S(1)}, u32[]{:S(2)}, u32[]{:S(2)}) collective-permute-start(f32[480,128]{1,0:T(8,128)S(1)} %add_add_fusion.1), channel_id=1, source_target_pairs={{0,8},{1,9},{2,3},{3,2},{4,12},{5,13},{6,7},{7,6},{8,0},{9,1},{10,... | collective-permute-start | bytes 737288 | tf_op jit(solution)/shard_map/ppermute | solution.py:202
  76.1 7.4 %collective-permute-start.14 = (f32[480,128]{1,0:T(8,128)S(1)}, f32[480,128]{1,0:T(8,128)S(1)}, u32[]{:S(2)}, u32[]{:S(2)}) collective-permute-start(f32[480,128]{1,0:T(8,128)S(1)} %add_add_fusion), channel_id=1, source_target_pairs={{0,5},{1,4},{2,26},{3,27},{4,1},{5,0},{6,30},{7,31},{8,13},{9,12},... | collective-permute-start | bytes 737288 | tf_op jit(solution)/shard_map/ppermute | solution.py:216
  79.3 7.4 %collective-permute-start.13 = (f32[480,128]{1,0:T(8,128)S(1)}, f32[480,128]{1,0:T(8,128)S(1)}, u32[]{:S(2)}, u32[]{:S(2)}) collective-permute-start(f32[480,128]{1,0:T(8,128)S(1)} %add_add_fusion), channel_id=1, source_target_pairs={{0,4},{1,5},{2,18},{3,19},{4,0},{5,1},{6,22},{7,23},{8,12},{9,13},... | collective-permute-start | bytes 737288 | tf_op jit(solution)/shard_map/ppermute | solution.py:216
  79.9 6.8 %collective-permute-start.12 = (f32[480,128]{1,0:T(8,128)S(1)}, f32[480,128]{1,0:T(8,128)S(1)}, u32[]{:S(2)}, u32[]{:S(2)}) collective-permute-start(f32[480,128]{1,0:T(8,128)S(1)} %add_add_fusion), channel_id=1, source_target_pairs={{0,1},{1,0},{2,10},{3,11},{4,5},{5,4},{6,14},{7,15},{8,9},{9,8},{1... | collective-permute-start | bytes 737288 | tf_op jit(solution)/shard_map/ppermute | solution.py:216
  86.9 1.8 %copy-start.4 = (f32[518,256]{1,0:T(8,128)S(1)}, f32[518,256]{1,0:T(8,128)}, u32[]{:S(2)}) copy-start(f32[518,256]{1,0:T(8,128)} %copy-done.3) | copy-start | bytes 1591300
  86.9 1.8 %copy-start.6 = (bf16[512,256]{1,0:T(8,128)(2,1)S(1)}, bf16[512,256]{1,0:T(8,128)(2,1)}, u32[]{:S(2)}) copy-start(bf16[512,256]{1,0:T(8,128)(2,1)} %copy-done.5) | copy-start | bytes 786436
  86.9 1.8 %copy-start.8 = (bf16[512,256]{1,0:T(8,128)(2,1)S(1)}, bf16[512,256]{1,0:T(8,128)(2,1)}, u32[]{:S(2)}) copy-start(bf16[512,256]{1,0:T(8,128)(2,1)} %copy-done.7) | copy-start | bytes 786436
  86.9 1.8 %copy-start.10 = (bf16[512,256]{1,0:T(8,128)(2,1)S(1)}, bf16[512,256]{1,0:T(8,128)(2,1)}, u32[]{:S(2)}) copy-start(bf16[512,256]{1,0:T(8,128)(2,1)} %copy-done.9) | copy-start | bytes 786436
  86.9 1.8 %copy-start.12 = (bf16[768,256]{1,0:T(8,128)(2,1)S(1)}, bf16[768,256]{1,0:T(8,128)(2,1)}, u32[]{:S(2)}) copy-start(bf16[768,256]{1,0:T(8,128)(2,1)} %param.20) | copy-start | bytes 1179652
  87.0 1.8 %copy-start.19 = (f32[256]{0:T(256)S(1)}, f32[256]{0:T(256)}, u32[]{:S(2)}) copy-start(f32[256]{0:T(256)} %param.21) | copy-start | bytes 3076
  87.1 3.8 %collective-permute-start.15 = (f32[1920,128]{1,0:T(8,128)S(1)}, f32[1920,128]{1,0:T(8,128)S(1)}, u32[]{:S(2)}, u32[]{:S(2)}) collective-permute-start(f32[1920,128]{1,0:T(8,128)S(1)} %pad_maximum_fusion.2), channel_id=1, source_target_pairs={{0,2},{1,3},{2,0},{3,1},{4,6},{5,7},{6,4},{7,5},{8,10},{9,11},{10,... | collective-permute-start | bytes 2949128 | tf_op jit(solution)/shard_map/ppermute | solution.py:225
  (7 other events, 7.4 us)
